TPU v7x, 32 devices: a whole 2x2x4 slice. The times are simulated.
32 devices in a mesh: depth: 4 (over y, core), tile: 2 (over x), angle: 4 (over z).
Axes of the slice: x: 2, y: 2, z: 4, core: 2. Of those that a mesh axis runs over, the one named last changes fastest.
Arguments:
- probe: bfloat16 [2, 512, 256], P(None, 'tile'), may hold values from -5 to 5
- phase: float32 [4, 1, 512, 256], P('depth', None, 'tile'), may hold values from -1.5 to 1.5
- forward_in: float32 [4, 4, 2, 512, 256], P('depth', 'angle', None, 'tile'), may hold values from -5 to 5
- adjoint_in: float32 [4, 4, 2, 512, 256], P('depth', 'angle', None, 'tile'), may hold values from -5 to 5
- held_waves: bfloat16 [4, 2, 4, 2, 512, 256], P('depth', None, 'angle', None, 'tile'), may hold values from -5 to 5
- measured: float32 [4, 512, 256], P('angle', 'tile'), may hold values from 0.1 to 2
- tilt_index: int32 [4], P('angle'), may hold values from 0 to 60
- positions: int32 [4, 2], P('angle'), may hold values from -8 to 8
Outputs:
- forward_out: float32 [4, 4, 2, 512, 256], P('depth', 'angle', None, 'tile')
- adjoint_out: float32 [4, 4, 2, 512, 256], P('depth', 'angle', None, 'tile')
- gradient: float32 [4, 1, 2, 512, 256], P('depth', None, None, 'tile')
All inputs are finite; a program needn't handle non-finite values.
Results may differ from a plain program's by a relative error of at most 0.0012.
Values sent between devices are 32-bit elements; how exact they have to be, the bound alone decides.
No kernel may reach another device: no remote copies, remote signals or barrier semaphores. Data moves between devices by JAX's collectives and lax.ppermute only.
A program may use at most 64 MiB of HBM per device.

v0:
```python
import math

import jax
import jax.numpy as jnp
from jax import lax
from jax.experimental import pallas as pl
from jax.experimental.pallas import tpu as pltpu
from jax.sharding import PartitionSpec as P

MARGIN = 32
TILTS = 61


fresnel = 24.0
slice_step = 6.0
tilt_step = math.pi / 90.0
highest = lax.Precision.HIGHEST
wave_precision = lax.Precision.HIGH


def padded_2(block, sides, width, periodic):
    for axis, dim in sides:
        count = lax.axis_size(axis)
        forward = [(i, i + 1) for i in range(count - 1)]
        if periodic:
            forward.append((count - 1, 0))
        backward = [(target, source) for source, target in forward]
        low = lax.ppermute(
            lax.slice_in_dim(block, block.shape[dim] - width, None, axis=dim), axis, forward
        )
        high = lax.ppermute(lax.slice_in_dim(block, 0, width, axis=dim), axis, backward)
        block = jnp.concatenate([low, block, high], axis=dim)
    return block


def contract(form, left, right):
    return jnp.einsum(form, left, right, precision=wave_precision)


def signed_freqs(length):
    ordinal = lax.iota(jnp.int32, length)
    signed = jnp.where(ordinal >= length // 2, ordinal - length, ordinal)
    return signed.astype(jnp.float32) / length


def kernel_lines(lines, length):
    ids = lax.iota(jnp.int32, length)
    angle = 2.0 * math.pi / length * (ids[:, None] * ids[None, :] % length).astype(jnp.float32)
    cos_grid = jnp.cos(angle)
    sin_grid = jnp.sin(angle)
    cos_line = jnp.cos(lines)
    sin_line = jnp.sin(lines)
    dot = lambda x, y: jnp.einsum("...f,nf->...n", x, y, precision=highest)
    real = (dot(cos_line, cos_grid) - dot(sin_line, sin_grid)) / length
    imag = (dot(sin_line, cos_grid) + dot(cos_line, sin_grid)) / length
    return real, imag


def toeplitz_kernel(q_ref, o_ref):
    count = q_ref.shape[0]
    rows, length = o_ref.shape[1], o_ref.shape[2]
    for t in range(count):
        line = jnp.broadcast_to(q_ref[t : t + 1, :], (rows, q_ref.shape[1]))
        rolled = pltpu.roll(line, MARGIN, 1, stride=1, stride_axis=0)
        o_ref[t] = rolled[:, :length]


def toeplitz(h, rows):
    count, length = h.shape
    flipped = jnp.roll(h[:, ::-1], 1, axis=-1)
    width = ((2 * length + 127) // 128) * 128
    reps = -(-width // length)
    doubled = jnp.concatenate([flipped] * reps, axis=-1)[:, :width]
    return pl.pallas_call(
        toeplitz_kernel,
        out_shape=jax.ShapeDtypeStruct((count, rows, length), jnp.float32),
    )(doubled)


def fold_rows(table, core_size):
    inner = table[..., MARGIN : MARGIN + core_size]
    top = table[..., :MARGIN]
    bottom = table[..., MARGIN + core_size :]
    zeros = jnp.zeros(inner.shape[:-1] + (core_size - MARGIN,), inner.dtype)
    return (
        inner
        + jnp.concatenate([zeros, top], axis=-1)
        + jnp.concatenate([bottom, zeros], axis=-1)
    )


def apply_operator(wave, padded_cols, row_table, col_table):
    wave_real = wave[:, 0]
    wave_imag = wave[:, 1]
    row_real = row_table[:, 0]
    row_imag = row_table[:, 1]
    first = contract("ajl,alk->ajk", row_real + row_imag, wave_real)
    second = contract("ajl,alk->ajk", row_real, wave_imag - wave_real)
    third = contract("ajl,alk->ajk", row_imag, wave_real + wave_imag)
    half = jnp.stack([first - third, first + second], axis=1)
    half = padded_cols(half)
    half_real = half[:, 0]
    half_imag = half[:, 1]
    col_real = col_table[:, 0]
    col_imag = col_table[:, 1]
    first = contract("ajk,aik->aji", half_real + half_imag, col_real)
    second = contract("ajk,aik->aji", half_real, col_imag - col_real)
    third = contract("ajk,aik->aji", half_imag, col_real + col_imag)
    return jnp.stack([first - third, first + second], axis=1)


def body(probe, phase, forward_in, adjoint_in, held_waves, measured, tilt_index, positions):
    core_size = phase.shape[-1]
    length = core_size + 2 * MARGIN
    angle_count = forward_in.shape[1]
    section = lax.axis_index("depth")
    sections = lax.axis_size("depth")
    is_first = section == 0
    frequency = signed_freqs(length)
    base_phase = -math.pi * fresnel * frequency * frequency

    tilt_angle = (tilt_index.astype(jnp.float32) - (TILTS - 1) / 2.0) * tilt_step
    lateral_drift = slice_step * jnp.tan(tilt_angle)
    shift_rows = jnp.where(is_first, positions[:, 0].astype(jnp.float32), 0.0)
    shift_cols = lateral_drift + jnp.where(is_first, positions[:, 1].astype(jnp.float32), 0.0)
    row_line = base_phase[None, :] - 2.0 * math.pi * frequency[None, :] * shift_rows[:, None]
    col_line = base_phase[None, :] - 2.0 * math.pi * frequency[None, :] * shift_cols[:, None]
    lines = jnp.stack([row_line, -row_line, col_line, -col_line], axis=1)
    h_real, h_imag = kernel_lines(lines, length)
    h_all = jnp.stack([h_real, h_imag], axis=2).reshape(angle_count * 8, length)
    tables = toeplitz(h_all, core_size).reshape(angle_count, 4, 2, core_size, length)
    rows_fwd = fold_rows(tables[:, 0], core_size)
    rows_back = fold_rows(tables[:, 1], core_size)
    cols_fwd = tables[:, 2]
    cols_back = tables[:, 3]

    cosine = jnp.cos(phase[0, 0])
    sine_part = jnp.sin(phase[0, 0])
    outgoing = jnp.concatenate([adjoint_in, forward_in], axis=0)
    received = padded_2(outgoing, (("depth", 0),), 1, False)
    probe_wave = probe.astype(jnp.float32)[None]
    wavefield = jnp.where(is_first, probe_wave, received[0])
    exit_wave = held_waves[0, 1].astype(jnp.float32)
    intensity = exit_wave[:, 0] * exit_wave[:, 0] + exit_wave[:, 1] * exit_wave[:, 1]
    residual = (intensity - measured)[:, None] * exit_wave
    returning = jnp.where(section == sections - 1, residual, received[3])
    transmitted = jnp.stack(
        [
            cosine * wavefield[:, 0] - sine_part * wavefield[:, 1],
            cosine * wavefield[:, 1] + sine_part * wavefield[:, 0],
        ],
        axis=1,
    )

    def side_halo(field):
        return padded_2(field, (("tile", 3),), MARGIN, True)

    spread = apply_operator(returning, side_halo, rows_back, cols_back)
    held_field = held_waves[0, 0].astype(jnp.float32)
    grad_real = spread[:, 0] * held_field[:, 0] + spread[:, 1] * held_field[:, 1]
    grad_imag = spread[:, 1] * held_field[:, 0] - spread[:, 0] * held_field[:, 1]
    gradient_term = jnp.stack([jnp.sum(grad_real, axis=0), jnp.sum(grad_imag, axis=0)])
    summed = lax.psum(gradient_term, "angle")
    returning = jnp.stack(
        [
            cosine * spread[:, 0] + sine_part * spread[:, 1],
            cosine * spread[:, 1] - sine_part * spread[:, 0],
        ],
        axis=1,
    )
    wavefield = apply_operator(transmitted, side_halo, rows_fwd, cols_fwd)
    return (wavefield[None], returning[None], summed[None, None])


def solution(mesh):
    in_specs = (
        P(None, "tile", None),
        P("depth", None, "tile", None),
        P("depth", "angle", None, "tile", None),
        P("depth", "angle", None, "tile", None),
        P("depth", None, "angle", None, "tile", None),
        P("angle", "tile", None),
        P("angle"),
        P("angle", None),
    )
    out_specs = (
        P("depth", "angle", None, "tile", None),
        P("depth", "angle", None, "tile", None),
        P("depth", None, None, "tile", None),
    )
    return jax.shard_map(body, mesh=mesh, in_specs=in_specs, out_specs=out_specs, check_vma=False)
```

profile of v0, /device:TPU:0, one launch (start us, length us, event | category | flops | bytes accessed | tf_op | source)
XLA Modules:
  0.0 103.9 jit_solution(17699328579946394483)
XLA Ops:
  7.2 1.3 %collective-permute-start.3 = (f32[1,1,2,256,256]{4,3,2,1,0:T(8,128)}, f32[1,1,2,256,256]{4,3,2,1,0:T(8,128)}, u32[]{:S(2)}, u32[]{:S(2)}) collective-permute-start(f32[1,1,2,256,256]{4,3,2,1,0:T(8,128)} %param.11), channel_id=1, source_target_pairs={{8,0},{16,8},{24,16},{9,1},{17,9},{25,17},{10,2},{18,10},{26,18},{... | collective-permute-start | bytes 1572872 | tf_op jit(solution)/shard_map/ppermute | solution.py:31
  8.5 3.8 %collective-permute-start = (f32[1,1,2,256,256]{4,3,2,1,0:T(8,128)}, f32[1,1,2,256,256]{4,3,2,1,0:T(8,128)}, u32[]{:S(2)}, u32[]{:S(2)}) collective-permute-start(f32[1,1,2,256,256]{4,3,2,1,0:T(8,128)} %param.10), channel_id=1, source_target_pairs={{0,8},{8,16},{16,24},{1,9},{9,17},{17,25},{2,10},{10,18},{18,26},{... | collective-permute-start | bytes 1572872 | tf_op jit(solution)/shard_map/ppermute | solution.py:28
  12.3 1.3 %fusion.145 = (s32[1,1]{1,0:T(1,128)}, s32[1,1]{1,0:T(1,128)}) fusion(s32[1,2]{1,0:T(1,128)} %param.15), kind=kLoop, calls=%fused_computation.183 | loop fusion | bytes 16 | tf_op jit(solution)/shard_map/slice | solution.py:124
  15.7 2.4 %fusion.21 = f32[4,320]{1,0:T(4,128)S(1)} fusion(f32[1,320]{1,0:T(1,128)S(1)} %get-tuple-element.30, f32[1,320]{1,0:T(1,128)S(1)} %get-tuple-element.29, f32[1,320]{1,0:T(1,128)S(1)} %get-tuple-element.32, f32[1,320]{1,0:T(1,128)S(1)} %get-tuple-element.31), kind=kOutput, calls=%fused_computation.45 | convolution fusion | flops 5840640 | bytes 10240 | tf_op jit(solution)/shard_map/...f,nf->...n/dot_general | solution.py:53
  18.1 2.4 %fusion.19 = f32[4,320]{1,0:T(4,128)S(1)} fusion(f32[1,320]{1,0:T(1,128)S(1)} %get-tuple-element.30, f32[1,320]{1,0:T(1,128)S(1)} %get-tuple-element.29, f32[1,320]{1,0:T(1,128)S(1)} %get-tuple-element.32, f32[1,320]{1,0:T(1,128)S(1)} %get-tuple-element.31), kind=kOutput, calls=%fused_computation.44 | convolution fusion | flops 5840640 | bytes 10240 | tf_op jit(solution)/shard_map/...f,nf->...n/dot_general | solution.py:53
  20.6 2.4 %fusion.7 = f32[1,4,1,320]{3,1,2,0:T(4,128)S(1)} fusion(f32[4,320]{1,0:T(4,128)S(1)} %fusion.21, f32[1,320]{1,0:T(1,128)S(1)} %get-tuple-element.30, f32[1,320]{1,0:T(1,128)S(1)} %get-tuple-element.29, f32[1,320]{1,0:T(1,128)S(1)} %get-tuple-element.32, f32[1,320]{1,0:T(1,128)S(1)} %get-tuple-element.31), kind=kOutput, calls=%fused_computation.17 | convolution fusion | flops 5843200 | bytes 15360 | tf_op jit(solution)/shard_map/...f,nf->...n/dot_general | solution.py:53
  23.0 2.4 %fusion.9 = f32[1,4,1,320]{3,1,2,0:T(4,128)S(1)} fusion(f32[4,320]{1,0:T(4,128)S(1)} %fusion.19, f32[1,320]{1,0:T(1,128)S(1)} %get-tuple-element.30, f32[1,320]{1,0:T(1,128)S(1)} %get-tuple-element.29, f32[1,320]{1,0:T(1,128)S(1)} %get-tuple-element.32, f32[1,320]{1,0:T(1,128)S(1)} %get-tuple-element.31), kind=kOutput, calls=%fused_computation.19 | convolution fusion | flops 5843200 | bytes 15360 | tf_op jit(solution)/shard_map/...f,nf->...n/dot_general | solution.py:53
  26.0 0.7 pad_maximum_fusion.6.q_ref
  26.7 3.1 %shard_map.103 = f32[8,256,320]{2,1,0:T(8,128)} custom-call(f32[8,640]{1,0:T(8,128)} %pad_maximum_fusion.6.q_ref), custom_call_target="tpu_custom_call" | custom-call | tf_op jit(solution)/shard_map/pallas_call | solution.py:74
  29.8 2.1 %slice_bitcast_fusion.1 = (f32[1,2,256,320]{3,2,1,0:T(8,128)S(1)}, f32[1,2,256,320]{3,2,1,0:T(8,128)S(1)}, f32[1,2,256,320]{3,2,1,0:T(8,128)S(1)}, f32[1,2,256,320]{3,2,1,0:T(8,128)S(1)}) fusion(f32[1,4,2,256,320]{4,3,2,1,0:T(8,128)} %bitcast.175), kind=kLoop, calls=%fused_computation.21 | loop fusion | bytes 5242880 | tf_op jit(solution)/shard_map/squeeze | solution.py:133
  31.9 0.9 fusion.142
  32.8 0.9 bitcast_convert_fusion
  33.7 1.6 %fusion.144 = (f32[1,1,256,256]{3,2,1,0:T(8,128)S(1)}, f32[1,1,256,256]{3,2,1,0:T(8,128)}) fusion(f32[1,1,256,256]{3,2,1,0:T(8,128)S(1)} %copy-done.6), kind=kLoop, calls=%fused_computation.182 | loop fusion | bytes 786432 | tf_op jit(solution)/shard_map/cos | solution.py:137
  35.3 0.9 fusion.143
  36.1 0.8 fusion.67
  36.9 1.4 %fusion.10 = f32[1,2,256,256]{3,2,1,0:T(8,128)S(1)} fusion(f32[1,2,256,320]{3,2,1,0:T(8,128)S(1)} %get-tuple-element.3, f32[1,2,256,32]{3,2,1,0:T(8,128)} %get-tuple-element.14, f32[1,2,256,32]{3,2,1,0:T(8,128)} %get-tuple-element.13), kind=kLoop, calls=%fused_computation.28 | loop fusion | flops 262144 | bytes 1179648 | tf_op jit(solution)/shard_map/add | solution.py:86
  38.3 1.3 %fusion.11 = f32[1,2,256,256]{3,2,1,0:T(8,128)S(1)} fusion(f32[1,2,256,320]{3,2,1,0:T(8,128)S(1)} %get-tuple-element.6, f32[1,2,256,32]{3,2,1,0:T(8,128)} %get-tuple-element.16, f32[1,2,256,32]{3,2,1,0:T(8,128)} %get-tuple-element.15), kind=kLoop, calls=%fused_computation.30 | loop fusion | flops 262144 | bytes 1179648 | tf_op jit(solution)/shard_map/add | solution.py:86
  39.7 1.2 %bitcast_select_fusion = f32[1,2,256,256]{3,2,1,0:T(8,128)S(1)} fusion(f32[1,1,2,256,256]{4,3,2,1,0:T(8,128)} %collective-permute-done.3, f32[256,256]{1,0:T(8,128)S(1)} %copy-done.5, pred[]{:T(512)S(6)} %eq.9, bf16[1,2,1,2,256,256]{5,4,3,2,1,0:T(8,128)(2,1)S(1)} %copy-done.3), kind=kLoop, calls=%fused_computation.34 | loop fusion | flops 393216 | bytes 1572865 | tf_op jit(solution)/shard_map/jit(_where)/select_n | solution.py:146
  42.0 1.1 %fusion.12 = f32[1,2,256,256]{3,2,1,0:T(8,128)S(1)} fusion(f32[1,1,2,256,256]{4,3,2,1,0:T(8,128)} %collective-permute-done, bf16[2,256,256]{2,1,0:T(8,128)(2,1)S(1)} %copy-done.7, pred[]{:T(512)} %eq.8), kind=kLoop, calls=%fused_computation.36 | loop fusion | flops 262144 | bytes 1310721 | tf_op jit(solution)/shard_map/jit(_where)/select_n | solution.py:142
  44.5 3.0 %collective-permute-start.4 = (f32[1,2,256,32]{2,3,1,0:T(8,128)S(1)}, f32[1,2,256,32]{2,3,1,0:T(8,128)S(1)}, u32[]{:S(2)}, u32[]{:S(2)}) collective-permute-start(f32[1,2,256,32]{2,3,1,0:T(8,128)S(1)} %get-tuple-element.21), channel_id=1, source_target_pairs={{0,4},{4,0},{1,5},{5,1},{2,6},{6,2},{3,7},{7,3},{8,12},{12,8},{9,1... | collective-permute-start | bytes 196616 | tf_op jit(solution)/shard_map/ppermute | solution.py:28
  47.5 2.0 %collective-permute-start.1 = (f32[1,2,256,32]{2,3,1,0:T(8,128)S(1)}, f32[1,2,256,32]{2,3,1,0:T(8,128)S(1)}, u32[]{:S(2)}, u32[]{:S(2)}) collective-permute-start(f32[1,2,256,32]{2,3,1,0:T(8,128)S(1)} %get-tuple-element.23), channel_id=1, source_target_pairs={{0,4},{4,0},{1,5},{5,1},{2,6},{6,2},{3,7},{7,3},{8,12},{12,8},{9,1... | collective-permute-start | bytes 196616 | tf_op jit(solution)/shard_map/ppermute | solution.py:28
  49.6 0.8 collective-permute-done.4
  50.4 2.1 %collective-permute-done.5 = f32[1,2,256,32]{2,3,1,0:T(8,128)S(1)} collective-permute-done((f32[1,2,256,32]{2,3,1,0:T(8,128)S(1)}, f32[1,2,256,32]{2,3,1,0:T(8,128)S(1)}, u32[]{:S(2)}, u32[]{:S(2)}) %collective-permute-start.5) | collective-permute-done | bytes 65568 | tf_op jit(solution)/shard_map/ppermute | solution.py:31
  52.5 0.5 fusion.28
  53.1 0.5 convolution_subtract_fusion
  53.6 1.3 %add_bitcast_fusion = (f32[1,256,256]{2,1,0:T(8,128)S(1)}, f32[1,256,256]{2,1,0:T(8,128)S(1)}, f32[1,1,256,256]{3,2,1,0:T(8,128)S(1)}, f32[1,1,256,256]{3,2,1,0:T(8,128)}) fusion(f32[256,256]{1,0:T(8,128)S(1)} %convolution_subtract_fusion, f32[1,2,256,256]{3,2,1,0:T(8,128)S(1)} %copy-done.1, f32[1,1,256,256]{3,2,1,0:T(8,128)S(1)} %copy-done, ...), kind=kOutput, calls=%fused_computation.118 | convolution fusion | flops 126763008 | bytes 3735552 | tf_op jit(solution)/shard_map/ajk,aik->aji/dot_general | solution.py:37
  54.9 0.8 maximum_bitcast_fusion.2
  55.8 0.5 fusion.32
  56.4 0.8 maximum_bitcast_fusion.1
  58.2 0.8 maximum_bitcast_fusion
  59.1 36.2 %all-reduce.6.cloned.1.call-done = f32[1,1,2,256,256]{4,3,2,1,0:T(8,128)} async-done(((f32[1,1,2,256,256]{4,3,2,1,0:T(8,128)}), f32[1,1,2,256,256]{4,3,2,1,0:T(8,128)}) %all-reduce.6.cloned.1.call-update) | async-done | bytes 524304 | tf_op jit(solution)/shard_map/psum | solution.py:163
  95.2 1.9 %copy.14 = f32[1,1,2,256,256]{4,3,2,1,0:T(8,128)} copy(f32[1,1,2,256,256]{4,3,2,1,0:T(8,128)} %all-reduce.6.cloned.1.call-done) | data formatting | bytes 1048576
  (48 shorter events, 4.4 us)
Async XLA Ops:
  7.2 88.1 %all-reduce.6.cloned.1.call-start = ((), (), s32[]{:S(2)}) async-start(), calls=%async_computation | async-start | bytes 1048576 | tf_op jit(solution)/shard_map/psum | solution.py:163
  7.2 32.4 %collective-permute-start.3 = (f32[1,1,2,256,256]{4,3,2,1,0:T(8,128)}, f32[1,1,2,256,256]{4,3,2,1,0:T(8,128)}, u32[]{:S(2)}, u32[]{:S(2)}) collective-permute-start(f32[1,1,2,256,256]{4,3,2,1,0:T(8,128)} %param.11), channel_id=1, source_target_pairs={{8,0},{16,8},{24,16},{9,1},{17,9},{25,17},{10,2},{18,10},{26,18},{... | collective-permute-start | bytes 1572872 | tf_op jit(solution)/shard_map/ppermute | solution.py:31
  8.5 33.5 %collective-permute-start = (f32[1,1,2,256,256]{4,3,2,1,0:T(8,128)}, f32[1,1,2,256,256]{4,3,2,1,0:T(8,128)}, u32[]{:S(2)}, u32[]{:S(2)}) collective-permute-start(f32[1,1,2,256,256]{4,3,2,1,0:T(8,128)} %param.10), channel_id=1, source_target_pairs={{0,8},{8,16},{16,24},{1,9},{9,17},{17,25},{2,10},{10,18},{18,26},{... | collective-permute-start | bytes 1572872 | tf_op jit(solution)/shard_map/ppermute | solution.py:28
  29.8 3.0 %copy-start.2 = (bf16[1,2,1,2,256,256]{5,4,3,2,1,0:T(8,128)(2,1)S(1)}, bf16[1,2,1,2,256,256]{5,4,3,2,1,0:T(8,128)(2,1)}, u32[]{:S(2)}) copy-start(bf16[1,2,1,2,256,256]{5,4,3,2,1,0:T(8,128)(2,1)} %param.12) | copy-start | bytes 1572868
  29.8 3.9 %copy-start.6 = (f32[1,1,256,256]{3,2,1,0:T(8,128)S(1)}, f32[1,1,256,256]{3,2,1,0:T(8,128)}, u32[]{:S(2)}) copy-start(f32[1,1,256,256]{3,2,1,0:T(8,128)} %param.9) | copy-start | bytes 786436
  31.9 4.2 %copy-start.8 = (f32[1,256,256]{2,1,0:T(8,128)S(1)}, f32[1,256,256]{2,1,0:T(8,128)}, u32[]{:S(2)}) copy-start(f32[1,256,256]{2,1,0:T(8,128)} %param.13) | copy-start | bytes 786436
  36.9 2.8 %copy-start.3 = (bf16[1,2,1,2,256,256]{5,4,3,2,1,0:T(8,128)(2,1)S(1)}, bf16[1,2,1,2,256,256]{5,4,3,2,1,0:T(8,128)(2,1)}, u32[]{:S(2)}) copy-start(bf16[1,2,1,2,256,256]{5,4,3,2,1,0:T(8,128)(2,1)} %param.12) | copy-start | bytes 1572868
  36.9 2.8 %copy-start.5 = (f32[256,256]{1,0:T(8,128)S(1)}, f32[256,256]{1,0:T(8,128)}, u32[]{:S(2)}) copy-start(f32[256,256]{1,0:T(8,128)} %fusion.67) | copy-start | bytes 786436
  38.3 3.8 %copy-start.7 = (bf16[2,256,256]{2,1,0:T(8,128)(2,1)S(1)}, bf16[2,256,256]{2,1,0:T(8,128)(2,1)}, u32[]{:S(2)}) copy-start(bf16[2,256,256]{2,1,0:T(8,128)(2,1)} %param.8) | copy-start | bytes 786436
  39.6 3.5 %copy-start = (f32[1,1,256,256]{3,2,1,0:T(8,128)S(1)}, f32[1,1,256,256]{3,2,1,0:T(8,128)}, u32[]{:S(2)}) copy-start(f32[1,1,256,256]{3,2,1,0:T(8,128)} %get-tuple-element.26) | copy-start | bytes 786436
  44.0 9.6 %copy-start.1 = (f32[1,2,256,256]{3,2,1,0:T(8,128)S(1)}, f32[1,2,256,256]{3,2,1,0:T(8,128)}, u32[]{:S(2)}) copy-start(f32[1,2,256,256]{3,2,1,0:T(8,128)} %get-tuple-element.19) | copy-start | bytes 1572868
  44.5 5.9 %collective-permute-start.4 = (f32[1,2,256,32]{2,3,1,0:T(8,128)S(1)}, f32[1,2,256,32]{2,3,1,0:T(8,128)S(1)}, u32[]{:S(2)}, u32[]{:S(2)}) collective-permute-start(f32[1,2,256,32]{2,3,1,0:T(8,128)S(1)} %get-tuple-element.21), channel_id=1, source_target_pairs={{0,4},{4,0},{1,5},{5,1},{2,6},{6,2},{3,7},{7,3},{8,12},{12,8},{9,1... | collective-permute-start | bytes 196616 | tf_op jit(solution)/shard_map/ppermute | solution.py:28
  47.5 5.0 %collective-permute-start.5 = (f32[1,2,256,32]{2,3,1,0:T(8,128)S(1)}, f32[1,2,256,32]{2,3,1,0:T(8,128)S(1)}, u32[]{:S(2)}, u32[]{:S(2)}) collective-permute-start(f32[1,2,256,32]{2,3,1,0:T(8,128)S(1)} %get-tuple-element.22), channel_id=1, source_target_pairs={{4,0},{0,4},{5,1},{1,5},{6,2},{2,6},{7,3},{3,7},{12,8},{8,12},{13,... | collective-permute-start | bytes 196616 | tf_op jit(solution)/shard_map/ppermute | solution.py:31
  47.5 8.2 %collective-permute-start.1 = (f32[1,2,256,32]{2,3,1,0:T(8,128)S(1)}, f32[1,2,256,32]{2,3,1,0:T(8,128)S(1)}, u32[]{:S(2)}, u32[]{:S(2)}) collective-permute-start(f32[1,2,256,32]{2,3,1,0:T(8,128)S(1)} %get-tuple-element.23), channel_id=1, source_target_pairs={{0,4},{4,0},{1,5},{5,1},{2,6},{6,2},{3,7},{7,3},{8,12},{12,8},{9,1... | collective-permute-start | bytes 196616 | tf_op jit(solution)/shard_map/ppermute | solution.py:28
  49.6 6.2 %collective-permute-start.2 = (f32[1,2,256,32]{2,3,1,0:T(8,128)S(1)}, f32[1,2,256,32]{2,3,1,0:T(8,128)S(1)}, u32[]{:S(2)}, u32[]{:S(2)}) collective-permute-start(f32[1,2,256,32]{2,3,1,0:T(8,128)S(1)} %get-tuple-element.24), channel_id=1, source_target_pairs={{4,0},{0,4},{5,1},{1,5},{6,2},{2,6},{7,3},{3,7},{12,8},{8,12},{13,... | collective-permute-start | bytes 196616 | tf_op jit(solution)/shard_map/ppermute | solution.py:31
  54.9 1.5 %copy-start.4 = (f32[1,1,256,256]{3,2,1,0:T(8,128)S(1)}, f32[1,1,256,256]{3,2,1,0:T(8,128)}, u32[]{:S(2)}) copy-start(f32[1,1,256,256]{3,2,1,0:T(8,128)} %get-tuple-element.18) | copy-start | bytes 786436
Sparse Core Ops, SparseCore 0:
  55.9 39.3 all-reduce.5
where the time goes:
time: 104 us
  waiting for transfers between devices  39 us (38%)
  between operations  16.4 us (16%)
  matrix products  15.9 us (15%)
  starting transfers between devices  10.3 us (10%)
  other arithmetic  9.96 us (10%)
  local copies, waits for them, and re-layouts  9.21 us (9%)
  Pallas kernels  3.1 us (3%)
    psum x1, waiting for transfers between devices, body(): summed = lax.psum(gradient_term, 'angle')  36.2 us
    dot_general x4, matrix products, kernel_lines(): dot = lambda x, y: jnp.einsum('...f,nf->...n', x, y, precision=highest)  9.66 us
    ppermute x3, starting transfers between devices, padded_2(): lax.ppermute(lax.slice_in_dim(block, block.shape[dim] - width, None, axis...  8.85 us
    dot_general x12, matrix products, contract(): return jnp.einsum(form, left, right, precision=wave_precision)  6.24 us
    pallas_call x1, Pallas kernels, toeplitz(): pl.pallas_call(toeplitz_kernel, out_shape=jax.ShapeDtypeStruct((count, ro...  3.1 us
    add x2, other arithmetic, fold_rows(): inner + jnp.concatenate([zeros, top], axis=-1)  2.71 us
    broadcast_in_dim x3, other arithmetic, body(): return (wavefield[None], returning[None], summed[None, None])  2.49 us
    unnamed x21, local copies, waits for them, and re-layouts  2.35 us
  transfers between devices with their start and end apart: 7, of which 3 were waited for; matrix products, arithmetic and copies ran while one was open for 30% of the time, Pallas kernels for 3%

commit v1 on v0

--- a/solution.py
+++ b/solution.py
@@ -1,6 +1,7 @@
 import math
 
 import jax
+import numpy as np
 import jax.numpy as jnp
 from jax import lax
 from jax.experimental import pallas as pl
@@ -44,16 +45,42 @@
 
 
 def kernel_lines(lines, length):
-    ids = lax.iota(jnp.int32, length)
-    angle = 2.0 * math.pi / length * (ids[:, None] * ids[None, :] % length).astype(jnp.float32)
-    cos_grid = jnp.cos(angle)
-    sin_grid = jnp.sin(angle)
-    cos_line = jnp.cos(lines)
-    sin_line = jnp.sin(lines)
-    dot = lambda x, y: jnp.einsum("...f,nf->...n", x, y, precision=highest)
-    real = (dot(cos_line, cos_grid) - dot(sin_line, sin_grid)) / length
-    imag = (dot(sin_line, cos_grid) + dot(cos_line, sin_grid)) / length
-    return real, imag
+    ids = np.arange(length)
+    angle = 2.0 * np.pi / length * (ids[None, :] * ids[:, None] % length)
+    grids = jnp.asarray(np.concatenate([np.cos(angle), np.sin(angle)], axis=1), jnp.float32)
+    both = jnp.concatenate([jnp.cos(lines), jnp.sin(lines)], axis=-2)
+    product = jnp.einsum("...f,fn->...n", both, grids, precision=highest)
+    count = lines.shape[-2]
+    cos_cos = product[..., :count, :length]
+    cos_sin = product[..., :count, length:]
+    sin_cos = product[..., count:, :length]
+    sin_sin = product[..., count:, length:]
+    return (cos_cos - sin_sin) / length, (sin_cos + cos_sin) / length
+
+
+def line_allreduce(value, axis, pieces):
+    count = lax.axis_size(axis)
+    if count == 1:
+        return value
+    if count % 2:
+        return lax.psum(value, axis)
+    half = count // 2
+    index = lax.axis_index(axis)
+    chunks = jnp.split(value, pieces, axis=-2)
+    done = []
+    for chunk in chunks:
+        total = chunk
+        for step in range(half - 1):
+            pairs = [(step, step + 1), (count - 1 - step, count - 2 - step)]
+            total = total + lax.ppermute(total, axis, pairs)
+        total = total + lax.ppermute(total, axis, [(half - 1, half), (half, half - 1)])
+        for step in range(half - 1):
+            pairs = [(half - 1 - step, half - 2 - step), (half + step, half + 1 + step)]
+            got = lax.ppermute(total, axis, pairs)
+            target = (index == half - 2 - step) | (index == half + 1 + step)
+            total = jnp.where(target, got, total)
+        done.append(total)
+    return jnp.concatenate(done, axis=-2)
 
 
 def toeplitz_kernel(q_ref, o_ref):
@@ -160,7 +187,7 @@
     grad_real = spread[:, 0] * held_field[:, 0] + spread[:, 1] * held_field[:, 1]
     grad_imag = spread[:, 1] * held_field[:, 0] - spread[:, 0] * held_field[:, 1]
     gradient_term = jnp.stack([jnp.sum(grad_real, axis=0), jnp.sum(grad_imag, axis=0)])
-    summed = lax.psum(gradient_term, "angle")
+    summed = line_allreduce(gradient_term, "angle", 4)
     returning = jnp.stack(
         [
             cosine * spread[:, 0] + sine_part * spread[:, 1],

time: 104 us -> 73.7 us (0.71)
  waiting for transfers between devices: 39 us -> 16.5 us
  starting transfers between devices: 10.3 us -> 25.5 us
  between operations: 16.4 us -> 3.19 us
  matrix products: 15.9 us -> 7.19 us
  local copies, waits for them, and re-layouts: 9.21 us -> 7.22 us
    psum x1 -> x0, waiting for transfers between devices: 36.2 us -> none  [body(): summed = lax.psum(gradient_term, 'angle')]
    ppermute x0 -> x12, starting transfers between devices: none -> 15.1 us  [the longest x4 7.31 us: line_allreduce(): total = total + lax.ppermute(total, axis, pairs)]
    ppermute x0 -> x12, waiting for transfers between devices: none -> 13.7 us  [the longest x4 11.6 us: line_allreduce(): got = lax.ppermute(total, axis, pairs)]
    dot_general x4 -> x1, matrix products: 9.66 us -> 1.65 us  [kernel_lines(): product = jnp.einsum('...f,fn->...n', both, grids, precision=highest)]
    unnamed x21 -> x18, local copies, waits for them, and re-layouts: 2.35 us -> 0.33 us
  transfers between devices with their start and end apart: 7 -> 18, of which waited for: 3 -> 9; matrix products, arithmetic and copies ran while one was open for 30% -> 29% of each run, Pallas kernels for 3% -> 4%
where the time goes in v1:
time: 73.7 us; the launch traced here: 73 us
  starting transfers between devices  25.5 us (35%)
  waiting for transfers between devices  16.5 us (22%)
  other arithmetic  10.4 us (14%)
  local copies, waits for them, and re-layouts  7.22 us (10%)
  matrix products  7.19 us (10%)
  between operations  3.19 us (4%)
  Pallas kernels  3.1 us (4%)
    ppermute x4, waiting for transfers between devices, line_allreduce(): got = lax.ppermute(total, axis, pairs)  11.6 us
    ppermute x3, starting transfers between devices, padded_2(): lax.ppermute(lax.slice_in_dim(block, block.shape[dim] - width, None, axis...  8.87 us
    ppermute x4, starting transfers between devices, line_allreduce(): total = total + lax.ppermute(total, axis, pairs)  7.31 us
    dot_general x12, matrix products, contract(): return jnp.einsum(form, left, right, precision=wave_precision)  5.54 us
    ppermute x4, starting transfers between devices, line_allreduce(): got = lax.ppermute(total, axis, pairs)  5.17 us
    pallas_call x1, Pallas kernels, toeplitz(): pl.pallas_call(toeplitz_kernel, out_shape=jax.ShapeDtypeStruct((count, ro...  3.1 us
    add x2, other arithmetic, fold_rows(): inner + jnp.concatenate([zeros, top], axis=-1)  2.71 us
    ppermute x4, starting transfers between devices, line_allreduce(): lax.ppermute(total, axis, [(half - 1, half), (half, half - 1)])  2.68 us
  transfers between devices with their start and end apart: 18, of which 9 were waited for; matrix products, arithmetic and copies ran while one was open for 29% of the time, Pallas kernels for 4%

profile of v1, /device:TPU:0, one launch (start us, length us, event | category | flops | bytes accessed | tf_op | source)
XLA Modules:
  0.0 73.0 jit_solution(14518340627521985607)
XLA Ops:
  0.6 1.3 %collective-permute-start.3 = (f32[1,1,2,256,256]{4,3,2,1,0:T(8,128)}, f32[1,1,2,256,256]{4,3,2,1,0:T(8,128)}, u32[]{:S(2)}, u32[]{:S(2)}) collective-permute-start(f32[1,1,2,256,256]{4,3,2,1,0:T(8,128)} %param.12), channel_id=1, source_target_pairs={{8,0},{16,8},{24,16},{9,1},{17,9},{25,17},{10,2},{18,10},{26,18},{... | collective-permute-start | bytes 1572872 | tf_op jit(solution)/shard_map/ppermute | solution.py:32
  1.9 3.8 %collective-permute-start = (f32[1,1,2,256,256]{4,3,2,1,0:T(8,128)}, f32[1,1,2,256,256]{4,3,2,1,0:T(8,128)}, u32[]{:S(2)}, u32[]{:S(2)}) collective-permute-start(f32[1,1,2,256,256]{4,3,2,1,0:T(8,128)} %param.11), channel_id=1, source_target_pairs={{0,8},{8,16},{16,24},{1,9},{9,17},{17,25},{2,10},{10,18},{18,26},{... | collective-permute-start | bytes 1572872 | tf_op jit(solution)/shard_map/ppermute | solution.py:29
  5.8 1.3 %fusion.106 = (s32[1,1]{1,0:T(1,128)}, s32[1,1]{1,0:T(1,128)}) fusion(s32[1,2]{1,0:T(1,128)} %param.16), kind=kLoop, calls=%fused_computation.169 | loop fusion | bytes 16 | tf_op jit(solution)/shard_map/slice | solution.py:151
  9.2 1.6 %convolution_bitcast_fusion = f32[1,8,640]{2,1,0:T(8,128)S(1)} fusion(f32[320,640]{1,0:T(8,128)} %constant.51.clone, f32[1,4,320]{2,1,0:T(4,128)S(1)} %get-tuple-element.34, f32[1,4,320]{2,1,0:T(4,128)S(1)} %get-tuple-element.33), kind=kOutput, calls=%fused_computation.14 | convolution fusion | flops 19663360 | bytes 849920 | tf_op jit(solution)/shard_map/...f,fn->...n/dot_general | solution.py:52
  12.1 3.1 %shard_map.112 = f32[8,256,320]{2,1,0:T(8,128)} custom-call(f32[8,640]{1,0:T(8,128)} %pad_maximum_fusion.7.q_ref), custom_call_target="tpu_custom_call" | custom-call | tf_op jit(solution)/shard_map/pallas_call | solution.py:101
  15.2 2.1 %slice_bitcast_fusion.1 = (f32[1,2,256,320]{3,2,1,0:T(8,128)S(1)}, f32[1,2,256,320]{3,2,1,0:T(8,128)S(1)}, f32[1,2,256,320]{3,2,1,0:T(8,128)S(1)}, f32[1,2,256,320]{3,2,1,0:T(8,128)S(1)}) fusion(f32[1,4,2,256,320]{4,3,2,1,0:T(8,128)} %bitcast.189), kind=kLoop, calls=%fused_computation.16 | loop fusion | bytes 5242880 | tf_op jit(solution)/shard_map/squeeze | solution.py:160
  17.3 0.9 %fusion.103 = (f32[1,2,256,32]{3,2,1,0:T(8,128)}, f32[1,2,256,32]{3,2,1,0:T(8,128)}) fusion(f32[1,2,256,320]{3,2,1,0:T(8,128)S(1)} %get-tuple-element.3), kind=kLoop, calls=%fused_computation.166 | loop fusion | bytes 262144 | tf_op jit(solution)/shard_map/slice | solution.py:109
  18.2 0.9 %bitcast_convert_fusion = (f32[1,2,256,256]{3,2,1,0:T(8,128)}, f32[1,2,256,256]{3,2,1,0:T(8,128)S(1)}) fusion(bf16[1,2,1,2,256,256]{5,4,3,2,1,0:T(8,128)(2,1)S(1)} %copy-done.2), kind=kLoop, calls=%fused_computation.83 | loop fusion | flops 262144 | bytes 1572864 | tf_op jit(solution)/shard_map/convert_element_type | solution.py:186
  19.1 1.6 %fusion.105 = (f32[1,1,256,256]{3,2,1,0:T(8,128)S(1)}, f32[1,1,256,256]{3,2,1,0:T(8,128)}) fusion(f32[1,1,256,256]{3,2,1,0:T(8,128)S(1)} %copy-done.5), kind=kLoop, calls=%fused_computation.168 | loop fusion | bytes 786432 | tf_op jit(solution)/shard_map/cos | solution.py:164
  20.7 0.9 %fusion.104 = (f32[1,2,256,32]{3,2,1,0:T(8,128)}, f32[1,2,256,32]{3,2,1,0:T(8,128)}) fusion(f32[1,2,256,320]{3,2,1,0:T(8,128)S(1)} %get-tuple-element.6), kind=kLoop, calls=%fused_computation.167 | loop fusion | bytes 262144 | tf_op jit(solution)/shard_map/slice | solution.py:109
  22.3 1.4 %fusion.6 = f32[1,2,256,256]{3,2,1,0:T(8,128)S(1)} fusion(f32[1,2,256,320]{3,2,1,0:T(8,128)S(1)} %get-tuple-element.3, f32[1,2,256,32]{3,2,1,0:T(8,128)} %get-tuple-element.14, f32[1,2,256,32]{3,2,1,0:T(8,128)} %get-tuple-element.13), kind=kLoop, calls=%fused_computation.28 | loop fusion | flops 262144 | bytes 1179648 | tf_op jit(solution)/shard_map/add | solution.py:113
  23.7 1.3 %fusion.7 = f32[1,2,256,256]{3,2,1,0:T(8,128)S(1)} fusion(f32[1,2,256,320]{3,2,1,0:T(8,128)S(1)} %get-tuple-element.6, f32[1,2,256,32]{3,2,1,0:T(8,128)} %get-tuple-element.16, f32[1,2,256,32]{3,2,1,0:T(8,128)} %get-tuple-element.15), kind=kLoop, calls=%fused_computation.30 | loop fusion | flops 262144 | bytes 1179648 | tf_op jit(solution)/shard_map/add | solution.py:113
  25.1 1.1 %bitcast_select_fusion = f32[1,2,256,256]{3,2,1,0:T(8,128)S(1)} fusion(f32[1,1,2,256,256]{4,3,2,1,0:T(8,128)} %collective-permute-done.3, f32[256,256]{1,0:T(8,128)S(1)} %copy-done.4, pred[]{:T(512)S(6)} %eq.9, bf16[1,2,1,2,256,256]{5,4,3,2,1,0:T(8,128)(2,1)S(1)} %copy-done.3), kind=kLoop, calls=%fused_computation.34 | loop fusion | flops 393216 | bytes 1572865 | tf_op jit(solution)/shard_map/jit(_where)/select_n | solution.py:173
  27.4 1.1 %fusion.8 = f32[1,2,256,256]{3,2,1,0:T(8,128)S(1)} fusion(f32[1,1,2,256,256]{4,3,2,1,0:T(8,128)} %collective-permute-done, bf16[2,256,256]{2,1,0:T(8,128)(2,1)S(1)} %copy-done.6, pred[]{:T(512)} %eq.8), kind=kLoop, calls=%fused_computation.36 | loop fusion | flops 262144 | bytes 1310721 | tf_op jit(solution)/shard_map/jit(_where)/select_n | solution.py:169
  29.9 3.0 %collective-permute-start.4 = (f32[1,2,256,32]{2,3,1,0:T(8,128)S(1)}, f32[1,2,256,32]{2,3,1,0:T(8,128)S(1)}, u32[]{:S(2)}, u32[]{:S(2)}) collective-permute-start(f32[1,2,256,32]{2,3,1,0:T(8,128)S(1)} %get-tuple-element.25), channel_id=1, source_target_pairs={{0,4},{4,0},{1,5},{5,1},{2,6},{6,2},{3,7},{7,3},{8,12},{12,8},{9,1... | collective-permute-start | bytes 196616 | tf_op jit(solution)/shard_map/ppermute | solution.py:29
  33.0 2.0 %collective-permute-start.1 = (f32[1,2,256,32]{2,3,1,0:T(8,128)S(1)}, f32[1,2,256,32]{2,3,1,0:T(8,128)S(1)}, u32[]{:S(2)}, u32[]{:S(2)}) collective-permute-start(f32[1,2,256,32]{2,3,1,0:T(8,128)S(1)} %get-tuple-element.27), channel_id=1, source_target_pairs={{0,4},{4,0},{1,5},{5,1},{2,6},{6,2},{3,7},{7,3},{8,12},{12,8},{9,1... | collective-permute-start | bytes 196616 | tf_op jit(solution)/shard_map/ppermute | solution.py:29
  35.8 2.1 %collective-permute-done.5 = f32[1,2,256,32]{2,3,1,0:T(8,128)S(1)} collective-permute-done((f32[1,2,256,32]{2,3,1,0:T(8,128)S(1)}, f32[1,2,256,32]{2,3,1,0:T(8,128)S(1)}, u32[]{:S(2)}, u32[]{:S(2)}) %collective-permute-start.5) | collective-permute-done | bytes 65568 | tf_op jit(solution)/shard_map/ppermute | solution.py:32
  39.7 3.4 %collective-permute-start.6 = (f32[2,64,256]{2,1,0:T(8,128)S(1)}, f32[2,64,256]{2,1,0:T(8,128)S(1)}, u32[]{:S(2)}, u32[]{:S(2)}) collective-permute-start(f32[2,64,256]{2,1,0:T(8,128)S(1)} %get-tuple-element.17), channel_id=1, source_target_pairs={{0,1},{3,2},{4,5},{7,6},{8,9},{11,10},{12,13},{15,14},{16,17},{19,... | collective-permute-start | bytes 393224 | tf_op jit(solution)/shard_map/ppermute | solution.py:75
  43.1 1.3 %collective-permute-start.9 = (f32[2,64,256]{2,1,0:T(8,128)S(1)}, f32[2,64,256]{2,1,0:T(8,128)S(1)}, u32[]{:S(2)}, u32[]{:S(2)}) collective-permute-start(f32[2,64,256]{2,1,0:T(8,128)S(1)} %get-tuple-element.18), channel_id=1, source_target_pairs={{0,1},{3,2},{4,5},{7,6},{8,9},{11,10},{12,13},{15,14},{16,17},{19,... | collective-permute-start | bytes 393224 | tf_op jit(solution)/shard_map/ppermute | solution.py:75
  44.4 1.3 %collective-permute-start.12 = (f32[2,64,256]{2,1,0:T(8,128)S(1)}, f32[2,64,256]{2,1,0:T(8,128)S(1)}, u32[]{:S(2)}, u32[]{:S(2)}) collective-permute-start(f32[2,64,256]{2,1,0:T(8,128)S(1)} %get-tuple-element.20), channel_id=1, source_target_pairs={{0,1},{3,2},{4,5},{7,6},{8,9},{11,10},{12,13},{15,14},{16,17},{19,... | collective-permute-start | bytes 393224 | tf_op jit(solution)/shard_map/ppermute | solution.py:75
  45.7 1.3 %collective-permute-start.15 = (f32[2,64,256]{2,1,0:T(8,128)S(1)}, f32[2,64,256]{2,1,0:T(8,128)S(1)}, u32[]{:S(2)}, u32[]{:S(2)}) collective-permute-start(f32[2,64,256]{2,1,0:T(8,128)S(1)} %get-tuple-element.19), channel_id=1, source_target_pairs={{0,1},{3,2},{4,5},{7,6},{8,9},{11,10},{12,13},{15,14},{16,17},{19,... | collective-permute-start | bytes 393224 | tf_op jit(solution)/shard_map/ppermute | solution.py:75
  50.5 0.9 %collective-permute-done.12 = f32[2,64,256]{2,1,0:T(8,128)S(1)} collective-permute-done((f32[2,64,256]{2,1,0:T(8,128)S(1)}, f32[2,64,256]{2,1,0:T(8,128)S(1)}, u32[]{:S(2)}, u32[]{:S(2)}) %collective-permute-start.12) | collective-permute-done | bytes 131104 | tf_op jit(solution)/shard_map/ppermute | solution.py:75
  53.6 1.3 %collective-permute-start.8 = (f32[2,64,256]{2,1,0:T(8,128)S(1)}, f32[2,64,256]{2,1,0:T(8,128)S(1)}, u32[]{:S(2)}, u32[]{:S(2)}) collective-permute-start(f32[2,64,256]{2,1,0:T(8,128)S(1)} %add.274), channel_id=1, source_target_pairs={{1,0},{2,3},{5,4},{6,7},{9,8},{10,11},{13,12},{14,15},{17,16},{18,... | collective-permute-start | bytes 393224 | tf_op jit(solution)/shard_map/ppermute | solution.py:79
  54.9 0.8 %maximum_bitcast_fusion.1 = f32[1,1,2,256,256]{4,3,2,1,0:T(8,128)} fusion(f32[1,1,256,256]{3,2,1,0:T(8,128)S(1)} %get-tuple-element.21, f32[1,1,256,256]{3,2,1,0:T(8,128)S(1)} %get-tuple-element.22), kind=kLoop, calls=%fused_computation.32 | loop fusion | flops 131072 | bytes 1048576 | tf_op jit(solution)/shard_map/broadcast_in_dim | solution.py:199
  56.6 1.3 %collective-permute-start.11 = (f32[2,64,256]{2,1,0:T(8,128)S(1)}, f32[2,64,256]{2,1,0:T(8,128)S(1)}, u32[]{:S(2)}, u32[]{:S(2)}) collective-permute-start(f32[2,64,256]{2,1,0:T(8,128)S(1)} %add.276), channel_id=1, source_target_pairs={{1,0},{2,3},{5,4},{6,7},{9,8},{10,11},{13,12},{14,15},{17,16},{18,... | collective-permute-start | bytes 393224 | tf_op jit(solution)/shard_map/ppermute | solution.py:79
  57.9 1.3 %collective-permute-start.14 = (f32[2,64,256]{2,1,0:T(8,128)S(1)}, f32[2,64,256]{2,1,0:T(8,128)S(1)}, u32[]{:S(2)}, u32[]{:S(2)}) collective-permute-start(f32[2,64,256]{2,1,0:T(8,128)S(1)} %add.278), channel_id=1, source_target_pairs={{1,0},{2,3},{5,4},{6,7},{9,8},{10,11},{13,12},{14,15},{17,16},{18,... | collective-permute-start | bytes 393224 | tf_op jit(solution)/shard_map/ppermute | solution.py:79
  59.2 1.3 %collective-permute-start.17 = (f32[2,64,256]{2,1,0:T(8,128)S(1)}, f32[2,64,256]{2,1,0:T(8,128)S(1)}, u32[]{:S(2)}, u32[]{:S(2)}) collective-permute-start(f32[2,64,256]{2,1,0:T(8,128)S(1)} %add.280), channel_id=1, source_target_pairs={{1,0},{2,3},{5,4},{6,7},{9,8},{10,11},{13,12},{14,15},{17,16},{18,... | collective-permute-start | bytes 393224 | tf_op jit(solution)/shard_map/ppermute | solution.py:79
  60.5 7.1 %collective-permute-done.8 = f32[2,64,256]{2,1,0:T(8,128)S(1)} collective-permute-done((f32[2,64,256]{2,1,0:T(8,128)S(1)}, f32[2,64,256]{2,1,0:T(8,128)S(1)}, u32[]{:S(2)}, u32[]{:S(2)}) %collective-permute-start.8) | collective-permute-done | bytes 131104 | tf_op jit(solution)/shard_map/ppermute | solution.py:79
  67.6 1.7 %collective-permute-done.11 = f32[2,64,256]{2,1,0:T(8,128)S(1)} collective-permute-done((f32[2,64,256]{2,1,0:T(8,128)S(1)}, f32[2,64,256]{2,1,0:T(8,128)S(1)}, u32[]{:S(2)}, u32[]{:S(2)}) %collective-permute-start.11) | collective-permute-done | bytes 131104 | tf_op jit(solution)/shard_map/ppermute | solution.py:79
  69.4 1.4 %collective-permute-done.14 = f32[2,64,256]{2,1,0:T(8,128)S(1)} collective-permute-done((f32[2,64,256]{2,1,0:T(8,128)S(1)}, f32[2,64,256]{2,1,0:T(8,128)S(1)}, u32[]{:S(2)}, u32[]{:S(2)}) %collective-permute-start.14) | collective-permute-done | bytes 131104 | tf_op jit(solution)/shard_map/ppermute | solution.py:79
  70.8 1.4 %collective-permute-done.17 = f32[2,64,256]{2,1,0:T(8,128)S(1)} collective-permute-done((f32[2,64,256]{2,1,0:T(8,128)S(1)}, f32[2,64,256]{2,1,0:T(8,128)S(1)}, u32[]{:S(2)}, u32[]{:S(2)}) %collective-permute-start.17) | collective-permute-done | bytes 131104 | tf_op jit(solution)/shard_map/ppermute | solution.py:79
  72.2 0.8 %maximum_bitcast_fusion.2 = f32[1,1,2,256,256]{4,3,2,1,0:T(8,128)} fusion(f32[2,64,256]{2,1,0:T(8,128)S(1)} %broadcast_select_fusion, f32[2,64,256]{2,1,0:T(8,128)S(1)} %broadcast_select_fusion.1, f32[2,64,256]{2,1,0:T(8,128)S(1)} %broadcast_select_fusion.2, f32[2,64,256]{2,1,0:T(8,128)S(1)} %broadcast_select_fusion.3), kind=kLoop, calls=%fused_computation.33 | loop fusion | flops 393216 | bytes 1048576 | tf_op jit(solution)/shard_map/broadcast_in_dim | solution.py:199
  (78 shorter events, 13.6 us)
Async XLA Ops:
  0.6 24.4 %collective-permute-start.3 = (f32[1,1,2,256,256]{4,3,2,1,0:T(8,128)}, f32[1,1,2,256,256]{4,3,2,1,0:T(8,128)}, u32[]{:S(2)}, u32[]{:S(2)}) collective-permute-start(f32[1,1,2,256,256]{4,3,2,1,0:T(8,128)} %param.12), channel_id=1, source_target_pairs={{8,0},{16,8},{24,16},{9,1},{17,9},{25,17},{10,2},{18,10},{26,18},{... | collective-permute-start | bytes 1572872 | tf_op jit(solution)/shard_map/ppermute | solution.py:32
  1.9 25.5 %collective-permute-start = (f32[1,1,2,256,256]{4,3,2,1,0:T(8,128)}, f32[1,1,2,256,256]{4,3,2,1,0:T(8,128)}, u32[]{:S(2)}, u32[]{:S(2)}) collective-permute-start(f32[1,1,2,256,256]{4,3,2,1,0:T(8,128)} %param.11), channel_id=1, source_target_pairs={{0,8},{8,16},{16,24},{1,9},{9,17},{17,25},{2,10},{10,18},{18,26},{... | collective-permute-start | bytes 1572872 | tf_op jit(solution)/shard_map/ppermute | solution.py:29
  15.2 3.1 %copy-start.2 = (bf16[1,2,1,2,256,256]{5,4,3,2,1,0:T(8,128)(2,1)S(1)}, bf16[1,2,1,2,256,256]{5,4,3,2,1,0:T(8,128)(2,1)}, u32[]{:S(2)}) copy-start(bf16[1,2,1,2,256,256]{5,4,3,2,1,0:T(8,128)(2,1)} %param.13) | copy-start | bytes 1572868
  15.2 3.9 %copy-start.5 = (f32[1,1,256,256]{3,2,1,0:T(8,128)S(1)}, f32[1,1,256,256]{3,2,1,0:T(8,128)}, u32[]{:S(2)}) copy-start(f32[1,1,256,256]{3,2,1,0:T(8,128)} %param.10) | copy-start | bytes 786436
  17.3 4.2 %copy-start.7 = (f32[1,256,256]{2,1,0:T(8,128)S(1)}, f32[1,256,256]{2,1,0:T(8,128)}, u32[]{:S(2)}) copy-start(f32[1,256,256]{2,1,0:T(8,128)} %param.14) | copy-start | bytes 786436
  22.3 2.8 %copy-start.3 = (bf16[1,2,1,2,256,256]{5,4,3,2,1,0:T(8,128)(2,1)S(1)}, bf16[1,2,1,2,256,256]{5,4,3,2,1,0:T(8,128)(2,1)}, u32[]{:S(2)}) copy-start(bf16[1,2,1,2,256,256]{5,4,3,2,1,0:T(8,128)(2,1)} %param.13) | copy-start | bytes 1572868
  22.3 2.8 %copy-start.4 = (f32[256,256]{1,0:T(8,128)S(1)}, f32[256,256]{1,0:T(8,128)}, u32[]{:S(2)}) copy-start(f32[256,256]{1,0:T(8,128)} %fusion.50) | copy-start | bytes 786436
  23.7 3.7 %copy-start.6 = (bf16[2,256,256]{2,1,0:T(8,128)(2,1)S(1)}, bf16[2,256,256]{2,1,0:T(8,128)(2,1)}, u32[]{:S(2)}) copy-start(bf16[2,256,256]{2,1,0:T(8,128)(2,1)} %param.9) | copy-start | bytes 786436
  25.0 3.5 %copy-start = (f32[1,1,256,256]{3,2,1,0:T(8,128)S(1)}, f32[1,1,256,256]{3,2,1,0:T(8,128)}, u32[]{:S(2)}) copy-start(f32[1,1,256,256]{3,2,1,0:T(8,128)} %get-tuple-element.30) | copy-start | bytes 786436
  29.4 9.6 %copy-start.1 = (f32[1,2,256,256]{3,2,1,0:T(8,128)S(1)}, f32[1,2,256,256]{3,2,1,0:T(8,128)}, u32[]{:S(2)}) copy-start(f32[1,2,256,256]{3,2,1,0:T(8,128)} %get-tuple-element.23) | copy-start | bytes 1572868
  29.9 5.9 %collective-permute-start.4 = (f32[1,2,256,32]{2,3,1,0:T(8,128)S(1)}, f32[1,2,256,32]{2,3,1,0:T(8,128)S(1)}, u32[]{:S(2)}, u32[]{:S(2)}) collective-permute-start(f32[1,2,256,32]{2,3,1,0:T(8,128)S(1)} %get-tuple-element.25), channel_id=1, source_target_pairs={{0,4},{4,0},{1,5},{5,1},{2,6},{6,2},{3,7},{7,3},{8,12},{12,8},{9,1... | collective-permute-start | bytes 196616 | tf_op jit(solution)/shard_map/ppermute | solution.py:29
  32.9 5.0 %collective-permute-start.5 = (f32[1,2,256,32]{2,3,1,0:T(8,128)S(1)}, f32[1,2,256,32]{2,3,1,0:T(8,128)S(1)}, u32[]{:S(2)}, u32[]{:S(2)}) collective-permute-start(f32[1,2,256,32]{2,3,1,0:T(8,128)S(1)} %get-tuple-element.26), channel_id=1, source_target_pairs={{4,0},{0,4},{5,1},{1,5},{6,2},{2,6},{7,3},{3,7},{12,8},{8,12},{13,... | collective-permute-start | bytes 196616 | tf_op jit(solution)/shard_map/ppermute | solution.py:32
  33.0 12.7 %collective-permute-start.1 = (f32[1,2,256,32]{2,3,1,0:T(8,128)S(1)}, f32[1,2,256,32]{2,3,1,0:T(8,128)S(1)}, u32[]{:S(2)}, u32[]{:S(2)}) collective-permute-start(f32[1,2,256,32]{2,3,1,0:T(8,128)S(1)} %get-tuple-element.27), channel_id=1, source_target_pairs={{0,4},{4,0},{1,5},{5,1},{2,6},{6,2},{3,7},{7,3},{8,12},{12,8},{9,1... | collective-permute-start | bytes 196616 | tf_op jit(solution)/shard_map/ppermute | solution.py:29
  35.0 12.0 %collective-permute-start.2 = (f32[1,2,256,32]{2,3,1,0:T(8,128)S(1)}, f32[1,2,256,32]{2,3,1,0:T(8,128)S(1)}, u32[]{:S(2)}, u32[]{:S(2)}) collective-permute-start(f32[1,2,256,32]{2,3,1,0:T(8,128)S(1)} %get-tuple-element.28), channel_id=1, source_target_pairs={{4,0},{0,4},{5,1},{1,5},{6,2},{2,6},{7,3},{3,7},{12,8},{8,12},{13,... | collective-permute-start | bytes 196616 | tf_op jit(solution)/shard_map/ppermute | solution.py:32
  39.7 8.5 %collective-permute-start.6 = (f32[2,64,256]{2,1,0:T(8,128)S(1)}, f32[2,64,256]{2,1,0:T(8,128)S(1)}, u32[]{:S(2)}, u32[]{:S(2)}) collective-permute-start(f32[2,64,256]{2,1,0:T(8,128)S(1)} %get-tuple-element.17), channel_id=1, source_target_pairs={{0,1},{3,2},{4,5},{7,6},{8,9},{11,10},{12,13},{15,14},{16,17},{19,... | collective-permute-start | bytes 393224 | tf_op jit(solution)/shard_map/ppermute | solution.py:75
  43.1 6.7 %collective-permute-start.9 = (f32[2,64,256]{2,1,0:T(8,128)S(1)}, f32[2,64,256]{2,1,0:T(8,128)S(1)}, u32[]{:S(2)}, u32[]{:S(2)}) collective-permute-start(f32[2,64,256]{2,1,0:T(8,128)S(1)} %get-tuple-element.18), channel_id=1, source_target_pairs={{0,1},{3,2},{4,5},{7,6},{8,9},{11,10},{12,13},{15,14},{16,17},{19,... | collective-permute-start | bytes 393224 | tf_op jit(solution)/shard_map/ppermute | solution.py:75
  44.4 7.0 %collective-permute-start.12 = (f32[2,64,256]{2,1,0:T(8,128)S(1)}, f32[2,64,256]{2,1,0:T(8,128)S(1)}, u32[]{:S(2)}, u32[]{:S(2)}) collective-permute-start(f32[2,64,256]{2,1,0:T(8,128)S(1)} %get-tuple-element.20), channel_id=1, source_target_pairs={{0,1},{3,2},{4,5},{7,6},{8,9},{11,10},{12,13},{15,14},{16,17},{19,... | collective-permute-start | bytes 393224 | tf_op jit(solution)/shard_map/ppermute | solution.py:75
  45.7 7.1 %collective-permute-start.15 = (f32[2,64,256]{2,1,0:T(8,128)S(1)}, f32[2,64,256]{2,1,0:T(8,128)S(1)}, u32[]{:S(2)}, u32[]{:S(2)}) collective-permute-start(f32[2,64,256]{2,1,0:T(8,128)S(1)} %get-tuple-element.19), channel_id=1, source_target_pairs={{0,1},{3,2},{4,5},{7,6},{8,9},{11,10},{12,13},{15,14},{16,17},{19,... | collective-permute-start | bytes 393224 | tf_op jit(solution)/shard_map/ppermute | solution.py:75
  48.2 5.4 %collective-permute-start.7 = (f32[2,64,256]{2,1,0:T(8,128)S(1)}, f32[2,64,256]{2,1,0:T(8,128)S(1)}, u32[]{:S(2)}, u32[]{:S(2)}) collective-permute-start(f32[2,64,256]{2,1,0:T(8,128)S(1)} %add.273), channel_id=1, source_target_pairs={{1,2},{2,1},{5,6},{6,5},{9,10},{10,9},{13,14},{14,13},{17,18},{18,... | collective-permute-start | bytes 393224 | tf_op jit(solution)/shard_map/ppermute | solution.py:76
  49.9 6.7 %collective-permute-start.10 = (f32[2,64,256]{2,1,0:T(8,128)S(1)}, f32[2,64,256]{2,1,0:T(8,128)S(1)}, u32[]{:S(2)}, u32[]{:S(2)}) collective-permute-start(f32[2,64,256]{2,1,0:T(8,128)S(1)} %add.275), channel_id=1, source_target_pairs={{1,2},{2,1},{5,6},{6,5},{9,10},{10,9},{13,14},{14,13},{17,18},{18,... | collective-permute-start | bytes 393224 | tf_op jit(solution)/shard_map/ppermute | solution.py:76
  51.5 6.4 %collective-permute-start.13 = (f32[2,64,256]{2,1,0:T(8,128)S(1)}, f32[2,64,256]{2,1,0:T(8,128)S(1)}, u32[]{:S(2)}, u32[]{:S(2)}) collective-permute-start(f32[2,64,256]{2,1,0:T(8,128)S(1)} %add.277), channel_id=1, source_target_pairs={{1,2},{2,1},{5,6},{6,5},{9,10},{10,9},{13,14},{14,13},{17,18},{18,... | collective-permute-start | bytes 393224 | tf_op jit(solution)/shard_map/ppermute | solution.py:76
  52.9 6.3 %collective-permute-start.16 = (f32[2,64,256]{2,1,0:T(8,128)S(1)}, f32[2,64,256]{2,1,0:T(8,128)S(1)}, u32[]{:S(2)}, u32[]{:S(2)}) collective-permute-start(f32[2,64,256]{2,1,0:T(8,128)S(1)} %add.279), channel_id=1, source_target_pairs={{1,2},{2,1},{5,6},{6,5},{9,10},{10,9},{13,14},{14,13},{17,18},{18,... | collective-permute-start | bytes 393224 | tf_op jit(solution)/shard_map/ppermute | solution.py:76
  53.6 14.0 %collective-permute-start.8 = (f32[2,64,256]{2,1,0:T(8,128)S(1)}, f32[2,64,256]{2,1,0:T(8,128)S(1)}, u32[]{:S(2)}, u32[]{:S(2)}) collective-permute-start(f32[2,64,256]{2,1,0:T(8,128)S(1)} %add.274), channel_id=1, source_target_pairs={{1,0},{2,3},{5,4},{6,7},{9,8},{10,11},{13,12},{14,15},{17,16},{18,... | collective-permute-start | bytes 393224 | tf_op jit(solution)/shard_map/ppermute | solution.py:79
  56.6 12.8 %collective-permute-start.11 = (f32[2,64,256]{2,1,0:T(8,128)S(1)}, f32[2,64,256]{2,1,0:T(8,128)S(1)}, u32[]{:S(2)}, u32[]{:S(2)}) collective-permute-start(f32[2,64,256]{2,1,0:T(8,128)S(1)} %add.276), channel_id=1, source_target_pairs={{1,0},{2,3},{5,4},{6,7},{9,8},{10,11},{13,12},{14,15},{17,16},{18,... | collective-permute-start | bytes 393224 | tf_op jit(solution)/shard_map/ppermute | solution.py:79
  57.9 12.9 %collective-permute-start.14 = (f32[2,64,256]{2,1,0:T(8,128)S(1)}, f32[2,64,256]{2,1,0:T(8,128)S(1)}, u32[]{:S(2)}, u32[]{:S(2)}) collective-permute-start(f32[2,64,256]{2,1,0:T(8,128)S(1)} %add.278), channel_id=1, source_target_pairs={{1,0},{2,3},{5,4},{6,7},{9,8},{10,11},{13,12},{14,15},{17,16},{18,... | collective-permute-start | bytes 393224 | tf_op jit(solution)/shard_map/ppermute | solution.py:79
  59.2 12.9 %collective-permute-start.17 = (f32[2,64,256]{2,1,0:T(8,128)S(1)}, f32[2,64,256]{2,1,0:T(8,128)S(1)}, u32[]{:S(2)}, u32[]{:S(2)}) collective-permute-start(f32[2,64,256]{2,1,0:T(8,128)S(1)} %add.280), channel_id=1, source_target_pairs={{1,0},{2,3},{5,4},{6,7},{9,8},{10,11},{13,12},{14,15},{17,16},{18,... | collective-permute-start | bytes 393224 | tf_op jit(solution)/shard_map/ppermute | solution.py:79

commit v2 on v1

--- a/solution.py
+++ b/solution.py
@@ -116,7 +116,7 @@
     )
 
 
-def apply_operator(wave, padded_cols, row_table, col_table):
+def apply_rows(wave, row_table):
     wave_real = wave[:, 0]
     wave_imag = wave[:, 1]
     row_real = row_table[:, 0]
@@ -124,8 +124,10 @@
     first = contract("ajl,alk->ajk", row_real + row_imag, wave_real)
     second = contract("ajl,alk->ajk", row_real, wave_imag - wave_real)
     third = contract("ajl,alk->ajk", row_imag, wave_real + wave_imag)
-    half = jnp.stack([first - third, first + second], axis=1)
-    half = padded_cols(half)
+    return jnp.stack([first - third, first + second], axis=1)
+
+
+def apply_cols(half, col_table):
     half_real = half[:, 0]
     half_imag = half[:, 1]
     col_real = col_table[:, 0]
@@ -134,6 +136,21 @@
     second = contract("ajk,aik->aji", half_real, col_imag - col_real)
     third = contract("ajk,aik->aji", half_imag, col_real + col_imag)
     return jnp.stack([first - third, first + second], axis=1)
+
+
+def side_halo(field, axis, dim):
+    count = lax.axis_size(axis)
+    if count > 2:
+        return padded_2(field, ((axis, dim),), MARGIN, True)
+    width = field.shape[dim]
+    left = lax.slice_in_dim(field, 0, MARGIN, axis=dim)
+    right = lax.slice_in_dim(field, width - MARGIN, None, axis=dim)
+    edges = jnp.concatenate([left, right], axis=dim)
+    if count == 2:
+        edges = lax.ppermute(edges, axis, [(0, 1), (1, 0)])
+    low = lax.slice_in_dim(edges, MARGIN, None, axis=dim)
+    high = lax.slice_in_dim(edges, 0, MARGIN, axis=dim)
+    return jnp.concatenate([low, field, high], axis=dim)
 
 
 def body(probe, phase, forward_in, adjoint_in, held_waves, measured, tilt_index, positions):
@@ -179,15 +196,16 @@
         axis=1,
     )
 
-    def side_halo(field):
-        return padded_2(field, (("tile", 3),), MARGIN, True)
-
-    spread = apply_operator(returning, side_halo, rows_back, cols_back)
+    halves = jnp.concatenate(
+        [apply_rows(returning, rows_back), apply_rows(transmitted, rows_fwd)], axis=1
+    )
+    halves = side_halo(halves, "tile", 3)
+    spread = apply_cols(halves[:, :2], cols_back)
     held_field = held_waves[0, 0].astype(jnp.float32)
     grad_real = spread[:, 0] * held_field[:, 0] + spread[:, 1] * held_field[:, 1]
     grad_imag = spread[:, 1] * held_field[:, 0] - spread[:, 0] * held_field[:, 1]
     gradient_term = jnp.stack([jnp.sum(grad_real, axis=0), jnp.sum(grad_imag, axis=0)])
-    summed = line_allreduce(gradient_term, "angle", 4)
+    summed = line_allreduce(gradient_term, "angle", 2)
     returning = jnp.stack(
         [
             cosine * spread[:, 0] + sine_part * spread[:, 1],
@@ -195,7 +213,7 @@
         ],
         axis=1,
     )
-    wavefield = apply_operator(transmitted, side_halo, rows_fwd, cols_fwd)
+    wavefield = apply_cols(halves[:, 2:], cols_fwd)
     return (wavefield[None], returning[None], summed[None, None])
 
 

time: 73.7 us -> 76.5 us (1.038)
  waiting for transfers between devices: 16.5 us -> 28 us
  starting transfers between devices: 25.5 us -> 16.9 us
  other arithmetic: 10.4 us -> 9.3 us
  matrix products: 7.19 us -> 8 us
    ppermute x0 -> x1, waiting for transfers between devices: none -> 7.07 us  [side_halo(): edges = lax.ppermute(edges, axis, [(0, 1), (1, 0)])]
    ppermute x4 -> x2, waiting for transfers between devices: 2.07 us -> 7.74 us  [line_allreduce(): total = total + lax.ppermute(total, axis, pairs)]
    ppermute x3 -> x1, starting transfers between devices: 8.87 us -> 3.84 us  [padded_2(): lax.ppermute(lax.slice_in_dim(block, block.shape[dim] - width, None, axis...]
    ppermute x0 -> x1, starting transfers between devices: none -> 3 us  [side_halo(): edges = lax.ppermute(edges, axis, [(0, 1), (1, 0)])]
    ppermute x4 -> x2, starting transfers between devices: 5.17 us -> 2.58 us  [line_allreduce(): got = lax.ppermute(total, axis, pairs)]
    ppermute x4 -> x2, starting transfers between devices: 7.31 us -> 4.8 us  [line_allreduce(): total = total + lax.ppermute(total, axis, pairs)]
    ppermute x3 -> x1, waiting for transfers between devices: 2.11 us -> 0.01 us  [padded_2(): lax.ppermute(lax.slice_in_dim(block, 0, width, axis=dim), axis, backward)]
    ppermute x4 -> x2, waiting for transfers between devices: 11.6 us -> 13.2 us  [line_allreduce(): got = lax.ppermute(total, axis, pairs)]
  transfers between devices with their start and end apart: 18 -> 9, of which waited for: 9 -> 5; matrix products, arithmetic and copies ran while one was open for 29% -> 24% of each run, Pallas kernels for 4% -> 4%
where the time goes in v2:
time: 76.5 us; the launch traced here: 75.9 us
  waiting for transfers between devices  28 us (37%)
  starting transfers between devices  16.9 us (22%)
  other arithmetic  9.3 us (12%)
  matrix products  8 us (10%)
  local copies, waits for them, and re-layouts  7.46 us (10%)
  between operations  3.11 us (4%)
  Pallas kernels  3.1 us (4%)
    ppermute x2, waiting for transfers between devices, line_allreduce(): got = lax.ppermute(total, axis, pairs)  13.2 us
    ppermute x2, waiting for transfers between devices, line_allreduce(): total = total + lax.ppermute(total, axis, pairs)  7.74 us
    ppermute x1, waiting for transfers between devices, side_halo(): edges = lax.ppermute(edges, axis, [(0, 1), (1, 0)])  7.07 us
    dot_general x12, matrix products, contract(): return jnp.einsum(form, left, right, precision=wave_precision)  6.35 us
    ppermute x2, starting transfers between devices, line_allreduce(): total = total + lax.ppermute(total, axis, pairs)  4.8 us
    ppermute x1, starting transfers between devices, padded_2(): lax.ppermute(lax.slice_in_dim(block, block.shape[dim] - width, None, axis...  3.84 us
    pallas_call x1, Pallas kernels, toeplitz(): pl.pallas_call(toeplitz_kernel, out_shape=jax.ShapeDtypeStruct((count, ro...  3.1 us
    ppermute x1, starting transfers between devices, side_halo(): edges = lax.ppermute(edges, axis, [(0, 1), (1, 0)])  3 us
  transfers between devices with their start and end apart: 9, of which 5 were waited for; matrix products, arithmetic and copies ran while one was open for 24% of the time, Pallas kernels for 4%

profile of v2, /device:TPU:0, one launch (start us, length us, event | category | flops | bytes accessed | tf_op | source)
XLA Modules:
  0.0 75.9 jit_solution(9229074638176813366)
XLA Ops:
  0.6 1.3 %collective-permute-start = (f32[1,1,2,256,256]{4,3,2,1,0:T(8,128)}, f32[1,1,2,256,256]{4,3,2,1,0:T(8,128)}, u32[]{:S(2)}, u32[]{:S(2)}) collective-permute-start(f32[1,1,2,256,256]{4,3,2,1,0:T(8,128)} %param.12), channel_id=1, source_target_pairs={{8,0},{16,8},{24,16},{9,1},{17,9},{25,17},{10,2},{18,10},{26,18},{... | collective-permute-start | bytes 1572872 | tf_op jit(solution)/shard_map/ppermute | solution.py:32
  1.9 3.8 %collective-permute-start.1 = (f32[1,1,2,256,256]{4,3,2,1,0:T(8,128)}, f32[1,1,2,256,256]{4,3,2,1,0:T(8,128)}, u32[]{:S(2)}, u32[]{:S(2)}) collective-permute-start(f32[1,1,2,256,256]{4,3,2,1,0:T(8,128)} %param.11), channel_id=1, source_target_pairs={{0,8},{8,16},{16,24},{1,9},{9,17},{17,25},{2,10},{10,18},{18,26},{... | collective-permute-start | bytes 1572872 | tf_op jit(solution)/shard_map/ppermute | solution.py:29
  5.8 1.3 %fusion.106 = (s32[1,1]{1,0:T(1,128)}, s32[1,1]{1,0:T(1,128)}) fusion(s32[1,2]{1,0:T(1,128)} %param.16), kind=kLoop, calls=%fused_computation.166 | loop fusion | bytes 16 | tf_op jit(solution)/shard_map/slice | solution.py:168
  9.2 1.6 %convolution_bitcast_fusion = f32[1,8,640]{2,1,0:T(8,128)S(1)} fusion(f32[320,640]{1,0:T(8,128)} %constant.51.clone, f32[1,4,320]{2,1,0:T(4,128)S(1)} %get-tuple-element.30, f32[1,4,320]{2,1,0:T(4,128)S(1)} %get-tuple-element.29), kind=kOutput, calls=%fused_computation.15 | convolution fusion | flops 19663360 | bytes 849920 | tf_op jit(solution)/shard_map/...f,fn->...n/dot_general | solution.py:52
  11.4 0.7 pad_maximum_fusion.2.q_ref
  12.1 3.1 %shard_map.112 = f32[8,256,320]{2,1,0:T(8,128)} custom-call(f32[8,640]{1,0:T(8,128)} %pad_maximum_fusion.2.q_ref), custom_call_target="tpu_custom_call" | custom-call | tf_op jit(solution)/shard_map/pallas_call | solution.py:101
  15.2 2.1 %slice_bitcast_fusion = (f32[1,2,256,320]{3,2,1,0:T(8,128)S(1)}, f32[1,2,256,320]{3,2,1,0:T(8,128)S(1)}, f32[1,2,256,320]{3,2,1,0:T(8,128)S(1)}, f32[1,2,256,320]{3,2,1,0:T(8,128)S(1)}) fusion(f32[1,4,2,256,320]{4,3,2,1,0:T(8,128)} %bitcast.189), kind=kLoop, calls=%fused_computation.16 | loop fusion | bytes 5242880 | tf_op jit(solution)/shard_map/squeeze | solution.py:179
  17.3 0.9 %fusion.102 = (f32[1,2,256,32]{3,2,1,0:T(8,128)}, f32[1,2,256,32]{3,2,1,0:T(8,128)}) fusion(f32[1,2,256,320]{3,2,1,0:T(8,128)S(1)} %get-tuple-element.6), kind=kLoop, calls=%fused_computation.162 | loop fusion | bytes 262144 | tf_op jit(solution)/shard_map/slice | solution.py:109
  18.5 0.9 %bitcast_convert_fusion = (f32[1,2,256,256]{3,2,1,0:T(8,128)}, f32[1,2,256,256]{3,2,1,0:T(8,128)S(1)}) fusion(bf16[1,2,1,2,256,256]{5,4,3,2,1,0:T(8,128)(2,1)S(1)} %copy-done.2), kind=kLoop, calls=%fused_computation.89 | loop fusion | flops 262144 | bytes 1572864 | tf_op jit(solution)/shard_map/convert_element_type | solution.py:204
  19.3 0.8 %fusion.103 = (f32[1,2,256,32]{3,2,1,0:T(8,128)}, f32[1,2,256,32]{3,2,1,0:T(8,128)}) fusion(f32[1,2,256,320]{3,2,1,0:T(8,128)S(1)} %get-tuple-element.5), kind=kLoop, calls=%fused_computation.163 | loop fusion | bytes 262144 | tf_op jit(solution)/shard_map/slice | solution.py:109
  20.2 1.6 %fusion.105 = (f32[1,1,256,256]{3,2,1,0:T(8,128)S(1)}, f32[1,1,256,256]{3,2,1,0:T(8,128)}) fusion(f32[1,1,256,256]{3,2,1,0:T(8,128)S(1)} %copy-done.9), kind=kLoop, calls=%fused_computation.165 | loop fusion | bytes 786432 | tf_op jit(solution)/shard_map/cos | solution.py:181
  21.8 0.8 %fusion.52 = f32[256,256]{1,0:T(8,128)} fusion(f32[1,256,256]{2,1,0:T(8,128)S(1)} %copy-done.11, f32[1,2,256,256]{3,2,1,0:T(8,128)S(1)} %get-tuple-element.22), kind=kLoop, calls=%fused_computation.87 | loop fusion | flops 262144 | bytes 1048576 | tf_op jit(solution)/shard_map/mul | solution.py:189
  22.5 1.4 %fusion.7 = f32[1,2,256,256]{3,2,1,0:T(8,128)S(1)} fusion(f32[1,2,256,320]{3,2,1,0:T(8,128)S(1)} %get-tuple-element.6, f32[1,2,256,32]{3,2,1,0:T(8,128)} %get-tuple-element.14, f32[1,2,256,32]{3,2,1,0:T(8,128)} %get-tuple-element.13), kind=kLoop, calls=%fused_computation.23 | loop fusion | flops 262144 | bytes 1179648 | tf_op jit(solution)/shard_map/add | solution.py:113
  24.3 1.1 %bitcast_select_fusion.1 = f32[1,2,256,256]{3,2,1,0:T(8,128)S(1)} fusion(f32[1,1,2,256,256]{4,3,2,1,0:T(8,128)} %collective-permute-done, f32[256,256]{1,0:T(8,128)S(1)} %copy-done.6, pred[]{:T(512)S(6)} %eq.15, bf16[1,2,1,2,256,256]{5,4,3,2,1,0:T(8,128)(2,1)S(1)} %copy-done.3), kind=kLoop, calls=%fused_computation.31 | loop fusion | flops 393216 | bytes 1572865 | tf_op jit(solution)/shard_map/jit(_where)/select_n | solution.py:190
  26.6 1.1 %fusion.8 = f32[1,2,256,256]{3,2,1,0:T(8,128)S(1)} fusion(f32[1,1,2,256,256]{4,3,2,1,0:T(8,128)} %collective-permute-done.1, bf16[2,256,256]{2,1,0:T(8,128)(2,1)S(1)} %copy-done.10, pred[]{:T(512)} %eq.14), kind=kLoop, calls=%fused_computation.30 | loop fusion | flops 262144 | bytes 1310721 | tf_op jit(solution)/shard_map/jit(_where)/select_n | solution.py:186
  29.1 3.0 %collective-permute-start.2 = (f32[1,4,256,64]{2,3,1,0:T(8,128)S(1)}, f32[1,4,256,64]{2,3,1,0:T(8,128)S(1)}, u32[]{:S(2)}, u32[]{:S(2)}) collective-permute-start(f32[1,4,256,64]{2,3,1,0:T(8,128)S(1)} %fusion.48), channel_id=1, source_target_pairs={{0,4},{4,0},{1,5},{5,1},{2,6},{6,2},{3,7},{7,3},{8,12},{12,8},{9,1... | collective-permute-start | bytes 786440 | tf_op jit(solution)/shard_map/ppermute | solution.py:150
  32.1 7.1 %collective-permute-done.2 = f32[1,4,256,64]{2,3,1,0:T(8,128)S(1)} collective-permute-done((f32[1,4,256,64]{2,3,1,0:T(8,128)S(1)}, f32[1,4,256,64]{2,3,1,0:T(8,128)S(1)}, u32[]{:S(2)}, u32[]{:S(2)}) %collective-permute-start.2) | collective-permute-done | bytes 262176 | tf_op jit(solution)/shard_map/ppermute | solution.py:150
  40.3 1.4 %add_bitcast_fusion = (f32[1,256,256]{2,1,0:T(8,128)S(1)}, f32[1,256,256]{2,1,0:T(8,128)S(1)}, f32[1,1,256,256]{3,2,1,0:T(8,128)}, f32[1,1,256,256]{3,2,1,0:T(8,128)}) fusion(f32[256,256]{1,0:T(8,128)S(1)} %convolution_subtract_fusion, f32[1,2,256,256]{3,2,1,0:T(8,128)S(1)} %copy-done.1, f32[1,1,256,256]{3,2,1,0:T(8,128)S(1)} %copy-done, ...), kind=kOutput, calls=%fused_computation.114 | convolution fusion | flops 126763008 | bytes 3735552 | tf_op jit(solution)/shard_map/ajk,aik->aji/dot_general | solution.py:38
  41.8 3.5 %collective-permute-start.3 = (f32[2,128,256]{2,1,0:T(8,128)S(1)}, f32[2,128,256]{2,1,0:T(8,128)S(1)}, u32[]{:S(2)}, u32[]{:S(2)}) collective-permute-start(f32[2,128,256]{2,1,0:T(8,128)S(1)} %get-tuple-element.17), channel_id=1, source_target_pairs={{0,1},{3,2},{4,5},{7,6},{8,9},{11,10},{12,13},{15,14},{16,17},{19,... | collective-permute-start | bytes 786440 | tf_op jit(solution)/shard_map/ppermute | solution.py:75
  45.3 1.3 %collective-permute-start.6 = (f32[2,128,256]{2,1,0:T(8,128)S(1)}, f32[2,128,256]{2,1,0:T(8,128)S(1)}, u32[]{:S(2)}, u32[]{:S(2)}) collective-permute-start(f32[2,128,256]{2,1,0:T(8,128)S(1)} %get-tuple-element.18), channel_id=1, source_target_pairs={{0,1},{3,2},{4,5},{7,6},{8,9},{11,10},{12,13},{15,14},{16,17},{19,... | collective-permute-start | bytes 786440 | tf_op jit(solution)/shard_map/ppermute | solution.py:75
  46.6 5.4 %collective-permute-done.3 = f32[2,128,256]{2,1,0:T(8,128)S(1)} collective-permute-done((f32[2,128,256]{2,1,0:T(8,128)S(1)}, f32[2,128,256]{2,1,0:T(8,128)S(1)}, u32[]{:S(2)}, u32[]{:S(2)}) %collective-permute-start.3) | collective-permute-done | bytes 262176 | tf_op jit(solution)/shard_map/ppermute | solution.py:75
  52.0 0.7 collective-permute-start.4
  53.8 2.3 %collective-permute-done.6 = f32[2,128,256]{2,1,0:T(8,128)S(1)} collective-permute-done((f32[2,128,256]{2,1,0:T(8,128)S(1)}, f32[2,128,256]{2,1,0:T(8,128)S(1)}, u32[]{:S(2)}, u32[]{:S(2)}) %collective-permute-start.6) | collective-permute-done | bytes 262176 | tf_op jit(solution)/shard_map/ppermute | solution.py:75
  56.2 0.7 collective-permute-start.7
  56.9 1.3 %collective-permute-start.5 = (f32[2,128,256]{2,1,0:T(8,128)S(1)}, f32[2,128,256]{2,1,0:T(8,128)S(1)}, u32[]{:S(2)}, u32[]{:S(2)}) collective-permute-start(f32[2,128,256]{2,1,0:T(8,128)S(1)} %add.262), channel_id=1, source_target_pairs={{1,0},{2,3},{5,4},{6,7},{9,8},{10,11},{13,12},{14,15},{17,16},{18,... | collective-permute-start | bytes 786440 | tf_op jit(solution)/shard_map/ppermute | solution.py:79
  58.2 0.5 fusion
  58.7 0.8 %maximum_bitcast_fusion.1 = f32[1,1,2,256,256]{4,3,2,1,0:T(8,128)} fusion(f32[1,1,256,256]{3,2,1,0:T(8,128)S(1)} %copy-done.4, f32[1,1,256,256]{3,2,1,0:T(8,128)S(1)} %copy-done.5), kind=kLoop, calls=%fused_computation.25 | loop fusion | flops 131072 | bytes 1048576 | tf_op jit(solution)/shard_map/broadcast_in_dim | solution.py:217
  59.6 1.3 %collective-permute-start.8 = (f32[2,128,256]{2,1,0:T(8,128)S(1)}, f32[2,128,256]{2,1,0:T(8,128)S(1)}, u32[]{:S(2)}, u32[]{:S(2)}) collective-permute-start(f32[2,128,256]{2,1,0:T(8,128)S(1)} %add.264), channel_id=1, source_target_pairs={{1,0},{2,3},{5,4},{6,7},{9,8},{10,11},{13,12},{14,15},{17,16},{18,... | collective-permute-start | bytes 786440 | tf_op jit(solution)/shard_map/ppermute | solution.py:79
  60.9 0.8 %maximum_bitcast_fusion = f32[1,1,2,256,256]{4,3,2,1,0:T(8,128)} fusion(f32[1,1,256,256]{3,2,1,0:T(8,128)S(1)} %fusion, f32[1,1,256,256]{3,2,1,0:T(8,128)S(1)} %fusion.1), kind=kLoop, calls=%fused_computation.24 | loop fusion | flops 131072 | bytes 1048576 | tf_op jit(solution)/shard_map/broadcast_in_dim | solution.py:217
  61.8 8.3 %collective-permute-done.5 = f32[2,128,256]{2,1,0:T(8,128)S(1)} collective-permute-done((f32[2,128,256]{2,1,0:T(8,128)S(1)}, f32[2,128,256]{2,1,0:T(8,128)S(1)}, u32[]{:S(2)}, u32[]{:S(2)}) %collective-permute-start.5) | collective-permute-done | bytes 262176 | tf_op jit(solution)/shard_map/ppermute | solution.py:79
  70.1 4.9 %collective-permute-done.8 = f32[2,128,256]{2,1,0:T(8,128)S(1)} collective-permute-done((f32[2,128,256]{2,1,0:T(8,128)S(1)}, f32[2,128,256]{2,1,0:T(8,128)S(1)}, u32[]{:S(2)}, u32[]{:S(2)}) %collective-permute-start.8) | collective-permute-done | bytes 262176 | tf_op jit(solution)/shard_map/ppermute | solution.py:79
  75.0 0.8 %maximum_bitcast_fusion.2 = f32[1,1,2,256,256]{4,3,2,1,0:T(8,128)} fusion(f32[2,128,256]{2,1,0:T(8,128)S(1)} %broadcast_select_fusion, f32[2,128,256]{2,1,0:T(8,128)S(1)} %broadcast_select_fusion.1), kind=kLoop, calls=%fused_computation.28 | loop fusion | flops 131072 | bytes 1048576 | tf_op jit(solution)/shard_map/broadcast_in_dim | solution.py:217
  (61 shorter events, 6.1 us)
Async XLA Ops:
  0.6 23.6 %collective-permute-start = (f32[1,1,2,256,256]{4,3,2,1,0:T(8,128)}, f32[1,1,2,256,256]{4,3,2,1,0:T(8,128)}, u32[]{:S(2)}, u32[]{:S(2)}) collective-permute-start(f32[1,1,2,256,256]{4,3,2,1,0:T(8,128)} %param.12), channel_id=1, source_target_pairs={{8,0},{16,8},{24,16},{9,1},{17,9},{25,17},{10,2},{18,10},{26,18},{... | collective-permute-start | bytes 1572872 | tf_op jit(solution)/shard_map/ppermute | solution.py:32
  1.9 24.7 %collective-permute-start.1 = (f32[1,1,2,256,256]{4,3,2,1,0:T(8,128)}, f32[1,1,2,256,256]{4,3,2,1,0:T(8,128)}, u32[]{:S(2)}, u32[]{:S(2)}) collective-permute-start(f32[1,1,2,256,256]{4,3,2,1,0:T(8,128)} %param.11), channel_id=1, source_target_pairs={{0,8},{8,16},{16,24},{1,9},{9,17},{17,25},{2,10},{10,18},{18,26},{... | collective-permute-start | bytes 1572872 | tf_op jit(solution)/shard_map/ppermute | solution.py:29
  17.3 1.2 %copy-start.2 = (bf16[1,2,1,2,256,256]{5,4,3,2,1,0:T(8,128)(2,1)S(1)}, bf16[1,2,1,2,256,256]{5,4,3,2,1,0:T(8,128)(2,1)}, u32[]{:S(2)}) copy-start(bf16[1,2,1,2,256,256]{5,4,3,2,1,0:T(8,128)(2,1)} %param.13) | copy-start | bytes 1572868
  18.4 1.7 %copy-start.9 = (f32[1,1,256,256]{3,2,1,0:T(8,128)S(1)}, f32[1,1,256,256]{3,2,1,0:T(8,128)}, u32[]{:S(2)}) copy-start(f32[1,1,256,256]{3,2,1,0:T(8,128)} %param.10) | copy-start | bytes 786436
  19.3 2.4 %copy-start.11 = (f32[1,256,256]{2,1,0:T(8,128)S(1)}, f32[1,256,256]{2,1,0:T(8,128)}, u32[]{:S(2)}) copy-start(f32[1,256,256]{2,1,0:T(8,128)} %param.14) | copy-start | bytes 786436
  22.5 1.4 %copy-start.7 = (f32[1,2,256,32]{3,2,1,0:T(8,128)S(1)}, f32[1,2,256,32]{3,2,1,0:T(8,128)}, u32[]{:S(2)}) copy-start(f32[1,2,256,32]{3,2,1,0:T(8,128)} %get-tuple-element.15) | copy-start | bytes 196612
  22.5 1.4 %copy-start.8 = (f32[1,2,256,32]{3,2,1,0:T(8,128)S(1)}, f32[1,2,256,32]{3,2,1,0:T(8,128)}, u32[]{:S(2)}) copy-start(f32[1,2,256,32]{3,2,1,0:T(8,128)} %get-tuple-element.16) | copy-start | bytes 196612
  22.5 1.7 %copy-start.3 = (bf16[1,2,1,2,256,256]{5,4,3,2,1,0:T(8,128)(2,1)S(1)}, bf16[1,2,1,2,256,256]{5,4,3,2,1,0:T(8,128)(2,1)}, u32[]{:S(2)}) copy-start(bf16[1,2,1,2,256,256]{5,4,3,2,1,0:T(8,128)(2,1)} %param.13) | copy-start | bytes 1572868
  22.5 1.7 %copy-start.6 = (f32[256,256]{1,0:T(8,128)S(1)}, f32[256,256]{1,0:T(8,128)}, u32[]{:S(2)}) copy-start(f32[256,256]{1,0:T(8,128)} %fusion.52) | copy-start | bytes 786436
  25.4 1.2 %copy-start.10 = (bf16[2,256,256]{2,1,0:T(8,128)(2,1)S(1)}, bf16[2,256,256]{2,1,0:T(8,128)(2,1)}, u32[]{:S(2)}) copy-start(bf16[2,256,256]{2,1,0:T(8,128)(2,1)} %param.9) | copy-start | bytes 786436
  26.2 1.5 %copy-start = (f32[1,1,256,256]{3,2,1,0:T(8,128)S(1)}, f32[1,1,256,256]{3,2,1,0:T(8,128)}, u32[]{:S(2)}) copy-start(f32[1,1,256,256]{3,2,1,0:T(8,128)} %get-tuple-element.26) | copy-start | bytes 786436
  29.1 10.1 %collective-permute-start.2 = (f32[1,4,256,64]{2,3,1,0:T(8,128)S(1)}, f32[1,4,256,64]{2,3,1,0:T(8,128)S(1)}, u32[]{:S(2)}, u32[]{:S(2)}) collective-permute-start(f32[1,4,256,64]{2,3,1,0:T(8,128)S(1)} %fusion.48), channel_id=1, source_target_pairs={{0,4},{4,0},{1,5},{5,1},{2,6},{6,2},{3,7},{7,3},{8,12},{12,8},{9,1... | collective-permute-start | bytes 786440 | tf_op jit(solution)/shard_map/ppermute | solution.py:150
  39.2 1.1 %copy-start.1 = (f32[1,2,256,256]{3,2,1,0:T(8,128)S(1)}, f32[1,2,256,256]{3,2,1,0:T(8,128)}, u32[]{:S(2)}) copy-start(f32[1,2,256,256]{3,2,1,0:T(8,128)} %get-tuple-element.21) | copy-start | bytes 1572868
  41.8 10.2 %collective-permute-start.3 = (f32[2,128,256]{2,1,0:T(8,128)S(1)}, f32[2,128,256]{2,1,0:T(8,128)S(1)}, u32[]{:S(2)}, u32[]{:S(2)}) collective-permute-start(f32[2,128,256]{2,1,0:T(8,128)S(1)} %get-tuple-element.17), channel_id=1, source_target_pairs={{0,1},{3,2},{4,5},{7,6},{8,9},{11,10},{12,13},{15,14},{16,17},{19,... | collective-permute-start | bytes 786440 | tf_op jit(solution)/shard_map/ppermute | solution.py:75
  45.3 10.8 %collective-permute-start.6 = (f32[2,128,256]{2,1,0:T(8,128)S(1)}, f32[2,128,256]{2,1,0:T(8,128)S(1)}, u32[]{:S(2)}, u32[]{:S(2)}) collective-permute-start(f32[2,128,256]{2,1,0:T(8,128)S(1)} %get-tuple-element.18), channel_id=1, source_target_pairs={{0,1},{3,2},{4,5},{7,6},{8,9},{11,10},{12,13},{15,14},{16,17},{19,... | collective-permute-start | bytes 786440 | tf_op jit(solution)/shard_map/ppermute | solution.py:75
  52.0 4.8 %collective-permute-start.4 = (f32[2,128,256]{2,1,0:T(8,128)S(1)}, f32[2,128,256]{2,1,0:T(8,128)S(1)}, u32[]{:S(2)}, u32[]{:S(2)}) collective-permute-start(f32[2,128,256]{2,1,0:T(8,128)S(1)} %add.261), channel_id=1, source_target_pairs={{1,2},{2,1},{5,6},{6,5},{9,10},{10,9},{13,14},{14,13},{17,18},{18,... | collective-permute-start | bytes 786440 | tf_op jit(solution)/shard_map/ppermute | solution.py:76
  53.8 5.0 %copy-start.4 = (f32[1,1,256,256]{3,2,1,0:T(8,128)S(1)}, f32[1,1,256,256]{3,2,1,0:T(8,128)}, u32[]{:S(2)}) copy-start(f32[1,1,256,256]{3,2,1,0:T(8,128)} %get-tuple-element.19) | copy-start | bytes 786436
  53.8 5.0 %copy-start.5 = (f32[1,1,256,256]{3,2,1,0:T(8,128)S(1)}, f32[1,1,256,256]{3,2,1,0:T(8,128)}, u32[]{:S(2)}) copy-start(f32[1,1,256,256]{3,2,1,0:T(8,128)} %get-tuple-element.20) | copy-start | bytes 786436
  56.2 3.4 %collective-permute-start.7 = (f32[2,128,256]{2,1,0:T(8,128)S(1)}, f32[2,128,256]{2,1,0:T(8,128)S(1)}, u32[]{:S(2)}, u32[]{:S(2)}) collective-permute-start(f32[2,128,256]{2,1,0:T(8,128)S(1)} %add.263), channel_id=1, source_target_pairs={{1,2},{2,1},{5,6},{6,5},{9,10},{10,9},{13,14},{14,13},{17,18},{18,... | collective-permute-start | bytes 786440 | tf_op jit(solution)/shard_map/ppermute | solution.py:76
  56.9 13.1 %collective-permute-start.5 = (f32[2,128,256]{2,1,0:T(8,128)S(1)}, f32[2,128,256]{2,1,0:T(8,128)S(1)}, u32[]{:S(2)}, u32[]{:S(2)}) collective-permute-start(f32[2,128,256]{2,1,0:T(8,128)S(1)} %add.262), channel_id=1, source_target_pairs={{1,0},{2,3},{5,4},{6,7},{9,8},{10,11},{13,12},{14,15},{17,16},{18,... | collective-permute-start | bytes 786440 | tf_op jit(solution)/shard_map/ppermute | solution.py:79
  59.6 15.4 %collective-permute-start.8 = (f32[2,128,256]{2,1,0:T(8,128)S(1)}, f32[2,128,256]{2,1,0:T(8,128)S(1)}, u32[]{:S(2)}, u32[]{:S(2)}) collective-permute-start(f32[2,128,256]{2,1,0:T(8,128)S(1)} %add.264), channel_id=1, source_target_pairs={{1,0},{2,3},{5,4},{6,7},{9,8},{10,11},{13,12},{14,15},{17,16},{18,... | collective-permute-start | bytes 786440 | tf_op jit(solution)/shard_map/ppermute | solution.py:79

commit v3 on v1

--- a/solution.py
+++ b/solution.py
@@ -154,12 +154,15 @@
     col_line = base_phase[None, :] - 2.0 * math.pi * frequency[None, :] * shift_cols[:, None]
     lines = jnp.stack([row_line, -row_line, col_line, -col_line], axis=1)
     h_real, h_imag = kernel_lines(lines, length)
-    h_all = jnp.stack([h_real, h_imag], axis=2).reshape(angle_count * 8, length)
-    tables = toeplitz(h_all, core_size).reshape(angle_count, 4, 2, core_size, length)
-    rows_fwd = fold_rows(tables[:, 0], core_size)
-    rows_back = fold_rows(tables[:, 1], core_size)
-    cols_fwd = tables[:, 2]
-    cols_back = tables[:, 3]
+    h_all = jnp.stack([h_real, h_imag], axis=2)
+
+    def build(which):
+        picked = jnp.stack([h_all[:, i] for i in which], axis=1).reshape(angle_count * 4, length)
+        return toeplitz(picked, core_size).reshape(angle_count, 2, 2, core_size, length)
+
+    back_tables = build((1, 3))
+    rows_back = fold_rows(back_tables[:, 0], core_size)
+    cols_back = back_tables[:, 1]
 
     cosine = jnp.cos(phase[0, 0])
     sine_part = jnp.sin(phase[0, 0])
@@ -171,14 +174,6 @@
     intensity = exit_wave[:, 0] * exit_wave[:, 0] + exit_wave[:, 1] * exit_wave[:, 1]
     residual = (intensity - measured)[:, None] * exit_wave
     returning = jnp.where(section == sections - 1, residual, received[3])
-    transmitted = jnp.stack(
-        [
-            cosine * wavefield[:, 0] - sine_part * wavefield[:, 1],
-            cosine * wavefield[:, 1] + sine_part * wavefield[:, 0],
-        ],
-        axis=1,
-    )
-
     def side_halo(field):
         return padded_2(field, (("tile", 3),), MARGIN, True)
 
@@ -187,6 +182,9 @@
     grad_real = spread[:, 0] * held_field[:, 0] + spread[:, 1] * held_field[:, 1]
     grad_imag = spread[:, 1] * held_field[:, 0] - spread[:, 0] * held_field[:, 1]
     gradient_term = jnp.stack([jnp.sum(grad_real, axis=0), jnp.sum(grad_imag, axis=0)])
+    gradient_term, cosine, sine_part, h_all = lax.optimization_barrier(
+        (gradient_term, cosine, sine_part, h_all)
+    )
     summed = line_allreduce(gradient_term, "angle", 4)
     returning = jnp.stack(
         [
@@ -195,6 +193,16 @@
         ],
         axis=1,
     )
+    transmitted = jnp.stack(
+        [
+            cosine * wavefield[:, 0] - sine_part * wavefield[:, 1],
+            cosine * wavefield[:, 1] + sine_part * wavefield[:, 0],
+        ],
+        axis=1,
+    )
+    fwd_tables = build((0, 2))
+    rows_fwd = fold_rows(fwd_tables[:, 0], core_size)
+    cols_fwd = fwd_tables[:, 1]
     wavefield = apply_operator(transmitted, side_halo, rows_fwd, cols_fwd)
     return (wavefield[None], returning[None], summed[None, None])
 

time: 73.7 us -> 81.9 us (1.11)
  waiting for transfers between devices: 16.5 us -> 22.5 us
  Pallas kernels: 3.1 us -> 4.59 us
  local copies, waits for them, and re-layouts: 7.22 us -> 8.42 us
  other arithmetic: 10.4 us -> 9.49 us
    ppermute x4, waiting for transfers between devices: 11.6 us -> 15.9 us  [line_allreduce(): got = lax.ppermute(total, axis, pairs)]
    ppermute x3, waiting for transfers between devices: 0.75 us -> 3.37 us  [padded_2(): lax.ppermute(lax.slice_in_dim(block, block.shape[dim] - width, None, axis...]
    sin x0 -> x1, local copies, waits for them, and re-layouts: none -> 1.62 us  [body(): sine_part = jnp.sin(phase[0, 0])]
    cos x1 -> x0, local copies, waits for them, and re-layouts: 1.59 us -> none  [body(): cosine = jnp.cos(phase[0, 0])]
    pallas_call x1 -> x2, Pallas kernels: 3.1 us -> 4.59 us  [toeplitz(): pl.pallas_call(toeplitz_kernel, out_shape=jax.ShapeDtypeStruct((count, ro...]
    add x2, other arithmetic: 2.71 us -> 1.57 us  [fold_rows(): inner + jnp.concatenate([zeros, top], axis=-1)]
    unnamed x18 -> x12, local copies, waits for them, and re-layouts: 0.33 us -> 1.24 us
    squeeze x1 -> x2, local copies, waits for them, and re-layouts: 2.14 us -> 3.02 us  [the longest x1 1.54 us: body(): rows_back = fold_rows(back_tables[:, 0], core_size)]
  transfers between devices with their start and end apart: 18 -> 18, of which waited for: 9 -> 8; matrix products, arithmetic and copies ran while one was open for 29% -> 22% of each run, Pallas kernels for 4% -> 3%
where the time goes in v3:
time: 81.9 us; the launch traced here: 81.1 us
  starting transfers between devices  25.8 us (32%)
  waiting for transfers between devices  22.5 us (27%)
  other arithmetic  9.49 us (12%)
  local copies, waits for them, and re-layouts  8.42 us (10%)
  matrix products  7.07 us (9%)
  Pallas kernels  4.59 us (6%)
  between operations  3.2 us (4%)
    ppermute x4, waiting for transfers between devices, line_allreduce(): got = lax.ppermute(total, axis, pairs)  15.9 us
    ppermute x3, starting transfers between devices, padded_2(): lax.ppermute(lax.slice_in_dim(block, block.shape[dim] - width, None, axis...  8.39 us
    ppermute x4, starting transfers between devices, line_allreduce(): total = total + lax.ppermute(total, axis, pairs)  7.63 us
    dot_general x12, matrix products, contract(): return jnp.einsum(form, left, right, precision=wave_precision)  5.42 us
    ppermute x4, starting transfers between devices, line_allreduce(): got = lax.ppermute(total, axis, pairs)  5.17 us
    pallas_call x2, Pallas kernels, toeplitz(): pl.pallas_call(toeplitz_kernel, out_shape=jax.ShapeDtypeStruct((count, ro...  4.59 us
    ppermute x3, waiting for transfers between devices, padded_2(): lax.ppermute(lax.slice_in_dim(block, block.shape[dim] - width, None, axis...  3.37 us
    ppermute x4, starting transfers between devices, line_allreduce(): lax.ppermute(total, axis, [(half - 1, half), (half, half - 1)])  2.68 us
  transfers between devices with their start and end apart: 18, of which 8 were waited for; matrix products, arithmetic and copies ran while one was open for 22% of the time, Pallas kernels for 3%

profile of v3, /device:TPU:0, one launch (start us, length us, event | category | flops | bytes accessed | tf_op | source)
XLA Modules:
  0.0 81.1 jit_solution(4648017560441489267)
XLA Ops:
  0.6 1.3 %collective-permute-start = (f32[1,1,2,256,256]{4,3,2,1,0:T(8,128)}, f32[1,1,2,256,256]{4,3,2,1,0:T(8,128)}, u32[]{:S(2)}, u32[]{:S(2)}) collective-permute-start(f32[1,1,2,256,256]{4,3,2,1,0:T(8,128)} %param.12), channel_id=1, source_target_pairs={{8,0},{16,8},{24,16},{9,1},{17,9},{25,17},{10,2},{18,10},{26,18},{... | collective-permute-start | bytes 1572872 | tf_op jit(solution)/shard_map/ppermute | solution.py:32
  1.9 3.8 %collective-permute-start.3 = (f32[1,1,2,256,256]{4,3,2,1,0:T(8,128)}, f32[1,1,2,256,256]{4,3,2,1,0:T(8,128)}, u32[]{:S(2)}, u32[]{:S(2)}) collective-permute-start(f32[1,1,2,256,256]{4,3,2,1,0:T(8,128)} %param.11), channel_id=1, source_target_pairs={{0,8},{8,16},{16,24},{1,9},{9,17},{17,25},{2,10},{10,18},{18,26},{... | collective-permute-start | bytes 1572872 | tf_op jit(solution)/shard_map/ppermute | solution.py:29
  5.8 1.3 %fusion.99 = (s32[1,1]{1,0:T(1,128)}, s32[1,1]{1,0:T(1,128)}) fusion(s32[1,2]{1,0:T(1,128)} %param.16), kind=kLoop, calls=%fused_computation.169 | loop fusion | bytes 16 | tf_op jit(solution)/shard_map/slice | solution.py:151
  9.2 1.6 %convolution_bitcast_fusion = f32[1,8,640]{2,1,0:T(8,128)S(1)} fusion(f32[320,640]{1,0:T(8,128)} %constant.51.clone, f32[1,4,320]{2,1,0:T(4,128)S(1)} %get-tuple-element.50, f32[1,4,320]{2,1,0:T(4,128)S(1)} %get-tuple-element.49), kind=kOutput, calls=%fused_computation.14 | convolution fusion | flops 19663360 | bytes 849920 | tf_op jit(solution)/shard_map/...f,fn->...n/dot_general | solution.py:52
  12.2 2.3 %shard_map.112 = f32[4,256,320]{2,1,0:T(8,128)} custom-call(f32[4,640]{1,0:T(4,128)} %pad_maximum_fusion.8.q_ref), custom_call_target="tpu_custom_call" | custom-call | tf_op jit(solution)/shard_map/pallas_call | solution.py:101
  14.4 1.5 %slice_bitcast_fusion.3 = (f32[1,2,256,320]{3,2,1,0:T(8,128)S(1)}, f32[1,2,256,320]{3,2,1,0:T(8,128)S(1)}) fusion(f32[1,2,2,256,320]{4,3,2,1,0:T(8,128)} %bitcast.177), kind=kLoop, calls=%fused_computation.18 | loop fusion | bytes 2621440 | tf_op jit(solution)/shard_map/squeeze | solution.py:164
  16.0 0.9 %fusion.96 = (f32[1,2,256,32]{3,2,1,0:T(8,128)}, f32[1,2,256,32]{3,2,1,0:T(8,128)}) fusion(f32[1,2,256,320]{3,2,1,0:T(8,128)S(1)} %get-tuple-element.13), kind=kLoop, calls=%fused_computation.166 | loop fusion | bytes 262144 | tf_op jit(solution)/shard_map/slice | solution.py:109
  17.0 1.6 %sine_bitcast_fusion = (f32[256,256]{1,0:T(8,128)S(1)}, f32[256,256]{1,0:T(8,128)}) fusion(f32[1,1,256,256]{3,2,1,0:T(8,128)S(1)} %copy-done.2), kind=kLoop, calls=%fused_computation.100 | loop fusion | bytes 786432 | tf_op jit(solution)/shard_map/sin | solution.py:168
  18.6 1.0 %fusion.50 = f32[256,256]{1,0:T(8,128)S(1)} fusion(f32[1,256,256]{2,1,0:T(8,128)} %param.14, f32[1,2,256,256]{3,2,1,0:T(8,128)S(1)} %get-tuple-element.38), kind=kLoop, calls=%fused_computation.78 | loop fusion | flops 262144 | bytes 1048576 | tf_op jit(solution)/shard_map/mul | solution.py:175
  19.6 1.3 %fusion.7 = f32[1,2,256,256]{3,2,1,0:T(8,128)S(1)} fusion(f32[1,2,256,320]{3,2,1,0:T(8,128)S(1)} %get-tuple-element.13, f32[1,2,256,32]{3,2,1,0:T(8,128)} %get-tuple-element.24, f32[1,2,256,32]{3,2,1,0:T(8,128)} %get-tuple-element.23), kind=kLoop, calls=%fused_computation.24 | loop fusion | flops 262144 | bytes 1179648 | tf_op jit(solution)/shard_map/add | solution.py:113
  20.9 1.1 %bitcast_select_fusion.1 = f32[1,2,256,256]{3,2,1,0:T(8,128)S(1)} fusion(f32[1,1,2,256,256]{4,3,2,1,0:T(8,128)} %collective-permute-done, f32[256,256]{1,0:T(8,128)S(1)} %fusion.50, pred[]{:T(512)S(6)} %eq.9, bf16[1,2,1,2,256,256]{5,4,3,2,1,0:T(8,128)(2,1)S(1)} %copy-done), kind=kLoop, calls=%fused_computation.31 | loop fusion | flops 393216 | bytes 1572865 | tf_op jit(solution)/shard_map/jit(_where)/select_n | solution.py:176
  23.2 3.0 %collective-permute-start.1 = (f32[1,2,256,32]{2,3,1,0:T(8,128)S(1)}, f32[1,2,256,32]{2,3,1,0:T(8,128)S(1)}, u32[]{:S(2)}, u32[]{:S(2)}) collective-permute-start(f32[1,2,256,32]{2,3,1,0:T(8,128)S(1)} %get-tuple-element.39), channel_id=1, source_target_pairs={{0,4},{4,0},{1,5},{5,1},{2,6},{6,2},{3,7},{7,3},{8,12},{12,8},{9,1... | collective-permute-start | bytes 196616 | tf_op jit(solution)/shard_map/ppermute | solution.py:29
  26.3 1.1 %fusion.8 = f32[1,2,256,256]{3,2,1,0:T(8,128)S(1)} fusion(f32[1,1,2,256,256]{4,3,2,1,0:T(8,128)} %collective-permute-done.3, bf16[2,256,256]{2,1,0:T(8,128)(2,1)S(1)} %copy-done.3, pred[]{:T(512)} %eq.8), kind=kLoop, calls=%fused_computation.30 | loop fusion | flops 262144 | bytes 1310721 | tf_op jit(solution)/shard_map/jit(_where)/select_n | solution.py:172
  27.4 1.8 %collective-permute-done.1 = f32[1,2,256,32]{2,3,1,0:T(8,128)S(1)} collective-permute-done((f32[1,2,256,32]{2,3,1,0:T(8,128)S(1)}, f32[1,2,256,32]{2,3,1,0:T(8,128)S(1)}, u32[]{:S(2)}, u32[]{:S(2)}) %collective-permute-start.1) | collective-permute-done | bytes 65568 | tf_op jit(solution)/shard_map/ppermute | solution.py:29
  29.2 1.3 %collective-permute-done.2 = f32[1,2,256,32]{2,3,1,0:T(8,128)S(1)} collective-permute-done((f32[1,2,256,32]{2,3,1,0:T(8,128)S(1)}, f32[1,2,256,32]{2,3,1,0:T(8,128)S(1)}, u32[]{:S(2)}, u32[]{:S(2)}) %collective-permute-start.2) | collective-permute-done | bytes 65568 | tf_op jit(solution)/shard_map/ppermute | solution.py:32
  33.4 2.3 %shard_map.113 = f32[4,256,320]{2,1,0:T(8,128)} custom-call(f32[4,640]{1,0:T(4,128)} %pad_maximum_fusion.9.q_ref), custom_call_target="tpu_custom_call" | custom-call | tf_op jit(solution)/shard_map/pallas_call | solution.py:101
  35.7 1.5 %slice_bitcast_fusion.1 = (f32[1,2,256,320]{3,2,1,0:T(8,128)S(1)}, f32[1,2,256,320]{3,2,1,0:T(8,128)S(1)}) fusion(f32[1,2,2,256,320]{4,3,2,1,0:T(8,128)} %bitcast.178), kind=kLoop, calls=%fused_computation.16 | loop fusion | bytes 2621440 | tf_op jit(solution)/shard_map/squeeze | solution.py:204
  39.5 3.5 %collective-permute-start.12 = (f32[2,64,256]{2,1,0:T(8,128)S(1)}, f32[2,64,256]{2,1,0:T(8,128)S(1)}, u32[]{:S(2)}, u32[]{:S(2)}) collective-permute-start(f32[2,64,256]{2,1,0:T(8,128)S(1)} %get-tuple-element.31), channel_id=1, source_target_pairs={{0,1},{3,2},{4,5},{7,6},{8,9},{11,10},{12,13},{15,14},{16,17},{19,... | collective-permute-start | bytes 393224 | tf_op jit(solution)/shard_map/ppermute | solution.py:75
  43.0 1.3 %collective-permute-start.15 = (f32[2,64,256]{2,1,0:T(8,128)S(1)}, f32[2,64,256]{2,1,0:T(8,128)S(1)}, u32[]{:S(2)}, u32[]{:S(2)}) collective-permute-start(f32[2,64,256]{2,1,0:T(8,128)S(1)} %get-tuple-element.30), channel_id=1, source_target_pairs={{0,1},{3,2},{4,5},{7,6},{8,9},{11,10},{12,13},{15,14},{16,17},{19,... | collective-permute-start | bytes 393224 | tf_op jit(solution)/shard_map/ppermute | solution.py:75
  44.3 1.3 %collective-permute-start.6 = (f32[2,64,256]{2,1,0:T(8,128)S(1)}, f32[2,64,256]{2,1,0:T(8,128)S(1)}, u32[]{:S(2)}, u32[]{:S(2)}) collective-permute-start(f32[2,64,256]{2,1,0:T(8,128)S(1)} %get-tuple-element.29), channel_id=1, source_target_pairs={{0,1},{3,2},{4,5},{7,6},{8,9},{11,10},{12,13},{15,14},{16,17},{19,... | collective-permute-start | bytes 393224 | tf_op jit(solution)/shard_map/ppermute | solution.py:75
  45.7 1.5 %collective-permute-start.4 = (f32[1,2,256,32]{2,3,1,0:T(8,128)S(1)}, f32[1,2,256,32]{2,3,1,0:T(8,128)S(1)}, u32[]{:S(2)}, u32[]{:S(2)}) collective-permute-start(f32[1,2,256,32]{2,3,1,0:T(8,128)S(1)} %get-tuple-element.35), channel_id=1, source_target_pairs={{0,4},{4,0},{1,5},{5,1},{2,6},{6,2},{3,7},{7,3},{8,12},{12,8},{9,1... | collective-permute-start | bytes 196616 | tf_op jit(solution)/shard_map/ppermute | solution.py:29
  48.6 1.6 %collective-permute-done.4 = f32[1,2,256,32]{2,3,1,0:T(8,128)S(1)} collective-permute-done((f32[1,2,256,32]{2,3,1,0:T(8,128)S(1)}, f32[1,2,256,32]{2,3,1,0:T(8,128)S(1)}, u32[]{:S(2)}, u32[]{:S(2)}) %collective-permute-start.4) | collective-permute-done | bytes 65568 | tf_op jit(solution)/shard_map/ppermute | solution.py:29
  50.2 1.6 %collective-permute-start.9 = (f32[2,64,256]{2,1,0:T(8,128)S(1)}, f32[2,64,256]{2,1,0:T(8,128)S(1)}, u32[]{:S(2)}, u32[]{:S(2)}) collective-permute-start(f32[2,64,256]{2,1,0:T(8,128)S(1)} %get-tuple-element.32), channel_id=1, source_target_pairs={{0,1},{3,2},{4,5},{7,6},{8,9},{11,10},{12,13},{15,14},{16,17},{19,... | collective-permute-start | bytes 393224 | tf_op jit(solution)/shard_map/ppermute | solution.py:75
  52.4 1.9 %collective-permute-done.9 = f32[2,64,256]{2,1,0:T(8,128)S(1)} collective-permute-done((f32[2,64,256]{2,1,0:T(8,128)S(1)}, f32[2,64,256]{2,1,0:T(8,128)S(1)}, u32[]{:S(2)}, u32[]{:S(2)}) %collective-permute-start.9) | collective-permute-done | bytes 131104 | tf_op jit(solution)/shard_map/ppermute | solution.py:75
  57.6 1.3 %collective-permute-start.8 = (f32[2,64,256]{2,1,0:T(8,128)S(1)}, f32[2,64,256]{2,1,0:T(8,128)S(1)}, u32[]{:S(2)}, u32[]{:S(2)}) collective-permute-start(f32[2,64,256]{2,1,0:T(8,128)S(1)} %add.262), channel_id=1, source_target_pairs={{1,0},{2,3},{5,4},{6,7},{9,8},{10,11},{13,12},{14,15},{17,16},{18,... | collective-permute-start | bytes 393224 | tf_op jit(solution)/shard_map/ppermute | solution.py:79
  60.3 1.3 %collective-permute-start.11 = (f32[2,64,256]{2,1,0:T(8,128)S(1)}, f32[2,64,256]{2,1,0:T(8,128)S(1)}, u32[]{:S(2)}, u32[]{:S(2)}) collective-permute-start(f32[2,64,256]{2,1,0:T(8,128)S(1)} %add.264), channel_id=1, source_target_pairs={{1,0},{2,3},{5,4},{6,7},{9,8},{10,11},{13,12},{14,15},{17,16},{18,... | collective-permute-start | bytes 393224 | tf_op jit(solution)/shard_map/ppermute | solution.py:79
  61.6 1.3 %collective-permute-start.14 = (f32[2,64,256]{2,1,0:T(8,128)S(1)}, f32[2,64,256]{2,1,0:T(8,128)S(1)}, u32[]{:S(2)}, u32[]{:S(2)}) collective-permute-start(f32[2,64,256]{2,1,0:T(8,128)S(1)} %add.266), channel_id=1, source_target_pairs={{1,0},{2,3},{5,4},{6,7},{9,8},{10,11},{13,12},{14,15},{17,16},{18,... | collective-permute-start | bytes 393224 | tf_op jit(solution)/shard_map/ppermute | solution.py:79
  62.9 1.3 %collective-permute-start.17 = (f32[2,64,256]{2,1,0:T(8,128)S(1)}, f32[2,64,256]{2,1,0:T(8,128)S(1)}, u32[]{:S(2)}, u32[]{:S(2)}) collective-permute-start(f32[2,64,256]{2,1,0:T(8,128)S(1)} %add.268), channel_id=1, source_target_pairs={{1,0},{2,3},{5,4},{6,7},{9,8},{10,11},{13,12},{14,15},{17,16},{18,... | collective-permute-start | bytes 393224 | tf_op jit(solution)/shard_map/ppermute | solution.py:79
  64.2 10.5 %collective-permute-done.8 = f32[2,64,256]{2,1,0:T(8,128)S(1)} collective-permute-done((f32[2,64,256]{2,1,0:T(8,128)S(1)}, f32[2,64,256]{2,1,0:T(8,128)S(1)}, u32[]{:S(2)}, u32[]{:S(2)}) %collective-permute-start.8) | collective-permute-done | bytes 131104 | tf_op jit(solution)/shard_map/ppermute | solution.py:79
  74.7 2.7 %collective-permute-done.11 = f32[2,64,256]{2,1,0:T(8,128)S(1)} collective-permute-done((f32[2,64,256]{2,1,0:T(8,128)S(1)}, f32[2,64,256]{2,1,0:T(8,128)S(1)}, u32[]{:S(2)}, u32[]{:S(2)}) %collective-permute-start.11) | collective-permute-done | bytes 131104 | tf_op jit(solution)/shard_map/ppermute | solution.py:79
  77.4 1.4 %collective-permute-done.14 = f32[2,64,256]{2,1,0:T(8,128)S(1)} collective-permute-done((f32[2,64,256]{2,1,0:T(8,128)S(1)}, f32[2,64,256]{2,1,0:T(8,128)S(1)}, u32[]{:S(2)}, u32[]{:S(2)}) %collective-permute-start.14) | collective-permute-done | bytes 131104 | tf_op jit(solution)/shard_map/ppermute | solution.py:79
  78.8 1.4 %collective-permute-done.17 = f32[2,64,256]{2,1,0:T(8,128)S(1)} collective-permute-done((f32[2,64,256]{2,1,0:T(8,128)S(1)}, f32[2,64,256]{2,1,0:T(8,128)S(1)}, u32[]{:S(2)}, u32[]{:S(2)}) %collective-permute-start.17) | collective-permute-done | bytes 131104 | tf_op jit(solution)/shard_map/ppermute | solution.py:79
  (82 shorter events, 15.3 us)
Async XLA Ops:
  0.6 20.3 %collective-permute-start = (f32[1,1,2,256,256]{4,3,2,1,0:T(8,128)}, f32[1,1,2,256,256]{4,3,2,1,0:T(8,128)}, u32[]{:S(2)}, u32[]{:S(2)}) collective-permute-start(f32[1,1,2,256,256]{4,3,2,1,0:T(8,128)} %param.12), channel_id=1, source_target_pairs={{8,0},{16,8},{24,16},{9,1},{17,9},{25,17},{10,2},{18,10},{26,18},{... | collective-permute-start | bytes 1572872 | tf_op jit(solution)/shard_map/ppermute | solution.py:32
  1.9 24.4 %collective-permute-start.3 = (f32[1,1,2,256,256]{4,3,2,1,0:T(8,128)}, f32[1,1,2,256,256]{4,3,2,1,0:T(8,128)}, u32[]{:S(2)}, u32[]{:S(2)}) collective-permute-start(f32[1,1,2,256,256]{4,3,2,1,0:T(8,128)} %param.11), channel_id=1, source_target_pairs={{0,8},{8,16},{16,24},{1,9},{9,17},{17,25},{2,10},{10,18},{18,26},{... | collective-permute-start | bytes 1572872 | tf_op jit(solution)/shard_map/ppermute | solution.py:29
  14.4 2.4 %copy-start = (bf16[1,2,1,2,256,256]{5,4,3,2,1,0:T(8,128)(2,1)S(1)}, bf16[1,2,1,2,256,256]{5,4,3,2,1,0:T(8,128)(2,1)}, u32[]{:S(2)}) copy-start(bf16[1,2,1,2,256,256]{5,4,3,2,1,0:T(8,128)(2,1)} %param.13) | copy-start | bytes 1572868
  16.0 1.0 %copy-start.2 = (f32[1,1,256,256]{3,2,1,0:T(8,128)S(1)}, f32[1,1,256,256]{3,2,1,0:T(8,128)}, u32[]{:S(2)}) copy-start(f32[1,1,256,256]{3,2,1,0:T(8,128)} %param.10) | copy-start | bytes 786436
  22.4 3.9 %copy-start.3 = (bf16[2,256,256]{2,1,0:T(8,128)(2,1)S(1)}, bf16[2,256,256]{2,1,0:T(8,128)(2,1)}, u32[]{:S(2)}) copy-start(bf16[2,256,256]{2,1,0:T(8,128)(2,1)} %param.9) | copy-start | bytes 786436
  23.2 5.9 %collective-permute-start.1 = (f32[1,2,256,32]{2,3,1,0:T(8,128)S(1)}, f32[1,2,256,32]{2,3,1,0:T(8,128)S(1)}, u32[]{:S(2)}, u32[]{:S(2)}) collective-permute-start(f32[1,2,256,32]{2,3,1,0:T(8,128)S(1)} %get-tuple-element.39), channel_id=1, source_target_pairs={{0,4},{4,0},{1,5},{5,1},{2,6},{6,2},{3,7},{7,3},{8,12},{12,8},{9,1... | collective-permute-start | bytes 196616 | tf_op jit(solution)/shard_map/ppermute | solution.py:29
  26.3 4.3 %collective-permute-start.2 = (f32[1,2,256,32]{2,3,1,0:T(8,128)S(1)}, f32[1,2,256,32]{2,3,1,0:T(8,128)S(1)}, u32[]{:S(2)}, u32[]{:S(2)}) collective-permute-start(f32[1,2,256,32]{2,3,1,0:T(8,128)S(1)} %get-tuple-element.40), channel_id=1, source_target_pairs={{4,0},{0,4},{5,1},{1,5},{6,2},{2,6},{7,3},{3,7},{12,8},{8,12},{13,... | collective-permute-start | bytes 196616 | tf_op jit(solution)/shard_map/ppermute | solution.py:32
  37.2 1.0 %copy-start.1 = (f32[256,256]{1,0:T(8,128)S(1)}, f32[256,256]{1,0:T(8,128)}, u32[]{:S(2)}) copy-start(f32[256,256]{1,0:T(8,128)} %get-tuple-element.8) | copy-start | bytes 786436
  39.5 12.8 %collective-permute-start.12 = (f32[2,64,256]{2,1,0:T(8,128)S(1)}, f32[2,64,256]{2,1,0:T(8,128)S(1)}, u32[]{:S(2)}, u32[]{:S(2)}) collective-permute-start(f32[2,64,256]{2,1,0:T(8,128)S(1)} %get-tuple-element.31), channel_id=1, source_target_pairs={{0,1},{3,2},{4,5},{7,6},{8,9},{11,10},{12,13},{15,14},{16,17},{19,... | collective-permute-start | bytes 393224 | tf_op jit(solution)/shard_map/ppermute | solution.py:75
  43.0 9.3 %collective-permute-start.15 = (f32[2,64,256]{2,1,0:T(8,128)S(1)}, f32[2,64,256]{2,1,0:T(8,128)S(1)}, u32[]{:S(2)}, u32[]{:S(2)}) collective-permute-start(f32[2,64,256]{2,1,0:T(8,128)S(1)} %get-tuple-element.30), channel_id=1, source_target_pairs={{0,1},{3,2},{4,5},{7,6},{8,9},{11,10},{12,13},{15,14},{16,17},{19,... | collective-permute-start | bytes 393224 | tf_op jit(solution)/shard_map/ppermute | solution.py:75
  44.3 8.0 %collective-permute-start.6 = (f32[2,64,256]{2,1,0:T(8,128)S(1)}, f32[2,64,256]{2,1,0:T(8,128)S(1)}, u32[]{:S(2)}, u32[]{:S(2)}) collective-permute-start(f32[2,64,256]{2,1,0:T(8,128)S(1)} %get-tuple-element.29), channel_id=1, source_target_pairs={{0,1},{3,2},{4,5},{7,6},{8,9},{11,10},{12,13},{15,14},{16,17},{19,... | collective-permute-start | bytes 393224 | tf_op jit(solution)/shard_map/ppermute | solution.py:75
  45.7 4.5 %collective-permute-start.4 = (f32[1,2,256,32]{2,3,1,0:T(8,128)S(1)}, f32[1,2,256,32]{2,3,1,0:T(8,128)S(1)}, u32[]{:S(2)}, u32[]{:S(2)}) collective-permute-start(f32[1,2,256,32]{2,3,1,0:T(8,128)S(1)} %get-tuple-element.35), channel_id=1, source_target_pairs={{0,4},{4,0},{1,5},{5,1},{2,6},{6,2},{3,7},{7,3},{8,12},{12,8},{9,1... | collective-permute-start | bytes 196616 | tf_op jit(solution)/shard_map/ppermute | solution.py:29
  47.2 4.5 %collective-permute-start.5 = (f32[1,2,256,32]{2,3,1,0:T(8,128)S(1)}, f32[1,2,256,32]{2,3,1,0:T(8,128)S(1)}, u32[]{:S(2)}, u32[]{:S(2)}) collective-permute-start(f32[1,2,256,32]{2,3,1,0:T(8,128)S(1)} %get-tuple-element.36), channel_id=1, source_target_pairs={{4,0},{0,4},{5,1},{1,5},{6,2},{2,6},{7,3},{3,7},{12,8},{8,12},{13,... | collective-permute-start | bytes 196616 | tf_op jit(solution)/shard_map/ppermute | solution.py:32
  50.2 4.1 %collective-permute-start.9 = (f32[2,64,256]{2,1,0:T(8,128)S(1)}, f32[2,64,256]{2,1,0:T(8,128)S(1)}, u32[]{:S(2)}, u32[]{:S(2)}) collective-permute-start(f32[2,64,256]{2,1,0:T(8,128)S(1)} %get-tuple-element.32), channel_id=1, source_target_pairs={{0,1},{3,2},{4,5},{7,6},{8,9},{11,10},{12,13},{15,14},{16,17},{19,... | collective-permute-start | bytes 393224 | tf_op jit(solution)/shard_map/ppermute | solution.py:75
  54.3 3.2 %collective-permute-start.7 = (f32[2,64,256]{2,1,0:T(8,128)S(1)}, f32[2,64,256]{2,1,0:T(8,128)S(1)}, u32[]{:S(2)}, u32[]{:S(2)}) collective-permute-start(f32[2,64,256]{2,1,0:T(8,128)S(1)} %get-tuple-element.25), channel_id=1, source_target_pairs={{1,2},{2,1},{5,6},{6,5},{9,10},{10,9},{13,14},{14,13},{17,18},{18,... | collective-permute-start | bytes 393224 | tf_op jit(solution)/shard_map/ppermute | solution.py:76
  55.5 4.7 %collective-permute-start.10 = (f32[2,64,256]{2,1,0:T(8,128)S(1)}, f32[2,64,256]{2,1,0:T(8,128)S(1)}, u32[]{:S(2)}, u32[]{:S(2)}) collective-permute-start(f32[2,64,256]{2,1,0:T(8,128)S(1)} %get-tuple-element.26), channel_id=1, source_target_pairs={{1,2},{2,1},{5,6},{6,5},{9,10},{10,9},{13,14},{14,13},{17,18},{18,... | collective-permute-start | bytes 393224 | tf_op jit(solution)/shard_map/ppermute | solution.py:76
  56.2 5.4 %collective-permute-start.13 = (f32[2,64,256]{2,1,0:T(8,128)S(1)}, f32[2,64,256]{2,1,0:T(8,128)S(1)}, u32[]{:S(2)}, u32[]{:S(2)}) collective-permute-start(f32[2,64,256]{2,1,0:T(8,128)S(1)} %get-tuple-element.27), channel_id=1, source_target_pairs={{1,2},{2,1},{5,6},{6,5},{9,10},{10,9},{13,14},{14,13},{17,18},{18,... | collective-permute-start | bytes 393224 | tf_op jit(solution)/shard_map/ppermute | solution.py:76
  56.9 6.0 %collective-permute-start.16 = (f32[2,64,256]{2,1,0:T(8,128)S(1)}, f32[2,64,256]{2,1,0:T(8,128)S(1)}, u32[]{:S(2)}, u32[]{:S(2)}) collective-permute-start(f32[2,64,256]{2,1,0:T(8,128)S(1)} %get-tuple-element.28), channel_id=1, source_target_pairs={{1,2},{2,1},{5,6},{6,5},{9,10},{10,9},{13,14},{14,13},{17,18},{18,... | collective-permute-start | bytes 393224 | tf_op jit(solution)/shard_map/ppermute | solution.py:76
  57.6 17.1 %collective-permute-start.8 = (f32[2,64,256]{2,1,0:T(8,128)S(1)}, f32[2,64,256]{2,1,0:T(8,128)S(1)}, u32[]{:S(2)}, u32[]{:S(2)}) collective-permute-start(f32[2,64,256]{2,1,0:T(8,128)S(1)} %add.262), channel_id=1, source_target_pairs={{1,0},{2,3},{5,4},{6,7},{9,8},{10,11},{13,12},{14,15},{17,16},{18,... | collective-permute-start | bytes 393224 | tf_op jit(solution)/shard_map/ppermute | solution.py:79
  60.3 17.2 %collective-permute-start.11 = (f32[2,64,256]{2,1,0:T(8,128)S(1)}, f32[2,64,256]{2,1,0:T(8,128)S(1)}, u32[]{:S(2)}, u32[]{:S(2)}) collective-permute-start(f32[2,64,256]{2,1,0:T(8,128)S(1)} %add.264), channel_id=1, source_target_pairs={{1,0},{2,3},{5,4},{6,7},{9,8},{10,11},{13,12},{14,15},{17,16},{18,... | collective-permute-start | bytes 393224 | tf_op jit(solution)/shard_map/ppermute | solution.py:79
  61.6 17.2 %collective-permute-start.14 = (f32[2,64,256]{2,1,0:T(8,128)S(1)}, f32[2,64,256]{2,1,0:T(8,128)S(1)}, u32[]{:S(2)}, u32[]{:S(2)}) collective-permute-start(f32[2,64,256]{2,1,0:T(8,128)S(1)} %add.266), channel_id=1, source_target_pairs={{1,0},{2,3},{5,4},{6,7},{9,8},{10,11},{13,12},{14,15},{17,16},{18,... | collective-permute-start | bytes 393224 | tf_op jit(solution)/shard_map/ppermute | solution.py:79
  62.9 17.3 %collective-permute-start.17 = (f32[2,64,256]{2,1,0:T(8,128)S(1)}, f32[2,64,256]{2,1,0:T(8,128)S(1)}, u32[]{:S(2)}, u32[]{:S(2)}) collective-permute-start(f32[2,64,256]{2,1,0:T(8,128)S(1)} %add.268), channel_id=1, source_target_pairs={{1,0},{2,3},{5,4},{6,7},{9,8},{10,11},{13,12},{14,15},{17,16},{18,... | collective-permute-start | bytes 393224 | tf_op jit(solution)/shard_map/ppermute | solution.py:79

commit v4 on v1

--- a/solution.py
+++ b/solution.py
@@ -42,20 +42,6 @@
     ordinal = lax.iota(jnp.int32, length)
     signed = jnp.where(ordinal >= length // 2, ordinal - length, ordinal)
     return signed.astype(jnp.float32) / length
-
-
-def kernel_lines(lines, length):
-    ids = np.arange(length)
-    angle = 2.0 * np.pi / length * (ids[None, :] * ids[:, None] % length)
-    grids = jnp.asarray(np.concatenate([np.cos(angle), np.sin(angle)], axis=1), jnp.float32)
-    both = jnp.concatenate([jnp.cos(lines), jnp.sin(lines)], axis=-2)
-    product = jnp.einsum("...f,fn->...n", both, grids, precision=highest)
-    count = lines.shape[-2]
-    cos_cos = product[..., :count, :length]
-    cos_sin = product[..., :count, length:]
-    sin_cos = product[..., count:, :length]
-    sin_sin = product[..., count:, length:]
-    return (cos_cos - sin_sin) / length, (sin_cos + cos_sin) / length
 
 
 def line_allreduce(value, axis, pieces):
@@ -83,56 +69,82 @@
     return jnp.concatenate(done, axis=-2)
 
 
-def toeplitz_kernel(q_ref, o_ref):
-    count = q_ref.shape[0]
-    rows, length = o_ref.shape[1], o_ref.shape[2]
-    for t in range(count):
-        line = jnp.broadcast_to(q_ref[t : t + 1, :], (rows, q_ref.shape[1]))
-        rolled = pltpu.roll(line, MARGIN, 1, stride=1, stride_axis=0)
-        o_ref[t] = rolled[:, :length]
-
-
-def toeplitz(h, rows):
-    count, length = h.shape
-    flipped = jnp.roll(h[:, ::-1], 1, axis=-1)
+def table_kernel(both_ref, grid_ref, rows_ref, cols_ref):
+    angle_count, doubled = both_ref.shape[0], both_ref.shape[1]
+    count = doubled // 2
+    length = both_ref.shape[2]
+    core_size = rows_ref.shape[-1]
+    width = grid_ref.shape[1] // 2
+    column = lax.broadcasted_iota(jnp.int32, (core_size, core_size), 1)
+    low_mask = column >= core_size - MARGIN
+    high_mask = column < MARGIN
+    for a in range(angle_count):
+        product = jnp.dot(
+            both_ref[a], grid_ref[...], precision=highest, preferred_element_type=jnp.float32
+        )
+        cos_cos = product[:count, :width]
+        cos_sin = product[:count, width:]
+        sin_cos = product[count:, :width]
+        sin_sin = product[count:, width:]
+        q_real = (cos_cos + sin_sin) * (1.0 / length)
+        q_imag = (sin_cos - cos_sin) * (1.0 / length)
+
+        def rolled(line, shift):
+            wide = jnp.broadcast_to(line, (core_size, width))
+            return pltpu.roll(wide, shift, 1, stride=1, stride_axis=0)
+
+        for t in range(count):
+            parts = []
+            for q in (q_real, q_imag):
+                line = q[t : t + 1, :]
+                if t < 2:
+                    inner = rolled(line, 0)[:, :core_size]
+                    low = rolled(line, core_size)[:, :core_size]
+                    high = rolled(line, width - core_size)[:, :core_size]
+                    folded = inner + jnp.where(low_mask, low, 0.0) + jnp.where(high_mask, high, 0.0)
+                    parts.append(folded)
+                else:
+                    parts.append(rolled(line, MARGIN)[:, :length])
+            real, imag = parts
+            if t < 2:
+                rows_ref[a, t, 0] = real + imag
+                rows_ref[a, t, 1] = real
+                rows_ref[a, t, 2] = imag
+            else:
+                cols_ref[a, t - 2, 0] = real
+                cols_ref[a, t - 2, 1] = imag - real
+                cols_ref[a, t - 2, 2] = real + imag
+
+
+def build_tables(lines, core_size):
+    angle_count, count, length = lines.shape
     width = ((2 * length + 127) // 128) * 128
-    reps = -(-width // length)
-    doubled = jnp.concatenate([flipped] * reps, axis=-1)[:, :width]
+    ids = np.arange(length)[:, None] * np.arange(width)[None, :] % length
+    angle = 2.0 * np.pi / length * ids
+    grid = jnp.asarray(np.concatenate([np.cos(angle), np.sin(angle)], axis=1), jnp.float32)
+    both = jnp.concatenate([jnp.cos(lines), jnp.sin(lines)], axis=1)
     return pl.pallas_call(
-        toeplitz_kernel,
-        out_shape=jax.ShapeDtypeStruct((count, rows, length), jnp.float32),
-    )(doubled)
-
-
-def fold_rows(table, core_size):
-    inner = table[..., MARGIN : MARGIN + core_size]
-    top = table[..., :MARGIN]
-    bottom = table[..., MARGIN + core_size :]
-    zeros = jnp.zeros(inner.shape[:-1] + (core_size - MARGIN,), inner.dtype)
-    return (
-        inner
-        + jnp.concatenate([zeros, top], axis=-1)
-        + jnp.concatenate([bottom, zeros], axis=-1)
-    )
+        table_kernel,
+        out_shape=(
+            jax.ShapeDtypeStruct((angle_count, 2, 3, core_size, core_size), jnp.float32),
+            jax.ShapeDtypeStruct((angle_count, 2, 3, core_size, length), jnp.float32),
+        ),
+    )(both, grid)
 
 
 def apply_operator(wave, padded_cols, row_table, col_table):
     wave_real = wave[:, 0]
     wave_imag = wave[:, 1]
-    row_real = row_table[:, 0]
-    row_imag = row_table[:, 1]
-    first = contract("ajl,alk->ajk", row_real + row_imag, wave_real)
-    second = contract("ajl,alk->ajk", row_real, wave_imag - wave_real)
-    third = contract("ajl,alk->ajk", row_imag, wave_real + wave_imag)
+    first = contract("ajl,alk->ajk", row_table[:, 0], wave_real)
+    second = contract("ajl,alk->ajk", row_table[:, 1], wave_imag - wave_real)
+    third = contract("ajl,alk->ajk", row_table[:, 2], wave_real + wave_imag)
     half = jnp.stack([first - third, first + second], axis=1)
     half = padded_cols(half)
     half_real = half[:, 0]
     half_imag = half[:, 1]
-    col_real = col_table[:, 0]
-    col_imag = col_table[:, 1]
-    first = contract("ajk,aik->aji", half_real + half_imag, col_real)
-    second = contract("ajk,aik->aji", half_real, col_imag - col_real)
-    third = contract("ajk,aik->aji", half_imag, col_real + col_imag)
+    first = contract("ajk,aik->aji", half_real + half_imag, col_table[:, 0])
+    second = contract("ajk,aik->aji", half_real, col_table[:, 1])
+    third = contract("ajk,aik->aji", half_imag, col_table[:, 2])
     return jnp.stack([first - third, first + second], axis=1)
 
 
@@ -153,13 +165,11 @@
     row_line = base_phase[None, :] - 2.0 * math.pi * frequency[None, :] * shift_rows[:, None]
     col_line = base_phase[None, :] - 2.0 * math.pi * frequency[None, :] * shift_cols[:, None]
     lines = jnp.stack([row_line, -row_line, col_line, -col_line], axis=1)
-    h_real, h_imag = kernel_lines(lines, length)
-    h_all = jnp.stack([h_real, h_imag], axis=2).reshape(angle_count * 8, length)
-    tables = toeplitz(h_all, core_size).reshape(angle_count, 4, 2, core_size, length)
-    rows_fwd = fold_rows(tables[:, 0], core_size)
-    rows_back = fold_rows(tables[:, 1], core_size)
-    cols_fwd = tables[:, 2]
-    cols_back = tables[:, 3]
+    row_tables, col_tables = build_tables(lines, core_size)
+    rows_fwd = row_tables[:, 0]
+    rows_back = row_tables[:, 1]
+    cols_fwd = col_tables[:, 0]
+    cols_back = col_tables[:, 1]
 
     cosine = jnp.cos(phase[0, 0])
     sine_part = jnp.sin(phase[0, 0])

time: 73.7 us -> 68.7 us (0.932)
  other arithmetic: 10.4 us -> 5.97 us
  waiting for transfers between devices: 16.5 us -> 18.5 us
  Pallas kernels: 3.1 us -> 4.79 us
  matrix products: 7.19 us -> 5.54 us
  local copies, waits for them, and re-layouts: 7.22 us -> 5.89 us
  starting transfers between devices: 25.5 us -> 24.2 us
    ppermute x3, starting transfers between devices: 8.87 us -> 3.32 us  [padded_2(): lax.ppermute(lax.slice_in_dim(block, block.shape[dim] - width, None, axis...]
    ppermute x3, starting transfers between devices: 1.43 us -> 5.68 us  [padded_2(): lax.ppermute(lax.slice_in_dim(block, 0, width, axis=dim), axis, backward)]
    add x2 -> x0, other arithmetic: 2.71 us -> none  [fold_rows(): inner + jnp.concatenate([zeros, top], axis=-1)]
    ppermute x4, waiting for transfers between devices: 2.07 us -> 4.37 us  [line_allreduce(): total = total + lax.ppermute(total, axis, pairs)]
    ppermute x3, waiting for transfers between devices: 2.11 us -> 0.07 us  [padded_2(): lax.ppermute(lax.slice_in_dim(block, 0, width, axis=dim), axis, backward)]
    slice x4 -> x0, local copies, waits for them, and re-layouts: 1.82 us -> none  [the longest x2 1.75 us: fold_rows(): top = table[..., :MARGIN]]
    pallas_call x1, Pallas kernels: 3.1 us -> 4.79 us  [build_tables(): pl.pallas_call(table_kernel, out_shape=(jax.ShapeDtypeStruct((angle_count...]
    ppermute x3, waiting for transfers between devices: 0.75 us -> 2.42 us  [padded_2(): lax.ppermute(lax.slice_in_dim(block, block.shape[dim] - width, None, axis...]
  transfers between devices with their start and end apart: 18 -> 18, of which waited for: 9 -> 9; matrix products, arithmetic and copies ran while one was open for 29% -> 21% of each run, Pallas kernels for 4% -> 7%
where the time goes in v4:
time: 68.7 us; the launch traced here: 68.1 us
  starting transfers between devices  24.2 us (35%)
  waiting for transfers between devices  18.5 us (27%)
  other arithmetic  5.97 us (9%)
  local copies, waits for them, and re-layouts  5.89 us (9%)
  matrix products  5.54 us (8%)
  Pallas kernels  4.79 us (7%)
  between operations  3.17 us (5%)
    ppermute x4, waiting for transfers between devices, line_allreduce(): got = lax.ppermute(total, axis, pairs)  11.6 us
    ppermute x4, starting transfers between devices, line_allreduce(): total = total + lax.ppermute(total, axis, pairs)  7.38 us
    ppermute x3, starting transfers between devices, padded_2(): lax.ppermute(lax.slice_in_dim(block, 0, width, axis=dim), axis, backward)  5.68 us
    dot_general x12, matrix products, contract(): return jnp.einsum(form, left, right, precision=wave_precision)  5.54 us
    ppermute x4, starting transfers between devices, line_allreduce(): got = lax.ppermute(total, axis, pairs)  5.17 us
    pallas_call x1, Pallas kernels, build_tables(): pl.pallas_call(table_kernel, out_shape=(jax.ShapeDtypeStruct((angle_count...  4.79 us
    ppermute x4, waiting for transfers between devices, line_allreduce(): total = total + lax.ppermute(total, axis, pairs)  4.37 us
    ppermute x3, starting transfers between devices, padded_2(): lax.ppermute(lax.slice_in_dim(block, block.shape[dim] - width, None, axis...  3.32 us
  transfers between devices with their start and end apart: 18, of which 9 were waited for; matrix products, arithmetic and copies ran while one was open for 21% of the time, Pallas kernels for 7%

profile of v4, /device:TPU:0, one launch (start us, length us, event | category | flops | bytes accessed | tf_op | source)
XLA Modules:
  0.0 68.1 jit_solution(7690153082366443388)
XLA Ops:
  0.6 3.2 %collective-permute-start = (f32[1,1,2,256,256]{4,3,2,1,0:T(8,128)}, f32[1,1,2,256,256]{4,3,2,1,0:T(8,128)}, u32[]{:S(2)}, u32[]{:S(2)}) collective-permute-start(f32[1,1,2,256,256]{4,3,2,1,0:T(8,128)} %param.11), channel_id=1, source_target_pairs={{0,8},{8,16},{16,24},{1,9},{9,17},{17,25},{2,10},{10,18},{18,26},{... | collective-permute-start | bytes 1572872 | tf_op jit(solution)/shard_map/ppermute | solution.py:29
  3.8 1.3 %collective-permute-start.3 = (f32[1,1,2,256,256]{4,3,2,1,0:T(8,128)}, f32[1,1,2,256,256]{4,3,2,1,0:T(8,128)}, u32[]{:S(2)}, u32[]{:S(2)}) collective-permute-start(f32[1,1,2,256,256]{4,3,2,1,0:T(8,128)} %param.12), channel_id=1, source_target_pairs={{8,0},{16,8},{24,16},{9,1},{17,9},{25,17},{10,2},{18,10},{26,18},{... | collective-permute-start | bytes 1572872 | tf_op jit(solution)/shard_map/ppermute | solution.py:32
  5.8 1.3 %fusion.59 = (s32[1,1]{1,0:T(1,128)}, s32[1,1]{1,0:T(1,128)}) fusion(s32[1,2]{1,0:T(1,128)} %param.16), kind=kLoop, calls=%fused_computation.127 | loop fusion | bytes 16 | tf_op jit(solution)/shard_map/slice | solution.py:163
  9.2 4.8 %shard_map.112 = (f32[1,2,3,256,256]{4,3,2,1,0:T(8,128)}, f32[1,2,3,256,320]{4,3,2,1,0:T(8,128)}) custom-call(f32[1,8,320]{2,1,0:T(8,128)} %pad_maximum_fusion.7.both_ref, f32[320,1280]{1,0:T(8,128)} %constant.46.clone.grid_ref), custom_call_target="tpu_custom_call" | custom-call | tf_op jit(solution)/shard_map/pallas_call | solution.py:126
  14.0 1.5 %slice_bitcast_fusion.2 = (f32[1,3,256,256]{3,2,1,0:T(8,128)S(1)}, f32[1,3,256,256]{3,2,1,0:T(8,128)S(1)}) fusion(f32[1,2,3,256,256]{4,3,2,1,0:T(8,128)} %get-tuple-element.5), kind=kLoop, calls=%fused_computation.16 | loop fusion | bytes 3145728 | tf_op jit(solution)/shard_map/squeeze | solution.py:170
  15.5 1.0 %fusion.58 = (f32[1,1,256,256]{3,2,1,0:T(8,128)S(1)}, f32[1,1,256,256]{3,2,1,0:T(8,128)S(1)}) fusion(f32[1,1,256,256]{3,2,1,0:T(8,128)S(1)} %copy-done.2), kind=kLoop, calls=%fused_computation.126 | loop fusion | bytes 786432 | tf_op jit(solution)/shard_map/cos | solution.py:174
  16.7 1.8 %slice_bitcast_fusion = (f32[1,3,256,320]{3,2,1,0:T(8,128)S(1)}, f32[1,3,256,320]{3,2,1,0:T(8,128)S(1)}) fusion(f32[1,2,3,256,320]{4,3,2,1,0:T(8,128)} %get-tuple-element.6), kind=kLoop, calls=%fused_computation | loop fusion | bytes 3932160 | tf_op jit(solution)/shard_map/squeeze | solution.py:172
  18.6 1.1 %fusion.6 = f32[1,2,256,256]{3,2,1,0:T(8,128)S(1)} fusion(f32[1,1,2,256,256]{4,3,2,1,0:T(8,128)} %collective-permute-done, bf16[2,256,256]{2,1,0:T(8,128)(2,1)S(1)} %copy-done.3, pred[]{:T(512)} %eq.8), kind=kLoop, calls=%fused_computation.31 | loop fusion | flops 262144 | bytes 1310721 | tf_op jit(solution)/shard_map/jit(_where)/select_n | solution.py:179
  21.2 1.1 %bitcast_select_fusion = f32[1,2,256,256]{3,2,1,0:T(8,128)S(1)} fusion(f32[1,1,2,256,256]{4,3,2,1,0:T(8,128)} %collective-permute-done.3, f32[256,256]{1,0:T(8,128)S(1)} %fusion.28, pred[]{:T(512)S(6)} %eq.9, bf16[1,2,1,2,256,256]{5,4,3,2,1,0:T(8,128)(2,1)S(1)} %copy-done.1), kind=kLoop, calls=%fused_computation.29 | loop fusion | flops 393216 | bytes 1572865 | tf_op jit(solution)/shard_map/jit(_where)/select_n | solution.py:183
  23.5 2.4 %collective-permute-start.5 = (f32[1,2,256,32]{2,3,1,0:T(8,128)S(1)}, f32[1,2,256,32]{2,3,1,0:T(8,128)S(1)}, u32[]{:S(2)}, u32[]{:S(2)}) collective-permute-start(f32[1,2,256,32]{2,3,1,0:T(8,128)S(1)} %get-tuple-element.26), channel_id=1, source_target_pairs={{4,0},{0,4},{5,1},{1,5},{6,2},{2,6},{7,3},{3,7},{12,8},{8,12},{13,... | collective-permute-start | bytes 196616 | tf_op jit(solution)/shard_map/ppermute | solution.py:32
  26.0 2.0 %collective-permute-start.2 = (f32[1,2,256,32]{2,3,1,0:T(8,128)S(1)}, f32[1,2,256,32]{2,3,1,0:T(8,128)S(1)}, u32[]{:S(2)}, u32[]{:S(2)}) collective-permute-start(f32[1,2,256,32]{2,3,1,0:T(8,128)S(1)} %get-tuple-element.28), channel_id=1, source_target_pairs={{4,0},{0,4},{5,1},{1,5},{6,2},{2,6},{7,3},{3,7},{12,8},{8,12},{13,... | collective-permute-start | bytes 196616 | tf_op jit(solution)/shard_map/ppermute | solution.py:32
  28.1 2.4 %collective-permute-done.4 = f32[1,2,256,32]{2,3,1,0:T(8,128)S(1)} collective-permute-done((f32[1,2,256,32]{2,3,1,0:T(8,128)S(1)}, f32[1,2,256,32]{2,3,1,0:T(8,128)S(1)}, u32[]{:S(2)}, u32[]{:S(2)}) %collective-permute-start.4) | collective-permute-done | bytes 65568 | tf_op jit(solution)/shard_map/ppermute | solution.py:29
  32.3 3.5 %collective-permute-start.15 = (f32[2,64,256]{2,1,0:T(8,128)S(1)}, f32[2,64,256]{2,1,0:T(8,128)S(1)}, u32[]{:S(2)}, u32[]{:S(2)}) collective-permute-start(f32[2,64,256]{2,1,0:T(8,128)S(1)} %get-tuple-element.19), channel_id=1, source_target_pairs={{0,1},{3,2},{4,5},{7,6},{8,9},{11,10},{12,13},{15,14},{16,17},{19,... | collective-permute-start | bytes 393224 | tf_op jit(solution)/shard_map/ppermute | solution.py:61
  35.8 1.3 %collective-permute-start.12 = (f32[2,64,256]{2,1,0:T(8,128)S(1)}, f32[2,64,256]{2,1,0:T(8,128)S(1)}, u32[]{:S(2)}, u32[]{:S(2)}) collective-permute-start(f32[2,64,256]{2,1,0:T(8,128)S(1)} %get-tuple-element.20), channel_id=1, source_target_pairs={{0,1},{3,2},{4,5},{7,6},{8,9},{11,10},{12,13},{15,14},{16,17},{19,... | collective-permute-start | bytes 393224 | tf_op jit(solution)/shard_map/ppermute | solution.py:61
  37.1 1.3 %collective-permute-start.9 = (f32[2,64,256]{2,1,0:T(8,128)S(1)}, f32[2,64,256]{2,1,0:T(8,128)S(1)}, u32[]{:S(2)}, u32[]{:S(2)}) collective-permute-start(f32[2,64,256]{2,1,0:T(8,128)S(1)} %get-tuple-element.18), channel_id=1, source_target_pairs={{0,1},{3,2},{4,5},{7,6},{8,9},{11,10},{12,13},{15,14},{16,17},{19,... | collective-permute-start | bytes 393224 | tf_op jit(solution)/shard_map/ppermute | solution.py:61
  38.4 1.3 %collective-permute-start.6 = (f32[2,64,256]{2,1,0:T(8,128)S(1)}, f32[2,64,256]{2,1,0:T(8,128)S(1)}, u32[]{:S(2)}, u32[]{:S(2)}) collective-permute-start(f32[2,64,256]{2,1,0:T(8,128)S(1)} %get-tuple-element.17), channel_id=1, source_target_pairs={{0,1},{3,2},{4,5},{7,6},{8,9},{11,10},{12,13},{15,14},{16,17},{19,... | collective-permute-start | bytes 393224 | tf_op jit(solution)/shard_map/ppermute | solution.py:61
  40.9 0.7 collective-permute-start.16
  42.5 0.7 collective-permute-start.13
  43.2 2.1 %collective-permute-done.9 = f32[2,64,256]{2,1,0:T(8,128)S(1)} collective-permute-done((f32[2,64,256]{2,1,0:T(8,128)S(1)}, f32[2,64,256]{2,1,0:T(8,128)S(1)}, u32[]{:S(2)}, u32[]{:S(2)}) %collective-permute-start.9) | collective-permute-done | bytes 131104 | tf_op jit(solution)/shard_map/ppermute | solution.py:61
  45.3 0.7 collective-permute-start.10
  46.0 1.9 %collective-permute-done.6 = f32[2,64,256]{2,1,0:T(8,128)S(1)} collective-permute-done((f32[2,64,256]{2,1,0:T(8,128)S(1)}, f32[2,64,256]{2,1,0:T(8,128)S(1)}, u32[]{:S(2)}, u32[]{:S(2)}) %collective-permute-start.6) | collective-permute-done | bytes 131104 | tf_op jit(solution)/shard_map/ppermute | solution.py:61
  48.6 1.3 %collective-permute-start.17 = (f32[2,64,256]{2,1,0:T(8,128)S(1)}, f32[2,64,256]{2,1,0:T(8,128)S(1)}, u32[]{:S(2)}, u32[]{:S(2)}) collective-permute-start(f32[2,64,256]{2,1,0:T(8,128)S(1)} %add.208), channel_id=1, source_target_pairs={{1,0},{2,3},{5,4},{6,7},{9,8},{10,11},{13,12},{14,15},{17,16},{18,... | collective-permute-start | bytes 393224 | tf_op jit(solution)/shard_map/ppermute | solution.py:65
  49.9 0.8 %maximum_bitcast_fusion = f32[1,1,2,256,256]{4,3,2,1,0:T(8,128)} fusion(f32[1,1,256,256]{3,2,1,0:T(8,128)S(1)} %fusion.2, f32[1,1,256,256]{3,2,1,0:T(8,128)S(1)} %fusion.3), kind=kLoop, calls=%fused_computation.26 | loop fusion | flops 131072 | bytes 1048576 | tf_op jit(solution)/shard_map/broadcast_in_dim | solution.py:209
  50.7 0.8 %maximum_bitcast_fusion.1 = f32[1,1,2,256,256]{4,3,2,1,0:T(8,128)} fusion(f32[1,1,256,256]{3,2,1,0:T(8,128)S(1)} %get-tuple-element.21, f32[1,1,256,256]{3,2,1,0:T(8,128)S(1)} %get-tuple-element.22), kind=kLoop, calls=%fused_computation.27 | loop fusion | flops 131072 | bytes 1048576 | tf_op jit(solution)/shard_map/broadcast_in_dim | solution.py:209
  51.6 1.3 %collective-permute-start.14 = (f32[2,64,256]{2,1,0:T(8,128)S(1)}, f32[2,64,256]{2,1,0:T(8,128)S(1)}, u32[]{:S(2)}, u32[]{:S(2)}) collective-permute-start(f32[2,64,256]{2,1,0:T(8,128)S(1)} %add.206), channel_id=1, source_target_pairs={{1,0},{2,3},{5,4},{6,7},{9,8},{10,11},{13,12},{14,15},{17,16},{18,... | collective-permute-start | bytes 393224 | tf_op jit(solution)/shard_map/ppermute | solution.py:65
  52.9 1.3 %collective-permute-start.11 = (f32[2,64,256]{2,1,0:T(8,128)S(1)}, f32[2,64,256]{2,1,0:T(8,128)S(1)}, u32[]{:S(2)}, u32[]{:S(2)}) collective-permute-start(f32[2,64,256]{2,1,0:T(8,128)S(1)} %add.204), channel_id=1, source_target_pairs={{1,0},{2,3},{5,4},{6,7},{9,8},{10,11},{13,12},{14,15},{17,16},{18,... | collective-permute-start | bytes 393224 | tf_op jit(solution)/shard_map/ppermute | solution.py:65
  54.2 1.3 %collective-permute-start.8 = (f32[2,64,256]{2,1,0:T(8,128)S(1)}, f32[2,64,256]{2,1,0:T(8,128)S(1)}, u32[]{:S(2)}, u32[]{:S(2)}) collective-permute-start(f32[2,64,256]{2,1,0:T(8,128)S(1)} %add.202), channel_id=1, source_target_pairs={{1,0},{2,3},{5,4},{6,7},{9,8},{10,11},{13,12},{14,15},{17,16},{18,... | collective-permute-start | bytes 393224 | tf_op jit(solution)/shard_map/ppermute | solution.py:65
  55.5 3.4 %collective-permute-done.17 = f32[2,64,256]{2,1,0:T(8,128)S(1)} collective-permute-done((f32[2,64,256]{2,1,0:T(8,128)S(1)}, f32[2,64,256]{2,1,0:T(8,128)S(1)}, u32[]{:S(2)}, u32[]{:S(2)}) %collective-permute-start.17) | collective-permute-done | bytes 131104 | tf_op jit(solution)/shard_map/ppermute | solution.py:65
  59.0 4.3 %collective-permute-done.14 = f32[2,64,256]{2,1,0:T(8,128)S(1)} collective-permute-done((f32[2,64,256]{2,1,0:T(8,128)S(1)}, f32[2,64,256]{2,1,0:T(8,128)S(1)}, u32[]{:S(2)}, u32[]{:S(2)}) %collective-permute-start.14) | collective-permute-done | bytes 131104 | tf_op jit(solution)/shard_map/ppermute | solution.py:65
  63.2 2.5 %collective-permute-done.11 = f32[2,64,256]{2,1,0:T(8,128)S(1)} collective-permute-done((f32[2,64,256]{2,1,0:T(8,128)S(1)}, f32[2,64,256]{2,1,0:T(8,128)S(1)}, u32[]{:S(2)}, u32[]{:S(2)}) %collective-permute-start.11) | collective-permute-done | bytes 131104 | tf_op jit(solution)/shard_map/ppermute | solution.py:65
  65.8 1.4 %collective-permute-done.8 = f32[2,64,256]{2,1,0:T(8,128)S(1)} collective-permute-done((f32[2,64,256]{2,1,0:T(8,128)S(1)}, f32[2,64,256]{2,1,0:T(8,128)S(1)}, u32[]{:S(2)}, u32[]{:S(2)}) %collective-permute-start.8) | collective-permute-done | bytes 131104 | tf_op jit(solution)/shard_map/ppermute | solution.py:65
  67.2 0.8 %maximum_bitcast_fusion.2 = f32[1,1,2,256,256]{4,3,2,1,0:T(8,128)} fusion(f32[2,64,256]{2,1,0:T(8,128)S(1)} %broadcast_select_fusion, f32[2,64,256]{2,1,0:T(8,128)S(1)} %broadcast_select_fusion.1, f32[2,64,256]{2,1,0:T(8,128)S(1)} %broadcast_select_fusion.2, f32[2,64,256]{2,1,0:T(8,128)S(1)} %broadcast_select_fusion.3), kind=kLoop, calls=%fused_computation.28 | loop fusion | flops 393216 | bytes 1048576 | tf_op jit(solution)/shard_map/broadcast_in_dim | solution.py:209
  (60 shorter events, 8.4 us)
Async XLA Ops:
  0.6 17.9 %collective-permute-start = (f32[1,1,2,256,256]{4,3,2,1,0:T(8,128)}, f32[1,1,2,256,256]{4,3,2,1,0:T(8,128)}, u32[]{:S(2)}, u32[]{:S(2)}) collective-permute-start(f32[1,1,2,256,256]{4,3,2,1,0:T(8,128)} %param.11), channel_id=1, source_target_pairs={{0,8},{8,16},{16,24},{1,9},{9,17},{17,25},{2,10},{10,18},{18,26},{... | collective-permute-start | bytes 1572872 | tf_op jit(solution)/shard_map/ppermute | solution.py:29
  3.8 17.2 %collective-permute-start.3 = (f32[1,1,2,256,256]{4,3,2,1,0:T(8,128)}, f32[1,1,2,256,256]{4,3,2,1,0:T(8,128)}, u32[]{:S(2)}, u32[]{:S(2)}) collective-permute-start(f32[1,1,2,256,256]{4,3,2,1,0:T(8,128)} %param.12), channel_id=1, source_target_pairs={{8,0},{16,8},{24,16},{9,1},{17,9},{25,17},{10,2},{18,10},{26,18},{... | collective-permute-start | bytes 1572872 | tf_op jit(solution)/shard_map/ppermute | solution.py:32
  14.0 1.6 %copy-start.2 = (f32[1,1,256,256]{3,2,1,0:T(8,128)S(1)}, f32[1,1,256,256]{3,2,1,0:T(8,128)}, u32[]{:S(2)}) copy-start(f32[1,1,256,256]{3,2,1,0:T(8,128)} %param.10) | copy-start | bytes 786436
  14.0 2.5 %copy-start = (bf16[1,2,1,2,256,256]{5,4,3,2,1,0:T(8,128)(2,1)S(1)}, bf16[1,2,1,2,256,256]{5,4,3,2,1,0:T(8,128)(2,1)}, u32[]{:S(2)}) copy-start(bf16[1,2,1,2,256,256]{5,4,3,2,1,0:T(8,128)(2,1)} %param.13) | copy-start | bytes 1572868
  15.5 1.1 %copy-start.4 = (f32[1,256,256]{2,1,0:T(8,128)S(1)}, f32[1,256,256]{2,1,0:T(8,128)}, u32[]{:S(2)}) copy-start(f32[1,256,256]{2,1,0:T(8,128)} %param.14) | copy-start | bytes 786436
  16.7 1.9 %copy-start.3 = (bf16[2,256,256]{2,1,0:T(8,128)(2,1)S(1)}, bf16[2,256,256]{2,1,0:T(8,128)(2,1)}, u32[]{:S(2)}) copy-start(bf16[2,256,256]{2,1,0:T(8,128)(2,1)} %param.9) | copy-start | bytes 786436
  20.1 1.0 %copy-start.1 = (bf16[1,2,1,2,256,256]{5,4,3,2,1,0:T(8,128)(2,1)S(1)}, bf16[1,2,1,2,256,256]{5,4,3,2,1,0:T(8,128)(2,1)}, u32[]{:S(2)}) copy-start(bf16[1,2,1,2,256,256]{5,4,3,2,1,0:T(8,128)(2,1)} %param.13) | copy-start | bytes 1572868
  23.5 4.6 %collective-permute-start.5 = (f32[1,2,256,32]{2,3,1,0:T(8,128)S(1)}, f32[1,2,256,32]{2,3,1,0:T(8,128)S(1)}, u32[]{:S(2)}, u32[]{:S(2)}) collective-permute-start(f32[1,2,256,32]{2,3,1,0:T(8,128)S(1)} %get-tuple-element.26), channel_id=1, source_target_pairs={{4,0},{0,4},{5,1},{1,5},{6,2},{2,6},{7,3},{3,7},{12,8},{8,12},{13,... | collective-permute-start | bytes 196616 | tf_op jit(solution)/shard_map/ppermute | solution.py:32
  25.9 4.7 %collective-permute-start.4 = (f32[1,2,256,32]{2,3,1,0:T(8,128)S(1)}, f32[1,2,256,32]{2,3,1,0:T(8,128)S(1)}, u32[]{:S(2)}, u32[]{:S(2)}) collective-permute-start(f32[1,2,256,32]{2,3,1,0:T(8,128)S(1)} %get-tuple-element.25), channel_id=1, source_target_pairs={{0,4},{4,0},{1,5},{5,1},{2,6},{6,2},{3,7},{7,3},{8,12},{12,8},{9,1... | collective-permute-start | bytes 196616 | tf_op jit(solution)/shard_map/ppermute | solution.py:29
  26.0 12.4 %collective-permute-start.2 = (f32[1,2,256,32]{2,3,1,0:T(8,128)S(1)}, f32[1,2,256,32]{2,3,1,0:T(8,128)S(1)}, u32[]{:S(2)}, u32[]{:S(2)}) collective-permute-start(f32[1,2,256,32]{2,3,1,0:T(8,128)S(1)} %get-tuple-element.28), channel_id=1, source_target_pairs={{4,0},{0,4},{5,1},{1,5},{6,2},{2,6},{7,3},{3,7},{12,8},{8,12},{13,... | collective-permute-start | bytes 196616 | tf_op jit(solution)/shard_map/ppermute | solution.py:32
  28.0 11.7 %collective-permute-start.1 = (f32[1,2,256,32]{2,3,1,0:T(8,128)S(1)}, f32[1,2,256,32]{2,3,1,0:T(8,128)S(1)}, u32[]{:S(2)}, u32[]{:S(2)}) collective-permute-start(f32[1,2,256,32]{2,3,1,0:T(8,128)S(1)} %get-tuple-element.27), channel_id=1, source_target_pairs={{0,4},{4,0},{1,5},{5,1},{2,6},{6,2},{3,7},{7,3},{8,12},{12,8},{9,1... | collective-permute-start | bytes 196616 | tf_op jit(solution)/shard_map/ppermute | solution.py:29
  32.3 8.5 %collective-permute-start.15 = (f32[2,64,256]{2,1,0:T(8,128)S(1)}, f32[2,64,256]{2,1,0:T(8,128)S(1)}, u32[]{:S(2)}, u32[]{:S(2)}) collective-permute-start(f32[2,64,256]{2,1,0:T(8,128)S(1)} %get-tuple-element.19), channel_id=1, source_target_pairs={{0,1},{3,2},{4,5},{7,6},{8,9},{11,10},{12,13},{15,14},{16,17},{19,... | collective-permute-start | bytes 393224 | tf_op jit(solution)/shard_map/ppermute | solution.py:61
  35.8 6.7 %collective-permute-start.12 = (f32[2,64,256]{2,1,0:T(8,128)S(1)}, f32[2,64,256]{2,1,0:T(8,128)S(1)}, u32[]{:S(2)}, u32[]{:S(2)}) collective-permute-start(f32[2,64,256]{2,1,0:T(8,128)S(1)} %get-tuple-element.20), channel_id=1, source_target_pairs={{0,1},{3,2},{4,5},{7,6},{8,9},{11,10},{12,13},{15,14},{16,17},{19,... | collective-permute-start | bytes 393224 | tf_op jit(solution)/shard_map/ppermute | solution.py:61
  37.1 8.2 %collective-permute-start.9 = (f32[2,64,256]{2,1,0:T(8,128)S(1)}, f32[2,64,256]{2,1,0:T(8,128)S(1)}, u32[]{:S(2)}, u32[]{:S(2)}) collective-permute-start(f32[2,64,256]{2,1,0:T(8,128)S(1)} %get-tuple-element.18), channel_id=1, source_target_pairs={{0,1},{3,2},{4,5},{7,6},{8,9},{11,10},{12,13},{15,14},{16,17},{19,... | collective-permute-start | bytes 393224 | tf_op jit(solution)/shard_map/ppermute | solution.py:61
  38.4 9.4 %collective-permute-start.6 = (f32[2,64,256]{2,1,0:T(8,128)S(1)}, f32[2,64,256]{2,1,0:T(8,128)S(1)}, u32[]{:S(2)}, u32[]{:S(2)}) collective-permute-start(f32[2,64,256]{2,1,0:T(8,128)S(1)} %get-tuple-element.17), channel_id=1, source_target_pairs={{0,1},{3,2},{4,5},{7,6},{8,9},{11,10},{12,13},{15,14},{16,17},{19,... | collective-permute-start | bytes 393224 | tf_op jit(solution)/shard_map/ppermute | solution.py:61
  40.9 7.7 %collective-permute-start.16 = (f32[2,64,256]{2,1,0:T(8,128)S(1)}, f32[2,64,256]{2,1,0:T(8,128)S(1)}, u32[]{:S(2)}, u32[]{:S(2)}) collective-permute-start(f32[2,64,256]{2,1,0:T(8,128)S(1)} %add.207), channel_id=1, source_target_pairs={{1,2},{2,1},{5,6},{6,5},{9,10},{10,9},{13,14},{14,13},{17,18},{18,... | collective-permute-start | bytes 393224 | tf_op jit(solution)/shard_map/ppermute | solution.py:62
  42.5 9.0 %collective-permute-start.13 = (f32[2,64,256]{2,1,0:T(8,128)S(1)}, f32[2,64,256]{2,1,0:T(8,128)S(1)}, u32[]{:S(2)}, u32[]{:S(2)}) collective-permute-start(f32[2,64,256]{2,1,0:T(8,128)S(1)} %add.205), channel_id=1, source_target_pairs={{1,2},{2,1},{5,6},{6,5},{9,10},{10,9},{13,14},{14,13},{17,18},{18,... | collective-permute-start | bytes 393224 | tf_op jit(solution)/shard_map/ppermute | solution.py:62
  45.3 7.6 %collective-permute-start.10 = (f32[2,64,256]{2,1,0:T(8,128)S(1)}, f32[2,64,256]{2,1,0:T(8,128)S(1)}, u32[]{:S(2)}, u32[]{:S(2)}) collective-permute-start(f32[2,64,256]{2,1,0:T(8,128)S(1)} %add.203), channel_id=1, source_target_pairs={{1,2},{2,1},{5,6},{6,5},{9,10},{10,9},{13,14},{14,13},{17,18},{18,... | collective-permute-start | bytes 393224 | tf_op jit(solution)/shard_map/ppermute | solution.py:62
  47.9 6.3 %collective-permute-start.7 = (f32[2,64,256]{2,1,0:T(8,128)S(1)}, f32[2,64,256]{2,1,0:T(8,128)S(1)}, u32[]{:S(2)}, u32[]{:S(2)}) collective-permute-start(f32[2,64,256]{2,1,0:T(8,128)S(1)} %add.201), channel_id=1, source_target_pairs={{1,2},{2,1},{5,6},{6,5},{9,10},{10,9},{13,14},{14,13},{17,18},{18,... | collective-permute-start | bytes 393224 | tf_op jit(solution)/shard_map/ppermute | solution.py:62
  48.6 10.4 %collective-permute-start.17 = (f32[2,64,256]{2,1,0:T(8,128)S(1)}, f32[2,64,256]{2,1,0:T(8,128)S(1)}, u32[]{:S(2)}, u32[]{:S(2)}) collective-permute-start(f32[2,64,256]{2,1,0:T(8,128)S(1)} %add.208), channel_id=1, source_target_pairs={{1,0},{2,3},{5,4},{6,7},{9,8},{10,11},{13,12},{14,15},{17,16},{18,... | collective-permute-start | bytes 393224 | tf_op jit(solution)/shard_map/ppermute | solution.py:65
  51.6 11.7 %collective-permute-start.14 = (f32[2,64,256]{2,1,0:T(8,128)S(1)}, f32[2,64,256]{2,1,0:T(8,128)S(1)}, u32[]{:S(2)}, u32[]{:S(2)}) collective-permute-start(f32[2,64,256]{2,1,0:T(8,128)S(1)} %add.206), channel_id=1, source_target_pairs={{1,0},{2,3},{5,4},{6,7},{9,8},{10,11},{13,12},{14,15},{17,16},{18,... | collective-permute-start | bytes 393224 | tf_op jit(solution)/shard_map/ppermute | solution.py:65
  52.9 12.9 %collective-permute-start.11 = (f32[2,64,256]{2,1,0:T(8,128)S(1)}, f32[2,64,256]{2,1,0:T(8,128)S(1)}, u32[]{:S(2)}, u32[]{:S(2)}) collective-permute-start(f32[2,64,256]{2,1,0:T(8,128)S(1)} %add.204), channel_id=1, source_target_pairs={{1,0},{2,3},{5,4},{6,7},{9,8},{10,11},{13,12},{14,15},{17,16},{18,... | collective-permute-start | bytes 393224 | tf_op jit(solution)/shard_map/ppermute | solution.py:65
  54.2 13.0 %collective-permute-start.8 = (f32[2,64,256]{2,1,0:T(8,128)S(1)}, f32[2,64,256]{2,1,0:T(8,128)S(1)}, u32[]{:S(2)}, u32[]{:S(2)}) collective-permute-start(f32[2,64,256]{2,1,0:T(8,128)S(1)} %add.202), channel_id=1, source_target_pairs={{1,0},{2,3},{5,4},{6,7},{9,8},{10,11},{13,12},{14,15},{17,16},{18,... | collective-permute-start | bytes 393224 | tf_op jit(solution)/shard_map/ppermute | solution.py:65

commit v5 on v4

--- a/solution.py
+++ b/solution.py
@@ -48,24 +48,67 @@
     count = lax.axis_size(axis)
     if count == 1:
         return value
-    if count % 2:
+    if count % 2 or count > 8:
         return lax.psum(value, axis)
     half = count // 2
     index = lax.axis_index(axis)
     chunks = jnp.split(value, pieces, axis=-2)
+    zero = jnp.zeros_like(chunks[0])
+
+    def own(c):
+        return chunks[c] if 0 <= c < pieces else zero
+
+    def by_role(candidates):
+        picked = candidates[-1]
+        for role in range(count - 2, -1, -1):
+            picked = jnp.where(index == role, candidates[role], picked)
+        return picked
+
+    from_left = []
+    from_right = []
+
+    def got(buffers, t):
+        return buffers[t] if t >= 0 else zero
+
+    right_pairs = [(j, j + 1) for j in range(count - 1)]
+    left_pairs = [(j + 1, j) for j in range(count - 1)]
+    for t in range(pieces + count - 2):
+        rightward = []
+        leftward = []
+        for role in range(count):
+            c = t - role
+            if role < half:
+                rightward.append(own(c) + got(from_left, t - 1))
+            elif role == half:
+                rightward.append(got(from_left, t - 1) + (own(c) + got(from_right, t - 2)))
+            else:
+                rightward.append(got(from_left, t - 1))
+            c = t - (count - 1 - role)
+            if role >= half:
+                leftward.append(own(c) + got(from_right, t - 1))
+            elif role == half - 1:
+                leftward.append((own(c) + got(from_left, t - 2)) + got(from_right, t - 1))
+            else:
+                leftward.append(got(from_right, t - 1))
+        from_left.append(lax.ppermute(by_role(rightward), axis, right_pairs))
+        from_right.append(lax.ppermute(by_role(leftward), axis, left_pairs))
     done = []
-    for chunk in chunks:
-        total = chunk
-        for step in range(half - 1):
-            pairs = [(step, step + 1), (count - 1 - step, count - 2 - step)]
-            total = total + lax.ppermute(total, axis, pairs)
-        total = total + lax.ppermute(total, axis, [(half - 1, half), (half, half - 1)])
-        for step in range(half - 1):
-            pairs = [(half - 1 - step, half - 2 - step), (half + step, half + 1 + step)]
-            got = lax.ppermute(total, axis, pairs)
-            target = (index == half - 2 - step) | (index == half + 1 + step)
-            total = jnp.where(target, got, total)
-        done.append(total)
+    for c in range(pieces):
+        finals = []
+        for role in range(count):
+            if role < half - 1:
+                finals.append(got(from_right, c + count - 2 - role))
+            elif role == half - 1:
+                finals.append(
+                    (own(c) + got(from_left, c + half - 2)) + got(from_right, c + half - 1)
+                )
+            elif role == half:
+                finals.append(
+                    got(from_left, c + half - 1) + (own(c) + got(from_right, c + half - 2))
+                )
+            else:
+                finals.append(got(from_left, c + role - 1))
+        done.append(by_role(finals))
     return jnp.concatenate(done, axis=-2)
 
 

time: 68.7 us -> 93.3 us (1.36)
  the two profiles are of different devices: /device:TPU:0 before, /device:TPU:22 now
where the time goes in v5:
time: 93.3 us; the launch traced here: 92.6 us
  starting transfers between devices  45 us (48%)
  waiting for transfers between devices  22.3 us (24%)
  other arithmetic  6.17 us (7%)
  local copies, waits for them, and re-layouts  5.69 us (6%)
  matrix products  5.52 us (6%)
  Pallas kernels  4.79 us (5%)
  between operations  3.13 us (3%)
    ppermute x6, starting transfers between devices, line_allreduce(): from_left.append(lax.ppermute(by_role(rightward), axis, right_pairs))  17.8 us
    ppermute x6, starting transfers between devices, line_allreduce(): from_right.append(lax.ppermute(by_role(leftward), axis, left_pairs))  17.5 us
    ppermute x6, waiting for transfers between devices, line_allreduce(): from_left.append(lax.ppermute(by_role(rightward), axis, right_pairs))  11.3 us
    ppermute x6, waiting for transfers between devices, line_allreduce(): from_right.append(lax.ppermute(by_role(leftward), axis, left_pairs))  9.66 us
    ppermute x3, starting transfers between devices, padded_2(): lax.ppermute(lax.slice_in_dim(block, 0, width, axis=dim), axis, backward)  5.62 us
    dot_general x12, matrix products, contract(): return jnp.einsum(form, left, right, precision=wave_precision)  5.52 us
    pallas_call x1, Pallas kernels, build_tables(): pl.pallas_call(table_kernel, out_shape=(jax.ShapeDtypeStruct((angle_count...  4.79 us
    ppermute x3, starting transfers between devices, padded_2(): lax.ppermute(lax.slice_in_dim(block, block.shape[dim] - width, None, axis...  4.13 us
  transfers between devices with their start and end apart: 18, of which 12 were waited for; matrix products, arithmetic and copies ran while one was open for 16% of the time, Pallas kernels for 5%

profile of v5, /device:TPU:22, one launch (start us, length us, event | category | flops | bytes accessed | tf_op | source)
XLA Modules:
  0.0 92.6 jit_solution(10345017712223833730)
XLA Ops:
  0.6 1.9 %collective-permute-start = (f32[1,1,2,256,256]{4,3,2,1,0:T(8,128)}, f32[1,1,2,256,256]{4,3,2,1,0:T(8,128)}, u32[]{:S(2)}, u32[]{:S(2)}) collective-permute-start(f32[1,1,2,256,256]{4,3,2,1,0:T(8,128)} %param.11), channel_id=1, source_target_pairs={{0,8},{8,16},{16,24},{1,9},{9,17},{17,25},{2,10},{10,18},{18,26},{... | collective-permute-start | bytes 1572872 | tf_op jit(solution)/shard_map/ppermute | solution.py:29
  2.6 3.6 %collective-permute-start.3 = (f32[1,1,2,256,256]{4,3,2,1,0:T(8,128)}, f32[1,1,2,256,256]{4,3,2,1,0:T(8,128)}, u32[]{:S(2)}, u32[]{:S(2)}) collective-permute-start(f32[1,1,2,256,256]{4,3,2,1,0:T(8,128)} %param.12), channel_id=1, source_target_pairs={{8,0},{16,8},{24,16},{9,1},{17,9},{25,17},{10,2},{18,10},{26,18},{... | collective-permute-start | bytes 1572872 | tf_op jit(solution)/shard_map/ppermute | solution.py:32
  6.9 1.3 %fusion.62 = (s32[1,1]{1,0:T(1,128)}, s32[1,1]{1,0:T(1,128)}) fusion(s32[1,2]{1,0:T(1,128)} %param.16), kind=kLoop, calls=%fused_computation.144 | loop fusion | bytes 16 | tf_op jit(solution)/shard_map/slice | solution.py:206
  10.3 4.8 %shard_map.112 = (f32[1,2,3,256,256]{4,3,2,1,0:T(8,128)}, f32[1,2,3,256,320]{4,3,2,1,0:T(8,128)}) custom-call(f32[1,8,320]{2,1,0:T(8,128)} %pad_maximum_fusion.7.both_ref, f32[320,1280]{1,0:T(8,128)} %constant.52.clone.grid_ref), custom_call_target="tpu_custom_call" | custom-call | tf_op jit(solution)/shard_map/pallas_call | solution.py:169
  15.1 1.5 %slice_bitcast_fusion.2 = (f32[1,3,256,256]{3,2,1,0:T(8,128)S(1)}, f32[1,3,256,256]{3,2,1,0:T(8,128)S(1)}) fusion(f32[1,2,3,256,256]{4,3,2,1,0:T(8,128)} %get-tuple-element.5), kind=kLoop, calls=%fused_computation.16 | loop fusion | bytes 3145728 | tf_op jit(solution)/shard_map/squeeze | solution.py:213
  16.7 1.0 %fusion.61 = (f32[1,1,256,256]{3,2,1,0:T(8,128)S(1)}, f32[1,1,256,256]{3,2,1,0:T(8,128)S(1)}) fusion(f32[1,1,256,256]{3,2,1,0:T(8,128)S(1)} %copy-done.2), kind=kLoop, calls=%fused_computation.143 | loop fusion | bytes 786432 | tf_op jit(solution)/shard_map/cos | solution.py:217
  17.8 1.8 %slice_bitcast_fusion = (f32[1,3,256,320]{3,2,1,0:T(8,128)S(1)}, f32[1,3,256,320]{3,2,1,0:T(8,128)S(1)}) fusion(f32[1,2,3,256,320]{4,3,2,1,0:T(8,128)} %get-tuple-element.6), kind=kLoop, calls=%fused_computation | loop fusion | bytes 3932160 | tf_op jit(solution)/shard_map/squeeze | solution.py:215
  19.7 1.1 %bitcast_select_fusion = f32[1,2,256,256]{3,2,1,0:T(8,128)S(1)} fusion(f32[1,1,2,256,256]{4,3,2,1,0:T(8,128)} %collective-permute-done.3, f32[256,256]{1,0:T(8,128)S(1)} %fusion.28, pred[]{:T(512)S(6)} %eq.11, bf16[1,2,1,2,256,256]{5,4,3,2,1,0:T(8,128)(2,1)S(1)} %copy-done.1), kind=kLoop, calls=%fused_computation.29 | loop fusion | flops 393216 | bytes 1572865 | tf_op jit(solution)/shard_map/jit(_where)/select_n | solution.py:226
  22.6 1.5 %collective-permute-start.4 = (f32[1,2,256,32]{2,3,1,0:T(8,128)S(1)}, f32[1,2,256,32]{2,3,1,0:T(8,128)S(1)}, u32[]{:S(2)}, u32[]{:S(2)}) collective-permute-start(f32[1,2,256,32]{2,3,1,0:T(8,128)S(1)} %get-tuple-element.33), channel_id=1, source_target_pairs={{0,4},{4,0},{1,5},{5,1},{2,6},{6,2},{3,7},{7,3},{8,12},{12,8},{9,1... | collective-permute-start | bytes 196616 | tf_op jit(solution)/shard_map/ppermute | solution.py:29
  24.1 1.1 %fusion.6 = f32[1,2,256,256]{3,2,1,0:T(8,128)S(1)} fusion(f32[1,1,2,256,256]{4,3,2,1,0:T(8,128)} %collective-permute-done, bf16[2,256,256]{2,1,0:T(8,128)(2,1)S(1)} %copy-done.3, pred[]{:T(512)} %eq.10), kind=kLoop, calls=%fused_computation.31 | loop fusion | flops 262144 | bytes 1310721 | tf_op jit(solution)/shard_map/jit(_where)/select_n | solution.py:222
  28.8 3.5 %collective-permute-start.8 = (f32[2,64,256]{2,1,0:T(8,128)S(1)}, f32[2,64,256]{2,1,0:T(8,128)S(1)}, u32[]{:S(2)}, u32[]{:S(2)}) collective-permute-start(f32[2,64,256]{2,1,0:T(8,128)S(1)} %get-tuple-element.13), channel_id=1, source_target_pairs={{0,1},{1,2},{2,3},{4,5},{5,6},{6,7},{8,9},{9,10},{10,11},{12,13},{... | collective-permute-start | bytes 393224 | tf_op jit(solution)/shard_map/ppermute | solution.py:93
  32.7 3.0 %collective-permute-done.8 = f32[2,64,256]{2,1,0:T(8,128)S(1)} collective-permute-done((f32[2,64,256]{2,1,0:T(8,128)S(1)}, f32[2,64,256]{2,1,0:T(8,128)S(1)}, u32[]{:S(2)}, u32[]{:S(2)}) %collective-permute-start.8) | collective-permute-done | bytes 131104 | tf_op jit(solution)/shard_map/ppermute | solution.py:93
  35.7 3.5 %collective-permute-start.10 = (f32[2,64,256]{2,1,0:T(8,128)S(1)}, f32[2,64,256]{2,1,0:T(8,128)S(1)}, u32[]{:S(2)}, u32[]{:S(2)}) collective-permute-start(f32[2,64,256]{2,1,0:T(8,128)S(1)} %get-tuple-element.11), channel_id=1, source_target_pairs={{0,1},{1,2},{2,3},{4,5},{5,6},{6,7},{8,9},{9,10},{10,11},{12,13},{... | collective-permute-start | bytes 393224 | tf_op jit(solution)/shard_map/ppermute | solution.py:93
  39.2 2.4 %collective-permute-start.6 = (f32[2,64,256]{2,1,0:T(8,128)S(1)}, f32[2,64,256]{2,1,0:T(8,128)S(1)}, u32[]{:S(2)}, u32[]{:S(2)}) collective-permute-start(f32[2,64,256]{2,1,0:T(8,128)S(1)} %get-tuple-element.45), channel_id=1, source_target_pairs={{1,0},{2,1},{3,2},{5,4},{6,5},{7,6},{9,8},{10,9},{11,10},{13,12},{... | collective-permute-start | bytes 393224 | tf_op jit(solution)/shard_map/ppermute | solution.py:94
  42.0 1.4 %collective-permute-start.2 = (f32[1,2,256,32]{2,3,1,0:T(8,128)S(1)}, f32[1,2,256,32]{2,3,1,0:T(8,128)S(1)}, u32[]{:S(2)}, u32[]{:S(2)}) collective-permute-start(f32[1,2,256,32]{2,3,1,0:T(8,128)S(1)} %get-tuple-element.36), channel_id=1, source_target_pairs={{4,0},{0,4},{5,1},{1,5},{6,2},{2,6},{7,3},{3,7},{12,8},{8,12},{13,... | collective-permute-start | bytes 196616 | tf_op jit(solution)/shard_map/ppermute | solution.py:32
  44.1 2.0 %collective-permute-done.6 = f32[2,64,256]{2,1,0:T(8,128)S(1)} collective-permute-done((f32[2,64,256]{2,1,0:T(8,128)S(1)}, f32[2,64,256]{2,1,0:T(8,128)S(1)}, u32[]{:S(2)}, u32[]{:S(2)}) %collective-permute-start.6) | collective-permute-done | bytes 131104 | tf_op jit(solution)/shard_map/ppermute | solution.py:94
  46.1 1.9 %collective-permute-start.11 = (f32[2,64,256]{2,1,0:T(8,128)S(1)}, f32[2,64,256]{2,1,0:T(8,128)S(1)}, u32[]{:S(2)}, u32[]{:S(2)}) collective-permute-start(f32[2,64,256]{2,1,0:T(8,128)S(1)} %get-tuple-element.9), channel_id=1, source_target_pairs={{0,1},{1,2},{2,3},{4,5},{5,6},{6,7},{8,9},{9,10},{10,11},{12,13},{... | collective-permute-start | bytes 393224 | tf_op jit(solution)/shard_map/ppermute | solution.py:93
  48.1 3.9 %collective-permute-start.7 = (f32[2,64,256]{2,1,0:T(8,128)S(1)}, f32[2,64,256]{2,1,0:T(8,128)S(1)}, u32[]{:S(2)}, u32[]{:S(2)}) collective-permute-start(f32[2,64,256]{2,1,0:T(8,128)S(1)} %get-tuple-element.40), channel_id=1, source_target_pairs={{1,0},{2,1},{3,2},{5,4},{6,5},{7,6},{9,8},{10,9},{11,10},{13,12},{... | collective-permute-start | bytes 393224 | tf_op jit(solution)/shard_map/ppermute | solution.py:94
  52.1 0.9 %collective-permute-done.11 = f32[2,64,256]{2,1,0:T(8,128)S(1)} collective-permute-done((f32[2,64,256]{2,1,0:T(8,128)S(1)}, f32[2,64,256]{2,1,0:T(8,128)S(1)}, u32[]{:S(2)}, u32[]{:S(2)}) %collective-permute-start.11) | collective-permute-done | bytes 131104 | tf_op jit(solution)/shard_map/ppermute | solution.py:93
  53.0 2.4 %collective-permute-done.7 = f32[2,64,256]{2,1,0:T(8,128)S(1)} collective-permute-done((f32[2,64,256]{2,1,0:T(8,128)S(1)}, f32[2,64,256]{2,1,0:T(8,128)S(1)}, u32[]{:S(2)}, u32[]{:S(2)}) %collective-permute-start.7) | collective-permute-done | bytes 131104 | tf_op jit(solution)/shard_map/ppermute | solution.py:94
  55.5 4.2 %collective-permute-start.9 = (f32[2,64,256]{2,1,0:T(8,128)S(1)}, f32[2,64,256]{2,1,0:T(8,128)S(1)}, u32[]{:S(2)}, u32[]{:S(2)}) collective-permute-start(f32[2,64,256]{2,1,0:T(8,128)S(1)} %get-tuple-element.39), channel_id=1, source_target_pairs={{1,0},{2,1},{3,2},{5,4},{6,5},{7,6},{9,8},{10,9},{11,10},{13,12},{... | collective-permute-start | bytes 393224 | tf_op jit(solution)/shard_map/ppermute | solution.py:94
  59.7 1.9 %collective-permute-start.13 = (f32[2,64,256]{2,1,0:T(8,128)S(1)}, f32[2,64,256]{2,1,0:T(8,128)S(1)}, u32[]{:S(2)}, u32[]{:S(2)}) collective-permute-start(f32[2,64,256]{2,1,0:T(8,128)S(1)} %get-tuple-element.7), channel_id=1, source_target_pairs={{0,1},{1,2},{2,3},{4,5},{5,6},{6,7},{8,9},{9,10},{10,11},{12,13},{... | collective-permute-start | bytes 393224 | tf_op jit(solution)/shard_map/ppermute | solution.py:93
  62.8 4.7 %collective-permute-done.13 = f32[2,64,256]{2,1,0:T(8,128)S(1)} collective-permute-done((f32[2,64,256]{2,1,0:T(8,128)S(1)}, f32[2,64,256]{2,1,0:T(8,128)S(1)}, u32[]{:S(2)}, u32[]{:S(2)}) %collective-permute-start.13) | collective-permute-done | bytes 131104 | tf_op jit(solution)/shard_map/ppermute | solution.py:93
  67.6 2.5 %collective-permute-start.12 = (f32[2,64,256]{2,1,0:T(8,128)S(1)}, f32[2,64,256]{2,1,0:T(8,128)S(1)}, u32[]{:S(2)}, u32[]{:S(2)}) collective-permute-start(f32[2,64,256]{2,1,0:T(8,128)S(1)} %get-tuple-element.38), channel_id=1, source_target_pairs={{1,0},{2,1},{3,2},{5,4},{6,5},{7,6},{9,8},{10,9},{11,10},{13,12},{... | collective-permute-start | bytes 393224 | tf_op jit(solution)/shard_map/ppermute | solution.py:94
  70.2 3.3 %collective-permute-start.15 = (f32[2,64,256]{2,1,0:T(8,128)S(1)}, f32[2,64,256]{2,1,0:T(8,128)S(1)}, u32[]{:S(2)}, u32[]{:S(2)}) collective-permute-start(f32[2,64,256]{2,1,0:T(8,128)S(1)} %get-tuple-element.37), channel_id=1, source_target_pairs={{0,1},{1,2},{2,3},{4,5},{5,6},{6,7},{8,9},{9,10},{10,11},{12,13},{... | collective-permute-start | bytes 393224 | tf_op jit(solution)/shard_map/ppermute | solution.py:93
  74.0 1.2 %collective-permute-done.12 = f32[2,64,256]{2,1,0:T(8,128)S(1)} collective-permute-done((f32[2,64,256]{2,1,0:T(8,128)S(1)}, f32[2,64,256]{2,1,0:T(8,128)S(1)}, u32[]{:S(2)}, u32[]{:S(2)}) %collective-permute-start.12) | collective-permute-done | bytes 131104 | tf_op jit(solution)/shard_map/ppermute | solution.py:94
  75.2 2.6 %collective-permute-done.15 = f32[2,64,256]{2,1,0:T(8,128)S(1)} collective-permute-done((f32[2,64,256]{2,1,0:T(8,128)S(1)}, f32[2,64,256]{2,1,0:T(8,128)S(1)}, u32[]{:S(2)}, u32[]{:S(2)}) %collective-permute-start.15) | collective-permute-done | bytes 131104 | tf_op jit(solution)/shard_map/ppermute | solution.py:93
  77.9 2.2 %collective-permute-start.14 = (f32[2,64,256]{2,1,0:T(8,128)S(1)}, f32[2,64,256]{2,1,0:T(8,128)S(1)}, u32[]{:S(2)}, u32[]{:S(2)}) collective-permute-start(f32[2,64,256]{2,1,0:T(8,128)S(1)} %get-tuple-element.42), channel_id=1, source_target_pairs={{1,0},{2,1},{3,2},{5,4},{6,5},{7,6},{9,8},{10,9},{11,10},{13,12},{... | collective-permute-start | bytes 393224 | tf_op jit(solution)/shard_map/ppermute | solution.py:94
  80.6 3.6 %collective-permute-start.17 = (f32[2,64,256]{2,1,0:T(8,128)S(1)}, f32[2,64,256]{2,1,0:T(8,128)S(1)}, u32[]{:S(2)}, u32[]{:S(2)}) collective-permute-start(f32[2,64,256]{2,1,0:T(8,128)S(1)} %get-tuple-element.41), channel_id=1, source_target_pairs={{0,1},{1,2},{2,3},{4,5},{5,6},{6,7},{8,9},{9,10},{10,11},{12,13},{... | collective-permute-start | bytes 393224 | tf_op jit(solution)/shard_map/ppermute | solution.py:93
  84.7 2.2 %collective-permute-start.16 = (f32[2,64,256]{2,1,0:T(8,128)S(1)}, f32[2,64,256]{2,1,0:T(8,128)S(1)}, u32[]{:S(2)}, u32[]{:S(2)}) collective-permute-start(f32[2,64,256]{2,1,0:T(8,128)S(1)} %select_select_fusion.1), channel_id=1, source_target_pairs={{1,0},{2,1},{3,2},{5,4},{6,5},{7,6},{9,8},{10,9},{11,10},{13,12},{... | collective-permute-start | bytes 393224 | tf_op jit(solution)/shard_map/ppermute | solution.py:94
  88.6 3.0 %collective-permute-done.16 = f32[2,64,256]{2,1,0:T(8,128)S(1)} collective-permute-done((f32[2,64,256]{2,1,0:T(8,128)S(1)}, f32[2,64,256]{2,1,0:T(8,128)S(1)}, u32[]{:S(2)}, u32[]{:S(2)}) %collective-permute-start.16) | collective-permute-done | bytes 131104 | tf_op jit(solution)/shard_map/ppermute | solution.py:94
  91.8 0.8 maximum_bitcast_fusion.2
  (55 shorter events, 12.5 us)
Async XLA Ops:
  0.6 23.5 %collective-permute-start = (f32[1,1,2,256,256]{4,3,2,1,0:T(8,128)}, f32[1,1,2,256,256]{4,3,2,1,0:T(8,128)}, u32[]{:S(2)}, u32[]{:S(2)}) collective-permute-start(f32[1,1,2,256,256]{4,3,2,1,0:T(8,128)} %param.11), channel_id=1, source_target_pairs={{0,8},{8,16},{16,24},{1,9},{9,17},{17,25},{2,10},{10,18},{18,26},{... | collective-permute-start | bytes 1572872 | tf_op jit(solution)/shard_map/ppermute | solution.py:29
  2.6 17.1 %collective-permute-start.3 = (f32[1,1,2,256,256]{4,3,2,1,0:T(8,128)}, f32[1,1,2,256,256]{4,3,2,1,0:T(8,128)}, u32[]{:S(2)}, u32[]{:S(2)}) collective-permute-start(f32[1,1,2,256,256]{4,3,2,1,0:T(8,128)} %param.12), channel_id=1, source_target_pairs={{8,0},{16,8},{24,16},{9,1},{17,9},{25,17},{10,2},{18,10},{26,18},{... | collective-permute-start | bytes 1572872 | tf_op jit(solution)/shard_map/ppermute | solution.py:32
  15.1 1.6 %copy-start.2 = (f32[1,1,256,256]{3,2,1,0:T(8,128)S(1)}, f32[1,1,256,256]{3,2,1,0:T(8,128)}, u32[]{:S(2)}) copy-start(f32[1,1,256,256]{3,2,1,0:T(8,128)} %param.10) | copy-start | bytes 786436
  15.1 2.5 %copy-start = (bf16[1,2,1,2,256,256]{5,4,3,2,1,0:T(8,128)(2,1)S(1)}, bf16[1,2,1,2,256,256]{5,4,3,2,1,0:T(8,128)(2,1)}, u32[]{:S(2)}) copy-start(bf16[1,2,1,2,256,256]{5,4,3,2,1,0:T(8,128)(2,1)} %param.13) | copy-start | bytes 1572868
  16.7 1.1 %copy-start.4 = (f32[1,256,256]{2,1,0:T(8,128)S(1)}, f32[1,256,256]{2,1,0:T(8,128)}, u32[]{:S(2)}) copy-start(f32[1,256,256]{2,1,0:T(8,128)} %param.14) | copy-start | bytes 786436
  17.8 1.9 %copy-start.1 = (bf16[1,2,1,2,256,256]{5,4,3,2,1,0:T(8,128)(2,1)S(1)}, bf16[1,2,1,2,256,256]{5,4,3,2,1,0:T(8,128)(2,1)}, u32[]{:S(2)}) copy-start(bf16[1,2,1,2,256,256]{5,4,3,2,1,0:T(8,128)(2,1)} %param.13) | copy-start | bytes 1572868
  21.2 2.9 %copy-start.3 = (bf16[2,256,256]{2,1,0:T(8,128)(2,1)S(1)}, bf16[2,256,256]{2,1,0:T(8,128)(2,1)}, u32[]{:S(2)}) copy-start(bf16[2,256,256]{2,1,0:T(8,128)(2,1)} %param.9) | copy-start | bytes 786436
  22.0 4.3 %collective-permute-start.5 = (f32[1,2,256,32]{2,3,1,0:T(8,128)S(1)}, f32[1,2,256,32]{2,3,1,0:T(8,128)S(1)}, u32[]{:S(2)}, u32[]{:S(2)}) collective-permute-start(f32[1,2,256,32]{2,3,1,0:T(8,128)S(1)} %get-tuple-element.34), channel_id=1, source_target_pairs={{4,0},{0,4},{5,1},{1,5},{6,2},{2,6},{7,3},{3,7},{12,8},{8,12},{13,... | collective-permute-start | bytes 196616 | tf_op jit(solution)/shard_map/ppermute | solution.py:32
  22.6 4.4 %collective-permute-start.4 = (f32[1,2,256,32]{2,3,1,0:T(8,128)S(1)}, f32[1,2,256,32]{2,3,1,0:T(8,128)S(1)}, u32[]{:S(2)}, u32[]{:S(2)}) collective-permute-start(f32[1,2,256,32]{2,3,1,0:T(8,128)S(1)} %get-tuple-element.33), channel_id=1, source_target_pairs={{0,4},{4,0},{1,5},{5,1},{2,6},{6,2},{3,7},{7,3},{8,12},{12,8},{9,1... | collective-permute-start | bytes 196616 | tf_op jit(solution)/shard_map/ppermute | solution.py:29
  28.8 6.9 %collective-permute-start.8 = (f32[2,64,256]{2,1,0:T(8,128)S(1)}, f32[2,64,256]{2,1,0:T(8,128)S(1)}, u32[]{:S(2)}, u32[]{:S(2)}) collective-permute-start(f32[2,64,256]{2,1,0:T(8,128)S(1)} %get-tuple-element.13), channel_id=1, source_target_pairs={{0,1},{1,2},{2,3},{4,5},{5,6},{6,7},{8,9},{9,10},{10,11},{12,13},{... | collective-permute-start | bytes 393224 | tf_op jit(solution)/shard_map/ppermute | solution.py:93
  35.7 8.4 %collective-permute-start.10 = (f32[2,64,256]{2,1,0:T(8,128)S(1)}, f32[2,64,256]{2,1,0:T(8,128)S(1)}, u32[]{:S(2)}, u32[]{:S(2)}) collective-permute-start(f32[2,64,256]{2,1,0:T(8,128)S(1)} %get-tuple-element.11), channel_id=1, source_target_pairs={{0,1},{1,2},{2,3},{4,5},{5,6},{6,7},{8,9},{9,10},{10,11},{12,13},{... | collective-permute-start | bytes 393224 | tf_op jit(solution)/shard_map/ppermute | solution.py:93
  39.2 6.9 %collective-permute-start.6 = (f32[2,64,256]{2,1,0:T(8,128)S(1)}, f32[2,64,256]{2,1,0:T(8,128)S(1)}, u32[]{:S(2)}, u32[]{:S(2)}) collective-permute-start(f32[2,64,256]{2,1,0:T(8,128)S(1)} %get-tuple-element.45), channel_id=1, source_target_pairs={{1,0},{2,1},{3,2},{5,4},{6,5},{7,6},{9,8},{10,9},{11,10},{13,12},{... | collective-permute-start | bytes 393224 | tf_op jit(solution)/shard_map/ppermute | solution.py:94
  42.0 10.0 %collective-permute-start.2 = (f32[1,2,256,32]{2,3,1,0:T(8,128)S(1)}, f32[1,2,256,32]{2,3,1,0:T(8,128)S(1)}, u32[]{:S(2)}, u32[]{:S(2)}) collective-permute-start(f32[1,2,256,32]{2,3,1,0:T(8,128)S(1)} %get-tuple-element.36), channel_id=1, source_target_pairs={{4,0},{0,4},{5,1},{1,5},{6,2},{2,6},{7,3},{3,7},{12,8},{8,12},{13,... | collective-permute-start | bytes 196616 | tf_op jit(solution)/shard_map/ppermute | solution.py:32
  43.4 8.6 %collective-permute-start.1 = (f32[1,2,256,32]{2,3,1,0:T(8,128)S(1)}, f32[1,2,256,32]{2,3,1,0:T(8,128)S(1)}, u32[]{:S(2)}, u32[]{:S(2)}) collective-permute-start(f32[1,2,256,32]{2,3,1,0:T(8,128)S(1)} %get-tuple-element.35), channel_id=1, source_target_pairs={{0,4},{4,0},{1,5},{5,1},{2,6},{6,2},{3,7},{7,3},{8,12},{12,8},{9,1... | collective-permute-start | bytes 196616 | tf_op jit(solution)/shard_map/ppermute | solution.py:29
  46.1 6.9 %collective-permute-start.11 = (f32[2,64,256]{2,1,0:T(8,128)S(1)}, f32[2,64,256]{2,1,0:T(8,128)S(1)}, u32[]{:S(2)}, u32[]{:S(2)}) collective-permute-start(f32[2,64,256]{2,1,0:T(8,128)S(1)} %get-tuple-element.9), channel_id=1, source_target_pairs={{0,1},{1,2},{2,3},{4,5},{5,6},{6,7},{8,9},{9,10},{10,11},{12,13},{... | collective-permute-start | bytes 393224 | tf_op jit(solution)/shard_map/ppermute | solution.py:93
  48.1 7.3 %collective-permute-start.7 = (f32[2,64,256]{2,1,0:T(8,128)S(1)}, f32[2,64,256]{2,1,0:T(8,128)S(1)}, u32[]{:S(2)}, u32[]{:S(2)}) collective-permute-start(f32[2,64,256]{2,1,0:T(8,128)S(1)} %get-tuple-element.40), channel_id=1, source_target_pairs={{1,0},{2,1},{3,2},{5,4},{6,5},{7,6},{9,8},{10,9},{11,10},{13,12},{... | collective-permute-start | bytes 393224 | tf_op jit(solution)/shard_map/ppermute | solution.py:94
  55.5 7.3 %collective-permute-start.9 = (f32[2,64,256]{2,1,0:T(8,128)S(1)}, f32[2,64,256]{2,1,0:T(8,128)S(1)}, u32[]{:S(2)}, u32[]{:S(2)}) collective-permute-start(f32[2,64,256]{2,1,0:T(8,128)S(1)} %get-tuple-element.39), channel_id=1, source_target_pairs={{1,0},{2,1},{3,2},{5,4},{6,5},{7,6},{9,8},{10,9},{11,10},{13,12},{... | collective-permute-start | bytes 393224 | tf_op jit(solution)/shard_map/ppermute | solution.py:94
  59.7 7.8 %collective-permute-start.13 = (f32[2,64,256]{2,1,0:T(8,128)S(1)}, f32[2,64,256]{2,1,0:T(8,128)S(1)}, u32[]{:S(2)}, u32[]{:S(2)}) collective-permute-start(f32[2,64,256]{2,1,0:T(8,128)S(1)} %get-tuple-element.7), channel_id=1, source_target_pairs={{0,1},{1,2},{2,3},{4,5},{5,6},{6,7},{8,9},{9,10},{10,11},{12,13},{... | collective-permute-start | bytes 393224 | tf_op jit(solution)/shard_map/ppermute | solution.py:93
  67.6 7.6 %collective-permute-start.12 = (f32[2,64,256]{2,1,0:T(8,128)S(1)}, f32[2,64,256]{2,1,0:T(8,128)S(1)}, u32[]{:S(2)}, u32[]{:S(2)}) collective-permute-start(f32[2,64,256]{2,1,0:T(8,128)S(1)} %get-tuple-element.38), channel_id=1, source_target_pairs={{1,0},{2,1},{3,2},{5,4},{6,5},{7,6},{9,8},{10,9},{11,10},{13,12},{... | collective-permute-start | bytes 393224 | tf_op jit(solution)/shard_map/ppermute | solution.py:94
  70.2 7.6 %collective-permute-start.15 = (f32[2,64,256]{2,1,0:T(8,128)S(1)}, f32[2,64,256]{2,1,0:T(8,128)S(1)}, u32[]{:S(2)}, u32[]{:S(2)}) collective-permute-start(f32[2,64,256]{2,1,0:T(8,128)S(1)} %get-tuple-element.37), channel_id=1, source_target_pairs={{0,1},{1,2},{2,3},{4,5},{5,6},{6,7},{8,9},{9,10},{10,11},{12,13},{... | collective-permute-start | bytes 393224 | tf_op jit(solution)/shard_map/ppermute | solution.py:93
  77.9 6.9 %collective-permute-start.14 = (f32[2,64,256]{2,1,0:T(8,128)S(1)}, f32[2,64,256]{2,1,0:T(8,128)S(1)}, u32[]{:S(2)}, u32[]{:S(2)}) collective-permute-start(f32[2,64,256]{2,1,0:T(8,128)S(1)} %get-tuple-element.42), channel_id=1, source_target_pairs={{1,0},{2,1},{3,2},{5,4},{6,5},{7,6},{9,8},{10,9},{11,10},{13,12},{... | collective-permute-start | bytes 393224 | tf_op jit(solution)/shard_map/ppermute | solution.py:94
  80.6 8.0 %collective-permute-start.17 = (f32[2,64,256]{2,1,0:T(8,128)S(1)}, f32[2,64,256]{2,1,0:T(8,128)S(1)}, u32[]{:S(2)}, u32[]{:S(2)}) collective-permute-start(f32[2,64,256]{2,1,0:T(8,128)S(1)} %get-tuple-element.41), channel_id=1, source_target_pairs={{0,1},{1,2},{2,3},{4,5},{5,6},{6,7},{8,9},{9,10},{10,11},{12,13},{... | collective-permute-start | bytes 393224 | tf_op jit(solution)/shard_map/ppermute | solution.py:93
  84.7 6.9 %collective-permute-start.16 = (f32[2,64,256]{2,1,0:T(8,128)S(1)}, f32[2,64,256]{2,1,0:T(8,128)S(1)}, u32[]{:S(2)}, u32[]{:S(2)}) collective-permute-start(f32[2,64,256]{2,1,0:T(8,128)S(1)} %select_select_fusion.1), channel_id=1, source_target_pairs={{1,0},{2,1},{3,2},{5,4},{6,5},{7,6},{9,8},{10,9},{11,10},{13,12},{... | collective-permute-start | bytes 393224 | tf_op jit(solution)/shard_map/ppermute | solution.py:94

commit v6 on v4

--- a/solution.py
+++ b/solution.py
@@ -44,29 +44,35 @@
     return signed.astype(jnp.float32) / length
 
 
-def line_allreduce(value, axis, pieces):
+def halving_allreduce(value, axis):
     count = lax.axis_size(axis)
     if count == 1:
         return value
-    if count % 2:
+    if count & (count - 1) or value.shape[-2] % count:
         return lax.psum(value, axis)
-    half = count // 2
     index = lax.axis_index(axis)
-    chunks = jnp.split(value, pieces, axis=-2)
-    done = []
-    for chunk in chunks:
-        total = chunk
-        for step in range(half - 1):
-            pairs = [(step, step + 1), (count - 1 - step, count - 2 - step)]
-            total = total + lax.ppermute(total, axis, pairs)
-        total = total + lax.ppermute(total, axis, [(half - 1, half), (half, half - 1)])
-        for step in range(half - 1):
-            pairs = [(half - 1 - step, half - 2 - step), (half + step, half + 1 + step)]
-            got = lax.ppermute(total, axis, pairs)
-            target = (index == half - 2 - step) | (index == half + 1 + step)
-            total = jnp.where(target, got, total)
-        done.append(total)
-    return jnp.concatenate(done, axis=-2)
+    steps = count.bit_length() - 1
+    dim = value.ndim - 2
+    held = value
+    for k in range(steps):
+        bit = (index >> k) & 1
+        size = held.shape[dim] // 2
+        low = lax.slice_in_dim(held, 0, size, axis=dim)
+        high = lax.slice_in_dim(held, size, None, axis=dim)
+        keep = jnp.where(bit == 0, low, high)
+        give = jnp.where(bit == 0, high, low)
+        pairs = [(j, j ^ (1 << k)) for j in range(count)]
+        held = keep + lax.ppermute(give, axis, pairs)
+    for k in reversed(range(steps)):
+        bit = (index >> k) & 1
+        pairs = [(j, j ^ (1 << k)) for j in range(count)]
+        other = lax.ppermute(held, axis, pairs)
+        held = jnp.where(
+            bit == 0,
+            jnp.concatenate([held, other], axis=dim),
+            jnp.concatenate([other, held], axis=dim),
+        )
+    return held
 
 
 def table_kernel(both_ref, grid_ref, rows_ref, cols_ref):
@@ -197,7 +203,7 @@
     grad_real = spread[:, 0] * held_field[:, 0] + spread[:, 1] * held_field[:, 1]
     grad_imag = spread[:, 1] * held_field[:, 0] - spread[:, 0] * held_field[:, 1]
     gradient_term = jnp.stack([jnp.sum(grad_real, axis=0), jnp.sum(grad_imag, axis=0)])
-    summed = line_allreduce(gradient_term, "angle", 4)
+    summed = halving_allreduce(gradient_term, "angle")
     returning = jnp.stack(
         [
             cosine * spread[:, 0] + sine_part * spread[:, 1],

time: 68.7 us -> 63.7 us (0.927)
  starting transfers between devices: 24.2 us -> 13.5 us
  waiting for transfers between devices: 18.5 us -> 24.2 us
  other arithmetic: 5.97 us -> 6.69 us
    ppermute x12 -> x4, starting transfers between devices: 15.2 us -> 4.48 us  [the longest x2 4.3 us: halving_allreduce(): held = keep + lax.ppermute(give, axis, pairs)]
    ppermute x3, waiting for transfers between devices: 0.07 us -> 2.94 us  [padded_2(): lax.ppermute(lax.slice_in_dim(block, 0, width, axis=dim), axis, backward)]
    ppermute x12 -> x4, waiting for transfers between devices: 16 us -> 18.4 us  [the longest x2 12.1 us: halving_allreduce(): other = lax.ppermute(held, axis, pairs)]
    ppermute x3, starting transfers between devices: 5.68 us -> 4.82 us  [padded_2(): lax.ppermute(lax.slice_in_dim(block, 0, width, axis=dim), axis, backward)]
    ppermute x3, starting transfers between devices: 3.32 us -> 4.18 us  [padded_2(): lax.ppermute(lax.slice_in_dim(block, block.shape[dim] - width, None, axis...]
    select_n x4, other arithmetic: 0.07 us -> 0.92 us  [the longest x2 0.86 us: halving_allreduce(): jnp.where(bit == 0, jnp.concatenate([held, other], axis=dim), jnp.concate...]
    broadcast_in_dim x3 -> x2, other arithmetic: 2.49 us -> 1.66 us  [body(): return (wavefield[None], returning[None], summed[None, None])]
    convert_element_type x1, other arithmetic: 0.08 us -> 0.88 us  [body(): held_field = held_waves[0, 0].astype(jnp.float32)]
  transfers between devices with their start and end apart: 18 -> 10, of which waited for: 9 -> 7; matrix products, arithmetic and copies ran while one was open for 21% -> 24% of each run, Pallas kernels for 7% -> 8%
where the time goes in v6:
time: 63.7 us; the launch traced here: 63.3 us
  waiting for transfers between devices  24.2 us (38%)
  starting transfers between devices  13.5 us (21%)
  other arithmetic  6.69 us (11%)
  local copies, waits for them, and re-layouts  5.7 us (9%)
  matrix products  5.52 us (9%)
  Pallas kernels  4.79 us (8%)
  between operations  2.98 us (5%)
    ppermute x2, waiting for transfers between devices, halving_allreduce(): other = lax.ppermute(held, axis, pairs)  12.1 us
    ppermute x2, waiting for transfers between devices, halving_allreduce(): held = keep + lax.ppermute(give, axis, pairs)  6.27 us
    dot_general x12, matrix products, contract(): return jnp.einsum(form, left, right, precision=wave_precision)  5.52 us
    ppermute x3, starting transfers between devices, padded_2(): lax.ppermute(lax.slice_in_dim(block, 0, width, axis=dim), axis, backward)  4.82 us
    pallas_call x1, Pallas kernels, build_tables(): pl.pallas_call(table_kernel, out_shape=(jax.ShapeDtypeStruct((angle_count...  4.79 us
    ppermute x2, starting transfers between devices, halving_allreduce(): held = keep + lax.ppermute(give, axis, pairs)  4.3 us
    ppermute x3, starting transfers between devices, padded_2(): lax.ppermute(lax.slice_in_dim(block, block.shape[dim] - width, None, axis...  4.18 us
    ppermute x3, waiting for transfers between devices, padded_2(): lax.ppermute(lax.slice_in_dim(block, 0, width, axis=dim), axis, backward)  2.94 us
  transfers between devices with their start and end apart: 10, of which 7 were waited for; matrix products, arithmetic and copies ran while one was open for 24% of the time, Pallas kernels for 8%

profile of v6, /device:TPU:0, one launch (start us, length us, event | category | flops | bytes accessed | tf_op | source)
XLA Modules:
  0.0 63.3 jit_solution(16066085398941201223)
XLA Ops:
  0.6 3.2 %collective-permute-start = (f32[1,1,2,256,256]{4,3,2,1,0:T(8,128)}, f32[1,1,2,256,256]{4,3,2,1,0:T(8,128)}, u32[]{:S(2)}, u32[]{:S(2)}) collective-permute-start(f32[1,1,2,256,256]{4,3,2,1,0:T(8,128)} %param.11), channel_id=1, source_target_pairs={{0,8},{8,16},{16,24},{1,9},{9,17},{17,25},{2,10},{10,18},{18,26},{... | collective-permute-start | bytes 1572872 | tf_op jit(solution)/shard_map/ppermute | solution.py:29
  3.8 1.3 %collective-permute-start.3 = (f32[1,1,2,256,256]{4,3,2,1,0:T(8,128)}, f32[1,1,2,256,256]{4,3,2,1,0:T(8,128)}, u32[]{:S(2)}, u32[]{:S(2)}) collective-permute-start(f32[1,1,2,256,256]{4,3,2,1,0:T(8,128)} %param.12), channel_id=1, source_target_pairs={{8,0},{16,8},{24,16},{9,1},{17,9},{25,17},{10,2},{18,10},{26,18},{... | collective-permute-start | bytes 1572872 | tf_op jit(solution)/shard_map/ppermute | solution.py:32
  5.8 1.3 %fusion.57 = (s32[1,1]{1,0:T(1,128)}, s32[1,1]{1,0:T(1,128)}) fusion(s32[1,2]{1,0:T(1,128)} %param.16), kind=kLoop, calls=%fused_computation.122 | loop fusion | bytes 16 | tf_op jit(solution)/shard_map/slice | solution.py:169
  8.6 0.6 pad_maximum_fusion.7.both_ref
  9.2 4.8 %shard_map.112 = (f32[1,2,3,256,256]{4,3,2,1,0:T(8,128)}, f32[1,2,3,256,320]{4,3,2,1,0:T(8,128)}) custom-call(f32[1,8,320]{2,1,0:T(8,128)} %pad_maximum_fusion.7.both_ref, f32[320,1280]{1,0:T(8,128)} %constant.48.clone.grid_ref), custom_call_target="tpu_custom_call" | custom-call | tf_op jit(solution)/shard_map/pallas_call | solution.py:132
  14.0 1.5 %slice_bitcast_fusion.2 = (f32[1,3,256,256]{3,2,1,0:T(8,128)S(1)}, f32[1,3,256,256]{3,2,1,0:T(8,128)S(1)}) fusion(f32[1,2,3,256,256]{4,3,2,1,0:T(8,128)} %get-tuple-element.5), kind=kLoop, calls=%fused_computation.16 | loop fusion | bytes 3145728 | tf_op jit(solution)/shard_map/squeeze | solution.py:176
  15.5 1.0 %fusion.56 = (f32[1,1,256,256]{3,2,1,0:T(8,128)S(1)}, f32[1,1,256,256]{3,2,1,0:T(8,128)S(1)}) fusion(f32[1,1,256,256]{3,2,1,0:T(8,128)S(1)} %copy-done.3), kind=kLoop, calls=%fused_computation.121 | loop fusion | bytes 786432 | tf_op jit(solution)/shard_map/cos | solution.py:180
  16.5 0.9 %bitcast_convert_fusion = (f32[1,2,256,256]{3,2,1,0:T(8,128)}, f32[1,2,256,256]{3,2,1,0:T(8,128)S(1)}) fusion(bf16[1,2,1,2,256,256]{5,4,3,2,1,0:T(8,128)(2,1)S(1)} %copy-done.1), kind=kLoop, calls=%fused_computation.71 | loop fusion | flops 262144 | bytes 1572864 | tf_op jit(solution)/shard_map/convert_element_type | solution.py:202
  17.5 1.8 %slice_bitcast_fusion = (f32[1,3,256,320]{3,2,1,0:T(8,128)S(1)}, f32[1,3,256,320]{3,2,1,0:T(8,128)S(1)}) fusion(f32[1,2,3,256,320]{4,3,2,1,0:T(8,128)} %get-tuple-element.6), kind=kLoop, calls=%fused_computation | loop fusion | bytes 3932160 | tf_op jit(solution)/shard_map/squeeze | solution.py:178
  19.3 1.1 %bitcast_select_fusion = f32[1,2,256,256]{3,2,1,0:T(8,128)S(1)} fusion(f32[1,1,2,256,256]{4,3,2,1,0:T(8,128)} %collective-permute-done.3, f32[256,256]{1,0:T(8,128)S(1)} %fusion.29, pred[]{:T(512)S(6)} %eq.17, bf16[1,2,1,2,256,256]{5,4,3,2,1,0:T(8,128)(2,1)S(1)} %copy-done.2), kind=kLoop, calls=%fused_computation.25 | loop fusion | flops 393216 | bytes 1572865 | tf_op jit(solution)/shard_map/jit(_where)/select_n | solution.py:189
  21.7 2.4 %collective-permute-start.5 = (f32[1,2,256,32]{2,3,1,0:T(8,128)S(1)}, f32[1,2,256,32]{2,3,1,0:T(8,128)S(1)}, u32[]{:S(2)}, u32[]{:S(2)}) collective-permute-start(f32[1,2,256,32]{2,3,1,0:T(8,128)S(1)} %get-tuple-element.22), channel_id=1, source_target_pairs={{4,0},{0,4},{5,1},{1,5},{6,2},{2,6},{7,3},{3,7},{12,8},{8,12},{13,... | collective-permute-start | bytes 196616 | tf_op jit(solution)/shard_map/ppermute | solution.py:32
  24.1 1.1 %fusion.6 = f32[1,2,256,256]{3,2,1,0:T(8,128)S(1)} fusion(f32[1,1,2,256,256]{4,3,2,1,0:T(8,128)} %collective-permute-done, bf16[2,256,256]{2,1,0:T(8,128)(2,1)S(1)} %copy-done.4, pred[]{:T(512)} %eq.16), kind=kLoop, calls=%fused_computation.27 | loop fusion | flops 262144 | bytes 1310721 | tf_op jit(solution)/shard_map/jit(_where)/select_n | solution.py:185
  26.5 2.2 %collective-permute-done.4 = f32[1,2,256,32]{2,3,1,0:T(8,128)S(1)} collective-permute-done((f32[1,2,256,32]{2,3,1,0:T(8,128)S(1)}, f32[1,2,256,32]{2,3,1,0:T(8,128)S(1)}, u32[]{:S(2)}, u32[]{:S(2)}) %collective-permute-start.4) | collective-permute-done | bytes 65568 | tf_op jit(solution)/shard_map/ppermute | solution.py:29
  28.8 0.5 fusion.7
  29.3 0.5 convolution_subtract_fusion
  29.8 0.6 add_bitcast_fusion
  30.5 1.6 %collective-permute-start.6 = (f32[2,128,256]{2,1,0:T(8,128)S(1)}, f32[2,128,256]{2,1,0:T(8,128)S(1)}, u32[]{:S(2)}, u32[]{:S(2)}) collective-permute-start(f32[2,128,256]{2,1,0:T(8,128)S(1)} %broadcast_select_fusion), channel_id=1, source_target_pairs={{0,1},{1,0},{2,3},{3,2},{4,5},{5,4},{6,7},{7,6},{8,9},{9,8},{10,11... | collective-permute-start | bytes 786440 | tf_op jit(solution)/shard_map/ppermute | solution.py:65
  32.2 1.1 %collective-permute-start.2 = (f32[1,2,256,32]{2,3,1,0:T(8,128)S(1)}, f32[1,2,256,32]{2,3,1,0:T(8,128)S(1)}, u32[]{:S(2)}, u32[]{:S(2)}) collective-permute-start(f32[1,2,256,32]{2,3,1,0:T(8,128)S(1)} %get-tuple-element.24), channel_id=1, source_target_pairs={{4,0},{0,4},{5,1},{1,5},{6,2},{2,6},{7,3},{3,7},{12,8},{8,12},{13,... | collective-permute-start | bytes 196616 | tf_op jit(solution)/shard_map/ppermute | solution.py:32
  33.3 0.9 %collective-permute-start.1 = (f32[1,2,256,32]{2,3,1,0:T(8,128)S(1)}, f32[1,2,256,32]{2,3,1,0:T(8,128)S(1)}, u32[]{:S(2)}, u32[]{:S(2)}) collective-permute-start(f32[1,2,256,32]{2,3,1,0:T(8,128)S(1)} %get-tuple-element.23), channel_id=1, source_target_pairs={{0,4},{4,0},{1,5},{5,1},{2,6},{6,2},{3,7},{7,3},{8,12},{12,8},{9,1... | collective-permute-start | bytes 196616 | tf_op jit(solution)/shard_map/ppermute | solution.py:29
  34.2 2.9 %collective-permute-done.2 = f32[1,2,256,32]{2,3,1,0:T(8,128)S(1)} collective-permute-done((f32[1,2,256,32]{2,3,1,0:T(8,128)S(1)}, f32[1,2,256,32]{2,3,1,0:T(8,128)S(1)}, u32[]{:S(2)}, u32[]{:S(2)}) %collective-permute-start.2) | collective-permute-done | bytes 65568 | tf_op jit(solution)/shard_map/ppermute | solution.py:32
  37.2 0.7 %collective-permute-done.1 = f32[1,2,256,32]{2,3,1,0:T(8,128)S(1)} collective-permute-done((f32[1,2,256,32]{2,3,1,0:T(8,128)S(1)}, f32[1,2,256,32]{2,3,1,0:T(8,128)S(1)}, u32[]{:S(2)}, u32[]{:S(2)}) %collective-permute-start.1) | collective-permute-done | bytes 65568 | tf_op jit(solution)/shard_map/ppermute | solution.py:29
  37.9 1.0 %collective-permute-done.6 = f32[2,128,256]{2,1,0:T(8,128)S(1)} collective-permute-done((f32[2,128,256]{2,1,0:T(8,128)S(1)}, f32[2,128,256]{2,1,0:T(8,128)S(1)}, u32[]{:S(2)}, u32[]{:S(2)}) %collective-permute-start.6) | collective-permute-done | bytes 262176 | tf_op jit(solution)/shard_map/ppermute | solution.py:65
  39.0 2.7 %collective-permute-start.7 = (f32[2,64,256]{2,1,0:T(8,128)S(1)}, f32[2,64,256]{2,1,0:T(8,128)S(1)}, u32[]{:S(2)}, u32[]{:S(2)}) collective-permute-start(f32[2,64,256]{2,1,0:T(8,128)S(1)} %slice_select_fusion), channel_id=1, source_target_pairs={{0,2},{1,3},{2,0},{3,1},{4,6},{5,7},{6,4},{7,5},{8,10},{9,11},{10,... | collective-permute-start | bytes 393224 | tf_op jit(solution)/shard_map/ppermute | solution.py:65
  41.6 0.5 fusion.8
  42.2 5.3 %collective-permute-done.7 = f32[2,64,256]{2,1,0:T(8,128)S(1)} collective-permute-done((f32[2,64,256]{2,1,0:T(8,128)S(1)}, f32[2,64,256]{2,1,0:T(8,128)S(1)}, u32[]{:S(2)}, u32[]{:S(2)}) %collective-permute-start.7) | collective-permute-done | bytes 131104 | tf_op jit(solution)/shard_map/ppermute | solution.py:65
  47.6 0.5 fusion.2
  48.1 7.9 %collective-permute-done.8 = f32[2,64,256]{2,1,0:T(8,128)S(1)} collective-permute-done((f32[2,64,256]{2,1,0:T(8,128)S(1)}, f32[2,64,256]{2,1,0:T(8,128)S(1)}, u32[]{:S(2)}, u32[]{:S(2)}) %collective-permute-start.8) | collective-permute-done | bytes 131104 | tf_op jit(solution)/shard_map/ppermute | solution.py:69
  56.1 0.5 fusion.3
  56.7 0.8 %maximum_bitcast_fusion = f32[1,1,2,256,256]{4,3,2,1,0:T(8,128)} fusion(f32[1,1,256,256]{3,2,1,0:T(8,128)S(1)} %fusion.2, f32[1,1,256,256]{3,2,1,0:T(8,128)S(1)} %fusion.3), kind=kLoop, calls=%fused_computation.20 | loop fusion | flops 131072 | bytes 1048576 | tf_op jit(solution)/shard_map/broadcast_in_dim | solution.py:215
  57.5 0.8 %maximum_bitcast_fusion.1 = f32[1,1,2,256,256]{4,3,2,1,0:T(8,128)} fusion(f32[1,1,256,256]{3,2,1,0:T(8,128)S(1)} %get-tuple-element.17, f32[1,1,256,256]{3,2,1,0:T(8,128)S(1)} %get-tuple-element.18), kind=kLoop, calls=%fused_computation.21 | loop fusion | flops 131072 | bytes 1048576 | tf_op jit(solution)/shard_map/broadcast_in_dim | solution.py:215
  58.3 4.2 %collective-permute-done.9 = f32[2,128,256]{2,1,0:T(8,128)S(1)} collective-permute-done((f32[2,128,256]{2,1,0:T(8,128)S(1)}, f32[2,128,256]{2,1,0:T(8,128)S(1)}, u32[]{:S(2)}, u32[]{:S(2)}) %collective-permute-start.9) | collective-permute-done | bytes 262176 | tf_op jit(solution)/shard_map/ppermute | solution.py:69
  62.5 0.8 %maximum_select_fusion = f32[1,1,2,256,256]{4,3,2,1,0:T(8,128)} fusion(f32[1,1,2,128,256]{4,3,2,1,0:T(8,128)S(1)} %bitcast.178, f32[1,1,2,128,256]{4,3,2,1,0:T(8,128)S(1)} %bitcast.177, pred[]{:T(512)S(6)} %eq.18), kind=kLoop, calls=%fused_computation.24 | loop fusion | flops 393216 | bytes 1048577 | tf_op jit(solution)/shard_map/jit(_where)/select_n | solution.py:70
  (38 shorter events, 3.1 us)
Async XLA Ops:
  0.6 23.5 %collective-permute-start = (f32[1,1,2,256,256]{4,3,2,1,0:T(8,128)}, f32[1,1,2,256,256]{4,3,2,1,0:T(8,128)}, u32[]{:S(2)}, u32[]{:S(2)}) collective-permute-start(f32[1,1,2,256,256]{4,3,2,1,0:T(8,128)} %param.11), channel_id=1, source_target_pairs={{0,8},{8,16},{16,24},{1,9},{9,17},{17,25},{2,10},{10,18},{18,26},{... | collective-permute-start | bytes 1572872 | tf_op jit(solution)/shard_map/ppermute | solution.py:29
  3.8 15.5 %collective-permute-start.3 = (f32[1,1,2,256,256]{4,3,2,1,0:T(8,128)}, f32[1,1,2,256,256]{4,3,2,1,0:T(8,128)}, u32[]{:S(2)}, u32[]{:S(2)}) collective-permute-start(f32[1,1,2,256,256]{4,3,2,1,0:T(8,128)} %param.12), channel_id=1, source_target_pairs={{8,0},{16,8},{24,16},{9,1},{17,9},{25,17},{10,2},{18,10},{26,18},{... | collective-permute-start | bytes 1572872 | tf_op jit(solution)/shard_map/ppermute | solution.py:32
  14.0 1.6 %copy-start.3 = (f32[1,1,256,256]{3,2,1,0:T(8,128)S(1)}, f32[1,1,256,256]{3,2,1,0:T(8,128)}, u32[]{:S(2)}) copy-start(f32[1,1,256,256]{3,2,1,0:T(8,128)} %param.10) | copy-start | bytes 786436
  14.0 2.5 %copy-start.1 = (bf16[1,2,1,2,256,256]{5,4,3,2,1,0:T(8,128)(2,1)S(1)}, bf16[1,2,1,2,256,256]{5,4,3,2,1,0:T(8,128)(2,1)}, u32[]{:S(2)}) copy-start(bf16[1,2,1,2,256,256]{5,4,3,2,1,0:T(8,128)(2,1)} %param.13) | copy-start | bytes 1572868
  15.5 1.9 %copy-start.5 = (f32[1,256,256]{2,1,0:T(8,128)S(1)}, f32[1,256,256]{2,1,0:T(8,128)}, u32[]{:S(2)}) copy-start(f32[1,256,256]{2,1,0:T(8,128)} %param.14) | copy-start | bytes 786436
  17.5 1.9 %copy-start.2 = (bf16[1,2,1,2,256,256]{5,4,3,2,1,0:T(8,128)(2,1)S(1)}, bf16[1,2,1,2,256,256]{5,4,3,2,1,0:T(8,128)(2,1)}, u32[]{:S(2)}) copy-start(bf16[1,2,1,2,256,256]{5,4,3,2,1,0:T(8,128)(2,1)} %param.13) | copy-start | bytes 1572868
  20.9 3.3 %copy-start.4 = (bf16[2,256,256]{2,1,0:T(8,128)(2,1)S(1)}, bf16[2,256,256]{2,1,0:T(8,128)(2,1)}, u32[]{:S(2)}) copy-start(bf16[2,256,256]{2,1,0:T(8,128)(2,1)} %param.9) | copy-start | bytes 786436
  21.7 4.9 %collective-permute-start.5 = (f32[1,2,256,32]{2,3,1,0:T(8,128)S(1)}, f32[1,2,256,32]{2,3,1,0:T(8,128)S(1)}, u32[]{:S(2)}, u32[]{:S(2)}) collective-permute-start(f32[1,2,256,32]{2,3,1,0:T(8,128)S(1)} %get-tuple-element.22), channel_id=1, source_target_pairs={{4,0},{0,4},{5,1},{1,5},{6,2},{2,6},{7,3},{3,7},{12,8},{8,12},{13,... | collective-permute-start | bytes 196616 | tf_op jit(solution)/shard_map/ppermute | solution.py:32
  24.1 4.7 %collective-permute-start.4 = (f32[1,2,256,32]{2,3,1,0:T(8,128)S(1)}, f32[1,2,256,32]{2,3,1,0:T(8,128)S(1)}, u32[]{:S(2)}, u32[]{:S(2)}) collective-permute-start(f32[1,2,256,32]{2,3,1,0:T(8,128)S(1)} %get-tuple-element.21), channel_id=1, source_target_pairs={{0,4},{4,0},{1,5},{5,1},{2,6},{6,2},{3,7},{7,3},{8,12},{12,8},{9,1... | collective-permute-start | bytes 196616 | tf_op jit(solution)/shard_map/ppermute | solution.py:29
  28.8 1.1 %copy-start = (f32[1,2,256,256]{3,2,1,0:T(8,128)S(1)}, f32[1,2,256,256]{3,2,1,0:T(8,128)}, u32[]{:S(2)}) copy-start(f32[1,2,256,256]{3,2,1,0:T(8,128)} %get-tuple-element.19) | copy-start | bytes 1572868
  30.5 8.4 %collective-permute-start.6 = (f32[2,128,256]{2,1,0:T(8,128)S(1)}, f32[2,128,256]{2,1,0:T(8,128)S(1)}, u32[]{:S(2)}, u32[]{:S(2)}) collective-permute-start(f32[2,128,256]{2,1,0:T(8,128)S(1)} %broadcast_select_fusion), channel_id=1, source_target_pairs={{0,1},{1,0},{2,3},{3,2},{4,5},{5,4},{6,7},{7,6},{8,9},{9,8},{10,11... | collective-permute-start | bytes 786440 | tf_op jit(solution)/shard_map/ppermute | solution.py:65
  32.2 5.0 %collective-permute-start.2 = (f32[1,2,256,32]{2,3,1,0:T(8,128)S(1)}, f32[1,2,256,32]{2,3,1,0:T(8,128)S(1)}, u32[]{:S(2)}, u32[]{:S(2)}) collective-permute-start(f32[1,2,256,32]{2,3,1,0:T(8,128)S(1)} %get-tuple-element.24), channel_id=1, source_target_pairs={{4,0},{0,4},{5,1},{1,5},{6,2},{2,6},{7,3},{3,7},{12,8},{8,12},{13,... | collective-permute-start | bytes 196616 | tf_op jit(solution)/shard_map/ppermute | solution.py:32
  33.3 4.6 %collective-permute-start.1 = (f32[1,2,256,32]{2,3,1,0:T(8,128)S(1)}, f32[1,2,256,32]{2,3,1,0:T(8,128)S(1)}, u32[]{:S(2)}, u32[]{:S(2)}) collective-permute-start(f32[1,2,256,32]{2,3,1,0:T(8,128)S(1)} %get-tuple-element.23), channel_id=1, source_target_pairs={{0,4},{4,0},{1,5},{5,1},{2,6},{6,2},{3,7},{7,3},{8,12},{12,8},{9,1... | collective-permute-start | bytes 196616 | tf_op jit(solution)/shard_map/ppermute | solution.py:29
  39.0 8.5 %collective-permute-start.7 = (f32[2,64,256]{2,1,0:T(8,128)S(1)}, f32[2,64,256]{2,1,0:T(8,128)S(1)}, u32[]{:S(2)}, u32[]{:S(2)}) collective-permute-start(f32[2,64,256]{2,1,0:T(8,128)S(1)} %slice_select_fusion), channel_id=1, source_target_pairs={{0,2},{1,3},{2,0},{3,1},{4,6},{5,7},{6,4},{7,5},{8,10},{9,11},{10,... | collective-permute-start | bytes 393224 | tf_op jit(solution)/shard_map/ppermute | solution.py:65
  47.5 8.5 %collective-permute-start.8 = (f32[2,64,256]{2,1,0:T(8,128)S(1)}, f32[2,64,256]{2,1,0:T(8,128)S(1)}, u32[]{:S(2)}, u32[]{:S(2)}) collective-permute-start(f32[2,64,256]{2,1,0:T(8,128)S(1)} %select_add_fusion.1), channel_id=1, source_target_pairs={{0,2},{1,3},{2,0},{3,1},{4,6},{5,7},{6,4},{7,5},{8,10},{9,11},{10,... | collective-permute-start | bytes 393224 | tf_op jit(solution)/shard_map/ppermute | solution.py:69
  56.1 6.4 %collective-permute-start.9 = (f32[2,128,256]{2,1,0:T(8,128)S(1)}, f32[2,128,256]{2,1,0:T(8,128)S(1)}, u32[]{:S(2)}, u32[]{:S(2)}) collective-permute-start(f32[2,128,256]{2,1,0:T(8,128)S(1)} %maximum_select_fusion.1), channel_id=1, source_target_pairs={{0,1},{1,0},{2,3},{3,2},{4,5},{5,4},{6,7},{7,6},{8,9},{9,8},{10,11... | collective-permute-start | bytes 786440 | tf_op jit(solution)/shard_map/ppermute | solution.py:69

commit v7 on v6

--- a/solution.py
+++ b/solution.py
@@ -75,19 +75,26 @@
     return held
 
 
-def table_kernel(both_ref, grid_ref, rows_ref, cols_ref):
-    angle_count, doubled = both_ref.shape[0], both_ref.shape[1]
-    count = doubled // 2
-    length = both_ref.shape[2]
-    core_size = rows_ref.shape[-1]
+def table_kernel(shift_ref, grid_ref, rows_fwd_ref, rows_back_ref, cols_fwd_ref, cols_back_ref):
+    angle_count = rows_fwd_ref.shape[0]
+    length = grid_ref.shape[0]
+    core_size = rows_fwd_ref.shape[-1]
     width = grid_ref.shape[1] // 2
+    lane = lax.broadcasted_iota(jnp.int32, (1, length), 1)
+    signed = jnp.where(lane >= length // 2, lane - length, lane)
+    frequency = signed.astype(jnp.float32) / length
+    base_phase = -math.pi * fresnel * frequency * frequency
     column = lax.broadcasted_iota(jnp.int32, (core_size, core_size), 1)
     low_mask = column >= core_size - MARGIN
     high_mask = column < MARGIN
+    outputs = (rows_fwd_ref, rows_back_ref, cols_fwd_ref, cols_back_ref)
     for a in range(angle_count):
-        product = jnp.dot(
-            both_ref[a], grid_ref[...], precision=highest, preferred_element_type=jnp.float32
-        )
+        row_line = base_phase - 2.0 * math.pi * frequency * shift_ref[2 * a]
+        col_line = base_phase - 2.0 * math.pi * frequency * shift_ref[2 * a + 1]
+        lines = jnp.concatenate([row_line, -row_line, col_line, -col_line], axis=0)
+        both = jnp.concatenate([jnp.cos(lines), jnp.sin(lines)], axis=0)
+        product = jnp.dot(both, grid_ref[...], precision=highest, preferred_element_type=jnp.float32)
+        count = 4
         cos_cos = product[:count, :width]
         cos_sin = product[:count, width:]
         sin_cos = product[count:, :width]
@@ -112,30 +119,33 @@
                 else:
                     parts.append(rolled(line, MARGIN)[:, :length])
             real, imag = parts
+            out = outputs[t]
             if t < 2:
-                rows_ref[a, t, 0] = real + imag
-                rows_ref[a, t, 1] = real
-                rows_ref[a, t, 2] = imag
+                out[a, 0] = real + imag
+                out[a, 1] = real
+                out[a, 2] = imag
             else:
-                cols_ref[a, t - 2, 0] = real
-                cols_ref[a, t - 2, 1] = imag - real
-                cols_ref[a, t - 2, 2] = real + imag
-
-
-def build_tables(lines, core_size):
-    angle_count, count, length = lines.shape
+                out[a, 0] = real
+                out[a, 1] = imag - real
+                out[a, 2] = real + imag
+
+
+def build_tables(shifts, core_size, length):
+    angle_count = shifts.shape[0]
     width = ((2 * length + 127) // 128) * 128
     ids = np.arange(length)[:, None] * np.arange(width)[None, :] % length
     angle = 2.0 * np.pi / length * ids
     grid = jnp.asarray(np.concatenate([np.cos(angle), np.sin(angle)], axis=1), jnp.float32)
-    both = jnp.concatenate([jnp.cos(lines), jnp.sin(lines)], axis=1)
+    rows = jax.ShapeDtypeStruct((angle_count, 3, core_size, core_size), jnp.float32)
+    cols = jax.ShapeDtypeStruct((angle_count, 3, core_size, length), jnp.float32)
     return pl.pallas_call(
         table_kernel,
-        out_shape=(
-            jax.ShapeDtypeStruct((angle_count, 2, 3, core_size, core_size), jnp.float32),
-            jax.ShapeDtypeStruct((angle_count, 2, 3, core_size, length), jnp.float32),
-        ),
-    )(both, grid)
+        out_shape=(rows, rows, cols, cols),
+        in_specs=[
+            pl.BlockSpec(memory_space=pltpu.SMEM),
+            pl.BlockSpec(memory_space=pltpu.VMEM),
+        ],
+    )(shifts.reshape(-1), grid)
 
 
 def apply_operator(wave, padded_cols, row_table, col_table):
@@ -161,21 +171,12 @@
     section = lax.axis_index("depth")
     sections = lax.axis_size("depth")
     is_first = section == 0
-    frequency = signed_freqs(length)
-    base_phase = -math.pi * fresnel * frequency * frequency
-
     tilt_angle = (tilt_index.astype(jnp.float32) - (TILTS - 1) / 2.0) * tilt_step
     lateral_drift = slice_step * jnp.tan(tilt_angle)
     shift_rows = jnp.where(is_first, positions[:, 0].astype(jnp.float32), 0.0)
     shift_cols = lateral_drift + jnp.where(is_first, positions[:, 1].astype(jnp.float32), 0.0)
-    row_line = base_phase[None, :] - 2.0 * math.pi * frequency[None, :] * shift_rows[:, None]
-    col_line = base_phase[None, :] - 2.0 * math.pi * frequency[None, :] * shift_cols[:, None]
-    lines = jnp.stack([row_line, -row_line, col_line, -col_line], axis=1)
-    row_tables, col_tables = build_tables(lines, core_size)
-    rows_fwd = row_tables[:, 0]
-    rows_back = row_tables[:, 1]
-    cols_fwd = col_tables[:, 0]
-    cols_back = col_tables[:, 1]
+    shifts = jnp.stack([shift_rows, shift_cols], axis=-1)
+    rows_fwd, rows_back, cols_fwd, cols_back = build_tables(shifts, core_size, length)
 
     cosine = jnp.cos(phase[0, 0])
     sine_part = jnp.sin(phase[0, 0])

time: 63.7 us -> 61.5 us (0.965)
  other arithmetic: 6.69 us -> 3.67 us
  waiting for transfers between devices: 24.2 us -> 25.5 us
  starting transfers between devices: 13.5 us -> 12.7 us
    squeeze x2 -> x0, local copies, waits for them, and re-layouts: 3.38 us -> none  [the longest x1 1.84 us: body(): cols_back = col_tables[:, 1]]
    unnamed x12 -> x14, local copies, waits for them, and re-layouts: 0.03 us -> 2.78 us
    ppermute x3, starting transfers between devices: 4.82 us -> 3.75 us  [padded_2(): lax.ppermute(lax.slice_in_dim(block, 0, width, axis=dim), axis, backward)]
    select_n x1, other arithmetic: 1.12 us -> 0.07 us  [body(): returning = jnp.where(section == sections - 1, residual, received[3])]
    select_n x1, other arithmetic: 1.1 us -> 0.06 us  [body(): wavefield = jnp.where(is_first, probe_wave, received[0])]
    cos x1, local copies, waits for them, and re-layouts: 0.97 us -> 1.91 us  [body(): cosine = jnp.cos(phase[0, 0])]
    convert_element_type x1, other arithmetic: 0.88 us -> 0.07 us  [body(): held_field = held_waves[0, 0].astype(jnp.float32)]
    ppermute x2, waiting for transfers between devices: 6.27 us -> 7.06 us  [halving_allreduce(): held = keep + lax.ppermute(give, axis, pairs)]
  transfers between devices with their start and end apart: 10 -> 10, of which waited for: 7 -> 7; matrix products, arithmetic and copies ran while one was open for 24% -> 16% of each run, Pallas kernels for 8% -> 8%
where the time goes in v7:
time: 61.5 us; the launch traced here: 61.2 us
  waiting for transfers between devices  25.5 us (41%)
  starting transfers between devices  12.7 us (21%)
  local copies, waits for them, and re-layouts  6.01 us (10%)
  matrix products  5.49 us (9%)
  Pallas kernels  4.86 us (8%)
  other arithmetic  3.67 us (6%)
  between operations  2.96 us (5%)
    ppermute x2, waiting for transfers between devices, halving_allreduce(): other = lax.ppermute(held, axis, pairs)  12.2 us
    ppermute x2, waiting for transfers between devices, halving_allreduce(): held = keep + lax.ppermute(give, axis, pairs)  7.06 us
    dot_general x12, matrix products, contract(): return jnp.einsum(form, left, right, precision=wave_precision)  5.49 us
    pallas_call x1, Pallas kernels, build_tables(): pl.pallas_call(table_kernel, out_shape=(rows, rows, cols, cols), in_specs...  4.86 us
    ppermute x3, starting transfers between devices, padded_2(): lax.ppermute(lax.slice_in_dim(block, block.shape[dim] - width, None, axis...  4.49 us
    ppermute x2, starting transfers between devices, halving_allreduce(): held = keep + lax.ppermute(give, axis, pairs)  4.29 us
    ppermute x3, starting transfers between devices, padded_2(): lax.ppermute(lax.slice_in_dim(block, 0, width, axis=dim), axis, backward)  3.75 us
    ppermute x3, waiting for transfers between devices, padded_2(): lax.ppermute(lax.slice_in_dim(block, block.shape[dim] - width, None, axis...  3.33 us
  transfers between devices with their start and end apart: 10, of which 7 were waited for; matrix products, arithmetic and copies ran while one was open for 16% of the time, Pallas kernels for 8%

profile of v7, /device:TPU:0, one launch (start us, length us, event | category | flops | bytes accessed | tf_op | source)
XLA Modules:
  0.0 61.2 jit_solution(3006483946257113467)
XLA Ops:
  0.6 2.4 %collective-permute-start = (f32[1,1,2,256,256]{4,3,2,1,0:T(8,128)}, f32[1,1,2,256,256]{4,3,2,1,0:T(8,128)S(1)}, u32[]{:S(2)}, u32[]{:S(2)}) collective-permute-start(f32[1,1,2,256,256]{4,3,2,1,0:T(8,128)} %param.11), channel_id=1, source_target_pairs={{0,8},{8,16},{16,24},{1,9},{9,17},{17,25},{2,10},{10,18},{18,26},{... | collective-permute-start | bytes 1572872 | tf_op jit(solution)/shard_map/ppermute | solution.py:29
  3.0 1.3 %collective-permute-start.3 = (f32[1,1,2,256,256]{4,3,2,1,0:T(8,128)}, f32[1,1,2,256,256]{4,3,2,1,0:T(8,128)S(1)}, u32[]{:S(2)}, u32[]{:S(2)}) collective-permute-start(f32[1,1,2,256,256]{4,3,2,1,0:T(8,128)} %param.12), channel_id=1, source_target_pairs={{8,0},{16,8},{24,16},{9,1},{17,9},{25,17},{10,2},{18,10},{26,18},{... | collective-permute-start | bytes 1572872 | tf_op jit(solution)/shard_map/ppermute | solution.py:32
  5.1 1.3 %fusion.76 = (s32[1,1]{1,0:T(1,128)}, s32[1,1]{1,0:T(1,128)}) fusion(s32[1,2]{1,0:T(1,128)} %param.16), kind=kLoop, calls=%fused_computation.118 | loop fusion | bytes 16 | tf_op jit(solution)/shard_map/slice | solution.py:176
  7.7 1.9 %fusion.75 = (f32[1,1,256,256]{3,2,1,0:T(8,128)S(1)}, f32[1,1,256,256]{3,2,1,0:T(8,128)S(1)}) fusion(f32[1,1,256,256]{3,2,1,0:T(8,128)} %param.10), kind=kLoop, calls=%fused_computation.117 | loop fusion | bytes 786432 | tf_op jit(solution)/shard_map/cos | solution.py:181
  9.6 0.6 maximum_bitcast_fusion.2.shift_ref
  10.2 4.9 %shard_map.112 = (f32[1,3,256,256]{3,2,1,0:T(8,128)}, f32[1,3,256,256]{3,2,1,0:T(8,128)}, f32[1,3,256,320]{3,2,1,0:T(8,128)}, f32[1,3,256,320]{3,2,1,0:T(8,128)}) custom-call(f32[2]{0:T(128)} %maximum_bitcast_fusion.2.shift_ref, f32[320,1280]{1,0:T(8,128)} %constant.25.clone.grid_ref), custom_call_target="tpu_custom_call" | custom-call | tf_op jit(solution)/shard_map/pallas_call | solution.py:141
  15.2 0.9 %copy-done.6 = f32[1,256,256]{2,1,0:T(8,128)S(1)} copy-done((f32[1,256,256]{2,1,0:T(8,128)S(1)}, f32[1,256,256]{2,1,0:T(8,128)}, u32[]{:S(2)}) %copy-start.6) | copy-done | bytes 262168
  16.2 1.0 %copy-done.4 = f32[1,3,256,256]{3,2,1,0:T(8,128)S(1)} copy-done((f32[1,3,256,256]{3,2,1,0:T(8,128)S(1)}, f32[1,3,256,256]{3,2,1,0:T(8,128)}, u32[]{:S(2)}) %copy-start.4) | copy-done | bytes 786456
  18.0 0.4 fusion.1
  18.4 2.4 %collective-permute-start.5 = (f32[1,2,256,32]{2,3,1,0:T(8,128)S(1)}, f32[1,2,256,32]{2,3,1,0:T(8,128)S(1)}, u32[]{:S(2)}, u32[]{:S(2)}) collective-permute-start(f32[1,2,256,32]{2,3,1,0:T(8,128)S(1)} %get-tuple-element.22), channel_id=1, source_target_pairs={{4,0},{0,4},{5,1},{1,5},{6,2},{2,6},{7,3},{3,7},{12,8},{8,12},{13,... | collective-permute-start | bytes 196616 | tf_op jit(solution)/shard_map/ppermute | solution.py:32
  21.0 0.9 %copy-done.3 = f32[1,3,256,256]{3,2,1,0:T(8,128)S(1)} copy-done((f32[1,3,256,256]{3,2,1,0:T(8,128)S(1)}, f32[1,3,256,256]{3,2,1,0:T(8,128)}, u32[]{:S(2)}) %copy-start.3) | copy-done | bytes 786456
  22.3 0.4 fusion.4
  22.7 0.4 fusion.5
  23.1 2.6 %collective-permute-done.4 = f32[1,2,256,32]{2,3,1,0:T(8,128)S(1)} collective-permute-done((f32[1,2,256,32]{2,3,1,0:T(8,128)S(1)}, f32[1,2,256,32]{2,3,1,0:T(8,128)S(1)}, u32[]{:S(2)}, u32[]{:S(2)}) %collective-permute-start.4) | collective-permute-done | bytes 65568 | tf_op jit(solution)/shard_map/ppermute | solution.py:29
  25.8 0.5 fusion.9
  26.3 0.5 convolution_subtract_fusion
  26.8 0.6 add_bitcast_fusion
  27.5 1.6 %collective-permute-start.6 = (f32[2,128,256]{2,1,0:T(8,128)S(1)}, f32[2,128,256]{2,1,0:T(8,128)S(1)}, u32[]{:S(2)}, u32[]{:S(2)}) collective-permute-start(f32[2,128,256]{2,1,0:T(8,128)S(1)} %broadcast_select_fusion), channel_id=1, source_target_pairs={{0,1},{1,0},{2,3},{3,2},{4,5},{5,4},{6,7},{7,6},{8,9},{9,8},{10,11... | collective-permute-start | bytes 786440 | tf_op jit(solution)/shard_map/ppermute | solution.py:65
  29.2 2.0 %collective-permute-start.1 = (f32[1,2,256,32]{2,3,1,0:T(8,128)S(1)}, f32[1,2,256,32]{2,3,1,0:T(8,128)S(1)}, u32[]{:S(2)}, u32[]{:S(2)}) collective-permute-start(f32[1,2,256,32]{2,3,1,0:T(8,128)S(1)} %get-tuple-element.23), channel_id=1, source_target_pairs={{0,4},{4,0},{1,5},{5,1},{2,6},{6,2},{3,7},{7,3},{8,12},{12,8},{9,1... | collective-permute-start | bytes 196616 | tf_op jit(solution)/shard_map/ppermute | solution.py:29
  31.2 2.9 %collective-permute-done.2 = f32[1,2,256,32]{2,3,1,0:T(8,128)S(1)} collective-permute-done((f32[1,2,256,32]{2,3,1,0:T(8,128)S(1)}, f32[1,2,256,32]{2,3,1,0:T(8,128)S(1)}, u32[]{:S(2)}, u32[]{:S(2)}) %collective-permute-start.2) | collective-permute-done | bytes 65568 | tf_op jit(solution)/shard_map/ppermute | solution.py:32
  34.1 0.7 %collective-permute-done.1 = f32[1,2,256,32]{2,3,1,0:T(8,128)S(1)} collective-permute-done((f32[1,2,256,32]{2,3,1,0:T(8,128)S(1)}, f32[1,2,256,32]{2,3,1,0:T(8,128)S(1)}, u32[]{:S(2)}, u32[]{:S(2)}) %collective-permute-start.1) | collective-permute-done | bytes 65568 | tf_op jit(solution)/shard_map/ppermute | solution.py:29
  34.9 1.4 %collective-permute-done.6 = f32[2,128,256]{2,1,0:T(8,128)S(1)} collective-permute-done((f32[2,128,256]{2,1,0:T(8,128)S(1)}, f32[2,128,256]{2,1,0:T(8,128)S(1)}, u32[]{:S(2)}, u32[]{:S(2)}) %collective-permute-start.6) | collective-permute-done | bytes 262176 | tf_op jit(solution)/shard_map/ppermute | solution.py:65
  36.3 2.7 %collective-permute-start.7 = (f32[2,64,256]{2,1,0:T(8,128)S(1)}, f32[2,64,256]{2,1,0:T(8,128)S(1)}, u32[]{:S(2)}, u32[]{:S(2)}) collective-permute-start(f32[2,64,256]{2,1,0:T(8,128)S(1)} %slice_select_fusion), channel_id=1, source_target_pairs={{0,2},{1,3},{2,0},{3,1},{4,6},{5,7},{6,4},{7,5},{8,10},{9,11},{10,... | collective-permute-start | bytes 393224 | tf_op jit(solution)/shard_map/ppermute | solution.py:65
  39.0 0.5 fusion.13
  39.5 5.7 %collective-permute-done.7 = f32[2,64,256]{2,1,0:T(8,128)S(1)} collective-permute-done((f32[2,64,256]{2,1,0:T(8,128)S(1)}, f32[2,64,256]{2,1,0:T(8,128)S(1)}, u32[]{:S(2)}, u32[]{:S(2)}) %collective-permute-start.7) | collective-permute-done | bytes 131104 | tf_op jit(solution)/shard_map/ppermute | solution.py:65
  45.3 0.5 fusion.2
  45.8 8.1 %collective-permute-done.8 = f32[2,64,256]{2,1,0:T(8,128)S(1)} collective-permute-done((f32[2,64,256]{2,1,0:T(8,128)S(1)}, f32[2,64,256]{2,1,0:T(8,128)S(1)}, u32[]{:S(2)}, u32[]{:S(2)}) %collective-permute-start.8) | collective-permute-done | bytes 131104 | tf_op jit(solution)/shard_map/ppermute | solution.py:69
  54.0 0.5 fusion.3
  54.5 0.8 %maximum_bitcast_fusion = f32[1,1,2,256,256]{4,3,2,1,0:T(8,128)} fusion(f32[1,1,256,256]{3,2,1,0:T(8,128)S(1)} %fusion.2, f32[1,1,256,256]{3,2,1,0:T(8,128)S(1)} %fusion.3), kind=kLoop, calls=%fused_computation.16 | loop fusion | flops 131072 | bytes 1048576 | tf_op jit(solution)/shard_map/broadcast_in_dim | solution.py:216
  55.3 0.8 %maximum_bitcast_fusion.1 = f32[1,1,2,256,256]{4,3,2,1,0:T(8,128)} fusion(f32[1,1,256,256]{3,2,1,0:T(8,128)S(1)} %get-tuple-element.17, f32[1,1,256,256]{3,2,1,0:T(8,128)S(1)} %get-tuple-element.18), kind=kLoop, calls=%fused_computation.17 | loop fusion | flops 131072 | bytes 1048576 | tf_op jit(solution)/shard_map/broadcast_in_dim | solution.py:216
  56.1 4.2 %collective-permute-done.9 = f32[2,128,256]{2,1,0:T(8,128)S(1)} collective-permute-done((f32[2,128,256]{2,1,0:T(8,128)S(1)}, f32[2,128,256]{2,1,0:T(8,128)S(1)}, u32[]{:S(2)}, u32[]{:S(2)}) %collective-permute-start.9) | collective-permute-done | bytes 262176 | tf_op jit(solution)/shard_map/ppermute | solution.py:69
  60.3 0.8 %maximum_select_fusion = f32[1,1,2,256,256]{4,3,2,1,0:T(8,128)} fusion(f32[1,1,2,128,256]{4,3,2,1,0:T(8,128)S(1)} %bitcast.164, f32[1,1,2,128,256]{4,3,2,1,0:T(8,128)S(1)} %bitcast.163, pred[]{:T(512)S(6)} %eq.18), kind=kLoop, calls=%fused_computation.20 | loop fusion | flops 393216 | bytes 1048577 | tf_op jit(solution)/shard_map/jit(_where)/select_n | solution.py:70
  (35 shorter events, 2.1 us)
Async XLA Ops:
  0.6 20.2 %collective-permute-start = (f32[1,1,2,256,256]{4,3,2,1,0:T(8,128)}, f32[1,1,2,256,256]{4,3,2,1,0:T(8,128)S(1)}, u32[]{:S(2)}, u32[]{:S(2)}) collective-permute-start(f32[1,1,2,256,256]{4,3,2,1,0:T(8,128)} %param.11), channel_id=1, source_target_pairs={{0,8},{8,16},{16,24},{1,9},{9,17},{17,25},{2,10},{10,18},{18,26},{... | collective-permute-start | bytes 1572872 | tf_op jit(solution)/shard_map/ppermute | solution.py:29
  3.0 13.1 %collective-permute-start.3 = (f32[1,1,2,256,256]{4,3,2,1,0:T(8,128)}, f32[1,1,2,256,256]{4,3,2,1,0:T(8,128)S(1)}, u32[]{:S(2)}, u32[]{:S(2)}) collective-permute-start(f32[1,1,2,256,256]{4,3,2,1,0:T(8,128)} %param.12), channel_id=1, source_target_pairs={{8,0},{16,8},{24,16},{9,1},{17,9},{25,17},{10,2},{18,10},{26,18},{... | collective-permute-start | bytes 1572872 | tf_op jit(solution)/shard_map/ppermute | solution.py:32
  7.7 7.4 %copy-start.2 = (bf16[1,2,1,2,256,256]{5,4,3,2,1,0:T(8,128)(2,1)S(1)}, bf16[1,2,1,2,256,256]{5,4,3,2,1,0:T(8,128)(2,1)}, u32[]{:S(2)}) copy-start(bf16[1,2,1,2,256,256]{5,4,3,2,1,0:T(8,128)(2,1)} %param.13) | copy-start | bytes 1572868
  15.1 1.0 %copy-start.6 = (f32[1,256,256]{2,1,0:T(8,128)S(1)}, f32[1,256,256]{2,1,0:T(8,128)}, u32[]{:S(2)}) copy-start(f32[1,256,256]{2,1,0:T(8,128)} %param.14) | copy-start | bytes 786436
  16.0 1.1 %copy-start.4 = (f32[1,3,256,256]{3,2,1,0:T(8,128)S(1)}, f32[1,3,256,256]{3,2,1,0:T(8,128)}, u32[]{:S(2)}) copy-start(f32[1,3,256,256]{3,2,1,0:T(8,128)} %get-tuple-element.9) | copy-start | bytes 2359300
  17.6 3.3 %copy-start.5 = (bf16[2,256,256]{2,1,0:T(8,128)(2,1)S(1)}, bf16[2,256,256]{2,1,0:T(8,128)(2,1)}, u32[]{:S(2)}) copy-start(bf16[2,256,256]{2,1,0:T(8,128)(2,1)} %param.9) | copy-start | bytes 786436
  18.4 4.7 %collective-permute-start.5 = (f32[1,2,256,32]{2,3,1,0:T(8,128)S(1)}, f32[1,2,256,32]{2,3,1,0:T(8,128)S(1)}, u32[]{:S(2)}, u32[]{:S(2)}) collective-permute-start(f32[1,2,256,32]{2,3,1,0:T(8,128)S(1)} %get-tuple-element.22), channel_id=1, source_target_pairs={{4,0},{0,4},{5,1},{1,5},{6,2},{2,6},{7,3},{3,7},{12,8},{8,12},{13,... | collective-permute-start | bytes 196616 | tf_op jit(solution)/shard_map/ppermute | solution.py:32
  20.8 1.1 %copy-start.3 = (f32[1,3,256,256]{3,2,1,0:T(8,128)S(1)}, f32[1,3,256,256]{3,2,1,0:T(8,128)}, u32[]{:S(2)}) copy-start(f32[1,3,256,256]{3,2,1,0:T(8,128)} %get-tuple-element.7) | copy-start | bytes 2359300
  20.8 5.0 %collective-permute-start.4 = (f32[1,2,256,32]{2,3,1,0:T(8,128)S(1)}, f32[1,2,256,32]{2,3,1,0:T(8,128)S(1)}, u32[]{:S(2)}, u32[]{:S(2)}) collective-permute-start(f32[1,2,256,32]{2,3,1,0:T(8,128)S(1)} %get-tuple-element.21), channel_id=1, source_target_pairs={{0,4},{4,0},{1,5},{5,1},{2,6},{6,2},{3,7},{7,3},{8,12},{12,8},{9,1... | collective-permute-start | bytes 196616 | tf_op jit(solution)/shard_map/ppermute | solution.py:29
  22.7 3.1 %copy-start.1 = (f32[1,3,256,320]{3,2,1,0:T(8,128)S(1)}, f32[1,3,256,320]{3,2,1,0:T(8,128)}, u32[]{:S(2)}) copy-start(f32[1,3,256,320]{3,2,1,0:T(8,128)} %get-tuple-element.10) | copy-start | bytes 2949124
  27.5 8.7 %collective-permute-start.6 = (f32[2,128,256]{2,1,0:T(8,128)S(1)}, f32[2,128,256]{2,1,0:T(8,128)S(1)}, u32[]{:S(2)}, u32[]{:S(2)}) collective-permute-start(f32[2,128,256]{2,1,0:T(8,128)S(1)} %broadcast_select_fusion), channel_id=1, source_target_pairs={{0,1},{1,0},{2,3},{3,2},{4,5},{5,4},{6,7},{7,6},{8,9},{9,8},{10,11... | collective-permute-start | bytes 786440 | tf_op jit(solution)/shard_map/ppermute | solution.py:65
  29.2 5.0 %collective-permute-start.2 = (f32[1,2,256,32]{2,3,1,0:T(8,128)S(1)}, f32[1,2,256,32]{2,3,1,0:T(8,128)S(1)}, u32[]{:S(2)}, u32[]{:S(2)}) collective-permute-start(f32[1,2,256,32]{2,3,1,0:T(8,128)S(1)} %get-tuple-element.24), channel_id=1, source_target_pairs={{4,0},{0,4},{5,1},{1,5},{6,2},{2,6},{7,3},{3,7},{12,8},{8,12},{13,... | collective-permute-start | bytes 196616 | tf_op jit(solution)/shard_map/ppermute | solution.py:32
  29.2 5.6 %collective-permute-start.1 = (f32[1,2,256,32]{2,3,1,0:T(8,128)S(1)}, f32[1,2,256,32]{2,3,1,0:T(8,128)S(1)}, u32[]{:S(2)}, u32[]{:S(2)}) collective-permute-start(f32[1,2,256,32]{2,3,1,0:T(8,128)S(1)} %get-tuple-element.23), channel_id=1, source_target_pairs={{0,4},{4,0},{1,5},{5,1},{2,6},{6,2},{3,7},{7,3},{8,12},{12,8},{9,1... | collective-permute-start | bytes 196616 | tf_op jit(solution)/shard_map/ppermute | solution.py:29
  31.2 7.7 %copy-start = (f32[1,3,256,320]{3,2,1,0:T(8,128)S(1)}, f32[1,3,256,320]{3,2,1,0:T(8,128)}, u32[]{:S(2)}) copy-start(f32[1,3,256,320]{3,2,1,0:T(8,128)} %get-tuple-element.8) | copy-start | bytes 2949124
  36.3 8.9 %collective-permute-start.7 = (f32[2,64,256]{2,1,0:T(8,128)S(1)}, f32[2,64,256]{2,1,0:T(8,128)S(1)}, u32[]{:S(2)}, u32[]{:S(2)}) collective-permute-start(f32[2,64,256]{2,1,0:T(8,128)S(1)} %slice_select_fusion), channel_id=1, source_target_pairs={{0,2},{1,3},{2,0},{3,1},{4,6},{5,7},{6,4},{7,5},{8,10},{9,11},{10,... | collective-permute-start | bytes 393224 | tf_op jit(solution)/shard_map/ppermute | solution.py:65
  45.2 8.7 %collective-permute-start.8 = (f32[2,64,256]{2,1,0:T(8,128)S(1)}, f32[2,64,256]{2,1,0:T(8,128)S(1)}, u32[]{:S(2)}, u32[]{:S(2)}) collective-permute-start(f32[2,64,256]{2,1,0:T(8,128)S(1)} %select_add_fusion.1), channel_id=1, source_target_pairs={{0,2},{1,3},{2,0},{3,1},{4,6},{5,7},{6,4},{7,5},{8,10},{9,11},{10,... | collective-permute-start | bytes 393224 | tf_op jit(solution)/shard_map/ppermute | solution.py:69
  53.9 6.4 %collective-permute-start.9 = (f32[2,128,256]{2,1,0:T(8,128)S(1)}, f32[2,128,256]{2,1,0:T(8,128)S(1)}, u32[]{:S(2)}, u32[]{:S(2)}) collective-permute-start(f32[2,128,256]{2,1,0:T(8,128)S(1)} %maximum_select_fusion.1), channel_id=1, source_target_pairs={{0,1},{1,0},{2,3},{3,2},{4,5},{5,4},{6,7},{7,6},{8,9},{9,8},{10,11... | collective-permute-start | bytes 786440 | tf_op jit(solution)/shard_map/ppermute | solution.py:69

commit v8 on v7

--- a/solution.py
+++ b/solution.py
@@ -75,7 +75,9 @@
     return held
 
 
-def table_kernel(shift_ref, grid_ref, rows_fwd_ref, rows_back_ref, cols_fwd_ref, cols_back_ref):
+def table_kernel(
+    tilt_ref, position_ref, first_ref, grid_ref, rows_fwd_ref, rows_back_ref, cols_fwd_ref, cols_back_ref
+):
     angle_count = rows_fwd_ref.shape[0]
     length = grid_ref.shape[0]
     core_size = rows_fwd_ref.shape[-1]
@@ -88,9 +90,17 @@
     low_mask = column >= core_size - MARGIN
     high_mask = column < MARGIN
     outputs = (rows_fwd_ref, rows_back_ref, cols_fwd_ref, cols_back_ref)
+    first = jnp.full((1, length), first_ref[0], jnp.int32).astype(jnp.float32)
     for a in range(angle_count):
-        row_line = base_phase - 2.0 * math.pi * frequency * shift_ref[2 * a]
-        col_line = base_phase - 2.0 * math.pi * frequency * shift_ref[2 * a + 1]
+        tilt = jnp.full((1, length), tilt_ref[a], jnp.int32).astype(jnp.float32)
+        tilt_angle = (tilt - (TILTS - 1) / 2.0) * tilt_step
+        drift = slice_step * (jnp.sin(tilt_angle) / jnp.cos(tilt_angle))
+        shift_rows = jnp.full((1, length), position_ref[2 * a], jnp.int32).astype(jnp.float32) * first
+        shift_cols = drift + jnp.full((1, length), position_ref[2 * a + 1], jnp.int32).astype(
+            jnp.float32
+        ) * first
+        row_line = base_phase - 2.0 * math.pi * frequency * shift_rows
+        col_line = base_phase - 2.0 * math.pi * frequency * shift_cols
         lines = jnp.concatenate([row_line, -row_line, col_line, -col_line], axis=0)
         both = jnp.concatenate([jnp.cos(lines), jnp.sin(lines)], axis=0)
         product = jnp.dot(both, grid_ref[...], precision=highest, preferred_element_type=jnp.float32)
@@ -130,8 +140,8 @@
                 out[a, 2] = real + imag
 
 
-def build_tables(shifts, core_size, length):
-    angle_count = shifts.shape[0]
+def build_tables(tilt_index, positions, is_first, core_size, length):
+    angle_count = tilt_index.shape[0]
     width = ((2 * length + 127) // 128) * 128
     ids = np.arange(length)[:, None] * np.arange(width)[None, :] % length
     angle = 2.0 * np.pi / length * ids
@@ -143,9 +153,11 @@
         out_shape=(rows, rows, cols, cols),
         in_specs=[
             pl.BlockSpec(memory_space=pltpu.SMEM),
+            pl.BlockSpec(memory_space=pltpu.SMEM),
+            pl.BlockSpec(memory_space=pltpu.SMEM),
             pl.BlockSpec(memory_space=pltpu.VMEM),
         ],
-    )(shifts.reshape(-1), grid)
+    )(tilt_index, positions.reshape(-1), is_first.astype(jnp.int32).reshape(1), grid)
 
 
 def apply_operator(wave, padded_cols, row_table, col_table):
@@ -171,12 +183,9 @@
     section = lax.axis_index("depth")
     sections = lax.axis_size("depth")
     is_first = section == 0
-    tilt_angle = (tilt_index.astype(jnp.float32) - (TILTS - 1) / 2.0) * tilt_step
-    lateral_drift = slice_step * jnp.tan(tilt_angle)
-    shift_rows = jnp.where(is_first, positions[:, 0].astype(jnp.float32), 0.0)
-    shift_cols = lateral_drift + jnp.where(is_first, positions[:, 1].astype(jnp.float32), 0.0)
-    shifts = jnp.stack([shift_rows, shift_cols], axis=-1)
-    rows_fwd, rows_back, cols_fwd, cols_back = build_tables(shifts, core_size, length)
+    rows_fwd, rows_back, cols_fwd, cols_back = build_tables(
+        tilt_index, positions, is_first, core_size, length
+    )
 
     cosine = jnp.cos(phase[0, 0])
     sine_part = jnp.sin(phase[0, 0])

time: 61.5 us -> 58.3 us (0.948)
  between operations: 2.96 us -> 1.57 us
  local copies, waits for them, and re-layouts: 6.01 us -> 4.63 us
    slice x1 -> x0, local copies, waits for them, and re-layouts: 1.31 us -> none  [body(): shift_rows = jnp.where(is_first, positions[:, 0].astype(jnp.float32), 0.0)]
  transfers between devices with their start and end apart: 10 -> 10, of which waited for: 7 -> 7; matrix products, arithmetic and copies ran while one was open for 16% -> 13% of each run, Pallas kernels for 8% -> 8%
where the time goes in v8:
time: 58.3 us; the launch traced here: 58 us
  waiting for transfers between devices  25.5 us (44%)
  starting transfers between devices  12.8 us (22%)
  matrix products  5.5 us (9%)
  Pallas kernels  4.9 us (8%)
  local copies, waits for them, and re-layouts  4.63 us (8%)
  other arithmetic  3.08 us (5%)
  between operations  1.57 us (3%)
    ppermute x2, waiting for transfers between devices, halving_allreduce(): other = lax.ppermute(held, axis, pairs)  12.2 us
    ppermute x2, waiting for transfers between devices, halving_allreduce(): held = keep + lax.ppermute(give, axis, pairs)  7.07 us
    dot_general x12, matrix products, contract(): return jnp.einsum(form, left, right, precision=wave_precision)  5.5 us
    pallas_call x1, Pallas kernels, build_tables(): pl.pallas_call(table_kernel, out_shape=(rows, rows, cols, cols), in_specs...  4.9 us
    ppermute x3, starting transfers between devices, padded_2(): lax.ppermute(lax.slice_in_dim(block, block.shape[dim] - width, None, axis...  4.62 us
    ppermute x2, starting transfers between devices, halving_allreduce(): held = keep + lax.ppermute(give, axis, pairs)  4.29 us
    ppermute x3, starting transfers between devices, padded_2(): lax.ppermute(lax.slice_in_dim(block, 0, width, axis=dim), axis, backward)  3.75 us
    ppermute x3, waiting for transfers between devices, padded_2(): lax.ppermute(lax.slice_in_dim(block, block.shape[dim] - width, None, axis...  3.33 us
  transfers between devices with their start and end apart: 10, of which 7 were waited for; matrix products, arithmetic and copies ran while one was open for 13% of the time, Pallas kernels for 8%

profile of v8, /device:TPU:0, one launch (start us, length us, event | category | flops | bytes accessed | tf_op | source)
XLA Modules:
  0.0 58.0 jit_solution(6817479641608163179)
XLA Ops:
  0.6 2.5 %collective-permute-start = (f32[1,1,2,256,256]{4,3,2,1,0:T(8,128)}, f32[1,1,2,256,256]{4,3,2,1,0:T(8,128)S(1)}, u32[]{:S(2)}, u32[]{:S(2)}) collective-permute-start(f32[1,1,2,256,256]{4,3,2,1,0:T(8,128)} %param.11), channel_id=1, source_target_pairs={{0,8},{8,16},{16,24},{1,9},{9,17},{17,25},{2,10},{10,18},{18,26},{... | collective-permute-start | bytes 1572872 | tf_op jit(solution)/shard_map/ppermute | solution.py:29
  3.2 1.3 %collective-permute-start.3 = (f32[1,1,2,256,256]{4,3,2,1,0:T(8,128)}, f32[1,1,2,256,256]{4,3,2,1,0:T(8,128)S(1)}, u32[]{:S(2)}, u32[]{:S(2)}) collective-permute-start(f32[1,1,2,256,256]{4,3,2,1,0:T(8,128)} %param.12), channel_id=1, source_target_pairs={{8,0},{16,8},{24,16},{9,1},{17,9},{25,17},{10,2},{18,10},{26,18},{... | collective-permute-start | bytes 1572872 | tf_op jit(solution)/shard_map/ppermute | solution.py:32
  4.5 1.9 %fusion.75 = (f32[1,1,256,256]{3,2,1,0:T(8,128)S(1)}, f32[1,1,256,256]{3,2,1,0:T(8,128)S(1)}) fusion(f32[1,1,256,256]{3,2,1,0:T(8,128)} %param.10), kind=kLoop, calls=%fused_computation.116 | loop fusion | bytes 786432 | tf_op jit(solution)/shard_map/cos | solution.py:190
  7.0 4.9 %shard_map.112 = (f32[1,3,256,256]{3,2,1,0:T(8,128)}, f32[1,3,256,256]{3,2,1,0:T(8,128)}, f32[1,3,256,320]{3,2,1,0:T(8,128)}, f32[1,3,256,320]{3,2,1,0:T(8,128)}) custom-call(s32[1]{0:T(128)S(6)} %copy.12.tilt_ref, s32[2]{0:T(128)} %bitcast.160, s32[1]{0:T(128)} %bitcast.1.first_ref, f32[320,1280]{1,0:T(8,128)} %constant.16.clone.grid_ref), custom_call_target="tpu_custom_call" | custom-call | tf_op jit(solution)/shard_map/pallas_call | solution.py:151
  12.0 0.9 %copy-done.6 = f32[1,256,256]{2,1,0:T(8,128)S(1)} copy-done((f32[1,256,256]{2,1,0:T(8,128)S(1)}, f32[1,256,256]{2,1,0:T(8,128)}, u32[]{:S(2)}) %copy-start.6) | copy-done | bytes 262168
  13.0 1.0 %copy-done.4 = f32[1,3,256,256]{3,2,1,0:T(8,128)S(1)} copy-done((f32[1,3,256,256]{3,2,1,0:T(8,128)S(1)}, f32[1,3,256,256]{3,2,1,0:T(8,128)}, u32[]{:S(2)}) %copy-start.4) | copy-done | bytes 786456
  14.4 0.4 fusion
  14.8 0.4 fusion.1
  15.2 2.4 %collective-permute-start.5 = (f32[1,2,256,32]{2,3,1,0:T(8,128)S(1)}, f32[1,2,256,32]{2,3,1,0:T(8,128)S(1)}, u32[]{:S(2)}, u32[]{:S(2)}) collective-permute-start(f32[1,2,256,32]{2,3,1,0:T(8,128)S(1)} %get-tuple-element.22), channel_id=1, source_target_pairs={{4,0},{0,4},{5,1},{1,5},{6,2},{2,6},{7,3},{3,7},{12,8},{8,12},{13,... | collective-permute-start | bytes 196616 | tf_op jit(solution)/shard_map/ppermute | solution.py:32
  17.8 0.9 %copy-done.3 = f32[1,3,256,256]{3,2,1,0:T(8,128)S(1)} copy-done((f32[1,3,256,256]{3,2,1,0:T(8,128)S(1)}, f32[1,3,256,256]{3,2,1,0:T(8,128)}, u32[]{:S(2)}) %copy-start.3) | copy-done | bytes 786456
  18.7 0.4 fusion.57
  19.1 0.4 fusion.4
  19.5 0.4 fusion.5
  19.9 2.6 %collective-permute-done.4 = f32[1,2,256,32]{2,3,1,0:T(8,128)S(1)} collective-permute-done((f32[1,2,256,32]{2,3,1,0:T(8,128)S(1)}, f32[1,2,256,32]{2,3,1,0:T(8,128)S(1)}, u32[]{:S(2)}, u32[]{:S(2)}) %collective-permute-start.4) | collective-permute-done | bytes 65568 | tf_op jit(solution)/shard_map/ppermute | solution.py:29
  22.6 0.5 fusion.9
  23.1 0.5 convolution_subtract_fusion
  23.7 0.6 %add_bitcast_fusion = (f32[1,256,256]{2,1,0:T(8,128)S(1)}, f32[1,256,256]{2,1,0:T(8,128)S(1)}, f32[1,1,256,256]{3,2,1,0:T(8,128)S(1)}, f32[1,1,256,256]{3,2,1,0:T(8,128)S(1)}) fusion(f32[256,256]{1,0:T(8,128)S(1)} %convolution_subtract_fusion, f32[1,2,256,256]{3,2,1,0:T(8,128)S(1)} %get-tuple-element.19, f32[1,1,256,256]{3,2,1,0:T(8,128)S(1)} %get-tuple-element.26, ...), kind=kOutput, calls=%fused_computation.91 | convolution fusion | flops 126681088 | bytes 3342336 | tf_op jit(solution)/shard_map/ajk,aik->aji/dot_general | solution.py:38
  24.3 1.6 %collective-permute-start.6 = (f32[2,128,256]{2,1,0:T(8,128)S(1)}, f32[2,128,256]{2,1,0:T(8,128)S(1)}, u32[]{:S(2)}, u32[]{:S(2)}) collective-permute-start(f32[2,128,256]{2,1,0:T(8,128)S(1)} %broadcast_select_fusion), channel_id=1, source_target_pairs={{0,1},{1,0},{2,3},{3,2},{4,5},{5,4},{6,7},{7,6},{8,9},{9,8},{10,11... | collective-permute-start | bytes 786440 | tf_op jit(solution)/shard_map/ppermute | solution.py:65
  26.0 2.0 %collective-permute-start.1 = (f32[1,2,256,32]{2,3,1,0:T(8,128)S(1)}, f32[1,2,256,32]{2,3,1,0:T(8,128)S(1)}, u32[]{:S(2)}, u32[]{:S(2)}) collective-permute-start(f32[1,2,256,32]{2,3,1,0:T(8,128)S(1)} %get-tuple-element.23), channel_id=1, source_target_pairs={{0,4},{4,0},{1,5},{5,1},{2,6},{6,2},{3,7},{7,3},{8,12},{12,8},{9,1... | collective-permute-start | bytes 196616 | tf_op jit(solution)/shard_map/ppermute | solution.py:29
  28.1 2.9 %collective-permute-done.2 = f32[1,2,256,32]{2,3,1,0:T(8,128)S(1)} collective-permute-done((f32[1,2,256,32]{2,3,1,0:T(8,128)S(1)}, f32[1,2,256,32]{2,3,1,0:T(8,128)S(1)}, u32[]{:S(2)}, u32[]{:S(2)}) %collective-permute-start.2) | collective-permute-done | bytes 65568 | tf_op jit(solution)/shard_map/ppermute | solution.py:32
  30.9 0.7 %collective-permute-done.1 = f32[1,2,256,32]{2,3,1,0:T(8,128)S(1)} collective-permute-done((f32[1,2,256,32]{2,3,1,0:T(8,128)S(1)}, f32[1,2,256,32]{2,3,1,0:T(8,128)S(1)}, u32[]{:S(2)}, u32[]{:S(2)}) %collective-permute-start.1) | collective-permute-done | bytes 65568 | tf_op jit(solution)/shard_map/ppermute | solution.py:29
  31.7 1.4 %collective-permute-done.6 = f32[2,128,256]{2,1,0:T(8,128)S(1)} collective-permute-done((f32[2,128,256]{2,1,0:T(8,128)S(1)}, f32[2,128,256]{2,1,0:T(8,128)S(1)}, u32[]{:S(2)}, u32[]{:S(2)}) %collective-permute-start.6) | collective-permute-done | bytes 262176 | tf_op jit(solution)/shard_map/ppermute | solution.py:65
  33.1 2.7 %collective-permute-start.7 = (f32[2,64,256]{2,1,0:T(8,128)S(1)}, f32[2,64,256]{2,1,0:T(8,128)S(1)}, u32[]{:S(2)}, u32[]{:S(2)}) collective-permute-start(f32[2,64,256]{2,1,0:T(8,128)S(1)} %slice_select_fusion), channel_id=1, source_target_pairs={{0,2},{1,3},{2,0},{3,1},{4,6},{5,7},{6,4},{7,5},{8,10},{9,11},{10,... | collective-permute-start | bytes 393224 | tf_op jit(solution)/shard_map/ppermute | solution.py:65
  35.8 0.5 fusion.13
  36.3 5.7 %collective-permute-done.7 = f32[2,64,256]{2,1,0:T(8,128)S(1)} collective-permute-done((f32[2,64,256]{2,1,0:T(8,128)S(1)}, f32[2,64,256]{2,1,0:T(8,128)S(1)}, u32[]{:S(2)}, u32[]{:S(2)}) %collective-permute-start.7) | collective-permute-done | bytes 131104 | tf_op jit(solution)/shard_map/ppermute | solution.py:65
  42.1 0.5 fusion.2
  42.6 8.1 %collective-permute-done.8 = f32[2,64,256]{2,1,0:T(8,128)S(1)} collective-permute-done((f32[2,64,256]{2,1,0:T(8,128)S(1)}, f32[2,64,256]{2,1,0:T(8,128)S(1)}, u32[]{:S(2)}, u32[]{:S(2)}) %collective-permute-start.8) | collective-permute-done | bytes 131104 | tf_op jit(solution)/shard_map/ppermute | solution.py:69
  50.8 0.5 fusion.3
  51.3 0.8 %maximum_bitcast_fusion = f32[1,1,2,256,256]{4,3,2,1,0:T(8,128)} fusion(f32[1,1,256,256]{3,2,1,0:T(8,128)S(1)} %fusion.2, f32[1,1,256,256]{3,2,1,0:T(8,128)S(1)} %fusion.3), kind=kLoop, calls=%fused_computation.16 | loop fusion | flops 131072 | bytes 1048576 | tf_op jit(solution)/shard_map/broadcast_in_dim | solution.py:225
  52.1 0.8 %maximum_bitcast_fusion.1 = f32[1,1,2,256,256]{4,3,2,1,0:T(8,128)} fusion(f32[1,1,256,256]{3,2,1,0:T(8,128)S(1)} %get-tuple-element.17, f32[1,1,256,256]{3,2,1,0:T(8,128)S(1)} %get-tuple-element.18), kind=kLoop, calls=%fused_computation.17 | loop fusion | flops 131072 | bytes 1048576 | tf_op jit(solution)/shard_map/broadcast_in_dim | solution.py:225
  53.0 4.2 %collective-permute-done.9 = f32[2,128,256]{2,1,0:T(8,128)S(1)} collective-permute-done((f32[2,128,256]{2,1,0:T(8,128)S(1)}, f32[2,128,256]{2,1,0:T(8,128)S(1)}, u32[]{:S(2)}, u32[]{:S(2)}) %collective-permute-start.9) | collective-permute-done | bytes 262176 | tf_op jit(solution)/shard_map/ppermute | solution.py:69
  57.1 0.8 %maximum_select_fusion = f32[1,1,2,256,256]{4,3,2,1,0:T(8,128)} fusion(f32[1,1,2,128,256]{4,3,2,1,0:T(8,128)S(1)} %bitcast.159, f32[1,1,2,128,256]{4,3,2,1,0:T(8,128)S(1)} %bitcast.158, pred[]{:T(512)S(6)} %eq.18), kind=kLoop, calls=%fused_computation.20 | loop fusion | flops 393216 | bytes 1048577 | tf_op jit(solution)/shard_map/jit(_where)/select_n | solution.py:70
  (33 shorter events, 1.3 us)
Async XLA Ops:
  0.6 11.3 %copy-start.2 = (bf16[1,2,1,2,256,256]{5,4,3,2,1,0:T(8,128)(2,1)S(1)}, bf16[1,2,1,2,256,256]{5,4,3,2,1,0:T(8,128)(2,1)}, u32[]{:S(2)}) copy-start(bf16[1,2,1,2,256,256]{5,4,3,2,1,0:T(8,128)(2,1)} %param.13) | copy-start | bytes 1572868
  0.6 17.0 %collective-permute-start = (f32[1,1,2,256,256]{4,3,2,1,0:T(8,128)}, f32[1,1,2,256,256]{4,3,2,1,0:T(8,128)S(1)}, u32[]{:S(2)}, u32[]{:S(2)}) collective-permute-start(f32[1,1,2,256,256]{4,3,2,1,0:T(8,128)} %param.11), channel_id=1, source_target_pairs={{0,8},{8,16},{16,24},{1,9},{9,17},{17,25},{2,10},{10,18},{18,26},{... | collective-permute-start | bytes 1572872 | tf_op jit(solution)/shard_map/ppermute | solution.py:29
  3.2 9.7 %collective-permute-start.3 = (f32[1,1,2,256,256]{4,3,2,1,0:T(8,128)}, f32[1,1,2,256,256]{4,3,2,1,0:T(8,128)S(1)}, u32[]{:S(2)}, u32[]{:S(2)}) collective-permute-start(f32[1,1,2,256,256]{4,3,2,1,0:T(8,128)} %param.12), channel_id=1, source_target_pairs={{8,0},{16,8},{24,16},{9,1},{17,9},{25,17},{10,2},{18,10},{26,18},{... | collective-permute-start | bytes 1572872 | tf_op jit(solution)/shard_map/ppermute | solution.py:32
  11.9 1.0 %copy-start.6 = (f32[1,256,256]{2,1,0:T(8,128)S(1)}, f32[1,256,256]{2,1,0:T(8,128)}, u32[]{:S(2)}) copy-start(f32[1,256,256]{2,1,0:T(8,128)} %param.14) | copy-start | bytes 786436
  12.8 1.1 %copy-start.4 = (f32[1,3,256,256]{3,2,1,0:T(8,128)S(1)}, f32[1,3,256,256]{3,2,1,0:T(8,128)}, u32[]{:S(2)}) copy-start(f32[1,3,256,256]{3,2,1,0:T(8,128)} %get-tuple-element.9) | copy-start | bytes 2359300
  14.4 3.3 %copy-start.5 = (bf16[2,256,256]{2,1,0:T(8,128)(2,1)S(1)}, bf16[2,256,256]{2,1,0:T(8,128)(2,1)}, u32[]{:S(2)}) copy-start(bf16[2,256,256]{2,1,0:T(8,128)(2,1)} %param.9) | copy-start | bytes 786436
  15.2 4.7 %collective-permute-start.5 = (f32[1,2,256,32]{2,3,1,0:T(8,128)S(1)}, f32[1,2,256,32]{2,3,1,0:T(8,128)S(1)}, u32[]{:S(2)}, u32[]{:S(2)}) collective-permute-start(f32[1,2,256,32]{2,3,1,0:T(8,128)S(1)} %get-tuple-element.22), channel_id=1, source_target_pairs={{4,0},{0,4},{5,1},{1,5},{6,2},{2,6},{7,3},{3,7},{12,8},{8,12},{13,... | collective-permute-start | bytes 196616 | tf_op jit(solution)/shard_map/ppermute | solution.py:32
  17.6 1.1 %copy-start.3 = (f32[1,3,256,256]{3,2,1,0:T(8,128)S(1)}, f32[1,3,256,256]{3,2,1,0:T(8,128)}, u32[]{:S(2)}) copy-start(f32[1,3,256,256]{3,2,1,0:T(8,128)} %get-tuple-element.7) | copy-start | bytes 2359300
  17.6 5.0 %collective-permute-start.4 = (f32[1,2,256,32]{2,3,1,0:T(8,128)S(1)}, f32[1,2,256,32]{2,3,1,0:T(8,128)S(1)}, u32[]{:S(2)}, u32[]{:S(2)}) collective-permute-start(f32[1,2,256,32]{2,3,1,0:T(8,128)S(1)} %get-tuple-element.21), channel_id=1, source_target_pairs={{0,4},{4,0},{1,5},{5,1},{2,6},{6,2},{3,7},{7,3},{8,12},{12,8},{9,1... | collective-permute-start | bytes 196616 | tf_op jit(solution)/shard_map/ppermute | solution.py:29
  19.5 3.1 %copy-start.1 = (f32[1,3,256,320]{3,2,1,0:T(8,128)S(1)}, f32[1,3,256,320]{3,2,1,0:T(8,128)}, u32[]{:S(2)}) copy-start(f32[1,3,256,320]{3,2,1,0:T(8,128)} %get-tuple-element.10) | copy-start | bytes 2949124
  24.3 8.7 %collective-permute-start.6 = (f32[2,128,256]{2,1,0:T(8,128)S(1)}, f32[2,128,256]{2,1,0:T(8,128)S(1)}, u32[]{:S(2)}, u32[]{:S(2)}) collective-permute-start(f32[2,128,256]{2,1,0:T(8,128)S(1)} %broadcast_select_fusion), channel_id=1, source_target_pairs={{0,1},{1,0},{2,3},{3,2},{4,5},{5,4},{6,7},{7,6},{8,9},{9,8},{10,11... | collective-permute-start | bytes 786440 | tf_op jit(solution)/shard_map/ppermute | solution.py:65
  26.0 4.9 %collective-permute-start.2 = (f32[1,2,256,32]{2,3,1,0:T(8,128)S(1)}, f32[1,2,256,32]{2,3,1,0:T(8,128)S(1)}, u32[]{:S(2)}, u32[]{:S(2)}) collective-permute-start(f32[1,2,256,32]{2,3,1,0:T(8,128)S(1)} %get-tuple-element.24), channel_id=1, source_target_pairs={{4,0},{0,4},{5,1},{1,5},{6,2},{2,6},{7,3},{3,7},{12,8},{8,12},{13,... | collective-permute-start | bytes 196616 | tf_op jit(solution)/shard_map/ppermute | solution.py:32
  26.0 5.6 %collective-permute-start.1 = (f32[1,2,256,32]{2,3,1,0:T(8,128)S(1)}, f32[1,2,256,32]{2,3,1,0:T(8,128)S(1)}, u32[]{:S(2)}, u32[]{:S(2)}) collective-permute-start(f32[1,2,256,32]{2,3,1,0:T(8,128)S(1)} %get-tuple-element.23), channel_id=1, source_target_pairs={{0,4},{4,0},{1,5},{5,1},{2,6},{6,2},{3,7},{7,3},{8,12},{12,8},{9,1... | collective-permute-start | bytes 196616 | tf_op jit(solution)/shard_map/ppermute | solution.py:29
  28.1 7.7 %copy-start = (f32[1,3,256,320]{3,2,1,0:T(8,128)S(1)}, f32[1,3,256,320]{3,2,1,0:T(8,128)}, u32[]{:S(2)}) copy-start(f32[1,3,256,320]{3,2,1,0:T(8,128)} %get-tuple-element.8) | copy-start | bytes 2949124
  33.1 8.9 %collective-permute-start.7 = (f32[2,64,256]{2,1,0:T(8,128)S(1)}, f32[2,64,256]{2,1,0:T(8,128)S(1)}, u32[]{:S(2)}, u32[]{:S(2)}) collective-permute-start(f32[2,64,256]{2,1,0:T(8,128)S(1)} %slice_select_fusion), channel_id=1, source_target_pairs={{0,2},{1,3},{2,0},{3,1},{4,6},{5,7},{6,4},{7,5},{8,10},{9,11},{10,... | collective-permute-start | bytes 393224 | tf_op jit(solution)/shard_map/ppermute | solution.py:65
  42.0 8.7 %collective-permute-start.8 = (f32[2,64,256]{2,1,0:T(8,128)S(1)}, f32[2,64,256]{2,1,0:T(8,128)S(1)}, u32[]{:S(2)}, u32[]{:S(2)}) collective-permute-start(f32[2,64,256]{2,1,0:T(8,128)S(1)} %select_add_fusion.1), channel_id=1, source_target_pairs={{0,2},{1,3},{2,0},{3,1},{4,6},{5,7},{6,4},{7,5},{8,10},{9,11},{10,... | collective-permute-start | bytes 393224 | tf_op jit(solution)/shard_map/ppermute | solution.py:69
  50.7 6.4 %collective-permute-start.9 = (f32[2,128,256]{2,1,0:T(8,128)S(1)}, f32[2,128,256]{2,1,0:T(8,128)S(1)}, u32[]{:S(2)}, u32[]{:S(2)}) collective-permute-start(f32[2,128,256]{2,1,0:T(8,128)S(1)} %maximum_select_fusion.1), channel_id=1, source_target_pairs={{0,1},{1,0},{2,3},{3,2},{4,5},{5,4},{6,7},{7,6},{8,9},{9,8},{10,11... | collective-permute-start | bytes 786440 | tf_op jit(solution)/shard_map/ppermute | solution.py:69

commit v9 on v8

--- a/solution.py
+++ b/solution.py
@@ -206,7 +206,14 @@
     )
 
     def side_halo(field):
-        return padded_2(field, (("tile", 3),), MARGIN, True)
+        count = lax.axis_size("tile")
+        if count > 2:
+            return padded_2(field, (("tile", 3),), MARGIN, True)
+        width = field.shape[3]
+        edges = jnp.concatenate([field[..., :MARGIN], field[..., width - MARGIN :]], axis=3)
+        if count == 2:
+            edges = lax.ppermute(edges, "tile", [(0, 1), (1, 0)])
+        return jnp.concatenate([edges[..., MARGIN:], field, edges[..., :MARGIN]], axis=3)
 
     spread = apply_operator(returning, side_halo, rows_back, cols_back)
     held_field = held_waves[0, 0].astype(jnp.float32)

time: 58.3 us -> 57.6 us (0.988)
  local copies, waits for them, and re-layouts: 4.63 us -> 3.76 us
    ppermute x2, waiting for transfers between devices: 7.07 us -> 12.4 us  [halving_allreduce(): held = keep + lax.ppermute(give, axis, pairs)]
    ppermute x0 -> x2, starting transfers between devices: none -> 3.38 us  [side_halo(): edges = lax.ppermute(edges, 'tile', [(0, 1), (1, 0)])]
    ppermute x3 -> x1, waiting for transfers between devices: 3.33 us -> 0.01 us  [padded_2(): lax.ppermute(lax.slice_in_dim(block, block.shape[dim] - width, None, axis...]
    ppermute x3 -> x1, waiting for transfers between devices: 2.86 us -> 0.01 us  [padded_2(): lax.ppermute(lax.slice_in_dim(block, 0, width, axis=dim), axis, backward)]
    ppermute x3 -> x1, starting transfers between devices: 3.75 us -> 1.29 us  [padded_2(): lax.ppermute(lax.slice_in_dim(block, 0, width, axis=dim), axis, backward)]
    ppermute x3 -> x1, starting transfers between devices: 4.62 us -> 2.52 us  [padded_2(): lax.ppermute(lax.slice_in_dim(block, block.shape[dim] - width, None, axis...]
    ppermute x2, starting transfers between devices: 4.29 us -> 5.67 us  [halving_allreduce(): held = keep + lax.ppermute(give, axis, pairs)]
    unnamed x14, local copies, waits for them, and re-layouts: 2.78 us -> 1.88 us
  transfers between devices with their start and end apart: 10 -> 8, of which waited for: 7 -> 5; matrix products, arithmetic and copies ran while one was open for 13% -> 17% of each run, Pallas kernels for 8% -> 9%
where the time goes in v9:
time: 57.6 us; the launch traced here: 57.3 us
  waiting for transfers between devices  25.4 us (44%)
  starting transfers between devices  13 us (23%)
  matrix products  5.51 us (10%)
  Pallas kernels  4.89 us (8%)
  local copies, waits for them, and re-layouts  3.76 us (7%)
  other arithmetic  3.07 us (5%)
  between operations  1.59 us (3%)
    ppermute x2, waiting for transfers between devices, halving_allreduce(): held = keep + lax.ppermute(give, axis, pairs)  12.4 us
    ppermute x2, waiting for transfers between devices, halving_allreduce(): other = lax.ppermute(held, axis, pairs)  12.4 us
    ppermute x2, starting transfers between devices, halving_allreduce(): held = keep + lax.ppermute(give, axis, pairs)  5.67 us
    dot_general x12, matrix products, contract(): return jnp.einsum(form, left, right, precision=wave_precision)  5.51 us
    pallas_call x1, Pallas kernels, build_tables(): pl.pallas_call(table_kernel, out_shape=(rows, rows, cols, cols), in_specs...  4.89 us
    ppermute x2, starting transfers between devices, side_halo(): edges = lax.ppermute(edges, 'tile', [(0, 1), (1, 0)])  3.38 us
    ppermute x1, starting transfers between devices, padded_2(): lax.ppermute(lax.slice_in_dim(block, block.shape[dim] - width, None, axis...  2.52 us
    unnamed x14, local copies, waits for them, and re-layouts  1.88 us
  transfers between devices with their start and end apart: 8, of which 5 were waited for; matrix products, arithmetic and copies ran while one was open for 17% of the time, Pallas kernels for 9%

profile of v9, /device:TPU:0, one launch (start us, length us, event | category | flops | bytes accessed | tf_op | source)
XLA Modules:
  0.0 57.3 jit_solution(11494240909729582737)
XLA Ops:
  0.6 2.5 %collective-permute-start = (f32[1,1,2,256,256]{4,3,2,1,0:T(8,128)}, f32[1,1,2,256,256]{4,3,2,1,0:T(8,128)S(1)}, u32[]{:S(2)}, u32[]{:S(2)}) collective-permute-start(f32[1,1,2,256,256]{4,3,2,1,0:T(8,128)} %param.11), channel_id=1, source_target_pairs={{0,8},{8,16},{16,24},{1,9},{9,17},{17,25},{2,10},{10,18},{18,26},{... | collective-permute-start | bytes 1572872 | tf_op jit(solution)/shard_map/ppermute | solution.py:29
  3.2 1.3 %collective-permute-start.2 = (f32[1,1,2,256,256]{4,3,2,1,0:T(8,128)}, f32[1,1,2,256,256]{4,3,2,1,0:T(8,128)S(1)}, u32[]{:S(2)}, u32[]{:S(2)}) collective-permute-start(f32[1,1,2,256,256]{4,3,2,1,0:T(8,128)} %param.12), channel_id=1, source_target_pairs={{8,0},{16,8},{24,16},{9,1},{17,9},{25,17},{10,2},{18,10},{26,18},{... | collective-permute-start | bytes 1572872 | tf_op jit(solution)/shard_map/ppermute | solution.py:32
  4.5 1.9 %fusion.77 = (f32[1,1,256,256]{3,2,1,0:T(8,128)S(1)}, f32[1,1,256,256]{3,2,1,0:T(8,128)S(1)}) fusion(f32[1,1,256,256]{3,2,1,0:T(8,128)} %param.10), kind=kLoop, calls=%fused_computation.120 | loop fusion | bytes 786432 | tf_op jit(solution)/shard_map/cos | solution.py:190
  7.0 4.9 %shard_map.112 = (f32[1,3,256,256]{3,2,1,0:T(8,128)}, f32[1,3,256,256]{3,2,1,0:T(8,128)}, f32[1,3,256,320]{3,2,1,0:T(8,128)}, f32[1,3,256,320]{3,2,1,0:T(8,128)}) custom-call(s32[1]{0:T(128)S(6)} %copy.12.tilt_ref, s32[2]{0:T(128)} %bitcast.160, s32[1]{0:T(128)} %bitcast.1.first_ref, f32[320,1280]{1,0:T(8,128)} %constant.16.clone.grid_ref), custom_call_target="tpu_custom_call" | custom-call | tf_op jit(solution)/shard_map/pallas_call | solution.py:151
  12.0 0.9 %copy-done.6 = f32[1,256,256]{2,1,0:T(8,128)S(1)} copy-done((f32[1,256,256]{2,1,0:T(8,128)S(1)}, f32[1,256,256]{2,1,0:T(8,128)}, u32[]{:S(2)}) %copy-start.6) | copy-done | bytes 262168
  12.9 0.1 bitcast_select_fusion
  13.0 1.0 %copy-done.4 = f32[1,3,256,256]{3,2,1,0:T(8,128)S(1)} copy-done((f32[1,3,256,256]{3,2,1,0:T(8,128)S(1)}, f32[1,3,256,256]{3,2,1,0:T(8,128)}, u32[]{:S(2)}) %copy-start.4) | copy-done | bytes 786456
  14.0 0.4 fusion.50
  14.4 0.4 fusion
  14.8 0.4 fusion.1
  15.2 2.4 %collective-permute-start.3 = (f32[1,2,256,64]{2,3,1,0:T(8,128)S(1)}, f32[1,2,256,64]{2,3,1,0:T(8,128)S(1)}, u32[]{:S(2)}, u32[]{:S(2)}) collective-permute-start(f32[1,2,256,64]{2,3,1,0:T(8,128)S(1)} %fusion.75), channel_id=1, source_target_pairs={{0,4},{4,0},{1,5},{5,1},{2,6},{6,2},{3,7},{7,3},{8,12},{12,8},{9,1... | collective-permute-start | bytes 393224 | tf_op jit(solution)/shard_map/ppermute | solution.py:215
  17.6 0.1 multiply_add_fusion
  17.7 0.4 fusion.57
  18.1 0.4 fusion.4
  18.5 0.4 fusion.5
  19.0 1.0 %collective-permute-start.1 = (f32[1,2,256,64]{2,3,1,0:T(8,128)S(1)}, f32[1,2,256,64]{2,3,1,0:T(8,128)S(1)}, u32[]{:S(2)}, u32[]{:S(2)}) collective-permute-start(f32[1,2,256,64]{2,3,1,0:T(8,128)S(1)} %fusion.76), channel_id=1, source_target_pairs={{0,4},{4,0},{1,5},{5,1},{2,6},{6,2},{3,7},{7,3},{8,12},{12,8},{9,1... | collective-permute-start | bytes 393224 | tf_op jit(solution)/shard_map/ppermute | solution.py:215
  19.9 0.6 %collective-permute-done.3 = f32[1,2,256,64]{2,3,1,0:T(8,128)S(1)} collective-permute-done((f32[1,2,256,64]{2,3,1,0:T(8,128)S(1)}, f32[1,2,256,64]{2,3,1,0:T(8,128)S(1)}, u32[]{:S(2)}, u32[]{:S(2)}) %collective-permute-start.3) | collective-permute-done | bytes 131104 | tf_op jit(solution)/shard_map/ppermute | solution.py:215
  20.6 0.5 fusion.9
  21.1 0.5 convolution_subtract_fusion
  21.7 0.6 %add_bitcast_fusion = (f32[1,256,256]{2,1,0:T(8,128)S(1)}, f32[1,256,256]{2,1,0:T(8,128)S(1)}, f32[1,1,256,256]{3,2,1,0:T(8,128)S(1)}, f32[1,1,256,256]{3,2,1,0:T(8,128)S(1)}) fusion(f32[256,256]{1,0:T(8,128)S(1)} %convolution_subtract_fusion, f32[1,2,256,256]{3,2,1,0:T(8,128)S(1)} %get-tuple-element.19, f32[1,1,256,256]{3,2,1,0:T(8,128)S(1)} %get-tuple-element.22, ...), kind=kOutput, calls=%fused_computation.91 | convolution fusion | flops 126681088 | bytes 3342336 | tf_op jit(solution)/shard_map/ajk,aik->aji/dot_general | solution.py:38
  22.3 2.2 %collective-permute-start.4 = (f32[2,128,256]{2,1,0:T(8,128)S(1)}, f32[2,128,256]{2,1,0:T(8,128)S(1)}, u32[]{:S(2)}, u32[]{:S(2)}) collective-permute-start(f32[2,128,256]{2,1,0:T(8,128)S(1)} %broadcast_select_fusion), channel_id=1, source_target_pairs={{0,1},{1,0},{2,3},{3,2},{4,5},{5,4},{6,7},{7,6},{8,9},{9,8},{10,11... | collective-permute-start | bytes 786440 | tf_op jit(solution)/shard_map/ppermute | solution.py:65
  24.6 6.4 %collective-permute-done.4 = f32[2,128,256]{2,1,0:T(8,128)S(1)} collective-permute-done((f32[2,128,256]{2,1,0:T(8,128)S(1)}, f32[2,128,256]{2,1,0:T(8,128)S(1)}, u32[]{:S(2)}, u32[]{:S(2)}) %collective-permute-start.4) | collective-permute-done | bytes 262176 | tf_op jit(solution)/shard_map/ppermute | solution.py:65
  31.0 3.5 %collective-permute-start.5 = (f32[2,64,256]{2,1,0:T(8,128)S(1)}, f32[2,64,256]{2,1,0:T(8,128)S(1)}, u32[]{:S(2)}, u32[]{:S(2)}) collective-permute-start(f32[2,64,256]{2,1,0:T(8,128)S(1)} %slice_select_fusion), channel_id=1, source_target_pairs={{0,2},{1,3},{2,0},{3,1},{4,6},{5,7},{6,4},{7,5},{8,10},{9,11},{10,... | collective-permute-start | bytes 393224 | tf_op jit(solution)/shard_map/ppermute | solution.py:65
  34.5 0.5 fusion.13
  35.1 6.1 %collective-permute-done.5 = f32[2,64,256]{2,1,0:T(8,128)S(1)} collective-permute-done((f32[2,64,256]{2,1,0:T(8,128)S(1)}, f32[2,64,256]{2,1,0:T(8,128)S(1)}, u32[]{:S(2)}, u32[]{:S(2)}) %collective-permute-start.5) | collective-permute-done | bytes 131104 | tf_op jit(solution)/shard_map/ppermute | solution.py:65
  41.2 0.5 fusion.2
  41.8 8.2 %collective-permute-done.6 = f32[2,64,256]{2,1,0:T(8,128)S(1)} collective-permute-done((f32[2,64,256]{2,1,0:T(8,128)S(1)}, f32[2,64,256]{2,1,0:T(8,128)S(1)}, u32[]{:S(2)}, u32[]{:S(2)}) %collective-permute-start.6) | collective-permute-done | bytes 131104 | tf_op jit(solution)/shard_map/ppermute | solution.py:69
  50.1 0.5 fusion.3
  50.6 0.8 %maximum_bitcast_fusion = f32[1,1,2,256,256]{4,3,2,1,0:T(8,128)} fusion(f32[1,1,256,256]{3,2,1,0:T(8,128)S(1)} %fusion.2, f32[1,1,256,256]{3,2,1,0:T(8,128)S(1)} %fusion.3), kind=kLoop, calls=%fused_computation.16 | loop fusion | flops 131072 | bytes 1048576 | tf_op jit(solution)/shard_map/broadcast_in_dim | solution.py:232
  51.4 0.8 %maximum_bitcast_fusion.1 = f32[1,1,2,256,256]{4,3,2,1,0:T(8,128)} fusion(f32[1,1,256,256]{3,2,1,0:T(8,128)S(1)} %get-tuple-element.17, f32[1,1,256,256]{3,2,1,0:T(8,128)S(1)} %get-tuple-element.18), kind=kLoop, calls=%fused_computation.17 | loop fusion | flops 131072 | bytes 1048576 | tf_op jit(solution)/shard_map/broadcast_in_dim | solution.py:232
  52.3 4.2 %collective-permute-done.7 = f32[2,128,256]{2,1,0:T(8,128)S(1)} collective-permute-done((f32[2,128,256]{2,1,0:T(8,128)S(1)}, f32[2,128,256]{2,1,0:T(8,128)S(1)}, u32[]{:S(2)}, u32[]{:S(2)}) %collective-permute-start.7) | collective-permute-done | bytes 262176 | tf_op jit(solution)/shard_map/ppermute | solution.py:69
  56.4 0.8 %maximum_select_fusion = f32[1,1,2,256,256]{4,3,2,1,0:T(8,128)} fusion(f32[1,1,2,128,256]{4,3,2,1,0:T(8,128)S(1)} %bitcast.159, f32[1,1,2,128,256]{4,3,2,1,0:T(8,128)S(1)} %bitcast.158, pred[]{:T(512)S(6)} %eq.18), kind=kLoop, calls=%fused_computation.20 | loop fusion | flops 393216 | bytes 1048577 | tf_op jit(solution)/shard_map/jit(_where)/select_n | solution.py:70
  (31 shorter events, 0.6 us)
Async XLA Ops:
  0.6 11.3 %copy-start.2 = (bf16[1,2,1,2,256,256]{5,4,3,2,1,0:T(8,128)(2,1)S(1)}, bf16[1,2,1,2,256,256]{5,4,3,2,1,0:T(8,128)(2,1)}, u32[]{:S(2)}) copy-start(bf16[1,2,1,2,256,256]{5,4,3,2,1,0:T(8,128)(2,1)} %param.13) | copy-start | bytes 1572868
  0.6 16.9 %collective-permute-start = (f32[1,1,2,256,256]{4,3,2,1,0:T(8,128)}, f32[1,1,2,256,256]{4,3,2,1,0:T(8,128)S(1)}, u32[]{:S(2)}, u32[]{:S(2)}) collective-permute-start(f32[1,1,2,256,256]{4,3,2,1,0:T(8,128)} %param.11), channel_id=1, source_target_pairs={{0,8},{8,16},{16,24},{1,9},{9,17},{17,25},{2,10},{10,18},{18,26},{... | collective-permute-start | bytes 1572872 | tf_op jit(solution)/shard_map/ppermute | solution.py:29
  3.2 9.7 %collective-permute-start.2 = (f32[1,1,2,256,256]{4,3,2,1,0:T(8,128)}, f32[1,1,2,256,256]{4,3,2,1,0:T(8,128)S(1)}, u32[]{:S(2)}, u32[]{:S(2)}) collective-permute-start(f32[1,1,2,256,256]{4,3,2,1,0:T(8,128)} %param.12), channel_id=1, source_target_pairs={{8,0},{16,8},{24,16},{9,1},{17,9},{25,17},{10,2},{18,10},{26,18},{... | collective-permute-start | bytes 1572872 | tf_op jit(solution)/shard_map/ppermute | solution.py:32
  11.9 1.0 %copy-start.6 = (f32[1,256,256]{2,1,0:T(8,128)S(1)}, f32[1,256,256]{2,1,0:T(8,128)}, u32[]{:S(2)}) copy-start(f32[1,256,256]{2,1,0:T(8,128)} %param.14) | copy-start | bytes 786436
  12.8 1.1 %copy-start.4 = (f32[1,3,256,256]{3,2,1,0:T(8,128)S(1)}, f32[1,3,256,256]{3,2,1,0:T(8,128)}, u32[]{:S(2)}) copy-start(f32[1,3,256,256]{3,2,1,0:T(8,128)} %get-tuple-element.9) | copy-start | bytes 2359300
  14.4 3.2 %copy-start.5 = (bf16[2,256,256]{2,1,0:T(8,128)(2,1)S(1)}, bf16[2,256,256]{2,1,0:T(8,128)(2,1)}, u32[]{:S(2)}) copy-start(bf16[2,256,256]{2,1,0:T(8,128)(2,1)} %param.9) | copy-start | bytes 786436
  15.2 2.5 %copy-start.3 = (f32[1,3,256,256]{3,2,1,0:T(8,128)S(1)}, f32[1,3,256,256]{3,2,1,0:T(8,128)}, u32[]{:S(2)}) copy-start(f32[1,3,256,256]{3,2,1,0:T(8,128)} %get-tuple-element.7) | copy-start | bytes 2359300
  15.2 5.3 %collective-permute-start.3 = (f32[1,2,256,64]{2,3,1,0:T(8,128)S(1)}, f32[1,2,256,64]{2,3,1,0:T(8,128)S(1)}, u32[]{:S(2)}, u32[]{:S(2)}) collective-permute-start(f32[1,2,256,64]{2,3,1,0:T(8,128)S(1)} %fusion.75), channel_id=1, source_target_pairs={{0,4},{4,0},{1,5},{5,1},{2,6},{6,2},{3,7},{7,3},{8,12},{12,8},{9,1... | collective-permute-start | bytes 393224 | tf_op jit(solution)/shard_map/ppermute | solution.py:215
  18.9 1.7 %copy-start.1 = (f32[1,3,256,320]{3,2,1,0:T(8,128)S(1)}, f32[1,3,256,320]{3,2,1,0:T(8,128)}, u32[]{:S(2)}) copy-start(f32[1,3,256,320]{3,2,1,0:T(8,128)} %get-tuple-element.10) | copy-start | bytes 2949124
  19.0 5.5 %collective-permute-start.1 = (f32[1,2,256,64]{2,3,1,0:T(8,128)S(1)}, f32[1,2,256,64]{2,3,1,0:T(8,128)S(1)}, u32[]{:S(2)}, u32[]{:S(2)}) collective-permute-start(f32[1,2,256,64]{2,3,1,0:T(8,128)S(1)} %fusion.76), channel_id=1, source_target_pairs={{0,4},{4,0},{1,5},{5,1},{2,6},{6,2},{3,7},{7,3},{8,12},{12,8},{9,1... | collective-permute-start | bytes 393224 | tf_op jit(solution)/shard_map/ppermute | solution.py:215
  22.3 8.6 %collective-permute-start.4 = (f32[2,128,256]{2,1,0:T(8,128)S(1)}, f32[2,128,256]{2,1,0:T(8,128)S(1)}, u32[]{:S(2)}, u32[]{:S(2)}) collective-permute-start(f32[2,128,256]{2,1,0:T(8,128)S(1)} %broadcast_select_fusion), channel_id=1, source_target_pairs={{0,1},{1,0},{2,3},{3,2},{4,5},{5,4},{6,7},{7,6},{8,9},{9,8},{10,11... | collective-permute-start | bytes 786440 | tf_op jit(solution)/shard_map/ppermute | solution.py:65
  24.5 10.0 %copy-start = (f32[1,3,256,320]{3,2,1,0:T(8,128)S(1)}, f32[1,3,256,320]{3,2,1,0:T(8,128)}, u32[]{:S(2)}) copy-start(f32[1,3,256,320]{3,2,1,0:T(8,128)} %get-tuple-element.8) | copy-start | bytes 2949124
  31.0 10.1 %collective-permute-start.5 = (f32[2,64,256]{2,1,0:T(8,128)S(1)}, f32[2,64,256]{2,1,0:T(8,128)S(1)}, u32[]{:S(2)}, u32[]{:S(2)}) collective-permute-start(f32[2,64,256]{2,1,0:T(8,128)S(1)} %slice_select_fusion), channel_id=1, source_target_pairs={{0,2},{1,3},{2,0},{3,1},{4,6},{5,7},{6,4},{7,5},{8,10},{9,11},{10,... | collective-permute-start | bytes 393224 | tf_op jit(solution)/shard_map/ppermute | solution.py:65
  41.1 8.8 %collective-permute-start.6 = (f32[2,64,256]{2,1,0:T(8,128)S(1)}, f32[2,64,256]{2,1,0:T(8,128)S(1)}, u32[]{:S(2)}, u32[]{:S(2)}) collective-permute-start(f32[2,64,256]{2,1,0:T(8,128)S(1)} %select_add_fusion.1), channel_id=1, source_target_pairs={{0,2},{1,3},{2,0},{3,1},{4,6},{5,7},{6,4},{7,5},{8,10},{9,11},{10,... | collective-permute-start | bytes 393224 | tf_op jit(solution)/shard_map/ppermute | solution.py:69
  50.0 6.4 %collective-permute-start.7 = (f32[2,128,256]{2,1,0:T(8,128)S(1)}, f32[2,128,256]{2,1,0:T(8,128)S(1)}, u32[]{:S(2)}, u32[]{:S(2)}) collective-permute-start(f32[2,128,256]{2,1,0:T(8,128)S(1)} %maximum_select_fusion.1), channel_id=1, source_target_pairs={{0,1},{1,0},{2,3},{3,2},{4,5},{5,4},{6,7},{7,6},{8,9},{9,8},{10,11... | collective-permute-start | bytes 786440 | tf_op jit(solution)/shard_map/ppermute | solution.py:69

commit v10 on v9

--- a/solution.py
+++ b/solution.py
@@ -44,33 +44,48 @@
     return signed.astype(jnp.float32) / length
 
 
-def halving_allreduce(value, axis):
+def halving_allreduce(value, axis, other):
     count = lax.axis_size(axis)
     if count == 1:
         return value
     if count & (count - 1) or value.shape[-2] % count:
         return lax.psum(value, axis)
+    groups = lax.axis_size(other)
     index = lax.axis_index(axis)
+    odd = lax.axis_index(other) % 2
     steps = count.bit_length() - 1
     dim = value.ndim - 2
+
+    def position(step, parity):
+        return step if parity == 0 else steps - 1 - step
+
+    def pairs(step):
+        return [
+            (g * count + j, g * count + (j ^ (1 << position(step, g % 2))))
+            for g in range(groups)
+            for j in range(count)
+        ]
+
+    def bit_of(step):
+        shift = jnp.where(odd == 0, position(step, 0), position(step, 1))
+        return (index >> shift) & 1
+
     held = value
     for k in range(steps):
-        bit = (index >> k) & 1
+        bit = bit_of(k)
         size = held.shape[dim] // 2
         low = lax.slice_in_dim(held, 0, size, axis=dim)
         high = lax.slice_in_dim(held, size, None, axis=dim)
         keep = jnp.where(bit == 0, low, high)
         give = jnp.where(bit == 0, high, low)
-        pairs = [(j, j ^ (1 << k)) for j in range(count)]
-        held = keep + lax.ppermute(give, axis, pairs)
+        held = keep + lax.ppermute(give, (other, axis), pairs(k))
     for k in reversed(range(steps)):
-        bit = (index >> k) & 1
-        pairs = [(j, j ^ (1 << k)) for j in range(count)]
-        other = lax.ppermute(held, axis, pairs)
+        bit = bit_of(k)
+        got = lax.ppermute(held, (other, axis), pairs(k))
         held = jnp.where(
             bit == 0,
-            jnp.concatenate([held, other], axis=dim),
-            jnp.concatenate([other, held], axis=dim),
+            jnp.concatenate([held, got], axis=dim),
+            jnp.concatenate([got, held], axis=dim),
         )
     return held
 
@@ -220,7 +235,7 @@
     grad_real = spread[:, 0] * held_field[:, 0] + spread[:, 1] * held_field[:, 1]
     grad_imag = spread[:, 1] * held_field[:, 0] - spread[:, 0] * held_field[:, 1]
     gradient_term = jnp.stack([jnp.sum(grad_real, axis=0), jnp.sum(grad_imag, axis=0)])
-    summed = halving_allreduce(gradient_term, "angle")
+    summed = halving_allreduce(gradient_term, "angle", "depth")
     returning = jnp.stack(
         [
             cosine * spread[:, 0] + sine_part * spread[:, 1],

time: 57.6 us -> 58.5 us (1.016)
  the two profiles are of different devices: /device:TPU:0 before, /device:TPU:6 now
where the time goes in v10:
time: 58.5 us; the launch traced here: 58.2 us
  waiting for transfers between devices  25.8 us (44%)
  starting transfers between devices  13.1 us (22%)
  matrix products  5.5 us (9%)
  Pallas kernels  4.89 us (8%)
  local copies, waits for them, and re-layouts  4.16 us (7%)
  other arithmetic  3.07 us (5%)
  between operations  1.6 us (3%)
    ppermute x2, waiting for transfers between devices, halving_allreduce(): got = lax.ppermute(held, (other, axis), pairs(k))  12.4 us
    ppermute x2, waiting for transfers between devices, halving_allreduce(): held = keep + lax.ppermute(give, (other, axis), pairs(k))  10.7 us
    dot_general x12, matrix products, contract(): return jnp.einsum(form, left, right, precision=wave_precision)  5.5 us
    pallas_call x1, Pallas kernels, build_tables(): pl.pallas_call(table_kernel, out_shape=(rows, rows, cols, cols), in_specs...  4.89 us
    ppermute x1, starting transfers between devices, padded_2(): lax.ppermute(lax.slice_in_dim(block, 0, width, axis=dim), axis, backward)  3.64 us
    ppermute x2, starting transfers between devices, halving_allreduce(): held = keep + lax.ppermute(give, (other, axis), pairs(k))  3.58 us
    ppermute x2, waiting for transfers between devices, side_halo(): edges = lax.ppermute(edges, 'tile', [(0, 1), (1, 0)])  2.72 us
    unnamed x14, local copies, waits for them, and re-layouts  2.29 us
  transfers between devices with their start and end apart: 8, of which 5 were waited for; matrix products, arithmetic and copies ran while one was open for 16% of the time, Pallas kernels for 8%

profile of v10, /device:TPU:6, one launch (start us, length us, event | category | flops | bytes accessed | tf_op | source)
XLA Modules:
  0.0 58.2 jit_solution(5729208730410153258)
XLA Ops:
  0.6 2.1 %collective-permute-start = (f32[1,1,2,256,256]{4,3,2,1,0:T(8,128)}, f32[1,1,2,256,256]{4,3,2,1,0:T(8,128)S(1)}, u32[]{:S(2)}, u32[]{:S(2)}) collective-permute-start(f32[1,1,2,256,256]{4,3,2,1,0:T(8,128)} %param.11), channel_id=1, source_target_pairs={{0,8},{8,16},{16,24},{1,9},{9,17},{17,25},{2,10},{10,18},{18,26},{... | collective-permute-start | bytes 1572872 | tf_op jit(solution)/shard_map/ppermute | solution.py:29
  2.7 3.6 %collective-permute-start.2 = (f32[1,1,2,256,256]{4,3,2,1,0:T(8,128)}, f32[1,1,2,256,256]{4,3,2,1,0:T(8,128)S(1)}, u32[]{:S(2)}, u32[]{:S(2)}) collective-permute-start(f32[1,1,2,256,256]{4,3,2,1,0:T(8,128)} %param.12), channel_id=1, source_target_pairs={{8,0},{16,8},{24,16},{9,1},{17,9},{25,17},{10,2},{18,10},{26,18},{... | collective-permute-start | bytes 1572872 | tf_op jit(solution)/shard_map/ppermute | solution.py:32
  6.3 1.9 %fusion.77 = (f32[1,1,256,256]{3,2,1,0:T(8,128)S(1)}, f32[1,1,256,256]{3,2,1,0:T(8,128)S(1)}) fusion(f32[1,1,256,256]{3,2,1,0:T(8,128)} %param.10), kind=kLoop, calls=%fused_computation.120 | loop fusion | bytes 786432 | tf_op jit(solution)/shard_map/cos | solution.py:205
  8.9 4.9 %shard_map.112 = (f32[1,3,256,256]{3,2,1,0:T(8,128)}, f32[1,3,256,256]{3,2,1,0:T(8,128)}, f32[1,3,256,320]{3,2,1,0:T(8,128)}, f32[1,3,256,320]{3,2,1,0:T(8,128)}) custom-call(s32[1]{0:T(128)S(6)} %copy.12.tilt_ref, s32[2]{0:T(128)} %bitcast.160, s32[1]{0:T(128)} %bitcast.1.first_ref, f32[320,1280]{1,0:T(8,128)} %constant.27.clone.grid_ref), custom_call_target="tpu_custom_call" | custom-call | tf_op jit(solution)/shard_map/pallas_call | solution.py:166
  13.9 0.9 %copy-done.6 = f32[1,256,256]{2,1,0:T(8,128)S(1)} copy-done((f32[1,256,256]{2,1,0:T(8,128)S(1)}, f32[1,256,256]{2,1,0:T(8,128)}, u32[]{:S(2)}) %copy-start.6) | copy-done | bytes 262168
  14.9 1.0 %copy-done.4 = f32[1,3,256,256]{3,2,1,0:T(8,128)S(1)} copy-done((f32[1,3,256,256]{3,2,1,0:T(8,128)S(1)}, f32[1,3,256,256]{3,2,1,0:T(8,128)}, u32[]{:S(2)}) %copy-start.4) | copy-done | bytes 786456
  15.9 0.4 fusion.50
  16.3 0.4 fusion
  16.7 0.4 fusion.1
  17.1 0.6 %collective-permute-start.3 = (f32[1,2,256,64]{2,3,1,0:T(8,128)S(1)}, f32[1,2,256,64]{2,3,1,0:T(8,128)S(1)}, u32[]{:S(2)}, u32[]{:S(2)}) collective-permute-start(f32[1,2,256,64]{2,3,1,0:T(8,128)S(1)} %fusion.75), channel_id=1, source_target_pairs={{0,4},{4,0},{1,5},{5,1},{2,6},{6,2},{3,7},{7,3},{8,12},{12,8},{9,1... | collective-permute-start | bytes 393224 | tf_op jit(solution)/shard_map/ppermute | solution.py:230
  17.8 0.4 copy-done.3
  18.2 0.4 fusion.57
  18.6 0.4 fusion.4
  19.0 0.4 fusion.5
  19.4 1.2 %collective-permute-start.1 = (f32[1,2,256,64]{2,3,1,0:T(8,128)S(1)}, f32[1,2,256,64]{2,3,1,0:T(8,128)S(1)}, u32[]{:S(2)}, u32[]{:S(2)}) collective-permute-start(f32[1,2,256,64]{2,3,1,0:T(8,128)S(1)} %fusion.76), channel_id=1, source_target_pairs={{0,4},{4,0},{1,5},{5,1},{2,6},{6,2},{3,7},{7,3},{8,12},{12,8},{9,1... | collective-permute-start | bytes 393224 | tf_op jit(solution)/shard_map/ppermute | solution.py:230
  20.6 2.7 %collective-permute-done.3 = f32[1,2,256,64]{2,3,1,0:T(8,128)S(1)} collective-permute-done((f32[1,2,256,64]{2,3,1,0:T(8,128)S(1)}, f32[1,2,256,64]{2,3,1,0:T(8,128)S(1)}, u32[]{:S(2)}, u32[]{:S(2)}) %collective-permute-start.3) | collective-permute-done | bytes 131104 | tf_op jit(solution)/shard_map/ppermute | solution.py:230
  23.4 0.5 fusion.9
  23.9 0.5 convolution_subtract_fusion
  24.5 0.6 %add_bitcast_fusion = (f32[1,256,256]{2,1,0:T(8,128)S(1)}, f32[1,256,256]{2,1,0:T(8,128)S(1)}, f32[1,1,256,256]{3,2,1,0:T(8,128)S(1)}, f32[1,1,256,256]{3,2,1,0:T(8,128)S(1)}) fusion(f32[256,256]{1,0:T(8,128)S(1)} %convolution_subtract_fusion, f32[1,2,256,256]{3,2,1,0:T(8,128)S(1)} %get-tuple-element.19, f32[1,1,256,256]{3,2,1,0:T(8,128)S(1)} %get-tuple-element.22, ...), kind=kOutput, calls=%fused_computation.91 | convolution fusion | flops 126681088 | bytes 3342336 | tf_op jit(solution)/shard_map/ajk,aik->aji/dot_general | solution.py:38
  25.1 1.6 %collective-permute-start.4 = (f32[2,128,256]{2,1,0:T(8,128)S(1)}, f32[2,128,256]{2,1,0:T(8,128)S(1)}, u32[]{:S(2)}, u32[]{:S(2)}) collective-permute-start(f32[2,128,256]{2,1,0:T(8,128)S(1)} %broadcast_select_fusion), channel_id=1, source_target_pairs={{0,1},{1,0},{2,3},{3,2},{8,10},{9,11},{10,8},{11,9},{16,17},{17,16... | collective-permute-start | bytes 786440 | tf_op jit(solution)/shard_map/ppermute | solution.py:81
  26.8 6.4 %collective-permute-done.4 = f32[2,128,256]{2,1,0:T(8,128)S(1)} collective-permute-done((f32[2,128,256]{2,1,0:T(8,128)S(1)}, f32[2,128,256]{2,1,0:T(8,128)S(1)}, u32[]{:S(2)}, u32[]{:S(2)}) %collective-permute-start.4) | collective-permute-done | bytes 262176 | tf_op jit(solution)/shard_map/ppermute | solution.py:81
  33.3 1.9 %collective-permute-start.5 = (f32[2,64,256]{2,1,0:T(8,128)S(1)}, f32[2,64,256]{2,1,0:T(8,128)S(1)}, u32[]{:S(2)}, u32[]{:S(2)}) collective-permute-start(f32[2,64,256]{2,1,0:T(8,128)S(1)} %slice_select_fusion), channel_id=1, source_target_pairs={{0,2},{1,3},{2,0},{3,1},{8,9},{9,8},{10,11},{11,10},{16,18},{17,19... | collective-permute-start | bytes 393224 | tf_op jit(solution)/shard_map/ppermute | solution.py:81
  35.3 0.5 fusion.13
  35.8 4.2 %collective-permute-done.5 = f32[2,64,256]{2,1,0:T(8,128)S(1)} collective-permute-done((f32[2,64,256]{2,1,0:T(8,128)S(1)}, f32[2,64,256]{2,1,0:T(8,128)S(1)}, u32[]{:S(2)}, u32[]{:S(2)}) %collective-permute-start.5) | collective-permute-done | bytes 131104 | tf_op jit(solution)/shard_map/ppermute | solution.py:81
  40.1 2.0 %collective-permute-start.6 = (f32[2,64,256]{2,1,0:T(8,128)S(1)}, f32[2,64,256]{2,1,0:T(8,128)S(1)}, u32[]{:S(2)}, u32[]{:S(2)}) collective-permute-start(f32[2,64,256]{2,1,0:T(8,128)S(1)} %select_add_fusion.1), channel_id=1, source_target_pairs={{0,2},{1,3},{2,0},{3,1},{8,9},{9,8},{10,11},{11,10},{16,18},{17,19... | collective-permute-start | bytes 393224 | tf_op jit(solution)/shard_map/ppermute | solution.py:84
  42.1 0.5 fusion.2
  42.6 8.3 %collective-permute-done.6 = f32[2,64,256]{2,1,0:T(8,128)S(1)} collective-permute-done((f32[2,64,256]{2,1,0:T(8,128)S(1)}, f32[2,64,256]{2,1,0:T(8,128)S(1)}, u32[]{:S(2)}, u32[]{:S(2)}) %collective-permute-start.6) | collective-permute-done | bytes 131104 | tf_op jit(solution)/shard_map/ppermute | solution.py:84
  51.0 0.5 fusion.3
  51.5 0.8 %maximum_bitcast_fusion = f32[1,1,2,256,256]{4,3,2,1,0:T(8,128)} fusion(f32[1,1,256,256]{3,2,1,0:T(8,128)S(1)} %fusion.2, f32[1,1,256,256]{3,2,1,0:T(8,128)S(1)} %fusion.3), kind=kLoop, calls=%fused_computation.16 | loop fusion | flops 131072 | bytes 1048576 | tf_op jit(solution)/shard_map/broadcast_in_dim | solution.py:247
  52.3 0.8 %maximum_bitcast_fusion.1 = f32[1,1,2,256,256]{4,3,2,1,0:T(8,128)} fusion(f32[1,1,256,256]{3,2,1,0:T(8,128)S(1)} %get-tuple-element.17, f32[1,1,256,256]{3,2,1,0:T(8,128)S(1)} %get-tuple-element.18), kind=kLoop, calls=%fused_computation.17 | loop fusion | flops 131072 | bytes 1048576 | tf_op jit(solution)/shard_map/broadcast_in_dim | solution.py:247
  53.2 4.2 %collective-permute-done.7 = f32[2,128,256]{2,1,0:T(8,128)S(1)} collective-permute-done((f32[2,128,256]{2,1,0:T(8,128)S(1)}, f32[2,128,256]{2,1,0:T(8,128)S(1)}, u32[]{:S(2)}, u32[]{:S(2)}) %collective-permute-start.7) | collective-permute-done | bytes 262176 | tf_op jit(solution)/shard_map/ppermute | solution.py:84
  57.3 0.8 %maximum_select_fusion = f32[1,1,2,256,256]{4,3,2,1,0:T(8,128)} fusion(f32[1,1,2,128,256]{4,3,2,1,0:T(8,128)S(1)} %bitcast.159, f32[1,1,2,128,256]{4,3,2,1,0:T(8,128)S(1)} %bitcast.158, pred[]{:T(512)S(6)} %eq.27), kind=kLoop, calls=%fused_computation.20 | loop fusion | flops 393216 | bytes 1048577 | tf_op jit(solution)/shard_map/jit(_where)/select_n | solution.py:85
  (31 shorter events, 0.7 us)
Async XLA Ops:
  0.6 13.2 %copy-start.2 = (bf16[1,2,1,2,256,256]{5,4,3,2,1,0:T(8,128)(2,1)S(1)}, bf16[1,2,1,2,256,256]{5,4,3,2,1,0:T(8,128)(2,1)}, u32[]{:S(2)}) copy-start(bf16[1,2,1,2,256,256]{5,4,3,2,1,0:T(8,128)(2,1)} %param.13) | copy-start | bytes 1572868
  0.6 17.1 %collective-permute-start = (f32[1,1,2,256,256]{4,3,2,1,0:T(8,128)}, f32[1,1,2,256,256]{4,3,2,1,0:T(8,128)S(1)}, u32[]{:S(2)}, u32[]{:S(2)}) collective-permute-start(f32[1,1,2,256,256]{4,3,2,1,0:T(8,128)} %param.11), channel_id=1, source_target_pairs={{0,8},{8,16},{16,24},{1,9},{9,17},{17,25},{2,10},{10,18},{18,26},{... | collective-permute-start | bytes 1572872 | tf_op jit(solution)/shard_map/ppermute | solution.py:29
  2.7 12.1 %collective-permute-start.2 = (f32[1,1,2,256,256]{4,3,2,1,0:T(8,128)}, f32[1,1,2,256,256]{4,3,2,1,0:T(8,128)S(1)}, u32[]{:S(2)}, u32[]{:S(2)}) collective-permute-start(f32[1,1,2,256,256]{4,3,2,1,0:T(8,128)} %param.12), channel_id=1, source_target_pairs={{8,0},{16,8},{24,16},{9,1},{17,9},{25,17},{10,2},{18,10},{26,18},{... | collective-permute-start | bytes 1572872 | tf_op jit(solution)/shard_map/ppermute | solution.py:32
  13.8 1.0 %copy-start.6 = (f32[1,256,256]{2,1,0:T(8,128)S(1)}, f32[1,256,256]{2,1,0:T(8,128)}, u32[]{:S(2)}) copy-start(f32[1,256,256]{2,1,0:T(8,128)} %param.14) | copy-start | bytes 786436
  14.7 1.1 %copy-start.4 = (f32[1,3,256,256]{3,2,1,0:T(8,128)S(1)}, f32[1,3,256,256]{3,2,1,0:T(8,128)}, u32[]{:S(2)}) copy-start(f32[1,3,256,256]{3,2,1,0:T(8,128)} %get-tuple-element.9) | copy-start | bytes 2359300
  16.3 1.4 %copy-start.5 = (bf16[2,256,256]{2,1,0:T(8,128)(2,1)S(1)}, bf16[2,256,256]{2,1,0:T(8,128)(2,1)}, u32[]{:S(2)}) copy-start(bf16[2,256,256]{2,1,0:T(8,128)(2,1)} %param.9) | copy-start | bytes 786436
  17.1 1.2 %copy-start.3 = (f32[1,3,256,256]{3,2,1,0:T(8,128)S(1)}, f32[1,3,256,256]{3,2,1,0:T(8,128)}, u32[]{:S(2)}) copy-start(f32[1,3,256,256]{3,2,1,0:T(8,128)} %get-tuple-element.7) | copy-start | bytes 2359300
  17.1 6.2 %collective-permute-start.3 = (f32[1,2,256,64]{2,3,1,0:T(8,128)S(1)}, f32[1,2,256,64]{2,3,1,0:T(8,128)S(1)}, u32[]{:S(2)}, u32[]{:S(2)}) collective-permute-start(f32[1,2,256,64]{2,3,1,0:T(8,128)S(1)} %fusion.75), channel_id=1, source_target_pairs={{0,4},{4,0},{1,5},{5,1},{2,6},{6,2},{3,7},{7,3},{8,12},{12,8},{9,1... | collective-permute-start | bytes 393224 | tf_op jit(solution)/shard_map/ppermute | solution.py:230
  19.4 4.0 %copy-start.1 = (f32[1,3,256,320]{3,2,1,0:T(8,128)S(1)}, f32[1,3,256,320]{3,2,1,0:T(8,128)}, u32[]{:S(2)}) copy-start(f32[1,3,256,320]{3,2,1,0:T(8,128)} %get-tuple-element.10) | copy-start | bytes 2949124
  19.4 7.3 %collective-permute-start.1 = (f32[1,2,256,64]{2,3,1,0:T(8,128)S(1)}, f32[1,2,256,64]{2,3,1,0:T(8,128)S(1)}, u32[]{:S(2)}, u32[]{:S(2)}) collective-permute-start(f32[1,2,256,64]{2,3,1,0:T(8,128)S(1)} %fusion.76), channel_id=1, source_target_pairs={{0,4},{4,0},{1,5},{5,1},{2,6},{6,2},{3,7},{7,3},{8,12},{12,8},{9,1... | collective-permute-start | bytes 393224 | tf_op jit(solution)/shard_map/ppermute | solution.py:230
  25.1 8.1 %collective-permute-start.4 = (f32[2,128,256]{2,1,0:T(8,128)S(1)}, f32[2,128,256]{2,1,0:T(8,128)S(1)}, u32[]{:S(2)}, u32[]{:S(2)}) collective-permute-start(f32[2,128,256]{2,1,0:T(8,128)S(1)} %broadcast_select_fusion), channel_id=1, source_target_pairs={{0,1},{1,0},{2,3},{3,2},{8,10},{9,11},{10,8},{11,9},{16,17},{17,16... | collective-permute-start | bytes 786440 | tf_op jit(solution)/shard_map/ppermute | solution.py:81
  26.8 8.5 %copy-start = (f32[1,3,256,320]{3,2,1,0:T(8,128)S(1)}, f32[1,3,256,320]{3,2,1,0:T(8,128)}, u32[]{:S(2)}) copy-start(f32[1,3,256,320]{3,2,1,0:T(8,128)} %get-tuple-element.8) | copy-start | bytes 2949124
  33.3 6.7 %collective-permute-start.5 = (f32[2,64,256]{2,1,0:T(8,128)S(1)}, f32[2,64,256]{2,1,0:T(8,128)S(1)}, u32[]{:S(2)}, u32[]{:S(2)}) collective-permute-start(f32[2,64,256]{2,1,0:T(8,128)S(1)} %slice_select_fusion), channel_id=1, source_target_pairs={{0,2},{1,3},{2,0},{3,1},{8,9},{9,8},{10,11},{11,10},{16,18},{17,19... | collective-permute-start | bytes 393224 | tf_op jit(solution)/shard_map/ppermute | solution.py:81
  40.1 10.8 %collective-permute-start.6 = (f32[2,64,256]{2,1,0:T(8,128)S(1)}, f32[2,64,256]{2,1,0:T(8,128)S(1)}, u32[]{:S(2)}, u32[]{:S(2)}) collective-permute-start(f32[2,64,256]{2,1,0:T(8,128)S(1)} %select_add_fusion.1), channel_id=1, source_target_pairs={{0,2},{1,3},{2,0},{3,1},{8,9},{9,8},{10,11},{11,10},{16,18},{17,19... | collective-permute-start | bytes 393224 | tf_op jit(solution)/shard_map/ppermute | solution.py:84
  50.9 6.4 %collective-permute-start.7 = (f32[2,128,256]{2,1,0:T(8,128)S(1)}, f32[2,128,256]{2,1,0:T(8,128)S(1)}, u32[]{:S(2)}, u32[]{:S(2)}) collective-permute-start(f32[2,128,256]{2,1,0:T(8,128)S(1)} %maximum_select_fusion.1), channel_id=1, source_target_pairs={{0,1},{1,0},{2,3},{3,2},{8,10},{9,11},{10,8},{11,9},{16,17},{17,16... | collective-permute-start | bytes 786440 | tf_op jit(solution)/shard_map/ppermute | solution.py:84

commit v11 on v9

--- a/solution.py
+++ b/solution.py
@@ -76,8 +76,20 @@
 
 
 def table_kernel(
-    tilt_ref, position_ref, first_ref, grid_ref, rows_fwd_ref, rows_back_ref, cols_fwd_ref, cols_back_ref
+    tilt_ref,
+    position_ref,
+    first_ref,
+    grid_ref,
+    phase_ref,
+    rows_fwd_ref,
+    rows_back_ref,
+    cols_fwd_ref,
+    cols_back_ref,
+    cosine_ref,
+    sine_ref,
 ):
+    cosine_ref[...] = jnp.cos(phase_ref[...])
+    sine_ref[...] = jnp.sin(phase_ref[...])
     angle_count = rows_fwd_ref.shape[0]
     length = grid_ref.shape[0]
     core_size = rows_fwd_ref.shape[-1]
@@ -140,7 +152,7 @@
                 out[a, 2] = real + imag
 
 
-def build_tables(tilt_index, positions, is_first, core_size, length):
+def build_tables(tilt_index, positions, is_first, phase_plane, core_size, length):
     angle_count = tilt_index.shape[0]
     width = ((2 * length + 127) // 128) * 128
     ids = np.arange(length)[:, None] * np.arange(width)[None, :] % length
@@ -148,16 +160,20 @@
     grid = jnp.asarray(np.concatenate([np.cos(angle), np.sin(angle)], axis=1), jnp.float32)
     rows = jax.ShapeDtypeStruct((angle_count, 3, core_size, core_size), jnp.float32)
     cols = jax.ShapeDtypeStruct((angle_count, 3, core_size, length), jnp.float32)
+    plane = jax.ShapeDtypeStruct(phase_plane.shape, jnp.float32)
+    in_vmem = pl.BlockSpec(memory_space=pltpu.VMEM)
     return pl.pallas_call(
         table_kernel,
-        out_shape=(rows, rows, cols, cols),
+        out_shape=(rows, rows, cols, cols, plane, plane),
         in_specs=[
             pl.BlockSpec(memory_space=pltpu.SMEM),
             pl.BlockSpec(memory_space=pltpu.SMEM),
             pl.BlockSpec(memory_space=pltpu.SMEM),
-            pl.BlockSpec(memory_space=pltpu.VMEM),
+            in_vmem,
+            in_vmem,
         ],
-    )(tilt_index, positions.reshape(-1), is_first.astype(jnp.int32).reshape(1), grid)
+        out_specs=tuple(pl.BlockSpec(memory_space=pltpu.VMEM) for _ in range(6)),
+    )(tilt_index, positions.reshape(-1), is_first.astype(jnp.int32).reshape(1), grid, phase_plane)
 
 
 def apply_operator(wave, padded_cols, row_table, col_table):
@@ -183,12 +199,10 @@
     section = lax.axis_index("depth")
     sections = lax.axis_size("depth")
     is_first = section == 0
-    rows_fwd, rows_back, cols_fwd, cols_back = build_tables(
-        tilt_index, positions, is_first, core_size, length
-    )
-
-    cosine = jnp.cos(phase[0, 0])
-    sine_part = jnp.sin(phase[0, 0])
+    rows_fwd, rows_back, cols_fwd, cols_back, cosine, sine_part = build_tables(
+        tilt_index, positions, is_first, phase[0, 0], core_size, length
+    )
+
     outgoing = jnp.concatenate([adjoint_in, forward_in], axis=0)
     received = padded_2(outgoing, (("depth", 0),), 1, False)
     probe_wave = probe.astype(jnp.float32)[None]

time: 57.6 us -> 58.1 us (level)
  starting transfers between devices: 13 us -> 16.9 us
  waiting for transfers between devices: 25.4 us -> 22.8 us
  local copies, waits for them, and re-layouts: 3.76 us -> 2.41 us
    ppermute x2, waiting for transfers between devices: 0.59 us -> 4.94 us  [side_halo(): edges = lax.ppermute(edges, 'tile', [(0, 1), (1, 0)])]
    ppermute x2, waiting for transfers between devices: 12.4 us -> 8.56 us  [halving_allreduce(): other = lax.ppermute(held, axis, pairs)]
    ppermute x2, waiting for transfers between devices: 12.4 us -> 9.25 us  [halving_allreduce(): held = keep + lax.ppermute(give, axis, pairs)]
    ppermute x2, starting transfers between devices: 0.14 us -> 2.57 us  [halving_allreduce(): other = lax.ppermute(held, axis, pairs)]
    ppermute x2, starting transfers between devices: 3.38 us -> 5.55 us  [side_halo(): edges = lax.ppermute(edges, 'tile', [(0, 1), (1, 0)])]
    cos x1 -> x0, local copies, waits for them, and re-layouts: 1.86 us -> none  [body(): cosine = jnp.cos(phase[0, 0])]
    ppermute x2, starting transfers between devices: 5.67 us -> 4.3 us  [halving_allreduce(): held = keep + lax.ppermute(give, axis, pairs)]
    unnamed x14 -> x18, local copies, waits for them, and re-layouts: 1.88 us -> 2.39 us
  transfers between devices with their start and end apart: 8 -> 8, of which waited for: 5 -> 6; matrix products, arithmetic and copies ran while one was open for 17% -> 8% of each run, Pallas kernels for 9% -> 9%
where the time goes in v11:
time: 58.1 us; the launch traced here: 57.5 us
  waiting for transfers between devices  22.8 us (39%)
  starting transfers between devices  16.9 us (29%)
  matrix products  5.52 us (10%)
  Pallas kernels  5.36 us (9%)
  other arithmetic  3.01 us (5%)
  local copies, waits for them, and re-layouts  2.41 us (4%)
  between operations  1.59 us (3%)
    ppermute x2, waiting for transfers between devices, halving_allreduce(): held = keep + lax.ppermute(give, axis, pairs)  9.25 us
    ppermute x2, waiting for transfers between devices, halving_allreduce(): other = lax.ppermute(held, axis, pairs)  8.56 us
    ppermute x2, starting transfers between devices, side_halo(): edges = lax.ppermute(edges, 'tile', [(0, 1), (1, 0)])  5.55 us
    dot_general x12, matrix products, contract(): return jnp.einsum(form, left, right, precision=wave_precision)  5.52 us
    pallas_call x1, Pallas kernels, build_tables(): pl.pallas_call(table_kernel, out_shape=(rows, rows, cols, cols, plane, pl...  5.36 us
    ppermute x2, waiting for transfers between devices, side_halo(): edges = lax.ppermute(edges, 'tile', [(0, 1), (1, 0)])  4.94 us
    ppermute x2, starting transfers between devices, halving_allreduce(): held = keep + lax.ppermute(give, axis, pairs)  4.3 us
    ppermute x1, starting transfers between devices, padded_2(): lax.ppermute(lax.slice_in_dim(block, block.shape[dim] - width, None, axis...  3.06 us
  transfers between devices with their start and end apart: 8, of which 6 were waited for; matrix products, arithmetic and copies ran while one was open for 8% of the time, Pallas kernels for 9%

profile of v11, /device:TPU:0, one launch (start us, length us, event | category | flops | bytes accessed | tf_op | source)
XLA Modules:
  0.0 57.5 jit_solution(10293330056403574251)
XLA Ops:
  0.6 1.4 %collective-permute-start.2 = (f32[1,1,2,256,256]{4,3,2,1,0:T(8,128)}, f32[1,1,2,256,256]{4,3,2,1,0:T(8,128)S(1)}, u32[]{:S(2)}, u32[]{:S(2)}) collective-permute-start(f32[1,1,2,256,256]{4,3,2,1,0:T(8,128)} %param.12), channel_id=1, source_target_pairs={{8,0},{16,8},{24,16},{9,1},{17,9},{25,17},{10,2},{18,10},{26,18},{... | collective-permute-start | bytes 1572872 | tf_op jit(solution)/shard_map/ppermute | solution.py:32
  2.1 3.1 %collective-permute-start = (f32[1,1,2,256,256]{4,3,2,1,0:T(8,128)}, f32[1,1,2,256,256]{4,3,2,1,0:T(8,128)S(1)}, u32[]{:S(2)}, u32[]{:S(2)}) collective-permute-start(f32[1,1,2,256,256]{4,3,2,1,0:T(8,128)} %param.11), channel_id=1, source_target_pairs={{0,8},{8,16},{16,24},{1,9},{9,17},{17,25},{2,10},{10,18},{18,26},{... | collective-permute-start | bytes 1572872 | tf_op jit(solution)/shard_map/ppermute | solution.py:29
  5.8 5.4 %shard_map.112 = (f32[1,3,256,256]{3,2,1,0:T(8,128)}, f32[1,3,256,256]{3,2,1,0:T(8,128)}, f32[1,3,256,320]{3,2,1,0:T(8,128)}, f32[1,3,256,320]{3,2,1,0:T(8,128)}...) custom-call(s32[1]{0:T(128)S(6)} %copy.12.tilt_ref, s32[2]{0:T(128)} %bitcast.148, s32[1]{0:T(128)} %bitcast.1.first_ref, ...), custom_call_target="tpu_custom_call" | custom-call | tf_op jit(solution)/shard_map/pallas_call | solution.py:165
  11.2 0.9 %copy-done.6 = f32[1,256,256]{2,1,0:T(8,128)S(1)} copy-done((f32[1,256,256]{2,1,0:T(8,128)S(1)}, f32[1,256,256]{2,1,0:T(8,128)}, u32[]{:S(2)}) %copy-start.6) | copy-done | bytes 262168
  12.3 1.0 %copy-done.4 = f32[1,3,256,256]{3,2,1,0:T(8,128)S(1)} copy-done((f32[1,3,256,256]{3,2,1,0:T(8,128)S(1)}, f32[1,3,256,256]{3,2,1,0:T(8,128)}, u32[]{:S(2)}) %copy-start.4) | copy-done | bytes 786456
  13.2 0.4 fusion.46
  13.7 0.4 fusion.1
  14.0 0.4 fusion
  14.5 3.0 %collective-permute-start.3 = (f32[1,2,256,64]{2,3,1,0:T(8,128)S(1)}, f32[1,2,256,64]{2,3,1,0:T(8,128)S(1)}, u32[]{:S(2)}, u32[]{:S(2)}) collective-permute-start(f32[1,2,256,64]{2,3,1,0:T(8,128)S(1)} %fusion.68), channel_id=1, source_target_pairs={{0,4},{4,0},{1,5},{5,1},{2,6},{6,2},{3,7},{7,3},{8,12},{12,8},{9,1... | collective-permute-start | bytes 393224 | tf_op jit(solution)/shard_map/ppermute | solution.py:229
  17.5 3.7 %collective-permute-done.3 = f32[1,2,256,64]{2,3,1,0:T(8,128)S(1)} collective-permute-done((f32[1,2,256,64]{2,3,1,0:T(8,128)S(1)}, f32[1,2,256,64]{2,3,1,0:T(8,128)S(1)}, u32[]{:S(2)}, u32[]{:S(2)}) %collective-permute-start.3) | collective-permute-done | bytes 131104 | tf_op jit(solution)/shard_map/ppermute | solution.py:229
  21.3 0.5 fusion.9
  21.8 0.5 convolution_subtract_fusion
  22.4 0.6 %add_bitcast_fusion = (f32[1,256,256]{2,1,0:T(8,128)S(1)}, f32[1,256,256]{2,1,0:T(8,128)S(1)}, f32[1,1,256,256]{3,2,1,0:T(8,128)S(1)}, f32[1,1,256,256]{3,2,1,0:...) fusion(f32[256,256]{1,0:T(8,128)S(1)} %convolution_subtract_fusion, ...), kind=kOutput, calls=%fused_computation.82 | convolution fusion | flops 127074304 | bytes 4390912 | tf_op jit(solution)/shard_map/ajk,aik->aji/dot_general | solution.py:38
  23.0 0.5 copy-done.3
  23.9 0.4 fusion.5
  24.3 0.4 fusion.4
  24.7 2.5 %collective-permute-start.1 = (f32[1,2,256,64]{2,3,1,0:T(8,128)S(1)}, f32[1,2,256,64]{2,3,1,0:T(8,128)S(1)}, u32[]{:S(2)}, u32[]{:S(2)}) collective-permute-start(f32[1,2,256,64]{2,3,1,0:T(8,128)S(1)} %fusion.69), channel_id=1, source_target_pairs={{0,4},{4,0},{1,5},{5,1},{2,6},{6,2},{3,7},{7,3},{8,12},{12,8},{9,1... | collective-permute-start | bytes 393224 | tf_op jit(solution)/shard_map/ppermute | solution.py:229
  27.3 1.6 %collective-permute-start.4 = (f32[2,128,256]{2,1,0:T(8,128)S(1)}, f32[2,128,256]{2,1,0:T(8,128)S(1)}, u32[]{:S(2)}, u32[]{:S(2)}) collective-permute-start(f32[2,128,256]{2,1,0:T(8,128)S(1)} %broadcast_select_fusion), channel_id=1, source_target_pairs={{0,1},{1,0},{2,3},{3,2},{4,5},{5,4},{6,7},{7,6},{8,9},{9,8},{10,11... | collective-permute-start | bytes 786440 | tf_op jit(solution)/shard_map/ppermute | solution.py:65
  29.0 0.8 %maximum_bitcast_fusion.1 = f32[1,1,2,256,256]{4,3,2,1,0:T(8,128)} fusion(f32[1,1,256,256]{3,2,1,0:T(8,128)S(1)} %get-tuple-element.21, f32[1,1,256,256]{3,2,1,0:T(8,128)S(1)} %get-tuple-element.22), kind=kLoop, calls=%fused_computation.17 | loop fusion | flops 131072 | bytes 1048576 | tf_op jit(solution)/shard_map/broadcast_in_dim | solution.py:246
  29.8 1.3 %collective-permute-done.1 = f32[1,2,256,64]{2,3,1,0:T(8,128)S(1)} collective-permute-done((f32[1,2,256,64]{2,3,1,0:T(8,128)S(1)}, f32[1,2,256,64]{2,3,1,0:T(8,128)S(1)}, u32[]{:S(2)}, u32[]{:S(2)}) %collective-permute-start.1) | collective-permute-done | bytes 131104 | tf_op jit(solution)/shard_map/ppermute | solution.py:229
  31.1 4.3 %collective-permute-done.4 = f32[2,128,256]{2,1,0:T(8,128)S(1)} collective-permute-done((f32[2,128,256]{2,1,0:T(8,128)S(1)}, f32[2,128,256]{2,1,0:T(8,128)S(1)}, u32[]{:S(2)}, u32[]{:S(2)}) %collective-permute-start.4) | collective-permute-done | bytes 262176 | tf_op jit(solution)/shard_map/ppermute | solution.py:65
  35.5 2.7 %collective-permute-start.5 = (f32[2,64,256]{2,1,0:T(8,128)S(1)}, f32[2,64,256]{2,1,0:T(8,128)S(1)}, u32[]{:S(2)}, u32[]{:S(2)}) collective-permute-start(f32[2,64,256]{2,1,0:T(8,128)S(1)} %slice_select_fusion), channel_id=1, source_target_pairs={{0,2},{1,3},{2,0},{3,1},{4,6},{5,7},{6,4},{7,5},{8,10},{9,11},{10,... | collective-permute-start | bytes 393224 | tf_op jit(solution)/shard_map/ppermute | solution.py:65
  38.2 0.5 fusion.13
  38.7 5.0 %collective-permute-done.5 = f32[2,64,256]{2,1,0:T(8,128)S(1)} collective-permute-done((f32[2,64,256]{2,1,0:T(8,128)S(1)}, f32[2,64,256]{2,1,0:T(8,128)S(1)}, u32[]{:S(2)}, u32[]{:S(2)}) %collective-permute-start.5) | collective-permute-done | bytes 131104 | tf_op jit(solution)/shard_map/ppermute | solution.py:65
  43.7 0.5 collective-permute-start.6
  44.2 0.5 fusion.3
  44.7 5.5 %collective-permute-done.6 = f32[2,64,256]{2,1,0:T(8,128)S(1)} collective-permute-done((f32[2,64,256]{2,1,0:T(8,128)S(1)}, f32[2,64,256]{2,1,0:T(8,128)S(1)}, u32[]{:S(2)}, u32[]{:S(2)}) %collective-permute-start.6) | collective-permute-done | bytes 131104 | tf_op jit(solution)/shard_map/ppermute | solution.py:69
  50.3 2.0 %collective-permute-start.7 = (f32[2,128,256]{2,1,0:T(8,128)S(1)}, f32[2,128,256]{2,1,0:T(8,128)S(1)}, u32[]{:S(2)}, u32[]{:S(2)}) collective-permute-start(f32[2,128,256]{2,1,0:T(8,128)S(1)} %maximum_select_fusion.1), channel_id=1, source_target_pairs={{0,1},{1,0},{2,3},{3,2},{4,5},{5,4},{6,7},{7,6},{8,9},{9,8},{10,11... | collective-permute-start | bytes 786440 | tf_op jit(solution)/shard_map/ppermute | solution.py:69
  52.3 0.5 fusion.2
  52.8 0.8 %maximum_bitcast_fusion = f32[1,1,2,256,256]{4,3,2,1,0:T(8,128)} fusion(f32[1,1,256,256]{3,2,1,0:T(8,128)S(1)} %fusion.2, f32[1,1,256,256]{3,2,1,0:T(8,128)S(1)} %fusion.3), kind=kLoop, calls=%fused_computation.16 | loop fusion | flops 131072 | bytes 1048576 | tf_op jit(solution)/shard_map/broadcast_in_dim | solution.py:246
  53.7 3.1 %collective-permute-done.7 = f32[2,128,256]{2,1,0:T(8,128)S(1)} collective-permute-done((f32[2,128,256]{2,1,0:T(8,128)S(1)}, f32[2,128,256]{2,1,0:T(8,128)S(1)}, u32[]{:S(2)}, u32[]{:S(2)}) %collective-permute-start.7) | collective-permute-done | bytes 262176 | tf_op jit(solution)/shard_map/ppermute | solution.py:69
  56.7 0.8 %maximum_select_fusion = f32[1,1,2,256,256]{4,3,2,1,0:T(8,128)} fusion(f32[1,1,2,128,256]{4,3,2,1,0:T(8,128)S(1)} %bitcast.147, f32[1,1,2,128,256]{4,3,2,1,0:T(8,128)S(1)} %bitcast.145, pred[]{:T(512)S(6)} %eq.18), kind=kLoop, calls=%fused_computation.20 | loop fusion | flops 393216 | bytes 1048577 | tf_op jit(solution)/shard_map/jit(_where)/select_n | solution.py:70
  (33 shorter events, 1.0 us)
Async XLA Ops:
  0.6 10.5 %copy-start.2 = (bf16[1,2,1,2,256,256]{5,4,3,2,1,0:T(8,128)(2,1)S(1)}, bf16[1,2,1,2,256,256]{5,4,3,2,1,0:T(8,128)(2,1)}, u32[]{:S(2)}) copy-start(bf16[1,2,1,2,256,256]{5,4,3,2,1,0:T(8,128)(2,1)} %param.13) | copy-start | bytes 1572868
  0.6 11.5 %collective-permute-start.2 = (f32[1,1,2,256,256]{4,3,2,1,0:T(8,128)}, f32[1,1,2,256,256]{4,3,2,1,0:T(8,128)S(1)}, u32[]{:S(2)}, u32[]{:S(2)}) collective-permute-start(f32[1,1,2,256,256]{4,3,2,1,0:T(8,128)} %param.12), channel_id=1, source_target_pairs={{8,0},{16,8},{24,16},{9,1},{17,9},{25,17},{10,2},{18,10},{26,18},{... | collective-permute-start | bytes 1572872 | tf_op jit(solution)/shard_map/ppermute | solution.py:32
  2.1 15.4 %collective-permute-start = (f32[1,1,2,256,256]{4,3,2,1,0:T(8,128)}, f32[1,1,2,256,256]{4,3,2,1,0:T(8,128)S(1)}, u32[]{:S(2)}, u32[]{:S(2)}) collective-permute-start(f32[1,1,2,256,256]{4,3,2,1,0:T(8,128)} %param.11), channel_id=1, source_target_pairs={{0,8},{8,16},{16,24},{1,9},{9,17},{17,25},{2,10},{10,18},{18,26},{... | collective-permute-start | bytes 1572872 | tf_op jit(solution)/shard_map/ppermute | solution.py:29
  11.2 1.0 %copy-start.6 = (f32[1,256,256]{2,1,0:T(8,128)S(1)}, f32[1,256,256]{2,1,0:T(8,128)}, u32[]{:S(2)}) copy-start(f32[1,256,256]{2,1,0:T(8,128)} %param.14) | copy-start | bytes 786436
  12.1 1.1 %copy-start.4 = (f32[1,3,256,256]{3,2,1,0:T(8,128)S(1)}, f32[1,3,256,256]{3,2,1,0:T(8,128)}, u32[]{:S(2)}) copy-start(f32[1,3,256,256]{3,2,1,0:T(8,128)} %get-tuple-element.13) | copy-start | bytes 2359300
  13.6 3.8 %copy-start.5 = (bf16[2,256,256]{2,1,0:T(8,128)(2,1)S(1)}, bf16[2,256,256]{2,1,0:T(8,128)(2,1)}, u32[]{:S(2)}) copy-start(bf16[2,256,256]{2,1,0:T(8,128)(2,1)} %param.9) | copy-start | bytes 786436
  14.5 6.9 %copy-start.1 = (f32[1,3,256,320]{3,2,1,0:T(8,128)S(1)}, f32[1,3,256,320]{3,2,1,0:T(8,128)}, u32[]{:S(2)}) copy-start(f32[1,3,256,320]{3,2,1,0:T(8,128)} %get-tuple-element.14) | copy-start | bytes 2949124
  14.5 6.8 %collective-permute-start.3 = (f32[1,2,256,64]{2,3,1,0:T(8,128)S(1)}, f32[1,2,256,64]{2,3,1,0:T(8,128)S(1)}, u32[]{:S(2)}, u32[]{:S(2)}) collective-permute-start(f32[1,2,256,64]{2,3,1,0:T(8,128)S(1)} %fusion.68), channel_id=1, source_target_pairs={{0,4},{4,0},{1,5},{5,1},{2,6},{6,2},{3,7},{7,3},{8,12},{12,8},{9,1... | collective-permute-start | bytes 393224 | tf_op jit(solution)/shard_map/ppermute | solution.py:229
  21.3 1.1 %copy-start.7 = (f32[256,256]{1,0:T(8,128)S(1)}, f32[256,256]{1,0:T(8,128)}, u32[]{:S(2)}) copy-start(f32[256,256]{1,0:T(8,128)} %get-tuple-element.10) | copy-start | bytes 786436
  21.3 1.1 %copy-start.8 = (f32[256,256]{1,0:T(8,128)S(1)}, f32[256,256]{1,0:T(8,128)}, u32[]{:S(2)}) copy-start(f32[256,256]{1,0:T(8,128)} %get-tuple-element.11) | copy-start | bytes 786436
  22.4 1.1 %copy-start.3 = (f32[1,3,256,256]{3,2,1,0:T(8,128)S(1)}, f32[1,3,256,256]{3,2,1,0:T(8,128)}, u32[]{:S(2)}) copy-start(f32[1,3,256,256]{3,2,1,0:T(8,128)} %get-tuple-element.9) | copy-start | bytes 2359300
  24.7 6.3 %collective-permute-start.1 = (f32[1,2,256,64]{2,3,1,0:T(8,128)S(1)}, f32[1,2,256,64]{2,3,1,0:T(8,128)S(1)}, u32[]{:S(2)}, u32[]{:S(2)}) collective-permute-start(f32[1,2,256,64]{2,3,1,0:T(8,128)S(1)} %fusion.69), channel_id=1, source_target_pairs={{0,4},{4,0},{1,5},{5,1},{2,6},{6,2},{3,7},{7,3},{8,12},{12,8},{9,1... | collective-permute-start | bytes 393224 | tf_op jit(solution)/shard_map/ppermute | solution.py:229
  27.3 8.1 %collective-permute-start.4 = (f32[2,128,256]{2,1,0:T(8,128)S(1)}, f32[2,128,256]{2,1,0:T(8,128)S(1)}, u32[]{:S(2)}, u32[]{:S(2)}) collective-permute-start(f32[2,128,256]{2,1,0:T(8,128)S(1)} %broadcast_select_fusion), channel_id=1, source_target_pairs={{0,1},{1,0},{2,3},{3,2},{4,5},{5,4},{6,7},{7,6},{8,9},{9,8},{10,11... | collective-permute-start | bytes 786440 | tf_op jit(solution)/shard_map/ppermute | solution.py:65
  31.1 7.1 %copy-start = (f32[1,3,256,320]{3,2,1,0:T(8,128)S(1)}, f32[1,3,256,320]{3,2,1,0:T(8,128)}, u32[]{:S(2)}) copy-start(f32[1,3,256,320]{3,2,1,0:T(8,128)} %get-tuple-element.12) | copy-start | bytes 2949124
  35.5 8.1 %collective-permute-start.5 = (f32[2,64,256]{2,1,0:T(8,128)S(1)}, f32[2,64,256]{2,1,0:T(8,128)S(1)}, u32[]{:S(2)}, u32[]{:S(2)}) collective-permute-start(f32[2,64,256]{2,1,0:T(8,128)S(1)} %slice_select_fusion), channel_id=1, source_target_pairs={{0,2},{1,3},{2,0},{3,1},{4,6},{5,7},{6,4},{7,5},{8,10},{9,11},{10,... | collective-permute-start | bytes 393224 | tf_op jit(solution)/shard_map/ppermute | solution.py:65
  43.7 6.6 %collective-permute-start.6 = (f32[2,64,256]{2,1,0:T(8,128)S(1)}, f32[2,64,256]{2,1,0:T(8,128)S(1)}, u32[]{:S(2)}, u32[]{:S(2)}) collective-permute-start(f32[2,64,256]{2,1,0:T(8,128)S(1)} %select_add_fusion.1), channel_id=1, source_target_pairs={{0,2},{1,3},{2,0},{3,1},{4,6},{5,7},{6,4},{7,5},{8,10},{9,11},{10,... | collective-permute-start | bytes 393224 | tf_op jit(solution)/shard_map/ppermute | solution.py:69
  50.3 6.4 %collective-permute-start.7 = (f32[2,128,256]{2,1,0:T(8,128)S(1)}, f32[2,128,256]{2,1,0:T(8,128)S(1)}, u32[]{:S(2)}, u32[]{:S(2)}) collective-permute-start(f32[2,128,256]{2,1,0:T(8,128)S(1)} %maximum_select_fusion.1), channel_id=1, source_target_pairs={{0,1},{1,0},{2,3},{3,2},{4,5},{5,4},{6,7},{7,6},{8,9},{9,8},{10,11... | collective-permute-start | bytes 786440 | tf_op jit(solution)/shard_map/ppermute | solution.py:69

commit v12 on v9

--- a/solution.py
+++ b/solution.py
@@ -73,6 +73,22 @@
             jnp.concatenate([other, held], axis=dim),
         )
     return held
+
+
+def exchange_allreduce(value, axis):
+    count = lax.axis_size(axis)
+    if count == 1:
+        return value
+    dim = value.ndim - 2
+    rows = value.shape[dim]
+    if rows % count:
+        return lax.psum(value, axis)
+    blocks = jnp.stack(jnp.split(value, count, axis=dim))
+    gathered = lax.all_to_all(blocks, axis, 0, 0)
+    share = jnp.sum(gathered, axis=0)
+    spread = jnp.broadcast_to(share[None], (count,) + share.shape)
+    everyone = lax.all_to_all(spread, axis, 0, 0)
+    return jnp.concatenate([everyone[j] for j in range(count)], axis=dim)
 
 
 def table_kernel(
@@ -220,7 +236,7 @@
     grad_real = spread[:, 0] * held_field[:, 0] + spread[:, 1] * held_field[:, 1]
     grad_imag = spread[:, 1] * held_field[:, 0] - spread[:, 0] * held_field[:, 1]
     gradient_term = jnp.stack([jnp.sum(grad_real, axis=0), jnp.sum(grad_imag, axis=0)])
-    summed = halving_allreduce(gradient_term, "angle")
+    summed = exchange_allreduce(gradient_term, "angle")
     returning = jnp.stack(
         [
             cosine * spread[:, 0] + sine_part * spread[:, 1],

time: 57.6 us -> 65.3 us (1.13)
  starting transfers between devices: 13 us -> 16.8 us
  waiting for transfers between devices: 25.4 us -> 28.3 us
  local copies, waits for them, and re-layouts: 3.76 us -> 4.64 us
    ppermute x4 -> x0, waiting for transfers between devices: 24.8 us -> none  [the longest x2 12.4 us: halving_allreduce(): held = keep + lax.ppermute(give, axis, pairs)]
    all_to_all x0 -> x2, waiting for transfers between devices: none -> 20.6 us  [the longest x1 12.3 us: exchange_allreduce(): everyone = lax.all_to_all(spread, axis, 0, 0)]
    all_to_all x0 -> x2, starting transfers between devices: none -> 9.01 us  [the longest x1 5.4 us: exchange_allreduce(): gathered = lax.all_to_all(blocks, axis, 0, 0)]
    ppermute x2, waiting for transfers between devices: 0.59 us -> 7.67 us  [side_halo(): edges = lax.ppermute(edges, 'tile', [(0, 1), (1, 0)])]
    ppermute x4 -> x0, starting transfers between devices: 5.82 us -> none  [the longest x2 5.67 us: halving_allreduce(): held = keep + lax.ppermute(give, axis, pairs)]
    select_n x4 -> x0, other arithmetic: 0.91 us -> none  [the longest x2 0.86 us: halving_allreduce(): jnp.where(bit == 0, jnp.concatenate([held, other], axis=dim), jnp.concate...]
    another operation x0 -> x2, other arithmetic: none -> 0.89 us  [exchange_allreduce(): blocks = jnp.stack(jnp.split(value, count, axis=dim))]
    broadcast_in_dim x0 -> x1, local copies, waits for them, and re-layouts: none -> 0.84 us  [exchange_allreduce(): spread = jnp.broadcast_to(share[None], (count,) + share.shape)]
  transfers between devices with their start and end apart: 8 -> 6, of which waited for: 5 -> 4; matrix products, arithmetic and copies ran while one was open for 17% -> 11% of each run, Pallas kernels for 9% -> 8%
where the time goes in v12:
time: 65.3 us; the launch traced here: 64.9 us
  waiting for transfers between devices  28.3 us (43%)
  starting transfers between devices  16.8 us (26%)
  matrix products  5.5 us (8%)
  Pallas kernels  4.9 us (8%)
  local copies, waits for them, and re-layouts  4.64 us (7%)
  other arithmetic  3.22 us (5%)
  between operations  1.56 us (2%)
    all_to_all x1, waiting for transfers between devices, exchange_allreduce(): everyone = lax.all_to_all(spread, axis, 0, 0)  12.3 us
    all_to_all x1, waiting for transfers between devices, exchange_allreduce(): gathered = lax.all_to_all(blocks, axis, 0, 0)  8.25 us
    ppermute x2, waiting for transfers between devices, side_halo(): edges = lax.ppermute(edges, 'tile', [(0, 1), (1, 0)])  7.67 us
    dot_general x12, matrix products, contract(): return jnp.einsum(form, left, right, precision=wave_precision)  5.5 us
    all_to_all x1, starting transfers between devices, exchange_allreduce(): gathered = lax.all_to_all(blocks, axis, 0, 0)  5.4 us
    pallas_call x1, Pallas kernels, build_tables(): pl.pallas_call(table_kernel, out_shape=(rows, rows, cols, cols), in_specs...  4.9 us
    ppermute x2, starting transfers between devices, side_halo(): edges = lax.ppermute(edges, 'tile', [(0, 1), (1, 0)])  3.94 us
    all_to_all x1, starting transfers between devices, exchange_allreduce(): everyone = lax.all_to_all(spread, axis, 0, 0)  3.6 us
  transfers between devices with their start and end apart: 6, of which 4 were waited for; matrix products, arithmetic and copies ran while one was open for 11% of the time, Pallas kernels for 8%

profile of v12, /device:TPU:0, one launch (start us, length us, event | category | flops | bytes accessed | tf_op | source)
XLA Modules:
  0.0 64.9 jit_solution(8347710829281308855)
XLA Ops:
  0.6 2.5 %collective-permute-start = (f32[1,1,2,256,256]{4,3,2,1,0:T(8,128)}, f32[1,1,2,256,256]{4,3,2,1,0:T(8,128)S(1)}, u32[]{:S(2)}, u32[]{:S(2)}) collective-permute-start(f32[1,1,2,256,256]{4,3,2,1,0:T(8,128)} %param.11), channel_id=1, source_target_pairs={{0,8},{8,16},{16,24},{1,9},{9,17},{17,25},{2,10},{10,18},{18,26},{... | collective-permute-start | bytes 1572872 | tf_op jit(solution)/shard_map/ppermute | solution.py:29
  3.2 1.3 %collective-permute-start.2 = (f32[1,1,2,256,256]{4,3,2,1,0:T(8,128)}, f32[1,1,2,256,256]{4,3,2,1,0:T(8,128)S(1)}, u32[]{:S(2)}, u32[]{:S(2)}) collective-permute-start(f32[1,1,2,256,256]{4,3,2,1,0:T(8,128)} %param.12), channel_id=1, source_target_pairs={{8,0},{16,8},{24,16},{9,1},{17,9},{25,17},{10,2},{18,10},{26,18},{... | collective-permute-start | bytes 1572872 | tf_op jit(solution)/shard_map/ppermute | solution.py:32
  4.5 1.9 %fusion.83 = (f32[1,1,256,256]{3,2,1,0:T(8,128)S(1)}, f32[1,1,256,256]{3,2,1,0:T(8,128)S(1)}) fusion(f32[1,1,256,256]{3,2,1,0:T(8,128)} %param.10), kind=kLoop, calls=%fused_computation.130 | loop fusion | bytes 786432 | tf_op jit(solution)/shard_map/cos | solution.py:206
  7.0 4.9 %shard_map.112 = (f32[1,3,256,256]{3,2,1,0:T(8,128)}, f32[1,3,256,256]{3,2,1,0:T(8,128)}, f32[1,3,256,320]{3,2,1,0:T(8,128)}, f32[1,3,256,320]{3,2,1,0:T(8,128)}) custom-call(s32[1]{0:T(128)S(6)} %copy.12.tilt_ref, s32[2]{0:T(128)} %bitcast.174, s32[1]{0:T(128)} %bitcast.1.first_ref, f32[320,1280]{1,0:T(8,128)} %constant.13.clone.grid_ref), custom_call_target="tpu_custom_call" | custom-call | tf_op jit(solution)/shard_map/pallas_call | solution.py:167
  11.9 0.1 bitcast_convert_fusion
  12.0 0.9 %copy-done.6 = f32[1,256,256]{2,1,0:T(8,128)S(1)} copy-done((f32[1,256,256]{2,1,0:T(8,128)S(1)}, f32[1,256,256]{2,1,0:T(8,128)}, u32[]{:S(2)}) %copy-start.6) | copy-done | bytes 262168
  13.0 1.0 %copy-done.4 = f32[1,3,256,256]{3,2,1,0:T(8,128)S(1)} copy-done((f32[1,3,256,256]{3,2,1,0:T(8,128)S(1)}, f32[1,3,256,256]{3,2,1,0:T(8,128)}, u32[]{:S(2)}) %copy-start.4) | copy-done | bytes 786456
  14.0 0.4 fusion.49
  14.4 0.4 fusion
  14.8 0.4 fusion.1
  15.2 2.4 %collective-permute-start.3 = (f32[1,2,256,64]{2,3,1,0:T(8,128)S(1)}, f32[1,2,256,64]{2,3,1,0:T(8,128)S(1)}, u32[]{:S(2)}, u32[]{:S(2)}) collective-permute-start(f32[1,2,256,64]{2,3,1,0:T(8,128)S(1)} %fusion.81), channel_id=1, source_target_pairs={{0,4},{4,0},{1,5},{5,1},{2,6},{6,2},{3,7},{7,3},{8,12},{12,8},{9,1... | collective-permute-start | bytes 393224 | tf_op jit(solution)/shard_map/ppermute | solution.py:231
  17.6 0.1 multiply_add_fusion
  17.7 2.8 %collective-permute-done.3 = f32[1,2,256,64]{2,3,1,0:T(8,128)S(1)} collective-permute-done((f32[1,2,256,64]{2,3,1,0:T(8,128)S(1)}, f32[1,2,256,64]{2,3,1,0:T(8,128)S(1)}, u32[]{:S(2)}, u32[]{:S(2)}) %collective-permute-start.3) | collective-permute-done | bytes 131104 | tf_op jit(solution)/shard_map/ppermute | solution.py:231
  20.6 0.5 fusion.9
  21.1 0.5 convolution_subtract_fusion
  21.6 0.6 add_bitcast_fusion
  22.3 0.8 %pad_maximum_fusion.2 = f32[4,2,64,256]{3,2,1,0:T(8,128)} fusion(f32[1,2,64,256]{3,2,1,0:T(8,128)S(1)} %get-tuple-element.23, f32[1,2,64,256]{3,2,1,0:T(8,128)S(1)} %get-tuple-element.24, f32[1,2,64,256]{3,2,1,0:T(8,128)S(1)} %get-tuple-element.22, f32[1,2,64,256]{3,2,1,0:T(8,128)S(1)} %get-tuple-element.21), kind=kLoop, calls=%fused_computation.24 | loop fusion | flops 393216 | bytes 1048576 | tf_op jit(solution)/shard_map/stack | solution.py:86
  23.2 5.4 %all-to-all-start = ((f32[4,2,64,256]{3,2,1,0:T(8,128)}), f32[4,2,64,256]{3,2,1,0:T(8,128)S(1)}, u32[]{:S(2)}, u32[]{:S(2)}) async-start(f32[4,2,64,256]{3,2,1,0:T(8,128)} %pad_maximum_fusion.2), calls=%async_computation | async-start | bytes 1048576 | tf_op jit(solution)/shard_map/all_to_all | solution.py:87
  28.6 0.4 fusion.56
  29.0 0.4 fusion.4
  29.4 0.4 fusion.5
  29.8 1.6 %collective-permute-start.1 = (f32[1,2,256,64]{2,3,1,0:T(8,128)S(1)}, f32[1,2,256,64]{2,3,1,0:T(8,128)S(1)}, u32[]{:S(2)}, u32[]{:S(2)}) collective-permute-start(f32[1,2,256,64]{2,3,1,0:T(8,128)S(1)} %fusion.82), channel_id=1, source_target_pairs={{0,4},{4,0},{1,5},{5,1},{2,6},{6,2},{3,7},{7,3},{8,12},{12,8},{9,1... | collective-permute-start | bytes 393224 | tf_op jit(solution)/shard_map/ppermute | solution.py:231
  31.3 4.9 %collective-permute-done.1 = f32[1,2,256,64]{2,3,1,0:T(8,128)S(1)} collective-permute-done((f32[1,2,256,64]{2,3,1,0:T(8,128)S(1)}, f32[1,2,256,64]{2,3,1,0:T(8,128)S(1)}, u32[]{:S(2)}, u32[]{:S(2)}) %collective-permute-start.1) | collective-permute-done | bytes 131104 | tf_op jit(solution)/shard_map/ppermute | solution.py:231
  36.2 8.2 %all-to-all-done = f32[4,2,64,256]{3,2,1,0:T(8,128)S(1)} async-done(((f32[4,2,64,256]{3,2,1,0:T(8,128)}), f32[4,2,64,256]{3,2,1,0:T(8,128)S(1)}, u32[]{:S(2)}, u32[]{:S(2)}) %all-to-all-start) | async-done | bytes 524320 | tf_op jit(solution)/shard_map/all_to_all | solution.py:87
  44.5 0.8 %broadcast_in_dim.10 = f32[4,2,64,256]{3,2,1,0:T(8,128)} broadcast(f32[2,64,256]{2,1,0:T(8,128)S(1)} %reduce_sum.8), dimensions={1,2,3} | broadcast | bytes 655360 | tf_op jit(solution)/shard_map/broadcast_in_dim | solution.py:89
  45.4 3.6 %all-to-all-start.1 = ((f32[4,2,64,256]{3,2,1,0:T(8,128)}), f32[4,2,64,256]{3,2,1,0:T(8,128)S(1)}, u32[]{:S(2)}, u32[]{:S(2)}) async-start(f32[4,2,64,256]{3,2,1,0:T(8,128)} %broadcast_in_dim.10), calls=%async_computation.1 | async-start | bytes 1048576 | tf_op jit(solution)/shard_map/all_to_all | solution.py:90
  49.0 0.5 fusion.13
  49.6 0.5 fusion.2
  50.1 0.5 fusion.3
  50.6 1.0 %maximum_bitcast_fusion = (f32[1,1,2,256,256]{4,3,2,1,0:T(8,128)}, f32[1,1,2,256,256]{4,3,2,1,0:T(8,128)}) fusion(f32[1,1,256,256]{3,2,1,0:T(8,128)S(1)} %fusion.2, f32[1,1,256,256]{3,2,1,0:T(8,128)S(1)} %fusion.3, f32[1,1,256,256]{3,2,1,0:T(8,128)S(1)} %get-tuple-element.25, f32[1,1,256,256]{3,2,1,0:T(8,128)S(1)} %get-tuple-element.26), kind=kLoop, calls=%fused_computation.22 | loop fusion | flops 262144 | bytes 2097152 | tf_op jit(solution)/shard_map/broadcast_in_dim | solution.py:248
  51.6 12.3 %all-to-all-done.1 = f32[4,2,64,256]{3,2,1,0:T(8,128)S(1)} async-done(((f32[4,2,64,256]{3,2,1,0:T(8,128)}), f32[4,2,64,256]{3,2,1,0:T(8,128)S(1)}, u32[]{:S(2)}, u32[]{:S(2)}) %all-to-all-start.1) | async-done | bytes 524320 | tf_op jit(solution)/shard_map/all_to_all | solution.py:90
  64.0 0.8 %maximum_bitcast_fusion.2 = f32[1,1,2,256,256]{4,3,2,1,0:T(8,128)} fusion(f32[2,64,256]{2,1,0:T(8,128)S(1)} %get-tuple-element.18, f32[2,64,256]{2,1,0:T(8,128)S(1)} %get-tuple-element.19, f32[2,64,256]{2,1,0:T(8,128)S(1)} %get-tuple-element.20, f32[2,64,256]{2,1,0:T(8,128)S(1)} %get-tuple-element.17), kind=kLoop, calls=%fused_computation.25 | loop fusion | flops 393216 | bytes 1048576 | tf_op jit(solution)/shard_map/broadcast_in_dim | solution.py:248
  (26 shorter events, 0.5 us)
Async XLA Ops:
  0.6 11.3 %copy-start.2 = (bf16[1,2,1,2,256,256]{5,4,3,2,1,0:T(8,128)(2,1)S(1)}, bf16[1,2,1,2,256,256]{5,4,3,2,1,0:T(8,128)(2,1)}, u32[]{:S(2)}) copy-start(bf16[1,2,1,2,256,256]{5,4,3,2,1,0:T(8,128)(2,1)} %param.13) | copy-start | bytes 1572868
  0.6 16.9 %collective-permute-start = (f32[1,1,2,256,256]{4,3,2,1,0:T(8,128)}, f32[1,1,2,256,256]{4,3,2,1,0:T(8,128)S(1)}, u32[]{:S(2)}, u32[]{:S(2)}) collective-permute-start(f32[1,1,2,256,256]{4,3,2,1,0:T(8,128)} %param.11), channel_id=1, source_target_pairs={{0,8},{8,16},{16,24},{1,9},{9,17},{17,25},{2,10},{10,18},{18,26},{... | collective-permute-start | bytes 1572872 | tf_op jit(solution)/shard_map/ppermute | solution.py:29
  3.2 9.7 %collective-permute-start.2 = (f32[1,1,2,256,256]{4,3,2,1,0:T(8,128)}, f32[1,1,2,256,256]{4,3,2,1,0:T(8,128)S(1)}, u32[]{:S(2)}, u32[]{:S(2)}) collective-permute-start(f32[1,1,2,256,256]{4,3,2,1,0:T(8,128)} %param.12), channel_id=1, source_target_pairs={{8,0},{16,8},{24,16},{9,1},{17,9},{25,17},{10,2},{18,10},{26,18},{... | collective-permute-start | bytes 1572872 | tf_op jit(solution)/shard_map/ppermute | solution.py:32
  11.9 1.0 %copy-start.6 = (f32[1,256,256]{2,1,0:T(8,128)S(1)}, f32[1,256,256]{2,1,0:T(8,128)}, u32[]{:S(2)}) copy-start(f32[1,256,256]{2,1,0:T(8,128)} %param.14) | copy-start | bytes 786436
  12.8 1.1 %copy-start.4 = (f32[1,3,256,256]{3,2,1,0:T(8,128)S(1)}, f32[1,3,256,256]{3,2,1,0:T(8,128)}, u32[]{:S(2)}) copy-start(f32[1,3,256,256]{3,2,1,0:T(8,128)} %get-tuple-element.9) | copy-start | bytes 2359300
  14.4 3.2 %copy-start.5 = (bf16[2,256,256]{2,1,0:T(8,128)(2,1)S(1)}, bf16[2,256,256]{2,1,0:T(8,128)(2,1)}, u32[]{:S(2)}) copy-start(bf16[2,256,256]{2,1,0:T(8,128)(2,1)} %param.9) | copy-start | bytes 786436
  15.2 5.3 %collective-permute-start.3 = (f32[1,2,256,64]{2,3,1,0:T(8,128)S(1)}, f32[1,2,256,64]{2,3,1,0:T(8,128)S(1)}, u32[]{:S(2)}, u32[]{:S(2)}) collective-permute-start(f32[1,2,256,64]{2,3,1,0:T(8,128)S(1)} %fusion.81), channel_id=1, source_target_pairs={{0,4},{4,0},{1,5},{5,1},{2,6},{6,2},{3,7},{7,3},{8,12},{12,8},{9,1... | collective-permute-start | bytes 393224 | tf_op jit(solution)/shard_map/ppermute | solution.py:231
  17.7 2.9 %copy-start.1 = (f32[1,3,256,320]{3,2,1,0:T(8,128)S(1)}, f32[1,3,256,320]{3,2,1,0:T(8,128)}, u32[]{:S(2)}) copy-start(f32[1,3,256,320]{3,2,1,0:T(8,128)} %get-tuple-element.10) | copy-start | bytes 2949124
  22.3 6.3 %copy-start.3 = (f32[1,3,256,256]{3,2,1,0:T(8,128)S(1)}, f32[1,3,256,256]{3,2,1,0:T(8,128)}, u32[]{:S(2)}) copy-start(f32[1,3,256,256]{3,2,1,0:T(8,128)} %get-tuple-element.7) | copy-start | bytes 2359300
  23.2 21.3 %all-to-all-start = ((f32[4,2,64,256]{3,2,1,0:T(8,128)}), f32[4,2,64,256]{3,2,1,0:T(8,128)S(1)}, u32[]{:S(2)}, u32[]{:S(2)}) async-start(f32[4,2,64,256]{3,2,1,0:T(8,128)} %pad_maximum_fusion.2), calls=%async_computation | async-start | bytes 1048576 | tf_op jit(solution)/shard_map/all_to_all | solution.py:87
  29.8 6.4 %collective-permute-start.1 = (f32[1,2,256,64]{2,3,1,0:T(8,128)S(1)}, f32[1,2,256,64]{2,3,1,0:T(8,128)S(1)}, u32[]{:S(2)}, u32[]{:S(2)}) collective-permute-start(f32[1,2,256,64]{2,3,1,0:T(8,128)S(1)} %fusion.82), channel_id=1, source_target_pairs={{0,4},{4,0},{1,5},{5,1},{2,6},{6,2},{3,7},{7,3},{8,12},{12,8},{9,1... | collective-permute-start | bytes 393224 | tf_op jit(solution)/shard_map/ppermute | solution.py:231
  45.3 3.7 %copy-start = (f32[1,3,256,320]{3,2,1,0:T(8,128)S(1)}, f32[1,3,256,320]{3,2,1,0:T(8,128)}, u32[]{:S(2)}) copy-start(f32[1,3,256,320]{3,2,1,0:T(8,128)} %get-tuple-element.8) | copy-start | bytes 2949124
  45.4 18.6 %all-to-all-start.1 = ((f32[4,2,64,256]{3,2,1,0:T(8,128)}), f32[4,2,64,256]{3,2,1,0:T(8,128)S(1)}, u32[]{:S(2)}, u32[]{:S(2)}) async-start(f32[4,2,64,256]{3,2,1,0:T(8,128)} %broadcast_in_dim.10), calls=%async_computation.1 | async-start | bytes 1048576 | tf_op jit(solution)/shard_map/all_to_all | solution.py:90

commit v13 on v9

--- a/solution.py
+++ b/solution.py
@@ -189,22 +189,13 @@
 
     cosine = jnp.cos(phase[0, 0])
     sine_part = jnp.sin(phase[0, 0])
-    outgoing = jnp.concatenate([adjoint_in, forward_in], axis=0)
-    received = padded_2(outgoing, (("depth", 0),), 1, False)
-    probe_wave = probe.astype(jnp.float32)[None]
-    wavefield = jnp.where(is_first, probe_wave, received[0])
+    down = [(i + 1, i) for i in range(sections - 1)]
+    up = [(i, i + 1) for i in range(sections - 1)]
+    received_back = lax.ppermute(adjoint_in[0], "depth", down)
     exit_wave = held_waves[0, 1].astype(jnp.float32)
     intensity = exit_wave[:, 0] * exit_wave[:, 0] + exit_wave[:, 1] * exit_wave[:, 1]
     residual = (intensity - measured)[:, None] * exit_wave
-    returning = jnp.where(section == sections - 1, residual, received[3])
-    transmitted = jnp.stack(
-        [
-            cosine * wavefield[:, 0] - sine_part * wavefield[:, 1],
-            cosine * wavefield[:, 1] + sine_part * wavefield[:, 0],
-        ],
-        axis=1,
-    )
-
+    returning = jnp.where(section == sections - 1, residual, received_back)
     def side_halo(field):
         count = lax.axis_size("tile")
         if count > 2:
@@ -220,7 +211,18 @@
     grad_real = spread[:, 0] * held_field[:, 0] + spread[:, 1] * held_field[:, 1]
     grad_imag = spread[:, 1] * held_field[:, 0] - spread[:, 0] * held_field[:, 1]
     gradient_term = jnp.stack([jnp.sum(grad_real, axis=0), jnp.sum(grad_imag, axis=0)])
+    gradient_term, forward_in = lax.optimization_barrier((gradient_term, forward_in))
     summed = halving_allreduce(gradient_term, "angle")
+    received_fwd = lax.ppermute(forward_in[0], "depth", up)
+    probe_wave = probe.astype(jnp.float32)[None]
+    wavefield = jnp.where(is_first, probe_wave, received_fwd)
+    transmitted = jnp.stack(
+        [
+            cosine * wavefield[:, 0] - sine_part * wavefield[:, 1],
+            cosine * wavefield[:, 1] + sine_part * wavefield[:, 0],
+        ],
+        axis=1,
+    )
     returning = jnp.stack(
         [
             cosine * spread[:, 0] + sine_part * spread[:, 1],

time: 57.6 us -> 54.2 us (0.941)
  waiting for transfers between devices: 25.4 us -> 21.8 us
  starting transfers between devices: 13 us -> 13.8 us
    ppermute x2, waiting for transfers between devices: 12.4 us -> 8.44 us  [halving_allreduce(): other = lax.ppermute(held, axis, pairs)]
    ppermute x2, waiting for transfers between devices: 0.59 us -> 2.19 us  [side_halo(): edges = lax.ppermute(edges, 'tile', [(0, 1), (1, 0)])]
    ppermute x2, waiting for transfers between devices: 12.4 us -> 11.2 us  [halving_allreduce(): held = keep + lax.ppermute(give, axis, pairs)]
    ppermute x2, starting transfers between devices: 3.38 us -> 4.52 us  [side_halo(): edges = lax.ppermute(edges, 'tile', [(0, 1), (1, 0)])]
    cos x1, local copies, waits for them, and re-layouts: 1.86 us -> 0.95 us  [body(): cosine = jnp.cos(phase[0, 0])]
    unnamed x14 -> x18, local copies, waits for them, and re-layouts: 1.88 us -> 2.78 us
    broadcast_in_dim x2 -> x1, other arithmetic: 1.66 us -> 1.03 us  [body(): return (wavefield[None], returning[None], summed[None, None])]
  transfers between devices with their start and end apart: 8 -> 8, of which waited for: 5 -> 5; matrix products, arithmetic and copies ran while one was open for 17% -> 10% of each run, Pallas kernels for 9% -> 9%
where the time goes in v13:
time: 54.2 us; the launch traced here: 53.8 us
  waiting for transfers between devices  21.8 us (40%)
  starting transfers between devices  13.8 us (25%)
  matrix products  5.51 us (10%)
  Pallas kernels  4.89 us (9%)
  local copies, waits for them, and re-layouts  3.74 us (7%)
  other arithmetic  2.5 us (5%)
  between operations  1.64 us (3%)
    ppermute x2, waiting for transfers between devices, halving_allreduce(): held = keep + lax.ppermute(give, axis, pairs)  11.2 us
    ppermute x2, waiting for transfers between devices, halving_allreduce(): other = lax.ppermute(held, axis, pairs)  8.44 us
    dot_general x12, matrix products, contract(): return jnp.einsum(form, left, right, precision=wave_precision)  5.51 us
    ppermute x2, starting transfers between devices, halving_allreduce(): held = keep + lax.ppermute(give, axis, pairs)  5.45 us
    pallas_call x1, Pallas kernels, build_tables(): pl.pallas_call(table_kernel, out_shape=(rows, rows, cols, cols), in_specs...  4.89 us
    ppermute x2, starting transfers between devices, side_halo(): edges = lax.ppermute(edges, 'tile', [(0, 1), (1, 0)])  4.52 us
    unnamed x18, local copies, waits for them, and re-layouts  2.78 us
    ppermute x1, starting transfers between devices, body(): received_fwd = lax.ppermute(forward_in[0], 'depth', up)  2.22 us
  transfers between devices with their start and end apart: 8, of which 5 were waited for; matrix products, arithmetic and copies ran while one was open for 10% of the time, Pallas kernels for 9%

profile of v13, /device:TPU:0, one launch (start us, length us, event | category | flops | bytes accessed | tf_op | source)
XLA Modules:
  0.0 53.8 jit_solution(5220445281950832862)
XLA Ops:
  0.6 1.4 %collective-permute-start = (f32[1,2,256,256]{3,2,1,0:T(8,128)}, f32[1,2,256,256]{3,2,1,0:T(8,128)S(1)}, u32[]{:S(2)}, u32[]{:S(2)}) collective-permute-start(f32[1,2,256,256]{3,2,1,0:T(8,128)} %bitcast.158), channel_id=1, source_target_pairs={{8,0},{16,8},{24,16},{9,1},{17,9},{25,17},{10,2},{18,10},{26,18},{... | collective-permute-start | bytes 1572872 | tf_op jit(solution)/shard_map/ppermute | solution.py:194
  2.7 4.9 %shard_map.112 = (f32[1,3,256,256]{3,2,1,0:T(8,128)}, f32[1,3,256,256]{3,2,1,0:T(8,128)}, f32[1,3,256,320]{3,2,1,0:T(8,128)}, f32[1,3,256,320]{3,2,1,0:T(8,128)}) custom-call(s32[1]{0:T(128)S(6)} %copy.12.tilt_ref, s32[2]{0:T(128)} %bitcast.157, s32[1]{0:T(128)} %bitcast.1.first_ref, f32[320,1280]{1,0:T(8,128)} %constant.16.clone.grid_ref), custom_call_target="tpu_custom_call" | custom-call | tf_op jit(solution)/shard_map/pallas_call | solution.py:151
  7.7 0.9 %copy-done.7 = f32[1,256,256]{2,1,0:T(8,128)S(1)} copy-done((f32[1,256,256]{2,1,0:T(8,128)S(1)}, f32[1,256,256]{2,1,0:T(8,128)}, u32[]{:S(2)}) %copy-start.7) | copy-done | bytes 262168
  8.6 0.1 multiply_select_fusion
  8.7 1.0 %copy-done.4 = f32[1,3,256,256]{3,2,1,0:T(8,128)S(1)} copy-done((f32[1,3,256,256]{3,2,1,0:T(8,128)S(1)}, f32[1,3,256,256]{3,2,1,0:T(8,128)}, u32[]{:S(2)}) %copy-start.4) | copy-done | bytes 786456
  9.7 0.4 fusion.54
  10.1 0.4 fusion.5
  10.5 0.4 fusion.4
  10.9 3.0 %collective-permute-start.1 = (f32[1,2,256,64]{2,3,1,0:T(8,128)S(1)}, f32[1,2,256,64]{2,3,1,0:T(8,128)S(1)}, u32[]{:S(2)}, u32[]{:S(2)}) collective-permute-start(f32[1,2,256,64]{2,3,1,0:T(8,128)S(1)} %fusion.77), channel_id=1, source_target_pairs={{0,4},{4,0},{1,5},{5,1},{2,6},{6,2},{3,7},{7,3},{8,12},{12,8},{9,1... | collective-permute-start | bytes 393224 | tf_op jit(solution)/shard_map/ppermute | solution.py:206
  13.9 0.9 %fusion.78 = (f32[1,1,256,256]{3,2,1,0:T(8,128)S(1)}, f32[1,1,256,256]{3,2,1,0:T(8,128)S(1)}) fusion(f32[1,1,256,256]{3,2,1,0:T(8,128)S(1)} %copy-done.5), kind=kLoop, calls=%fused_computation.118 | loop fusion | bytes 786432 | tf_op jit(solution)/shard_map/cos | solution.py:190
  14.9 2.2 %collective-permute-done.1 = f32[1,2,256,64]{2,3,1,0:T(8,128)S(1)} collective-permute-done((f32[1,2,256,64]{2,3,1,0:T(8,128)S(1)}, f32[1,2,256,64]{2,3,1,0:T(8,128)S(1)}, u32[]{:S(2)}, u32[]{:S(2)}) %collective-permute-start.1) | collective-permute-done | bytes 131104 | tf_op jit(solution)/shard_map/ppermute | solution.py:206
  17.2 0.5 fusion.12
  17.7 0.5 convolution_subtract_fusion.2
  18.2 0.6 %fusion.41 = (f32[1,1,256,256]{3,2,1,0:T(8,128)S(1)}, f32[1,1,256,256]{3,2,1,0:T(8,128)S(1)}, f32[1,256,256]{2,1,0:T(8,128)S(1)}, f32[1,256,256]{2,1,0:T(8,128)S(1)}) fusion(f32[1,1,256,256]{3,2,1,0:T(8,128)S(1)} %get-tuple-element.26, f32[256,256]{1,0:T(8,128)S(1)} %convolution_subtract_fusion.2, f32[1,1,256,256]{3,2,1,0:T(8,128)S(1)} %get-tuple-element.25, ...), kind=kOutput, calls=%fused_computation.64 | convolution fusion | flops 126681088 | bytes 3342336 | tf_op jit(solution)/shard_map/ajk,aik->aji/dot_general | solution.py:38
  18.9 2.6 %collective-permute-start.4 = (f32[2,128,256]{2,1,0:T(8,128)S(1)}, f32[2,128,256]{2,1,0:T(8,128)S(1)}, u32[]{:S(2)}, u32[]{:S(2)}) collective-permute-start(f32[2,128,256]{2,1,0:T(8,128)S(1)} %slice_select_fusion), channel_id=1, source_target_pairs={{0,1},{1,0},{2,3},{3,2},{4,5},{5,4},{6,7},{7,6},{8,9},{9,8},{10,11... | collective-permute-start | bytes 786440 | tf_op jit(solution)/shard_map/ppermute | solution.py:65
  21.6 2.2 %collective-permute-start.2 = (f32[1,2,256,256]{3,2,1,0:T(8,128)S(1)}, f32[1,2,256,256]{3,2,1,0:T(8,128)S(1)}, u32[]{:S(2)}, u32[]{:S(2)}) collective-permute-start(f32[1,2,256,256]{3,2,1,0:T(8,128)S(1)} %bitcast.159), channel_id=1, source_target_pairs={{0,8},{8,16},{16,24},{1,9},{9,17},{17,25},{2,10},{10,18},{18,26},{... | collective-permute-start | bytes 1572872 | tf_op jit(solution)/shard_map/ppermute | solution.py:216
  23.8 4.8 %collective-permute-done.4 = f32[2,128,256]{2,1,0:T(8,128)S(1)} collective-permute-done((f32[2,128,256]{2,1,0:T(8,128)S(1)}, f32[2,128,256]{2,1,0:T(8,128)S(1)}, u32[]{:S(2)}, u32[]{:S(2)}) %collective-permute-start.4) | collective-permute-done | bytes 262176 | tf_op jit(solution)/shard_map/ppermute | solution.py:65
  28.7 2.8 %collective-permute-start.5 = (f32[2,64,256]{2,1,0:T(8,128)S(1)}, f32[2,64,256]{2,1,0:T(8,128)S(1)}, u32[]{:S(2)}, u32[]{:S(2)}) collective-permute-start(f32[2,64,256]{2,1,0:T(8,128)S(1)} %slice_select_fusion.1), channel_id=1, source_target_pairs={{0,2},{1,3},{2,0},{3,1},{4,6},{5,7},{6,4},{7,5},{8,10},{9,11},{10,... | collective-permute-start | bytes 393224 | tf_op jit(solution)/shard_map/ppermute | solution.py:65
  31.5 6.4 %collective-permute-done.5 = f32[2,64,256]{2,1,0:T(8,128)S(1)} collective-permute-done((f32[2,64,256]{2,1,0:T(8,128)S(1)}, f32[2,64,256]{2,1,0:T(8,128)S(1)}, u32[]{:S(2)}, u32[]{:S(2)}) %collective-permute-start.5) | collective-permute-done | bytes 131104 | tf_op jit(solution)/shard_map/ppermute | solution.py:65
  38.1 0.1 multiply_add_fusion
  38.1 0.9 %copy-done.3 = f32[1,3,256,256]{3,2,1,0:T(8,128)S(1)} copy-done((f32[1,3,256,256]{3,2,1,0:T(8,128)S(1)}, f32[1,3,256,256]{3,2,1,0:T(8,128)}, u32[]{:S(2)}) %copy-start.3) | copy-done | bytes 786456
  39.0 0.4 fusion.48
  39.4 0.4 fusion.3
  39.8 0.4 fusion.2
  40.2 1.5 %collective-permute-start.3 = (f32[1,2,256,64]{2,3,1,0:T(8,128)S(1)}, f32[1,2,256,64]{2,3,1,0:T(8,128)S(1)}, u32[]{:S(2)}, u32[]{:S(2)}) collective-permute-start(f32[1,2,256,64]{2,3,1,0:T(8,128)S(1)} %fusion.73), channel_id=1, source_target_pairs={{0,4},{4,0},{1,5},{5,1},{2,6},{6,2},{3,7},{7,3},{8,12},{12,8},{9,1... | collective-permute-start | bytes 393224 | tf_op jit(solution)/shard_map/ppermute | solution.py:206
  41.7 4.8 %collective-permute-done.6 = f32[2,64,256]{2,1,0:T(8,128)S(1)} collective-permute-done((f32[2,64,256]{2,1,0:T(8,128)S(1)}, f32[2,64,256]{2,1,0:T(8,128)S(1)}, u32[]{:S(2)}, u32[]{:S(2)}) %collective-permute-start.6) | collective-permute-done | bytes 131104 | tf_op jit(solution)/shard_map/ppermute | solution.py:69
  46.7 0.5 fusion.8
  47.3 0.5 fusion.1
  47.8 0.5 fusion
  48.3 1.0 %maximum_bitcast_fusion = (f32[1,1,2,256,256]{4,3,2,1,0:T(8,128)}, f32[1,1,2,256,256]{4,3,2,1,0:T(8,128)}) fusion(f32[1,1,256,256]{3,2,1,0:T(8,128)S(1)} %fusion, f32[1,1,256,256]{3,2,1,0:T(8,128)S(1)} %fusion.1, f32[1,1,256,256]{3,2,1,0:T(8,128)S(1)} %get-tuple-element.16, f32[1,1,256,256]{3,2,1,0:T(8,128)S(1)} %get-tuple-element.15), kind=kLoop, calls=%fused_computation.17 | loop fusion | flops 262144 | bytes 2097152 | tf_op jit(solution)/shard_map/broadcast_in_dim | solution.py:234
  49.3 3.7 %collective-permute-done.7 = f32[2,128,256]{2,1,0:T(8,128)S(1)} collective-permute-done((f32[2,128,256]{2,1,0:T(8,128)S(1)}, f32[2,128,256]{2,1,0:T(8,128)S(1)}, u32[]{:S(2)}, u32[]{:S(2)}) %collective-permute-start.7) | collective-permute-done | bytes 262176 | tf_op jit(solution)/shard_map/ppermute | solution.py:69
  53.0 0.8 %maximum_select_fusion = f32[1,1,2,256,256]{4,3,2,1,0:T(8,128)} fusion(f32[1,1,2,128,256]{4,3,2,1,0:T(8,128)S(1)} %bitcast.156, f32[1,1,2,128,256]{4,3,2,1,0:T(8,128)S(1)} %bitcast.155, pred[]{:T(512)S(6)} %eq.18), kind=kLoop, calls=%fused_computation.19 | loop fusion | flops 393216 | bytes 1048577 | tf_op jit(solution)/shard_map/jit(_where)/select_n | solution.py:70
  (35 shorter events, 0.7 us)
Async XLA Ops:
  0.6 7.0 %copy-start.2 = (bf16[1,2,1,2,256,256]{5,4,3,2,1,0:T(8,128)(2,1)S(1)}, bf16[1,2,1,2,256,256]{5,4,3,2,1,0:T(8,128)(2,1)}, u32[]{:S(2)}) copy-start(bf16[1,2,1,2,256,256]{5,4,3,2,1,0:T(8,128)(2,1)} %param.13) | copy-start | bytes 1572868
  0.6 8.0 %collective-permute-start = (f32[1,2,256,256]{3,2,1,0:T(8,128)}, f32[1,2,256,256]{3,2,1,0:T(8,128)S(1)}, u32[]{:S(2)}, u32[]{:S(2)}) collective-permute-start(f32[1,2,256,256]{3,2,1,0:T(8,128)} %bitcast.158), channel_id=1, source_target_pairs={{8,0},{16,8},{24,16},{9,1},{17,9},{25,17},{10,2},{18,10},{26,18},{... | collective-permute-start | bytes 1572872 | tf_op jit(solution)/shard_map/ppermute | solution.py:194
  7.6 1.0 %copy-start.7 = (f32[1,256,256]{2,1,0:T(8,128)S(1)}, f32[1,256,256]{2,1,0:T(8,128)}, u32[]{:S(2)}) copy-start(f32[1,256,256]{2,1,0:T(8,128)} %param.14) | copy-start | bytes 786436
  8.6 1.1 %copy-start.4 = (f32[1,3,256,256]{3,2,1,0:T(8,128)S(1)}, f32[1,3,256,256]{3,2,1,0:T(8,128)}, u32[]{:S(2)}) copy-start(f32[1,3,256,256]{3,2,1,0:T(8,128)} %get-tuple-element.10) | copy-start | bytes 2359300
  10.1 3.8 %copy-start.5 = (f32[1,1,256,256]{3,2,1,0:T(8,128)S(1)}, f32[1,1,256,256]{3,2,1,0:T(8,128)}, u32[]{:S(2)}) copy-start(f32[1,1,256,256]{3,2,1,0:T(8,128)} %param.10) | copy-start | bytes 786436
  10.9 6.2 %copy-start.1 = (f32[1,3,256,320]{3,2,1,0:T(8,128)S(1)}, f32[1,3,256,320]{3,2,1,0:T(8,128)}, u32[]{:S(2)}) copy-start(f32[1,3,256,320]{3,2,1,0:T(8,128)} %get-tuple-element.11) | copy-start | bytes 2949124
  10.9 6.1 %collective-permute-start.1 = (f32[1,2,256,64]{2,3,1,0:T(8,128)S(1)}, f32[1,2,256,64]{2,3,1,0:T(8,128)S(1)}, u32[]{:S(2)}, u32[]{:S(2)}) collective-permute-start(f32[1,2,256,64]{2,3,1,0:T(8,128)S(1)} %fusion.77), channel_id=1, source_target_pairs={{0,4},{4,0},{1,5},{5,1},{2,6},{6,2},{3,7},{7,3},{8,12},{12,8},{9,1... | collective-permute-start | bytes 393224 | tf_op jit(solution)/shard_map/ppermute | solution.py:206
  18.8 2.7 %copy-start.8 = (f32[1,1,2,256,256]{4,3,2,1,0:T(8,128)S(1)}, f32[1,1,2,256,256]{4,3,2,1,0:T(8,128)}, u32[]{:S(2)}) copy-start(f32[1,1,2,256,256]{4,3,2,1,0:T(8,128)} %param.11) | copy-start | bytes 1572868
  18.9 19.1 %copy-start.6 = (bf16[2,256,256]{2,1,0:T(8,128)(2,1)S(1)}, bf16[2,256,256]{2,1,0:T(8,128)(2,1)}, u32[]{:S(2)}) copy-start(bf16[2,256,256]{2,1,0:T(8,128)(2,1)} %param.9) | copy-start | bytes 786436
  18.9 9.7 %collective-permute-start.4 = (f32[2,128,256]{2,1,0:T(8,128)S(1)}, f32[2,128,256]{2,1,0:T(8,128)S(1)}, u32[]{:S(2)}, u32[]{:S(2)}) collective-permute-start(f32[2,128,256]{2,1,0:T(8,128)S(1)} %slice_select_fusion), channel_id=1, source_target_pairs={{0,1},{1,0},{2,3},{3,2},{4,5},{5,4},{6,7},{7,6},{8,9},{9,8},{10,11... | collective-permute-start | bytes 786440 | tf_op jit(solution)/shard_map/ppermute | solution.py:65
  21.6 16.4 %collective-permute-start.2 = (f32[1,2,256,256]{3,2,1,0:T(8,128)S(1)}, f32[1,2,256,256]{3,2,1,0:T(8,128)S(1)}, u32[]{:S(2)}, u32[]{:S(2)}) collective-permute-start(f32[1,2,256,256]{3,2,1,0:T(8,128)S(1)} %bitcast.159), channel_id=1, source_target_pairs={{0,8},{8,16},{16,24},{1,9},{9,17},{17,25},{2,10},{10,18},{18,26},{... | collective-permute-start | bytes 1572872 | tf_op jit(solution)/shard_map/ppermute | solution.py:216
  28.7 9.2 %collective-permute-start.5 = (f32[2,64,256]{2,1,0:T(8,128)S(1)}, f32[2,64,256]{2,1,0:T(8,128)S(1)}, u32[]{:S(2)}, u32[]{:S(2)}) collective-permute-start(f32[2,64,256]{2,1,0:T(8,128)S(1)} %slice_select_fusion.1), channel_id=1, source_target_pairs={{0,2},{1,3},{2,0},{3,1},{4,6},{5,7},{6,4},{7,5},{8,10},{9,11},{10,... | collective-permute-start | bytes 393224 | tf_op jit(solution)/shard_map/ppermute | solution.py:65
  37.9 1.1 %copy-start.3 = (f32[1,3,256,256]{3,2,1,0:T(8,128)S(1)}, f32[1,3,256,256]{3,2,1,0:T(8,128)}, u32[]{:S(2)}) copy-start(f32[1,3,256,256]{3,2,1,0:T(8,128)} %get-tuple-element.9) | copy-start | bytes 2359300
  37.9 8.6 %collective-permute-start.6 = (f32[2,64,256]{2,1,0:T(8,128)S(1)}, f32[2,64,256]{2,1,0:T(8,128)S(1)}, u32[]{:S(2)}, u32[]{:S(2)}) collective-permute-start(f32[2,64,256]{2,1,0:T(8,128)S(1)} %select_add_fusion.1), channel_id=1, source_target_pairs={{0,2},{1,3},{2,0},{3,1},{4,6},{5,7},{6,4},{7,5},{8,10},{9,11},{10,... | collective-permute-start | bytes 393224 | tf_op jit(solution)/shard_map/ppermute | solution.py:69
  40.2 6.5 %copy-start = (f32[1,3,256,320]{3,2,1,0:T(8,128)S(1)}, f32[1,3,256,320]{3,2,1,0:T(8,128)}, u32[]{:S(2)}) copy-start(f32[1,3,256,320]{3,2,1,0:T(8,128)} %get-tuple-element.13) | copy-start | bytes 2949124
  40.2 6.4 %collective-permute-start.3 = (f32[1,2,256,64]{2,3,1,0:T(8,128)S(1)}, f32[1,2,256,64]{2,3,1,0:T(8,128)S(1)}, u32[]{:S(2)}, u32[]{:S(2)}) collective-permute-start(f32[1,2,256,64]{2,3,1,0:T(8,128)S(1)} %fusion.73), channel_id=1, source_target_pairs={{0,4},{4,0},{1,5},{5,1},{2,6},{6,2},{3,7},{7,3},{8,12},{12,8},{9,1... | collective-permute-start | bytes 393224 | tf_op jit(solution)/shard_map/ppermute | solution.py:206
  46.6 6.4 %collective-permute-start.7 = (f32[2,128,256]{2,1,0:T(8,128)S(1)}, f32[2,128,256]{2,1,0:T(8,128)S(1)}, u32[]{:S(2)}, u32[]{:S(2)}) collective-permute-start(f32[2,128,256]{2,1,0:T(8,128)S(1)} %maximum_select_fusion.1), channel_id=1, source_target_pairs={{0,1},{1,0},{2,3},{3,2},{4,5},{5,4},{6,7},{7,6},{8,9},{9,8},{10,11... | collective-permute-start | bytes 786440 | tf_op jit(solution)/shard_map/ppermute | solution.py:69

commit v14 on v13

--- a/solution.py
+++ b/solution.py
@@ -1,3 +1,4 @@
+import functools
 import math
 
 import jax
@@ -75,12 +76,10 @@
     return held
 
 
-def table_kernel(
-    tilt_ref, position_ref, first_ref, grid_ref, rows_fwd_ref, rows_back_ref, cols_fwd_ref, cols_back_ref
-):
-    angle_count = rows_fwd_ref.shape[0]
+def table_kernel(sign, tilt_ref, position_ref, first_ref, grid_ref, rows_ref, cols_ref):
+    angle_count = rows_ref.shape[0]
     length = grid_ref.shape[0]
-    core_size = rows_fwd_ref.shape[-1]
+    core_size = rows_ref.shape[-1]
     width = grid_ref.shape[1] // 2
     lane = lax.broadcasted_iota(jnp.int32, (1, length), 1)
     signed = jnp.where(lane >= length // 2, lane - length, lane)
@@ -89,7 +88,7 @@
     column = lax.broadcasted_iota(jnp.int32, (core_size, core_size), 1)
     low_mask = column >= core_size - MARGIN
     high_mask = column < MARGIN
-    outputs = (rows_fwd_ref, rows_back_ref, cols_fwd_ref, cols_back_ref)
+    outputs = (rows_ref, cols_ref)
     first = jnp.full((1, length), first_ref[0], jnp.int32).astype(jnp.float32)
     for a in range(angle_count):
         tilt = jnp.full((1, length), tilt_ref[a], jnp.int32).astype(jnp.float32)
@@ -101,10 +100,10 @@
         ) * first
         row_line = base_phase - 2.0 * math.pi * frequency * shift_rows
         col_line = base_phase - 2.0 * math.pi * frequency * shift_cols
-        lines = jnp.concatenate([row_line, -row_line, col_line, -col_line], axis=0)
+        lines = sign * jnp.concatenate([row_line, col_line], axis=0)
         both = jnp.concatenate([jnp.cos(lines), jnp.sin(lines)], axis=0)
         product = jnp.dot(both, grid_ref[...], precision=highest, preferred_element_type=jnp.float32)
-        count = 4
+        count = 2
         cos_cos = product[:count, :width]
         cos_sin = product[:count, width:]
         sin_cos = product[count:, :width]
@@ -120,7 +119,7 @@
             parts = []
             for q in (q_real, q_imag):
                 line = q[t : t + 1, :]
-                if t < 2:
+                if t < 1:
                     inner = rolled(line, 0)[:, :core_size]
                     low = rolled(line, core_size)[:, :core_size]
                     high = rolled(line, width - core_size)[:, :core_size]
@@ -130,7 +129,7 @@
                     parts.append(rolled(line, MARGIN)[:, :length])
             real, imag = parts
             out = outputs[t]
-            if t < 2:
+            if t < 1:
                 out[a, 0] = real + imag
                 out[a, 1] = real
                 out[a, 2] = imag
@@ -140,7 +139,7 @@
                 out[a, 2] = real + imag
 
 
-def build_tables(tilt_index, positions, is_first, core_size, length):
+def build_tables(sign, tilt_index, positions, is_first, core_size, length):
     angle_count = tilt_index.shape[0]
     width = ((2 * length + 127) // 128) * 128
     ids = np.arange(length)[:, None] * np.arange(width)[None, :] % length
@@ -149,8 +148,8 @@
     rows = jax.ShapeDtypeStruct((angle_count, 3, core_size, core_size), jnp.float32)
     cols = jax.ShapeDtypeStruct((angle_count, 3, core_size, length), jnp.float32)
     return pl.pallas_call(
-        table_kernel,
-        out_shape=(rows, rows, cols, cols),
+        functools.partial(table_kernel, sign),
+        out_shape=(rows, cols),
         in_specs=[
             pl.BlockSpec(memory_space=pltpu.SMEM),
             pl.BlockSpec(memory_space=pltpu.SMEM),
@@ -183,9 +182,7 @@
     section = lax.axis_index("depth")
     sections = lax.axis_size("depth")
     is_first = section == 0
-    rows_fwd, rows_back, cols_fwd, cols_back = build_tables(
-        tilt_index, positions, is_first, core_size, length
-    )
+    rows_back, cols_back = build_tables(-1.0, tilt_index, positions, is_first, core_size, length)
 
     cosine = jnp.cos(phase[0, 0])
     sine_part = jnp.sin(phase[0, 0])
@@ -211,7 +208,10 @@
     grad_real = spread[:, 0] * held_field[:, 0] + spread[:, 1] * held_field[:, 1]
     grad_imag = spread[:, 1] * held_field[:, 0] - spread[:, 0] * held_field[:, 1]
     gradient_term = jnp.stack([jnp.sum(grad_real, axis=0), jnp.sum(grad_imag, axis=0)])
-    gradient_term, forward_in = lax.optimization_barrier((gradient_term, forward_in))
+    gradient_term, forward_in, tilt_index = lax.optimization_barrier(
+        (gradient_term, forward_in, tilt_index)
+    )
+    rows_fwd, cols_fwd = build_tables(1.0, tilt_index, positions, is_first, core_size, length)
     summed = halving_allreduce(gradient_term, "angle")
     received_fwd = lax.ppermute(forward_in[0], "depth", up)
     probe_wave = probe.astype(jnp.float32)[None]

time: 54.2 us -> 54 us (level)
  waiting for transfers between devices: 21.8 us -> 17.2 us
  Pallas kernels: 4.89 us -> 8 us
  starting transfers between devices: 13.8 us -> 15 us
    ppermute x2, waiting for transfers between devices: 11.2 us -> 5.85 us  [halving_allreduce(): held = keep + lax.ppermute(give, axis, pairs)]
    pallas_call x1 -> x2, Pallas kernels: 4.89 us -> 8 us  [build_tables(): pl.pallas_call(functools.partial(table_kernel, sign), out_shape=(rows, co...]
    ppermute x2, waiting for transfers between devices: 8.44 us -> 9.4 us  [halving_allreduce(): other = lax.ppermute(held, axis, pairs)]
    ppermute x1, starting transfers between devices: 2.22 us -> 3.14 us  [body(): received_fwd = lax.ppermute(forward_in[0], 'depth', up)]
  transfers between devices with their start and end apart: 8 -> 8, of which waited for: 5 -> 5; matrix products, arithmetic and copies ran while one was open for 10% -> 10% of each run, Pallas kernels for 9% -> 15%
where the time goes in v14:
time: 54 us; the launch traced here: 53.7 us
  waiting for transfers between devices  17.2 us (32%)
  starting transfers between devices  15 us (28%)
  Pallas kernels  8 us (15%)
  matrix products  5.5 us (10%)
  local copies, waits for them, and re-layouts  3.75 us (7%)
  other arithmetic  2.49 us (5%)
  between operations  1.64 us (3%)
    ppermute x2, waiting for transfers between devices, halving_allreduce(): other = lax.ppermute(held, axis, pairs)  9.4 us
    pallas_call x2, Pallas kernels, build_tables(): pl.pallas_call(functools.partial(table_kernel, sign), out_shape=(rows, co...  8 us
    ppermute x2, waiting for transfers between devices, halving_allreduce(): held = keep + lax.ppermute(give, axis, pairs)  5.85 us
    ppermute x2, starting transfers between devices, halving_allreduce(): held = keep + lax.ppermute(give, axis, pairs)  5.73 us
    dot_general x12, matrix products, contract(): return jnp.einsum(form, left, right, precision=wave_precision)  5.5 us
    ppermute x2, starting transfers between devices, side_halo(): edges = lax.ppermute(edges, 'tile', [(0, 1), (1, 0)])  4.61 us
    ppermute x1, starting transfers between devices, body(): received_fwd = lax.ppermute(forward_in[0], 'depth', up)  3.14 us
    unnamed x18, local copies, waits for them, and re-layouts  2.78 us
  transfers between devices with their start and end apart: 8, of which 5 were waited for; matrix products, arithmetic and copies ran while one was open for 10% of the time, Pallas kernels for 15%

profile of v14, /device:TPU:0, one launch (start us, length us, event | category | flops | bytes accessed | tf_op | source)
XLA Modules:
  0.0 53.7 jit_solution(1359627583177758080)
XLA Ops:
  0.6 1.4 %collective-permute-start = (f32[1,2,256,256]{3,2,1,0:T(8,128)}, f32[1,2,256,256]{3,2,1,0:T(8,128)S(1)}, u32[]{:S(2)}, u32[]{:S(2)}) collective-permute-start(f32[1,2,256,256]{3,2,1,0:T(8,128)} %bitcast.159), channel_id=1, source_target_pairs={{8,0},{16,8},{24,16},{9,1},{17,9},{25,17},{10,2},{18,10},{26,18},{... | collective-permute-start | bytes 1572872 | tf_op jit(solution)/shard_map/ppermute | solution.py:191
  2.7 4.0 %shard_map.121 = (f32[1,3,256,256]{3,2,1,0:T(8,128)}, f32[1,3,256,320]{3,2,1,0:T(8,128)}) custom-call(s32[1]{0:T(128)S(6)} %copy.13.tilt_ref, s32[2]{0:T(128)} %bitcast.157, s32[1]{0:T(128)} %bitcast.1.first_ref, f32[320,1280]{1,0:T(8,128)} %constant.16.clone.grid_ref), custom_call_target="tpu_custom_call" | custom-call | tf_op jit(solution)/shard_map/pallas_call | solution.py:150
  6.8 0.9 %copy-done.7 = f32[1,256,256]{2,1,0:T(8,128)S(1)} copy-done((f32[1,256,256]{2,1,0:T(8,128)S(1)}, f32[1,256,256]{2,1,0:T(8,128)}, u32[]{:S(2)}) %copy-start.7) | copy-done | bytes 262168
  7.8 0.1 multiply_select_fusion
  7.8 1.0 %copy-done.4 = f32[1,3,256,256]{3,2,1,0:T(8,128)S(1)} copy-done((f32[1,3,256,256]{3,2,1,0:T(8,128)S(1)}, f32[1,3,256,256]{3,2,1,0:T(8,128)}, u32[]{:S(2)}) %copy-start.4) | copy-done | bytes 786456
  8.8 0.4 fusion.55
  9.2 0.4 fusion.5
  9.6 0.4 fusion.4
  10.0 3.0 %collective-permute-start.1 = (f32[1,2,256,64]{2,3,1,0:T(8,128)S(1)}, f32[1,2,256,64]{2,3,1,0:T(8,128)S(1)}, u32[]{:S(2)}, u32[]{:S(2)}) collective-permute-start(f32[1,2,256,64]{2,3,1,0:T(8,128)S(1)} %fusion.77), channel_id=1, source_target_pairs={{0,4},{4,0},{1,5},{5,1},{2,6},{6,2},{3,7},{7,3},{8,12},{12,8},{9,1... | collective-permute-start | bytes 393224 | tf_op jit(solution)/shard_map/ppermute | solution.py:203
  13.1 0.9 %fusion.78 = (f32[1,1,256,256]{3,2,1,0:T(8,128)S(1)}, f32[1,1,256,256]{3,2,1,0:T(8,128)S(1)}) fusion(f32[1,1,256,256]{3,2,1,0:T(8,128)S(1)} %copy-done.5), kind=kLoop, calls=%fused_computation.118 | loop fusion | bytes 786432 | tf_op jit(solution)/shard_map/cos | solution.py:187
  14.0 2.0 %collective-permute-done.1 = f32[1,2,256,64]{2,3,1,0:T(8,128)S(1)} collective-permute-done((f32[1,2,256,64]{2,3,1,0:T(8,128)S(1)}, f32[1,2,256,64]{2,3,1,0:T(8,128)S(1)}, u32[]{:S(2)}, u32[]{:S(2)}) %collective-permute-start.1) | collective-permute-done | bytes 131104 | tf_op jit(solution)/shard_map/ppermute | solution.py:203
  16.1 0.5 fusion.12
  16.6 0.5 convolution_subtract_fusion.2
  17.1 0.6 %fusion.41 = (f32[1,1,256,256]{3,2,1,0:T(8,128)S(1)}, f32[1,1,256,256]{3,2,1,0:T(8,128)S(1)}, f32[1,256,256]{2,1,0:T(8,128)S(1)}, f32[1,256,256]{2,1,0:T(8,128)S(1)}) fusion(f32[1,1,256,256]{3,2,1,0:T(8,128)S(1)} %get-tuple-element.28, f32[256,256]{1,0:T(8,128)S(1)} %convolution_subtract_fusion.2, f32[1,1,256,256]{3,2,1,0:T(8,128)S(1)} %get-tuple-element.27, ...), kind=kOutput, calls=%fused_computation.64 | convolution fusion | flops 126681088 | bytes 3342336 | tf_op jit(solution)/shard_map/ajk,aik->aji/dot_general | solution.py:39
  17.8 2.2 %collective-permute-start.4 = (f32[2,128,256]{2,1,0:T(8,128)S(1)}, f32[2,128,256]{2,1,0:T(8,128)S(1)}, u32[]{:S(2)}, u32[]{:S(2)}) collective-permute-start(f32[2,128,256]{2,1,0:T(8,128)S(1)} %slice_select_fusion), channel_id=1, source_target_pairs={{0,1},{1,0},{2,3},{3,2},{4,5},{5,4},{6,7},{7,6},{8,9},{9,8},{10,11... | collective-permute-start | bytes 786440 | tf_op jit(solution)/shard_map/ppermute | solution.py:66
  20.0 3.1 %collective-permute-start.2 = (f32[1,2,256,256]{3,2,1,0:T(8,128)S(1)}, f32[1,2,256,256]{3,2,1,0:T(8,128)S(1)}, u32[]{:S(2)}, u32[]{:S(2)}) collective-permute-start(f32[1,2,256,256]{3,2,1,0:T(8,128)S(1)} %bitcast.160), channel_id=1, source_target_pairs={{0,8},{8,16},{16,24},{1,9},{9,17},{17,25},{2,10},{10,18},{18,26},{... | collective-permute-start | bytes 1572872 | tf_op jit(solution)/shard_map/ppermute | solution.py:216
  23.2 3.1 %collective-permute-done.4 = f32[2,128,256]{2,1,0:T(8,128)S(1)} collective-permute-done((f32[2,128,256]{2,1,0:T(8,128)S(1)}, f32[2,128,256]{2,1,0:T(8,128)S(1)}, u32[]{:S(2)}, u32[]{:S(2)}) %collective-permute-start.4) | collective-permute-done | bytes 262176 | tf_op jit(solution)/shard_map/ppermute | solution.py:66
  26.3 3.6 %collective-permute-start.5 = (f32[2,64,256]{2,1,0:T(8,128)S(1)}, f32[2,64,256]{2,1,0:T(8,128)S(1)}, u32[]{:S(2)}, u32[]{:S(2)}) collective-permute-start(f32[2,64,256]{2,1,0:T(8,128)S(1)} %slice_select_fusion.1), channel_id=1, source_target_pairs={{0,2},{1,3},{2,0},{3,1},{4,6},{5,7},{6,4},{7,5},{8,10},{9,11},{10,... | collective-permute-start | bytes 393224 | tf_op jit(solution)/shard_map/ppermute | solution.py:66
  29.9 4.0 %shard_map.122 = (f32[1,3,256,256]{3,2,1,0:T(8,128)}, f32[1,3,256,320]{3,2,1,0:T(8,128)}) custom-call(s32[1]{0:T(128)S(6)} %copy.13.tilt_ref, s32[2]{0:T(128)} %bitcast.158, s32[1]{0:T(128)} %bitcast.1.first_ref, f32[320,1280]{1,0:T(8,128)} %constant.16.clone.grid_ref), custom_call_target="tpu_custom_call" | custom-call | tf_op jit(solution)/shard_map/pallas_call | solution.py:150
  33.9 2.7 %collective-permute-done.5 = f32[2,64,256]{2,1,0:T(8,128)S(1)} collective-permute-done((f32[2,64,256]{2,1,0:T(8,128)S(1)}, f32[2,64,256]{2,1,0:T(8,128)S(1)}, u32[]{:S(2)}, u32[]{:S(2)}) %collective-permute-start.5) | collective-permute-done | bytes 131104 | tf_op jit(solution)/shard_map/ppermute | solution.py:66
  36.9 0.9 %copy-done.3 = f32[1,3,256,256]{3,2,1,0:T(8,128)S(1)} copy-done((f32[1,3,256,256]{3,2,1,0:T(8,128)S(1)}, f32[1,3,256,256]{3,2,1,0:T(8,128)}, u32[]{:S(2)}) %copy-start.3) | copy-done | bytes 786456
  37.8 0.4 fusion.48
  38.2 0.4 fusion.3
  38.6 0.4 fusion.2
  39.0 1.6 %collective-permute-start.3 = (f32[1,2,256,64]{2,3,1,0:T(8,128)S(1)}, f32[1,2,256,64]{2,3,1,0:T(8,128)S(1)}, u32[]{:S(2)}, u32[]{:S(2)}) collective-permute-start(f32[1,2,256,64]{2,3,1,0:T(8,128)S(1)} %fusion.73), channel_id=1, source_target_pairs={{0,4},{4,0},{1,5},{5,1},{2,6},{6,2},{3,7},{7,3},{8,12},{12,8},{9,1... | collective-permute-start | bytes 393224 | tf_op jit(solution)/shard_map/ppermute | solution.py:203
  40.6 5.0 %collective-permute-done.6 = f32[2,64,256]{2,1,0:T(8,128)S(1)} collective-permute-done((f32[2,64,256]{2,1,0:T(8,128)S(1)}, f32[2,64,256]{2,1,0:T(8,128)S(1)}, u32[]{:S(2)}, u32[]{:S(2)}) %collective-permute-start.6) | collective-permute-done | bytes 131104 | tf_op jit(solution)/shard_map/ppermute | solution.py:70
  45.8 0.5 fusion.8
  46.4 0.5 fusion.1
  46.9 0.5 fusion
  47.4 1.0 %maximum_bitcast_fusion = (f32[1,1,2,256,256]{4,3,2,1,0:T(8,128)}, f32[1,1,2,256,256]{4,3,2,1,0:T(8,128)}) fusion(f32[1,1,256,256]{3,2,1,0:T(8,128)S(1)} %fusion, f32[1,1,256,256]{3,2,1,0:T(8,128)S(1)} %fusion.1, f32[1,1,256,256]{3,2,1,0:T(8,128)S(1)} %get-tuple-element.18, f32[1,1,256,256]{3,2,1,0:T(8,128)S(1)} %get-tuple-element.17), kind=kLoop, calls=%fused_computation.17 | loop fusion | flops 262144 | bytes 2097152 | tf_op jit(solution)/shard_map/broadcast_in_dim | solution.py:234
  48.4 4.4 %collective-permute-done.7 = f32[2,128,256]{2,1,0:T(8,128)S(1)} collective-permute-done((f32[2,128,256]{2,1,0:T(8,128)S(1)}, f32[2,128,256]{2,1,0:T(8,128)S(1)}, u32[]{:S(2)}, u32[]{:S(2)}) %collective-permute-start.7) | collective-permute-done | bytes 262176 | tf_op jit(solution)/shard_map/ppermute | solution.py:70
  52.8 0.8 %maximum_select_fusion = f32[1,1,2,256,256]{4,3,2,1,0:T(8,128)} fusion(f32[1,1,2,128,256]{4,3,2,1,0:T(8,128)S(1)} %bitcast.156, f32[1,1,2,128,256]{4,3,2,1,0:T(8,128)S(1)} %bitcast.155, pred[]{:T(512)S(6)} %eq.18), kind=kLoop, calls=%fused_computation.19 | loop fusion | flops 393216 | bytes 1048577 | tf_op jit(solution)/shard_map/jit(_where)/select_n | solution.py:71
  (36 shorter events, 0.8 us)
Async XLA Ops:
  0.6 6.1 %copy-start.2 = (bf16[1,2,1,2,256,256]{5,4,3,2,1,0:T(8,128)(2,1)S(1)}, bf16[1,2,1,2,256,256]{5,4,3,2,1,0:T(8,128)(2,1)}, u32[]{:S(2)}) copy-start(bf16[1,2,1,2,256,256]{5,4,3,2,1,0:T(8,128)(2,1)} %param.14) | copy-start | bytes 1572868
  0.6 7.1 %collective-permute-start = (f32[1,2,256,256]{3,2,1,0:T(8,128)}, f32[1,2,256,256]{3,2,1,0:T(8,128)S(1)}, u32[]{:S(2)}, u32[]{:S(2)}) collective-permute-start(f32[1,2,256,256]{3,2,1,0:T(8,128)} %bitcast.159), channel_id=1, source_target_pairs={{8,0},{16,8},{24,16},{9,1},{17,9},{25,17},{10,2},{18,10},{26,18},{... | collective-permute-start | bytes 1572872 | tf_op jit(solution)/shard_map/ppermute | solution.py:191
  6.7 1.0 %copy-start.7 = (f32[1,256,256]{2,1,0:T(8,128)S(1)}, f32[1,256,256]{2,1,0:T(8,128)}, u32[]{:S(2)}) copy-start(f32[1,256,256]{2,1,0:T(8,128)} %param.15) | copy-start | bytes 786436
  7.7 1.1 %copy-start.4 = (f32[1,3,256,256]{3,2,1,0:T(8,128)S(1)}, f32[1,3,256,256]{3,2,1,0:T(8,128)}, u32[]{:S(2)}) copy-start(f32[1,3,256,256]{3,2,1,0:T(8,128)} %get-tuple-element.10) | copy-start | bytes 2359300
  9.2 3.8 %copy-start.5 = (f32[1,1,256,256]{3,2,1,0:T(8,128)S(1)}, f32[1,1,256,256]{3,2,1,0:T(8,128)}, u32[]{:S(2)}) copy-start(f32[1,1,256,256]{3,2,1,0:T(8,128)} %param.11) | copy-start | bytes 786436
  10.0 6.0 %copy-start.1 = (f32[1,3,256,320]{3,2,1,0:T(8,128)S(1)}, f32[1,3,256,320]{3,2,1,0:T(8,128)}, u32[]{:S(2)}) copy-start(f32[1,3,256,320]{3,2,1,0:T(8,128)} %get-tuple-element.11) | copy-start | bytes 2949124
  10.0 6.0 %collective-permute-start.1 = (f32[1,2,256,64]{2,3,1,0:T(8,128)S(1)}, f32[1,2,256,64]{2,3,1,0:T(8,128)S(1)}, u32[]{:S(2)}, u32[]{:S(2)}) collective-permute-start(f32[1,2,256,64]{2,3,1,0:T(8,128)S(1)} %fusion.77), channel_id=1, source_target_pairs={{0,4},{4,0},{1,5},{5,1},{2,6},{6,2},{3,7},{7,3},{8,12},{12,8},{9,1... | collective-permute-start | bytes 393224 | tf_op jit(solution)/shard_map/ppermute | solution.py:203
  17.7 2.3 %copy-start.8 = (f32[1,1,2,256,256]{4,3,2,1,0:T(8,128)S(1)}, f32[1,1,2,256,256]{4,3,2,1,0:T(8,128)}, u32[]{:S(2)}) copy-start(f32[1,1,2,256,256]{4,3,2,1,0:T(8,128)} %param.12) | copy-start | bytes 1572868
  17.8 8.4 %collective-permute-start.4 = (f32[2,128,256]{2,1,0:T(8,128)S(1)}, f32[2,128,256]{2,1,0:T(8,128)S(1)}, u32[]{:S(2)}, u32[]{:S(2)}) collective-permute-start(f32[2,128,256]{2,1,0:T(8,128)S(1)} %slice_select_fusion), channel_id=1, source_target_pairs={{0,1},{1,0},{2,3},{3,2},{4,5},{5,4},{6,7},{7,6},{8,9},{9,8},{10,11... | collective-permute-start | bytes 786440 | tf_op jit(solution)/shard_map/ppermute | solution.py:66
  20.0 16.8 %collective-permute-start.2 = (f32[1,2,256,256]{3,2,1,0:T(8,128)S(1)}, f32[1,2,256,256]{3,2,1,0:T(8,128)S(1)}, u32[]{:S(2)}, u32[]{:S(2)}) collective-permute-start(f32[1,2,256,256]{3,2,1,0:T(8,128)S(1)} %bitcast.160), channel_id=1, source_target_pairs={{0,8},{8,16},{16,24},{1,9},{9,17},{17,25},{2,10},{10,18},{18,26},{... | collective-permute-start | bytes 1572872 | tf_op jit(solution)/shard_map/ppermute | solution.py:216
  26.3 10.4 %copy-start.6 = (bf16[2,256,256]{2,1,0:T(8,128)(2,1)S(1)}, bf16[2,256,256]{2,1,0:T(8,128)(2,1)}, u32[]{:S(2)}) copy-start(bf16[2,256,256]{2,1,0:T(8,128)(2,1)} %param.10) | copy-start | bytes 786436
  26.3 10.3 %collective-permute-start.5 = (f32[2,64,256]{2,1,0:T(8,128)S(1)}, f32[2,64,256]{2,1,0:T(8,128)S(1)}, u32[]{:S(2)}, u32[]{:S(2)}) collective-permute-start(f32[2,64,256]{2,1,0:T(8,128)S(1)} %slice_select_fusion.1), channel_id=1, source_target_pairs={{0,2},{1,3},{2,0},{3,1},{4,6},{5,7},{6,4},{7,5},{8,10},{9,11},{10,... | collective-permute-start | bytes 393224 | tf_op jit(solution)/shard_map/ppermute | solution.py:66
  36.7 1.1 %copy-start.3 = (f32[1,3,256,256]{3,2,1,0:T(8,128)S(1)}, f32[1,3,256,256]{3,2,1,0:T(8,128)}, u32[]{:S(2)}) copy-start(f32[1,3,256,256]{3,2,1,0:T(8,128)} %get-tuple-element.13) | copy-start | bytes 2359300
  36.7 9.0 %collective-permute-start.6 = (f32[2,64,256]{2,1,0:T(8,128)S(1)}, f32[2,64,256]{2,1,0:T(8,128)S(1)}, u32[]{:S(2)}, u32[]{:S(2)}) collective-permute-start(f32[2,64,256]{2,1,0:T(8,128)S(1)} %select_add_fusion.1), channel_id=1, source_target_pairs={{0,2},{1,3},{2,0},{3,1},{4,6},{5,7},{6,4},{7,5},{8,10},{9,11},{10,... | collective-permute-start | bytes 393224 | tf_op jit(solution)/shard_map/ppermute | solution.py:70
  39.0 6.8 %copy-start = (f32[1,3,256,320]{3,2,1,0:T(8,128)S(1)}, f32[1,3,256,320]{3,2,1,0:T(8,128)}, u32[]{:S(2)}) copy-start(f32[1,3,256,320]{3,2,1,0:T(8,128)} %get-tuple-element.15) | copy-start | bytes 2949124
  39.0 6.7 %collective-permute-start.3 = (f32[1,2,256,64]{2,3,1,0:T(8,128)S(1)}, f32[1,2,256,64]{2,3,1,0:T(8,128)S(1)}, u32[]{:S(2)}, u32[]{:S(2)}) collective-permute-start(f32[1,2,256,64]{2,3,1,0:T(8,128)S(1)} %fusion.73), channel_id=1, source_target_pairs={{0,4},{4,0},{1,5},{5,1},{2,6},{6,2},{3,7},{7,3},{8,12},{12,8},{9,1... | collective-permute-start | bytes 393224 | tf_op jit(solution)/shard_map/ppermute | solution.py:203
  45.7 7.2 %collective-permute-start.7 = (f32[2,128,256]{2,1,0:T(8,128)S(1)}, f32[2,128,256]{2,1,0:T(8,128)S(1)}, u32[]{:S(2)}, u32[]{:S(2)}) collective-permute-start(f32[2,128,256]{2,1,0:T(8,128)S(1)} %maximum_select_fusion.1), channel_id=1, source_target_pairs={{0,1},{1,0},{2,3},{3,2},{4,5},{5,4},{6,7},{7,6},{8,9},{9,8},{10,11... | collective-permute-start | bytes 786440 | tf_op jit(solution)/shard_map/ppermute | solution.py:70

commit v15 on v14

--- a/solution.py
+++ b/solution.py
@@ -80,7 +80,8 @@
     angle_count = rows_ref.shape[0]
     length = grid_ref.shape[0]
     core_size = rows_ref.shape[-1]
-    width = grid_ref.shape[1] // 2
+    period = grid_ref.shape[1] // 2
+    width = 2 * period
     lane = lax.broadcasted_iota(jnp.int32, (1, length), 1)
     signed = jnp.where(lane >= length // 2, lane - length, lane)
     frequency = signed.astype(jnp.float32) / length
@@ -102,14 +103,18 @@
         col_line = base_phase - 2.0 * math.pi * frequency * shift_cols
         lines = sign * jnp.concatenate([row_line, col_line], axis=0)
         both = jnp.concatenate([jnp.cos(lines), jnp.sin(lines)], axis=0)
-        product = jnp.dot(both, grid_ref[...], precision=highest, preferred_element_type=jnp.float32)
+        product = jnp.dot(
+            both, grid_ref[...], precision=lax.Precision.HIGH, preferred_element_type=jnp.float32
+        )
         count = 2
-        cos_cos = product[:count, :width]
-        cos_sin = product[:count, width:]
-        sin_cos = product[count:, :width]
-        sin_sin = product[count:, width:]
+        cos_cos = product[:count, :period]
+        cos_sin = product[:count, period:]
+        sin_cos = product[count:, :period]
+        sin_sin = product[count:, period:]
         q_real = (cos_cos + sin_sin) * (1.0 / length)
         q_imag = (sin_cos - cos_sin) * (1.0 / length)
+        q_real = jnp.concatenate([q_real, q_real], axis=1)
+        q_imag = jnp.concatenate([q_imag, q_imag], axis=1)
 
         def rolled(line, shift):
             wide = jnp.broadcast_to(line, (core_size, width))
@@ -141,8 +146,7 @@
 
 def build_tables(sign, tilt_index, positions, is_first, core_size, length):
     angle_count = tilt_index.shape[0]
-    width = ((2 * length + 127) // 128) * 128
-    ids = np.arange(length)[:, None] * np.arange(width)[None, :] % length
+    ids = np.arange(length)[:, None] * np.arange(length)[None, :] % length
     angle = 2.0 * np.pi / length * ids
     grid = jnp.asarray(np.concatenate([np.cos(angle), np.sin(angle)], axis=1), jnp.float32)
     rows = jax.ShapeDtypeStruct((angle_count, 3, core_size, core_size), jnp.float32)

time: 54 us -> 52.1 us (0.965)
  starting transfers between devices: 15 us -> 17.6 us
  waiting for transfers between devices: 17.2 us -> 15.6 us
  Pallas kernels: 8 us -> 6.59 us
  local copies, waits for them, and re-layouts: 3.75 us -> 2.36 us
    ppermute x2, waiting for transfers between devices: 5.85 us -> 2.59 us  [halving_allreduce(): held = keep + lax.ppermute(give, axis, pairs)]
    ppermute x1, starting transfers between devices: 3.14 us -> 4.81 us  [body(): received_fwd = lax.ppermute(forward_in[0], 'depth', up)]
    ppermute x2, waiting for transfers between devices: 9.4 us -> 11.1 us  [halving_allreduce(): other = lax.ppermute(held, axis, pairs)]
    pallas_call x2, Pallas kernels: 8 us -> 6.59 us  [build_tables(): pl.pallas_call(functools.partial(table_kernel, sign), out_shape=(rows, co...]
    unnamed x18, local copies, waits for them, and re-layouts: 2.78 us -> 1.4 us
    ppermute x2, starting transfers between devices: 4.61 us -> 5.21 us  [side_halo(): edges = lax.ppermute(edges, 'tile', [(0, 1), (1, 0)])]
  transfers between devices with their start and end apart: 8 -> 8, of which waited for: 5 -> 4; matrix products, arithmetic and copies ran while one was open for 10% -> 10% of each run, Pallas kernels for 15% -> 13%
where the time goes in v15:
time: 52.1 us; the launch traced here: 51.8 us
  starting transfers between devices  17.6 us (34%)
  waiting for transfers between devices  15.6 us (30%)
  Pallas kernels  6.59 us (13%)
  matrix products  5.51 us (11%)
  other arithmetic  2.49 us (5%)
  local copies, waits for them, and re-layouts  2.36 us (5%)
  between operations  1.65 us (3%)
    ppermute x2, waiting for transfers between devices, halving_allreduce(): other = lax.ppermute(held, axis, pairs)  11.1 us
    pallas_call x2, Pallas kernels, build_tables(): pl.pallas_call(functools.partial(table_kernel, sign), out_shape=(rows, co...  6.59 us
    dot_general x12, matrix products, contract(): return jnp.einsum(form, left, right, precision=wave_precision)  5.51 us
    ppermute x2, starting transfers between devices, halving_allreduce(): held = keep + lax.ppermute(give, axis, pairs)  5.45 us
    ppermute x2, starting transfers between devices, side_halo(): edges = lax.ppermute(edges, 'tile', [(0, 1), (1, 0)])  5.21 us
    ppermute x1, starting transfers between devices, body(): received_fwd = lax.ppermute(forward_in[0], 'depth', up)  4.81 us
    ppermute x2, waiting for transfers between devices, halving_allreduce(): held = keep + lax.ppermute(give, axis, pairs)  2.59 us
    ppermute x2, waiting for transfers between devices, side_halo(): edges = lax.ppermute(edges, 'tile', [(0, 1), (1, 0)])  1.99 us
  transfers between devices with their start and end apart: 8, of which 4 were waited for; matrix products, arithmetic and copies ran while one was open for 10% of the time, Pallas kernels for 13%

profile of v15, /device:TPU:0, one launch (start us, length us, event | category | flops | bytes accessed | tf_op | source)
XLA Modules:
  0.0 51.8 jit_solution(15891938369039286393)
XLA Ops:
  0.6 1.4 %collective-permute-start = (f32[1,2,256,256]{3,2,1,0:T(8,128)}, f32[1,2,256,256]{3,2,1,0:T(8,128)S(1)}, u32[]{:S(2)}, u32[]{:S(2)}) collective-permute-start(f32[1,2,256,256]{3,2,1,0:T(8,128)} %bitcast.159), channel_id=1, source_target_pairs={{8,0},{16,8},{24,16},{9,1},{17,9},{25,17},{10,2},{18,10},{26,18},{... | collective-permute-start | bytes 1572872 | tf_op jit(solution)/shard_map/ppermute | solution.py:195
  2.7 3.3 %shard_map.121 = (f32[1,3,256,256]{3,2,1,0:T(8,128)}, f32[1,3,256,320]{3,2,1,0:T(8,128)}) custom-call(s32[1]{0:T(128)S(6)} %copy.13.tilt_ref, s32[2]{0:T(128)} %bitcast.157, s32[1]{0:T(128)} %bitcast.1.first_ref, f32[320,640]{1,0:T(8,128)} %constant.16.clone.grid_ref), custom_call_target="tpu_custom_call" | custom-call | tf_op jit(solution)/shard_map/pallas_call | solution.py:154
  6.2 0.1 multiply_select_fusion
  6.3 1.0 %copy-done.4 = f32[1,3,256,256]{3,2,1,0:T(8,128)S(1)} copy-done((f32[1,3,256,256]{3,2,1,0:T(8,128)S(1)}, f32[1,3,256,256]{3,2,1,0:T(8,128)}, u32[]{:S(2)}) %copy-start.4) | copy-done | bytes 786456
  7.3 0.4 fusion.55
  7.7 0.4 fusion.5
  8.1 0.4 fusion.4
  8.5 3.0 %collective-permute-start.1 = (f32[1,2,256,64]{2,3,1,0:T(8,128)S(1)}, f32[1,2,256,64]{2,3,1,0:T(8,128)S(1)}, u32[]{:S(2)}, u32[]{:S(2)}) collective-permute-start(f32[1,2,256,64]{2,3,1,0:T(8,128)S(1)} %fusion.77), channel_id=1, source_target_pairs={{0,4},{4,0},{1,5},{5,1},{2,6},{6,2},{3,7},{7,3},{8,12},{12,8},{9,1... | collective-permute-start | bytes 393224 | tf_op jit(solution)/shard_map/ppermute | solution.py:207
  11.5 0.9 %fusion.78 = (f32[1,1,256,256]{3,2,1,0:T(8,128)S(1)}, f32[1,1,256,256]{3,2,1,0:T(8,128)S(1)}) fusion(f32[1,1,256,256]{3,2,1,0:T(8,128)S(1)} %copy-done.5), kind=kLoop, calls=%fused_computation.118 | loop fusion | bytes 786432 | tf_op jit(solution)/shard_map/cos | solution.py:191
  12.5 2.0 %collective-permute-done.1 = f32[1,2,256,64]{2,3,1,0:T(8,128)S(1)} collective-permute-done((f32[1,2,256,64]{2,3,1,0:T(8,128)S(1)}, f32[1,2,256,64]{2,3,1,0:T(8,128)S(1)}, u32[]{:S(2)}, u32[]{:S(2)}) %collective-permute-start.1) | collective-permute-done | bytes 131104 | tf_op jit(solution)/shard_map/ppermute | solution.py:207
  14.5 0.5 fusion.12
  15.1 0.5 convolution_subtract_fusion.2
  15.6 0.6 %fusion.41 = (f32[1,1,256,256]{3,2,1,0:T(8,128)S(1)}, f32[1,1,256,256]{3,2,1,0:T(8,128)S(1)}, f32[1,256,256]{2,1,0:T(8,128)S(1)}, f32[1,256,256]{2,1,0:T(8,128)S(1)}) fusion(f32[1,1,256,256]{3,2,1,0:T(8,128)S(1)} %get-tuple-element.28, f32[256,256]{1,0:T(8,128)S(1)} %convolution_subtract_fusion.2, f32[1,1,256,256]{3,2,1,0:T(8,128)S(1)} %get-tuple-element.27, ...), kind=kOutput, calls=%fused_computation.64 | convolution fusion | flops 126681088 | bytes 3342336 | tf_op jit(solution)/shard_map/ajk,aik->aji/dot_general | solution.py:39
  16.3 2.2 %collective-permute-start.4 = (f32[2,128,256]{2,1,0:T(8,128)S(1)}, f32[2,128,256]{2,1,0:T(8,128)S(1)}, u32[]{:S(2)}, u32[]{:S(2)}) collective-permute-start(f32[2,128,256]{2,1,0:T(8,128)S(1)} %slice_select_fusion), channel_id=1, source_target_pairs={{0,1},{1,0},{2,3},{3,2},{4,5},{5,4},{6,7},{7,6},{8,9},{9,8},{10,11... | collective-permute-start | bytes 786440 | tf_op jit(solution)/shard_map/ppermute | solution.py:66
  18.5 4.8 %collective-permute-start.2 = (f32[1,2,256,256]{3,2,1,0:T(8,128)S(1)}, f32[1,2,256,256]{3,2,1,0:T(8,128)S(1)}, u32[]{:S(2)}, u32[]{:S(2)}) collective-permute-start(f32[1,2,256,256]{3,2,1,0:T(8,128)S(1)} %bitcast.160), channel_id=1, source_target_pairs={{0,8},{8,16},{16,24},{1,9},{9,17},{17,25},{2,10},{10,18},{18,26},{... | collective-permute-start | bytes 1572872 | tf_op jit(solution)/shard_map/ppermute | solution.py:220
  23.4 3.3 %collective-permute-start.5 = (f32[2,64,256]{2,1,0:T(8,128)S(1)}, f32[2,64,256]{2,1,0:T(8,128)S(1)}, u32[]{:S(2)}, u32[]{:S(2)}) collective-permute-start(f32[2,64,256]{2,1,0:T(8,128)S(1)} %slice_select_fusion.1), channel_id=1, source_target_pairs={{0,2},{1,3},{2,0},{3,1},{4,6},{5,7},{6,4},{7,5},{8,10},{9,11},{10,... | collective-permute-start | bytes 393224 | tf_op jit(solution)/shard_map/ppermute | solution.py:66
  26.7 3.3 %shard_map.122 = (f32[1,3,256,256]{3,2,1,0:T(8,128)}, f32[1,3,256,320]{3,2,1,0:T(8,128)}) custom-call(s32[1]{0:T(128)S(6)} %copy.13.tilt_ref, s32[2]{0:T(128)} %bitcast.158, s32[1]{0:T(128)} %bitcast.1.first_ref, f32[320,640]{1,0:T(8,128)} %constant.16.clone.grid_ref), custom_call_target="tpu_custom_call" | custom-call | tf_op jit(solution)/shard_map/pallas_call | solution.py:154
  29.9 2.6 %collective-permute-done.5 = f32[2,64,256]{2,1,0:T(8,128)S(1)} collective-permute-done((f32[2,64,256]{2,1,0:T(8,128)S(1)}, f32[2,64,256]{2,1,0:T(8,128)S(1)}, u32[]{:S(2)}, u32[]{:S(2)}) %collective-permute-start.5) | collective-permute-done | bytes 131104 | tf_op jit(solution)/shard_map/ppermute | solution.py:66
  32.6 0.6 %collective-permute-start.6 = (f32[2,64,256]{2,1,0:T(8,128)S(1)}, f32[2,64,256]{2,1,0:T(8,128)S(1)}, u32[]{:S(2)}, u32[]{:S(2)}) collective-permute-start(f32[2,64,256]{2,1,0:T(8,128)S(1)} %select_add_fusion.1), channel_id=1, source_target_pairs={{0,2},{1,3},{2,0},{3,1},{4,6},{5,7},{6,4},{7,5},{8,10},{9,11},{10,... | collective-permute-start | bytes 393224 | tf_op jit(solution)/shard_map/ppermute | solution.py:70
  33.2 0.1 multiply_add_fusion
  33.3 0.4 copy-done.3
  33.7 0.4 fusion.48
  34.1 0.4 fusion.3
  34.5 0.4 fusion.2
  34.9 2.2 %collective-permute-start.3 = (f32[1,2,256,64]{2,3,1,0:T(8,128)S(1)}, f32[1,2,256,64]{2,3,1,0:T(8,128)S(1)}, u32[]{:S(2)}, u32[]{:S(2)}) collective-permute-start(f32[1,2,256,64]{2,3,1,0:T(8,128)S(1)} %fusion.73), channel_id=1, source_target_pairs={{0,4},{4,0},{1,5},{5,1},{2,6},{6,2},{3,7},{7,3},{8,12},{12,8},{9,1... | collective-permute-start | bytes 393224 | tf_op jit(solution)/shard_map/ppermute | solution.py:207
  37.1 5.4 %collective-permute-done.6 = f32[2,64,256]{2,1,0:T(8,128)S(1)} collective-permute-done((f32[2,64,256]{2,1,0:T(8,128)S(1)}, f32[2,64,256]{2,1,0:T(8,128)S(1)}, u32[]{:S(2)}, u32[]{:S(2)}) %collective-permute-start.6) | collective-permute-done | bytes 131104 | tf_op jit(solution)/shard_map/ppermute | solution.py:70
  42.8 0.5 %fusion.8 = f32[256,256]{1,0:T(8,128)S(1)} fusion(f32[1,3,256,320]{3,2,1,0:T(8,128)S(1)} %copy-done, f32[1,2,256,320]{2,3,1,0:T(8,128)S(1)} %pad_maximum_fusion.1), kind=kOutput, calls=%fused_computation.24 | convolution fusion | flops 125911040 | bytes 1310720 | tf_op jit(solution)/shard_map/ajk,aik->aji/dot_general | solution.py:39
  43.3 0.5 %fusion.1 = f32[1,1,256,256]{3,2,1,0:T(8,128)S(1)} fusion(f32[256,256]{1,0:T(8,128)S(1)} %fusion.8, f32[1,3,256,320]{3,2,1,0:T(8,128)S(1)} %copy-done, f32[1,2,256,320]{2,3,1,0:T(8,128)S(1)} %pad_maximum_fusion.1), kind=kOutput, calls=%fused_computation.3 | convolution fusion | flops 125894656 | bytes 1245184 | tf_op jit(solution)/shard_map/ajk,aik->aji/dot_general | solution.py:39
  43.8 0.5 fusion
  44.3 1.0 %maximum_bitcast_fusion = (f32[1,1,2,256,256]{4,3,2,1,0:T(8,128)}, f32[1,1,2,256,256]{4,3,2,1,0:T(8,128)}) fusion(f32[1,1,256,256]{3,2,1,0:T(8,128)S(1)} %fusion, f32[1,1,256,256]{3,2,1,0:T(8,128)S(1)} %fusion.1, f32[1,1,256,256]{3,2,1,0:T(8,128)S(1)} %get-tuple-element.18, f32[1,1,256,256]{3,2,1,0:T(8,128)S(1)} %get-tuple-element.17), kind=kLoop, calls=%fused_computation.17 | loop fusion | flops 262144 | bytes 2097152 | tf_op jit(solution)/shard_map/broadcast_in_dim | solution.py:238
  45.4 5.6 %collective-permute-done.7 = f32[2,128,256]{2,1,0:T(8,128)S(1)} collective-permute-done((f32[2,128,256]{2,1,0:T(8,128)S(1)}, f32[2,128,256]{2,1,0:T(8,128)S(1)}, u32[]{:S(2)}, u32[]{:S(2)}) %collective-permute-start.7) | collective-permute-done | bytes 262176 | tf_op jit(solution)/shard_map/ppermute | solution.py:70
  51.0 0.8 %maximum_select_fusion = f32[1,1,2,256,256]{4,3,2,1,0:T(8,128)} fusion(f32[1,1,2,128,256]{4,3,2,1,0:T(8,128)S(1)} %bitcast.156, f32[1,1,2,128,256]{4,3,2,1,0:T(8,128)S(1)} %bitcast.155, pred[]{:T(512)S(6)} %eq.18), kind=kLoop, calls=%fused_computation.19 | loop fusion | flops 393216 | bytes 1048577 | tf_op jit(solution)/shard_map/jit(_where)/select_n | solution.py:71
  (36 shorter events, 0.6 us)
Async XLA Ops:
  0.6 5.4 %copy-start.2 = (bf16[1,2,1,2,256,256]{5,4,3,2,1,0:T(8,128)(2,1)S(1)}, bf16[1,2,1,2,256,256]{5,4,3,2,1,0:T(8,128)(2,1)}, u32[]{:S(2)}) copy-start(bf16[1,2,1,2,256,256]{5,4,3,2,1,0:T(8,128)(2,1)} %param.14) | copy-start | bytes 1572868
  0.6 5.6 %collective-permute-start = (f32[1,2,256,256]{3,2,1,0:T(8,128)}, f32[1,2,256,256]{3,2,1,0:T(8,128)S(1)}, u32[]{:S(2)}, u32[]{:S(2)}) collective-permute-start(f32[1,2,256,256]{3,2,1,0:T(8,128)} %bitcast.159), channel_id=1, source_target_pairs={{8,0},{16,8},{24,16},{9,1},{17,9},{25,17},{10,2},{18,10},{26,18},{... | collective-permute-start | bytes 1572872 | tf_op jit(solution)/shard_map/ppermute | solution.py:195
  2.7 3.4 %copy-start.7 = (f32[1,256,256]{2,1,0:T(8,128)S(1)}, f32[1,256,256]{2,1,0:T(8,128)}, u32[]{:S(2)}) copy-start(f32[1,256,256]{2,1,0:T(8,128)} %param.15) | copy-start | bytes 786436
  6.1 1.1 %copy-start.4 = (f32[1,3,256,256]{3,2,1,0:T(8,128)S(1)}, f32[1,3,256,256]{3,2,1,0:T(8,128)}, u32[]{:S(2)}) copy-start(f32[1,3,256,256]{3,2,1,0:T(8,128)} %get-tuple-element.10) | copy-start | bytes 2359300
  7.7 3.8 %copy-start.5 = (f32[1,1,256,256]{3,2,1,0:T(8,128)S(1)}, f32[1,1,256,256]{3,2,1,0:T(8,128)}, u32[]{:S(2)}) copy-start(f32[1,1,256,256]{3,2,1,0:T(8,128)} %param.11) | copy-start | bytes 786436
  8.5 6.0 %copy-start.1 = (f32[1,3,256,320]{3,2,1,0:T(8,128)S(1)}, f32[1,3,256,320]{3,2,1,0:T(8,128)}, u32[]{:S(2)}) copy-start(f32[1,3,256,320]{3,2,1,0:T(8,128)} %get-tuple-element.11) | copy-start | bytes 2949124
  8.5 6.0 %collective-permute-start.1 = (f32[1,2,256,64]{2,3,1,0:T(8,128)S(1)}, f32[1,2,256,64]{2,3,1,0:T(8,128)S(1)}, u32[]{:S(2)}, u32[]{:S(2)}) collective-permute-start(f32[1,2,256,64]{2,3,1,0:T(8,128)S(1)} %fusion.77), channel_id=1, source_target_pairs={{0,4},{4,0},{1,5},{5,1},{2,6},{6,2},{3,7},{7,3},{8,12},{12,8},{9,1... | collective-permute-start | bytes 393224 | tf_op jit(solution)/shard_map/ppermute | solution.py:207
  16.2 2.3 %copy-start.8 = (f32[1,1,2,256,256]{4,3,2,1,0:T(8,128)S(1)}, f32[1,1,2,256,256]{4,3,2,1,0:T(8,128)}, u32[]{:S(2)}) copy-start(f32[1,1,2,256,256]{4,3,2,1,0:T(8,128)} %param.12) | copy-start | bytes 1572868
  16.3 7.0 %collective-permute-start.4 = (f32[2,128,256]{2,1,0:T(8,128)S(1)}, f32[2,128,256]{2,1,0:T(8,128)S(1)}, u32[]{:S(2)}, u32[]{:S(2)}) collective-permute-start(f32[2,128,256]{2,1,0:T(8,128)S(1)} %slice_select_fusion), channel_id=1, source_target_pairs={{0,1},{1,0},{2,3},{3,2},{4,5},{5,4},{6,7},{7,6},{8,9},{9,8},{10,11... | collective-permute-start | bytes 786440 | tf_op jit(solution)/shard_map/ppermute | solution.py:66
  18.5 14.7 %copy-start.6 = (bf16[2,256,256]{2,1,0:T(8,128)(2,1)S(1)}, bf16[2,256,256]{2,1,0:T(8,128)(2,1)}, u32[]{:S(2)}) copy-start(bf16[2,256,256]{2,1,0:T(8,128)(2,1)} %param.10) | copy-start | bytes 786436
  18.5 14.7 %collective-permute-start.2 = (f32[1,2,256,256]{3,2,1,0:T(8,128)S(1)}, f32[1,2,256,256]{3,2,1,0:T(8,128)S(1)}, u32[]{:S(2)}, u32[]{:S(2)}) collective-permute-start(f32[1,2,256,256]{3,2,1,0:T(8,128)S(1)} %bitcast.160), channel_id=1, source_target_pairs={{0,8},{8,16},{16,24},{1,9},{9,17},{17,25},{2,10},{10,18},{18,26},{... | collective-permute-start | bytes 1572872 | tf_op jit(solution)/shard_map/ppermute | solution.py:220
  23.4 9.1 %collective-permute-start.5 = (f32[2,64,256]{2,1,0:T(8,128)S(1)}, f32[2,64,256]{2,1,0:T(8,128)S(1)}, u32[]{:S(2)}, u32[]{:S(2)}) collective-permute-start(f32[2,64,256]{2,1,0:T(8,128)S(1)} %slice_select_fusion.1), channel_id=1, source_target_pairs={{0,2},{1,3},{2,0},{3,1},{4,6},{5,7},{6,4},{7,5},{8,10},{9,11},{10,... | collective-permute-start | bytes 393224 | tf_op jit(solution)/shard_map/ppermute | solution.py:66
  32.6 1.1 %copy-start.3 = (f32[1,3,256,256]{3,2,1,0:T(8,128)S(1)}, f32[1,3,256,256]{3,2,1,0:T(8,128)}, u32[]{:S(2)}) copy-start(f32[1,3,256,256]{3,2,1,0:T(8,128)} %get-tuple-element.13) | copy-start | bytes 2359300
  32.6 10.0 %collective-permute-start.6 = (f32[2,64,256]{2,1,0:T(8,128)S(1)}, f32[2,64,256]{2,1,0:T(8,128)S(1)}, u32[]{:S(2)}, u32[]{:S(2)}) collective-permute-start(f32[2,64,256]{2,1,0:T(8,128)S(1)} %select_add_fusion.1), channel_id=1, source_target_pairs={{0,2},{1,3},{2,0},{3,1},{4,6},{5,7},{6,4},{7,5},{8,10},{9,11},{10,... | collective-permute-start | bytes 393224 | tf_op jit(solution)/shard_map/ppermute | solution.py:70
  34.9 7.9 %copy-start = (f32[1,3,256,320]{3,2,1,0:T(8,128)S(1)}, f32[1,3,256,320]{3,2,1,0:T(8,128)}, u32[]{:S(2)}) copy-start(f32[1,3,256,320]{3,2,1,0:T(8,128)} %get-tuple-element.15) | copy-start | bytes 2949124
  34.9 7.8 %collective-permute-start.3 = (f32[1,2,256,64]{2,3,1,0:T(8,128)S(1)}, f32[1,2,256,64]{2,3,1,0:T(8,128)S(1)}, u32[]{:S(2)}, u32[]{:S(2)}) collective-permute-start(f32[1,2,256,64]{2,3,1,0:T(8,128)S(1)} %fusion.73), channel_id=1, source_target_pairs={{0,4},{4,0},{1,5},{5,1},{2,6},{6,2},{3,7},{7,3},{8,12},{12,8},{9,1... | collective-permute-start | bytes 393224 | tf_op jit(solution)/shard_map/ppermute | solution.py:207
  42.6 8.4 %collective-permute-start.7 = (f32[2,128,256]{2,1,0:T(8,128)S(1)}, f32[2,128,256]{2,1,0:T(8,128)S(1)}, u32[]{:S(2)}, u32[]{:S(2)}) collective-permute-start(f32[2,128,256]{2,1,0:T(8,128)S(1)} %maximum_select_fusion.1), channel_id=1, source_target_pairs={{0,1},{1,0},{2,3},{3,2},{4,5},{5,4},{6,7},{7,6},{8,9},{9,8},{10,11... | collective-permute-start | bytes 786440 | tf_op jit(solution)/shard_map/ppermute | solution.py:70

commit v16 on v15

--- a/solution.py
+++ b/solution.py
@@ -68,11 +68,14 @@
         bit = (index >> k) & 1
         pairs = [(j, j ^ (1 << k)) for j in range(count)]
         other = lax.ppermute(held, axis, pairs)
-        held = jnp.where(
+        size = held.shape[dim]
+        blank = jnp.zeros_like(held)
+        placed = jnp.where(
             bit == 0,
-            jnp.concatenate([held, other], axis=dim),
-            jnp.concatenate([other, held], axis=dim),
+            jnp.concatenate([held, blank], axis=dim),
+            jnp.concatenate([blank, held], axis=dim),
         )
+        held = lax.dynamic_update_slice_in_dim(placed, other, (1 - bit) * size, axis=dim)
     return held
 
 

time: 52.1 us -> 52.2 us (level)
  local copies, waits for them, and re-layouts: 2.36 us -> 4.81 us
  waiting for transfers between devices: 15.6 us -> 14.5 us
  other arithmetic: 2.49 us -> 1.7 us
    unnamed x18 -> x20, local copies, waits for them, and re-layouts: 1.4 us -> 3.81 us
    ppermute x2, waiting for transfers between devices: 11.1 us -> 9.87 us  [halving_allreduce(): other = lax.ppermute(held, axis, pairs)]
    select_n x2 -> x1, other arithmetic: 0.86 us -> 0.02 us  [halving_allreduce(): jnp.where(bit == 0, jnp.concatenate([held, blank], axis=dim), jnp.concate...]
    broadcast_in_dim x1 -> x2, other arithmetic: 1.03 us -> 1.07 us  [body(): return (wavefield[None], returning[None], summed[None, None])]
where the time goes in v16:
time: 52.2 us; the launch traced here: 51.8 us
  starting transfers between devices  17.1 us (33%)
  waiting for transfers between devices  14.5 us (28%)
  Pallas kernels  6.61 us (13%)
  matrix products  5.5 us (11%)
  local copies, waits for them, and re-layouts  4.81 us (9%)
  other arithmetic  1.7 us (3%)
  between operations  1.69 us (3%)
    ppermute x2, waiting for transfers between devices, halving_allreduce(): other = lax.ppermute(held, axis, pairs)  9.87 us
    pallas_call x2, Pallas kernels, build_tables(): pl.pallas_call(functools.partial(table_kernel, sign), out_shape=(rows, co...  6.61 us
    ppermute x2, starting transfers between devices, halving_allreduce(): held = keep + lax.ppermute(give, axis, pairs)  5.61 us
    dot_general x12, matrix products, contract(): return jnp.einsum(form, left, right, precision=wave_precision)  5.5 us
    ppermute x2, starting transfers between devices, side_halo(): edges = lax.ppermute(edges, 'tile', [(0, 1), (1, 0)])  4.7 us
    ppermute x1, starting transfers between devices, body(): received_fwd = lax.ppermute(forward_in[0], 'depth', up)  4.67 us
    unnamed x20, local copies, waits for them, and re-layouts  3.81 us
    ppermute x2, waiting for transfers between devices, halving_allreduce(): held = keep + lax.ppermute(give, axis, pairs)  2.59 us
  transfers between devices with their start and end apart: 8, of which 4 were waited for; matrix products, arithmetic and copies ran while one was open for 10% of the time, Pallas kernels for 13%

profile of v16, /device:TPU:0, one launch (start us, length us, event | category | flops | bytes accessed | tf_op | source)
XLA Modules:
  0.0 51.8 jit_solution(3840299387720102334)
XLA Ops:
  0.6 1.4 %collective-permute-start = (f32[1,2,256,256]{3,2,1,0:T(8,128)}, f32[1,2,256,256]{3,2,1,0:T(8,128)S(1)}, u32[]{:S(2)}, u32[]{:S(2)}) collective-permute-start(f32[1,2,256,256]{3,2,1,0:T(8,128)} %bitcast.159), channel_id=1, source_target_pairs={{8,0},{16,8},{24,16},{9,1},{17,9},{25,17},{10,2},{18,10},{26,18},{... | collective-permute-start | bytes 1572872 | tf_op jit(solution)/shard_map/ppermute | solution.py:198
  2.7 3.3 %shard_map.121 = (f32[1,3,256,256]{3,2,1,0:T(8,128)}, f32[1,3,256,320]{3,2,1,0:T(8,128)}) custom-call(s32[1]{0:T(128)S(6)} %copy.15.tilt_ref, s32[2]{0:T(128)} %bitcast.157, s32[1]{0:T(128)} %bitcast.1.first_ref, f32[320,640]{1,0:T(8,128)} %constant.26.clone.grid_ref), custom_call_target="tpu_custom_call" | custom-call | tf_op jit(solution)/shard_map/pallas_call | solution.py:157
  6.2 0.1 multiply_select_fusion
  6.3 1.0 %copy-done.4 = f32[1,3,256,256]{3,2,1,0:T(8,128)S(1)} copy-done((f32[1,3,256,256]{3,2,1,0:T(8,128)S(1)}, f32[1,3,256,256]{3,2,1,0:T(8,128)}, u32[]{:S(2)}) %copy-start.4) | copy-done | bytes 786456
  7.3 0.4 fusion.55
  7.7 0.4 fusion.5
  8.1 0.4 fusion.4
  8.5 3.0 %collective-permute-start.1 = (f32[1,2,256,64]{2,3,1,0:T(8,128)S(1)}, f32[1,2,256,64]{2,3,1,0:T(8,128)S(1)}, u32[]{:S(2)}, u32[]{:S(2)}) collective-permute-start(f32[1,2,256,64]{2,3,1,0:T(8,128)S(1)} %fusion.77), channel_id=1, source_target_pairs={{0,4},{4,0},{1,5},{5,1},{2,6},{6,2},{3,7},{7,3},{8,12},{12,8},{9,1... | collective-permute-start | bytes 393224 | tf_op jit(solution)/shard_map/ppermute | solution.py:210
  11.5 0.9 %fusion.78 = (f32[1,1,256,256]{3,2,1,0:T(8,128)S(1)}, f32[1,1,256,256]{3,2,1,0:T(8,128)S(1)}) fusion(f32[1,1,256,256]{3,2,1,0:T(8,128)S(1)} %copy-done.6), kind=kLoop, calls=%fused_computation.120 | loop fusion | bytes 786432 | tf_op jit(solution)/shard_map/cos | solution.py:194
  12.5 2.0 %collective-permute-done.1 = f32[1,2,256,64]{2,3,1,0:T(8,128)S(1)} collective-permute-done((f32[1,2,256,64]{2,3,1,0:T(8,128)S(1)}, f32[1,2,256,64]{2,3,1,0:T(8,128)S(1)}, u32[]{:S(2)}, u32[]{:S(2)}) %collective-permute-start.1) | collective-permute-done | bytes 131104 | tf_op jit(solution)/shard_map/ppermute | solution.py:210
  14.5 0.5 fusion.12
  15.1 0.5 convolution_subtract_fusion.2
  15.6 0.6 %fusion.41 = (f32[1,1,256,256]{3,2,1,0:T(8,128)S(1)}, f32[1,1,256,256]{3,2,1,0:T(8,128)S(1)}, f32[1,256,256]{2,1,0:T(8,128)S(1)}, f32[1,256,256]{2,1,0:T(8,128)S(1)}) fusion(f32[1,1,256,256]{3,2,1,0:T(8,128)S(1)} %get-tuple-element.28, f32[256,256]{1,0:T(8,128)S(1)} %convolution_subtract_fusion.2, f32[1,1,256,256]{3,2,1,0:T(8,128)S(1)} %get-tuple-element.27, ...), kind=kOutput, calls=%fused_computation.64 | convolution fusion | flops 126681088 | bytes 3342336 | tf_op jit(solution)/shard_map/ajk,aik->aji/dot_general | solution.py:39
  16.3 2.2 %collective-permute-start.4 = (f32[2,128,256]{2,1,0:T(8,128)S(1)}, f32[2,128,256]{2,1,0:T(8,128)S(1)}, u32[]{:S(2)}, u32[]{:S(2)}) collective-permute-start(f32[2,128,256]{2,1,0:T(8,128)S(1)} %slice_select_fusion), channel_id=1, source_target_pairs={{0,1},{1,0},{2,3},{3,2},{4,5},{5,4},{6,7},{7,6},{8,9},{9,8},{10,11... | collective-permute-start | bytes 786440 | tf_op jit(solution)/shard_map/ppermute | solution.py:66
  18.5 4.7 %collective-permute-start.2 = (f32[1,2,256,256]{3,2,1,0:T(8,128)S(1)}, f32[1,2,256,256]{3,2,1,0:T(8,128)S(1)}, u32[]{:S(2)}, u32[]{:S(2)}) collective-permute-start(f32[1,2,256,256]{3,2,1,0:T(8,128)S(1)} %bitcast.160), channel_id=1, source_target_pairs={{0,8},{8,16},{16,24},{1,9},{9,17},{17,25},{2,10},{10,18},{18,26},{... | collective-permute-start | bytes 1572872 | tf_op jit(solution)/shard_map/ppermute | solution.py:223
  23.3 3.4 %collective-permute-start.5 = (f32[2,64,256]{2,1,0:T(8,128)S(1)}, f32[2,64,256]{2,1,0:T(8,128)S(1)}, u32[]{:S(2)}, u32[]{:S(2)}) collective-permute-start(f32[2,64,256]{2,1,0:T(8,128)S(1)} %slice_select_fusion.1), channel_id=1, source_target_pairs={{0,2},{1,3},{2,0},{3,1},{4,6},{5,7},{6,4},{7,5},{8,10},{9,11},{10,... | collective-permute-start | bytes 393224 | tf_op jit(solution)/shard_map/ppermute | solution.py:66
  26.7 3.3 %shard_map.122 = (f32[1,3,256,256]{3,2,1,0:T(8,128)}, f32[1,3,256,320]{3,2,1,0:T(8,128)}) custom-call(s32[1]{0:T(128)S(6)} %copy.15.tilt_ref, s32[2]{0:T(128)} %bitcast.158, s32[1]{0:T(128)} %bitcast.1.first_ref, f32[320,640]{1,0:T(8,128)} %constant.26.clone.grid_ref), custom_call_target="tpu_custom_call" | custom-call | tf_op jit(solution)/shard_map/pallas_call | solution.py:157
  30.0 2.6 %collective-permute-done.5 = f32[2,64,256]{2,1,0:T(8,128)S(1)} collective-permute-done((f32[2,64,256]{2,1,0:T(8,128)S(1)}, f32[2,64,256]{2,1,0:T(8,128)S(1)}, u32[]{:S(2)}, u32[]{:S(2)}) %collective-permute-start.5) | collective-permute-done | bytes 131104 | tf_op jit(solution)/shard_map/ppermute | solution.py:66
  32.6 0.6 %collective-permute-start.6 = (f32[2,64,256]{2,1,0:T(8,128)S(1)}, f32[2,64,256]{2,1,0:T(8,128)S(1)}, u32[]{:S(2)}, u32[]{:S(2)}) collective-permute-start(f32[2,64,256]{2,1,0:T(8,128)S(1)} %select_add_fusion.1), channel_id=1, source_target_pairs={{0,2},{1,3},{2,0},{3,1},{4,6},{5,7},{6,4},{7,5},{8,10},{9,11},{10,... | collective-permute-start | bytes 393224 | tf_op jit(solution)/shard_map/ppermute | solution.py:70
  33.4 1.0 %copy-done.3 = f32[1,3,256,256]{3,2,1,0:T(8,128)S(1)} copy-done((f32[1,3,256,256]{3,2,1,0:T(8,128)S(1)}, f32[1,3,256,256]{3,2,1,0:T(8,128)}, u32[]{:S(2)}) %copy-start.3) | copy-done | bytes 786456
  34.4 0.4 fusion.48
  34.7 0.4 fusion.3
  35.1 0.4 fusion.2
  35.6 1.7 %collective-permute-start.3 = (f32[1,2,256,64]{2,3,1,0:T(8,128)S(1)}, f32[1,2,256,64]{2,3,1,0:T(8,128)S(1)}, u32[]{:S(2)}, u32[]{:S(2)}) collective-permute-start(f32[1,2,256,64]{2,3,1,0:T(8,128)S(1)} %fusion.73), channel_id=1, source_target_pairs={{0,4},{4,0},{1,5},{5,1},{2,6},{6,2},{3,7},{7,3},{8,12},{12,8},{9,1... | collective-permute-start | bytes 393224 | tf_op jit(solution)/shard_map/ppermute | solution.py:210
  37.2 5.4 %collective-permute-done.6 = f32[2,64,256]{2,1,0:T(8,128)S(1)} collective-permute-done((f32[2,64,256]{2,1,0:T(8,128)S(1)}, f32[2,64,256]{2,1,0:T(8,128)S(1)}, u32[]{:S(2)}, u32[]{:S(2)}) %collective-permute-start.6) | collective-permute-done | bytes 131104 | tf_op jit(solution)/shard_map/ppermute | solution.py:70
  42.8 1.1 %copy-done = f32[1,3,256,320]{3,2,1,0:T(8,128)S(1)} copy-done((f32[1,3,256,320]{3,2,1,0:T(8,128)S(1)}, f32[1,3,256,320]{3,2,1,0:T(8,128)}, u32[]{:S(2)}) %copy-start) | copy-done | bytes 983064
  43.9 0.5 fusion.8
  44.4 0.5 fusion.1
  44.9 0.5 fusion
  45.5 1.0 %maximum_bitcast_fusion = (f32[1,1,2,256,256]{4,3,2,1,0:T(8,128)}, f32[1,1,2,256,256]{4,3,2,1,0:T(8,128)}) fusion(f32[1,1,256,256]{3,2,1,0:T(8,128)S(1)} %fusion, f32[1,1,256,256]{3,2,1,0:T(8,128)S(1)} %fusion.1, f32[1,1,256,256]{3,2,1,0:T(8,128)S(1)} %get-tuple-element.18, f32[1,1,256,256]{3,2,1,0:T(8,128)S(1)} %get-tuple-element.17), kind=kLoop, calls=%fused_computation.17 | loop fusion | flops 262144 | bytes 2097152 | tf_op jit(solution)/shard_map/broadcast_in_dim | solution.py:241
  46.5 4.5 %collective-permute-done.7 = f32[2,128,256]{2,1,0:T(8,128)S(1)} collective-permute-done((f32[2,128,256]{2,1,0:T(8,128)S(1)}, f32[2,128,256]{2,1,0:T(8,128)S(1)}, u32[]{:S(2)}, u32[]{:S(2)}) %collective-permute-start.7) | collective-permute-done | bytes 262176 | tf_op jit(solution)/shard_map/ppermute | solution.py:70
  51.1 0.8 %copy-done.5 = f32[1,1,2,256,256]{4,3,2,1,0:T(8,128)} copy-done((f32[1,1,2,256,256]{4,3,2,1,0:T(8,128)}, f32[1,1,2,256,256]{4,3,2,1,0:T(8,128)S(1)}, u32[]{:S(2)}) %copy-start.5) | copy-done | bytes 524312
  (40 shorter events, 0.8 us)
Async XLA Ops:
  0.6 5.4 %copy-start.2 = (bf16[1,2,1,2,256,256]{5,4,3,2,1,0:T(8,128)(2,1)S(1)}, bf16[1,2,1,2,256,256]{5,4,3,2,1,0:T(8,128)(2,1)}, u32[]{:S(2)}) copy-start(bf16[1,2,1,2,256,256]{5,4,3,2,1,0:T(8,128)(2,1)} %param.14) | copy-start | bytes 1572868
  0.6 5.6 %collective-permute-start = (f32[1,2,256,256]{3,2,1,0:T(8,128)}, f32[1,2,256,256]{3,2,1,0:T(8,128)S(1)}, u32[]{:S(2)}, u32[]{:S(2)}) collective-permute-start(f32[1,2,256,256]{3,2,1,0:T(8,128)} %bitcast.159), channel_id=1, source_target_pairs={{8,0},{16,8},{24,16},{9,1},{17,9},{25,17},{10,2},{18,10},{26,18},{... | collective-permute-start | bytes 1572872 | tf_op jit(solution)/shard_map/ppermute | solution.py:198
  2.7 3.4 %copy-start.8 = (f32[1,256,256]{2,1,0:T(8,128)S(1)}, f32[1,256,256]{2,1,0:T(8,128)}, u32[]{:S(2)}) copy-start(f32[1,256,256]{2,1,0:T(8,128)} %param.15) | copy-start | bytes 786436
  6.2 1.1 %copy-start.4 = (f32[1,3,256,256]{3,2,1,0:T(8,128)S(1)}, f32[1,3,256,256]{3,2,1,0:T(8,128)}, u32[]{:S(2)}) copy-start(f32[1,3,256,256]{3,2,1,0:T(8,128)} %get-tuple-element.10) | copy-start | bytes 2359300
  7.7 3.8 %copy-start.6 = (f32[1,1,256,256]{3,2,1,0:T(8,128)S(1)}, f32[1,1,256,256]{3,2,1,0:T(8,128)}, u32[]{:S(2)}) copy-start(f32[1,1,256,256]{3,2,1,0:T(8,128)} %param.11) | copy-start | bytes 786436
  8.5 6.0 %copy-start.1 = (f32[1,3,256,320]{3,2,1,0:T(8,128)S(1)}, f32[1,3,256,320]{3,2,1,0:T(8,128)}, u32[]{:S(2)}) copy-start(f32[1,3,256,320]{3,2,1,0:T(8,128)} %get-tuple-element.11) | copy-start | bytes 2949124
  8.5 6.0 %collective-permute-start.1 = (f32[1,2,256,64]{2,3,1,0:T(8,128)S(1)}, f32[1,2,256,64]{2,3,1,0:T(8,128)S(1)}, u32[]{:S(2)}, u32[]{:S(2)}) collective-permute-start(f32[1,2,256,64]{2,3,1,0:T(8,128)S(1)} %fusion.77), channel_id=1, source_target_pairs={{0,4},{4,0},{1,5},{5,1},{2,6},{6,2},{3,7},{7,3},{8,12},{12,8},{9,1... | collective-permute-start | bytes 393224 | tf_op jit(solution)/shard_map/ppermute | solution.py:210
  16.2 2.3 %copy-start.9 = (f32[1,1,2,256,256]{4,3,2,1,0:T(8,128)S(1)}, f32[1,1,2,256,256]{4,3,2,1,0:T(8,128)}, u32[]{:S(2)}) copy-start(f32[1,1,2,256,256]{4,3,2,1,0:T(8,128)} %param.12) | copy-start | bytes 1572868
  16.3 6.9 %collective-permute-start.4 = (f32[2,128,256]{2,1,0:T(8,128)S(1)}, f32[2,128,256]{2,1,0:T(8,128)S(1)}, u32[]{:S(2)}, u32[]{:S(2)}) collective-permute-start(f32[2,128,256]{2,1,0:T(8,128)S(1)} %slice_select_fusion), channel_id=1, source_target_pairs={{0,1},{1,0},{2,3},{3,2},{4,5},{5,4},{6,7},{7,6},{8,9},{9,8},{10,11... | collective-permute-start | bytes 786440 | tf_op jit(solution)/shard_map/ppermute | solution.py:66
  18.5 14.8 %collective-permute-start.2 = (f32[1,2,256,256]{3,2,1,0:T(8,128)S(1)}, f32[1,2,256,256]{3,2,1,0:T(8,128)S(1)}, u32[]{:S(2)}, u32[]{:S(2)}) collective-permute-start(f32[1,2,256,256]{3,2,1,0:T(8,128)S(1)} %bitcast.160), channel_id=1, source_target_pairs={{0,8},{8,16},{16,24},{1,9},{9,17},{17,25},{2,10},{10,18},{18,26},{... | collective-permute-start | bytes 1572872 | tf_op jit(solution)/shard_map/ppermute | solution.py:223
  23.2 10.0 %copy-start.7 = (bf16[2,256,256]{2,1,0:T(8,128)(2,1)S(1)}, bf16[2,256,256]{2,1,0:T(8,128)(2,1)}, u32[]{:S(2)}) copy-start(bf16[2,256,256]{2,1,0:T(8,128)(2,1)} %param.10) | copy-start | bytes 786436
  23.3 9.3 %collective-permute-start.5 = (f32[2,64,256]{2,1,0:T(8,128)S(1)}, f32[2,64,256]{2,1,0:T(8,128)S(1)}, u32[]{:S(2)}, u32[]{:S(2)}) collective-permute-start(f32[2,64,256]{2,1,0:T(8,128)S(1)} %slice_select_fusion.1), channel_id=1, source_target_pairs={{0,2},{1,3},{2,0},{3,1},{4,6},{5,7},{6,4},{7,5},{8,10},{9,11},{10,... | collective-permute-start | bytes 393224 | tf_op jit(solution)/shard_map/ppermute | solution.py:66
  32.6 10.0 %collective-permute-start.6 = (f32[2,64,256]{2,1,0:T(8,128)S(1)}, f32[2,64,256]{2,1,0:T(8,128)S(1)}, u32[]{:S(2)}, u32[]{:S(2)}) collective-permute-start(f32[2,64,256]{2,1,0:T(8,128)S(1)} %select_add_fusion.1), channel_id=1, source_target_pairs={{0,2},{1,3},{2,0},{3,1},{4,6},{5,7},{6,4},{7,5},{8,10},{9,11},{10,... | collective-permute-start | bytes 393224 | tf_op jit(solution)/shard_map/ppermute | solution.py:70
  33.2 1.1 %copy-start.3 = (f32[1,3,256,256]{3,2,1,0:T(8,128)S(1)}, f32[1,3,256,256]{3,2,1,0:T(8,128)}, u32[]{:S(2)}) copy-start(f32[1,3,256,256]{3,2,1,0:T(8,128)} %get-tuple-element.13) | copy-start | bytes 2359300
  35.6 7.2 %collective-permute-start.3 = (f32[1,2,256,64]{2,3,1,0:T(8,128)S(1)}, f32[1,2,256,64]{2,3,1,0:T(8,128)S(1)}, u32[]{:S(2)}, u32[]{:S(2)}) collective-permute-start(f32[1,2,256,64]{2,3,1,0:T(8,128)S(1)} %fusion.73), channel_id=1, source_target_pairs={{0,4},{4,0},{1,5},{5,1},{2,6},{6,2},{3,7},{7,3},{8,12},{12,8},{9,1... | collective-permute-start | bytes 393224 | tf_op jit(solution)/shard_map/ppermute | solution.py:210
  42.6 1.3 %copy-start = (f32[1,3,256,320]{3,2,1,0:T(8,128)S(1)}, f32[1,3,256,320]{3,2,1,0:T(8,128)}, u32[]{:S(2)}) copy-start(f32[1,3,256,320]{3,2,1,0:T(8,128)} %get-tuple-element.15) | copy-start | bytes 2949124
  42.6 8.4 %collective-permute-start.7 = (f32[2,128,256]{2,1,0:T(8,128)S(1)}, f32[2,128,256]{2,1,0:T(8,128)S(1)}, u32[]{:S(2)}, u32[]{:S(2)}) collective-permute-start(f32[2,128,256]{2,1,0:T(8,128)S(1)} %constant_dynamic-update-slice_fusion), channel_id=1, source_target_pairs={{0,1},{1,0},{2,3},{3,2},{4,5},{5,4},{6,7},{7,6},{8,9},{9,8},{10,11... | collective-permute-start | bytes 786440 | tf_op jit(solution)/shard_map/ppermute | solution.py:70
  51.0 0.8 %copy-start.5 = (f32[1,1,2,256,256]{4,3,2,1,0:T(8,128)}, f32[1,1,2,256,256]{4,3,2,1,0:T(8,128)S(1)}, u32[]{:S(2)}) copy-start(f32[1,1,2,256,256]{4,3,2,1,0:T(8,128)S(1)} %bitcast_dynamic-update-slice_fusion) | copy-start | bytes 1572868

commit v17 on v15

--- a/solution.py
+++ b/solution.py
@@ -163,14 +163,24 @@
     )(tilt_index, positions.reshape(-1), is_first.astype(jnp.int32).reshape(1), grid)
 
 
-def apply_operator(wave, padded_cols, row_table, col_table):
+def apply_rows(wave, row_table):
     wave_real = wave[:, 0]
     wave_imag = wave[:, 1]
     first = contract("ajl,alk->ajk", row_table[:, 0], wave_real)
     second = contract("ajl,alk->ajk", row_table[:, 1], wave_imag - wave_real)
     third = contract("ajl,alk->ajk", row_table[:, 2], wave_real + wave_imag)
-    half = jnp.stack([first - third, first + second], axis=1)
-    half = padded_cols(half)
+    return jnp.stack([first - third, first + second], axis=1)
+
+
+def apply_operator(wave, padded_cols, row_table, col_table):
+    if lax.axis_size("tile") == 2:
+        width = wave.shape[-1]
+        edges = jnp.concatenate([wave[..., :MARGIN], wave[..., width - MARGIN :]], axis=-1)
+        edges = lax.ppermute(apply_rows(edges, row_table), "tile", [(0, 1), (1, 0)])
+        half = apply_rows(wave, row_table)
+        half = jnp.concatenate([edges[..., MARGIN:], half, edges[..., :MARGIN]], axis=-1)
+    else:
+        half = padded_cols(apply_rows(wave, row_table))
     half_real = half[:, 0]
     half_imag = half[:, 1]
     first = contract("ajk,aik->aji", half_real + half_imag, col_table[:, 0])

time: 52.1 us -> 55.6 us (1.067)
  matrix products: 5.51 us -> 7.44 us
  waiting for transfers between devices: 15.6 us -> 16.6 us
  local copies, waits for them, and re-layouts: 2.36 us -> 3.35 us
  starting transfers between devices: 17.6 us -> 16.8 us
    ppermute x2, waiting for transfers between devices: 11.1 us -> 6.79 us  [halving_allreduce(): other = lax.ppermute(held, axis, pairs)]
    ppermute x2, waiting for transfers between devices: 1.99 us -> 4.68 us  [apply_operator(): edges = lax.ppermute(apply_rows(edges, row_table), 'tile', [(0, 1), (1, 0)])]
    ppermute x2, waiting for transfers between devices: 2.59 us -> 5.15 us  [halving_allreduce(): held = keep + lax.ppermute(give, axis, pairs)]
    dot_general x12 -> x18, matrix products: 5.51 us -> 7.44 us  [contract(): return jnp.einsum(form, left, right, precision=wave_precision)]
    cos x1, local copies, waits for them, and re-layouts: 0.95 us -> 1.86 us  [body(): cosine = jnp.cos(phase[0, 0])]
    ppermute x1, starting transfers between devices: 4.81 us -> 3.91 us  [body(): received_fwd = lax.ppermute(forward_in[0], 'depth', up)]
    unnamed x18 -> x16, local copies, waits for them, and re-layouts: 1.4 us -> 1.34 us
  transfers between devices with their start and end apart: 8 -> 8, of which waited for: 4 -> 5; matrix products, arithmetic and copies ran while one was open for 10% -> 14% of each run, Pallas kernels for 13% -> 12%
where the time goes in v17:
time: 55.6 us; the launch traced here: 55.2 us
  starting transfers between devices  16.8 us (30%)
  waiting for transfers between devices  16.6 us (30%)
  matrix products  7.44 us (13%)
  Pallas kernels  6.59 us (12%)
  local copies, waits for them, and re-layouts  3.35 us (6%)
  other arithmetic  2.75 us (5%)
  between operations  1.65 us (3%)
    dot_general x18, matrix products, contract(): return jnp.einsum(form, left, right, precision=wave_precision)  7.44 us
    ppermute x2, waiting for transfers between devices, halving_allreduce(): other = lax.ppermute(held, axis, pairs)  6.79 us
    pallas_call x2, Pallas kernels, build_tables(): pl.pallas_call(functools.partial(table_kernel, sign), out_shape=(rows, co...  6.59 us
    ppermute x2, starting transfers between devices, halving_allreduce(): held = keep + lax.ppermute(give, axis, pairs)  5.73 us
    ppermute x2, waiting for transfers between devices, halving_allreduce(): held = keep + lax.ppermute(give, axis, pairs)  5.15 us
    ppermute x2, starting transfers between devices, apply_operator(): edges = lax.ppermute(apply_rows(edges, row_table), 'tile', [(0, 1), (1, 0)])  5.14 us
    ppermute x2, waiting for transfers between devices, apply_operator(): edges = lax.ppermute(apply_rows(edges, row_table), 'tile', [(0, 1), (1, 0)])  4.68 us
    ppermute x1, starting transfers between devices, body(): received_fwd = lax.ppermute(forward_in[0], 'depth', up)  3.91 us
  transfers between devices with their start and end apart: 8, of which 5 were waited for; matrix products, arithmetic and copies ran while one was open for 14% of the time, Pallas kernels for 12%

profile of v17, /device:TPU:0, one launch (start us, length us, event | category | flops | bytes accessed | tf_op | source)
XLA Modules:
  0.0 55.2 jit_solution(6562446917828346134)
XLA Ops:
  0.6 1.4 %collective-permute-start = (f32[1,2,256,256]{3,2,1,0:T(8,128)}, f32[1,2,256,256]{3,2,1,0:T(8,128)S(1)}, u32[]{:S(2)}, u32[]{:S(2)}) collective-permute-start(f32[1,2,256,256]{3,2,1,0:T(8,128)} %bitcast.197), channel_id=1, source_target_pairs={{8,0},{16,8},{24,16},{9,1},{17,9},{25,17},{10,2},{18,10},{26,18},{... | collective-permute-start | bytes 1572872 | tf_op jit(solution)/shard_map/ppermute | solution.py:205
  2.1 1.9 %fusion.113 = (f32[1,1,256,256]{3,2,1,0:T(8,128)S(1)}, f32[1,1,256,256]{3,2,1,0:T(8,128)S(1)}) fusion(f32[1,1,256,256]{3,2,1,0:T(8,128)} %param.11), kind=kLoop, calls=%fused_computation.158 | loop fusion | bytes 786432 | tf_op jit(solution)/shard_map/cos | solution.py:201
  4.6 3.3 %shard_map.121 = (f32[1,3,256,256]{3,2,1,0:T(8,128)}, f32[1,3,256,320]{3,2,1,0:T(8,128)}) custom-call(s32[1]{0:T(128)S(6)} %copy.13.tilt_ref, s32[2]{0:T(128)} %bitcast.195, s32[1]{0:T(128)} %bitcast.1.first_ref, f32[320,640]{1,0:T(8,128)} %constant.16.clone.grid_ref), custom_call_target="tpu_custom_call" | custom-call | tf_op jit(solution)/shard_map/pallas_call | solution.py:154
  8.4 0.9 %copy-done.1 = f32[1,3,256,256]{3,2,1,0:T(8,128)S(1)} copy-done((f32[1,3,256,256]{3,2,1,0:T(8,128)S(1)}, f32[1,3,256,256]{3,2,1,0:T(8,128)}, u32[]{:S(2)}) %copy-start.1) | copy-done | bytes 786456
  10.0 0.4 fusion.8
  10.4 0.4 fusion.63
  10.8 3.0 %collective-permute-start.1 = (f32[1,2,256,64]{2,3,1,0:T(8,128)S(1)}, f32[1,2,256,64]{2,3,1,0:T(8,128)S(1)}, u32[]{:S(2)}, u32[]{:S(2)}) collective-permute-start(f32[1,2,256,64]{2,3,1,0:T(8,128)S(1)} %pad_maximum_fusion.4), channel_id=1, source_target_pairs={{0,4},{4,0},{1,5},{5,1},{2,6},{6,2},{3,7},{7,3},{8,12},{12,8},{9,1... | collective-permute-start | bytes 393224 | tf_op jit(solution)/shard_map/ppermute | solution.py:179
  13.8 0.4 fusion.5
  14.2 0.4 fusion.4
  14.6 2.1 %collective-permute-done.1 = f32[1,2,256,64]{2,3,1,0:T(8,128)S(1)} collective-permute-done((f32[1,2,256,64]{2,3,1,0:T(8,128)S(1)}, f32[1,2,256,64]{2,3,1,0:T(8,128)S(1)}, u32[]{:S(2)}, u32[]{:S(2)}) %collective-permute-start.1) | collective-permute-done | bytes 131104 | tf_op jit(solution)/shard_map/ppermute | solution.py:179
  16.8 0.5 fusion.16
  17.3 0.5 convolution_subtract_fusion.2
  17.9 0.6 %fusion.47 = (f32[1,1,256,256]{3,2,1,0:T(8,128)S(1)}, f32[1,1,256,256]{3,2,1,0:T(8,128)S(1)}, f32[1,256,256]{2,1,0:T(8,128)S(1)}, f32[1,256,256]{2,1,0:T(8,128)S(1)}) fusion(f32[1,1,256,256]{3,2,1,0:T(8,128)S(1)} %get-tuple-element.30, f32[256,256]{1,0:T(8,128)S(1)} %convolution_subtract_fusion.2, f32[1,1,256,256]{3,2,1,0:T(8,128)S(1)} %get-tuple-element.29, ...), kind=kOutput, calls=%fused_computation.80 | convolution fusion | flops 126681088 | bytes 3342336 | tf_op jit(solution)/shard_map/ajk,aik->aji/dot_general | solution.py:39
  18.6 2.2 %collective-permute-start.4 = (f32[2,128,256]{2,1,0:T(8,128)S(1)}, f32[2,128,256]{2,1,0:T(8,128)S(1)}, u32[]{:S(2)}, u32[]{:S(2)}) collective-permute-start(f32[2,128,256]{2,1,0:T(8,128)S(1)} %slice_select_fusion), channel_id=1, source_target_pairs={{0,1},{1,0},{2,3},{3,2},{4,5},{5,4},{6,7},{7,6},{8,9},{9,8},{10,11... | collective-permute-start | bytes 786440 | tf_op jit(solution)/shard_map/ppermute | solution.py:66
  20.8 3.9 %collective-permute-start.2 = (f32[1,2,256,256]{3,2,1,0:T(8,128)S(1)}, f32[1,2,256,256]{3,2,1,0:T(8,128)S(1)}, u32[]{:S(2)}, u32[]{:S(2)}) collective-permute-start(f32[1,2,256,256]{3,2,1,0:T(8,128)S(1)} %bitcast.198), channel_id=1, source_target_pairs={{0,8},{8,16},{16,24},{1,9},{9,17},{17,25},{2,10},{10,18},{18,26},{... | collective-permute-start | bytes 1572872 | tf_op jit(solution)/shard_map/ppermute | solution.py:230
  24.7 1.6 %collective-permute-done.4 = f32[2,128,256]{2,1,0:T(8,128)S(1)} collective-permute-done((f32[2,128,256]{2,1,0:T(8,128)S(1)}, f32[2,128,256]{2,1,0:T(8,128)S(1)}, u32[]{:S(2)}, u32[]{:S(2)}) %collective-permute-start.4) | collective-permute-done | bytes 262176 | tf_op jit(solution)/shard_map/ppermute | solution.py:66
  26.3 3.6 %collective-permute-start.5 = (f32[2,64,256]{2,1,0:T(8,128)S(1)}, f32[2,64,256]{2,1,0:T(8,128)S(1)}, u32[]{:S(2)}, u32[]{:S(2)}) collective-permute-start(f32[2,64,256]{2,1,0:T(8,128)S(1)} %slice_select_fusion.1), channel_id=1, source_target_pairs={{0,2},{1,3},{2,0},{3,1},{4,6},{5,7},{6,4},{7,5},{8,10},{9,11},{10,... | collective-permute-start | bytes 393224 | tf_op jit(solution)/shard_map/ppermute | solution.py:66
  29.9 3.3 %shard_map.122 = (f32[1,3,256,256]{3,2,1,0:T(8,128)}, f32[1,3,256,320]{3,2,1,0:T(8,128)}) custom-call(s32[1]{0:T(128)S(6)} %copy.13.tilt_ref, s32[2]{0:T(128)} %bitcast.196, s32[1]{0:T(128)} %bitcast.1.first_ref, f32[320,640]{1,0:T(8,128)} %constant.16.clone.grid_ref), custom_call_target="tpu_custom_call" | custom-call | tf_op jit(solution)/shard_map/pallas_call | solution.py:154
  33.2 3.6 %collective-permute-done.5 = f32[2,64,256]{2,1,0:T(8,128)S(1)} collective-permute-done((f32[2,64,256]{2,1,0:T(8,128)S(1)}, f32[2,64,256]{2,1,0:T(8,128)S(1)}, u32[]{:S(2)}, u32[]{:S(2)}) %collective-permute-start.5) | collective-permute-done | bytes 131104 | tf_op jit(solution)/shard_map/ppermute | solution.py:66
  36.8 0.6 %collective-permute-start.6 = (f32[2,64,256]{2,1,0:T(8,128)S(1)}, f32[2,64,256]{2,1,0:T(8,128)S(1)}, u32[]{:S(2)}, u32[]{:S(2)}) collective-permute-start(f32[2,64,256]{2,1,0:T(8,128)S(1)} %select_add_fusion.1), channel_id=1, source_target_pairs={{0,2},{1,3},{2,0},{3,1},{4,6},{5,7},{6,4},{7,5},{8,10},{9,11},{10,... | collective-permute-start | bytes 393224 | tf_op jit(solution)/shard_map/ppermute | solution.py:70
  37.5 0.4 copy-done
  37.9 0.4 fusion.52
  39.3 6.8 %collective-permute-done.6 = f32[2,64,256]{2,1,0:T(8,128)S(1)} collective-permute-done((f32[2,64,256]{2,1,0:T(8,128)S(1)}, f32[2,64,256]{2,1,0:T(8,128)S(1)}, u32[]{:S(2)}, u32[]{:S(2)}) %collective-permute-start.6) | collective-permute-done | bytes 131104 | tf_op jit(solution)/shard_map/ppermute | solution.py:70
  46.2 0.4 fusion.3
  46.6 2.1 %collective-permute-start.3 = (f32[1,2,256,64]{2,3,1,0:T(8,128)S(1)}, f32[1,2,256,64]{2,3,1,0:T(8,128)S(1)}, u32[]{:S(2)}, u32[]{:S(2)}) collective-permute-start(f32[1,2,256,64]{2,3,1,0:T(8,128)S(1)} %pad_maximum_fusion.5), channel_id=1, source_target_pairs={{0,4},{4,0},{1,5},{5,1},{2,6},{6,2},{3,7},{7,3},{8,12},{12,8},{9,1... | collective-permute-start | bytes 393224 | tf_op jit(solution)/shard_map/ppermute | solution.py:179
  48.8 0.4 fusion.2
  49.2 2.6 %collective-permute-done.3 = f32[1,2,256,64]{2,3,1,0:T(8,128)S(1)} collective-permute-done((f32[1,2,256,64]{2,3,1,0:T(8,128)S(1)}, f32[1,2,256,64]{2,3,1,0:T(8,128)S(1)}, u32[]{:S(2)}, u32[]{:S(2)}) %collective-permute-start.3) | collective-permute-done | bytes 131104 | tf_op jit(solution)/shard_map/ppermute | solution.py:179
  51.8 0.5 fusion.12
  52.3 0.5 fusion.1
  52.8 0.5 fusion
  53.4 1.0 %maximum_bitcast_fusion = (f32[1,1,2,256,256]{4,3,2,1,0:T(8,128)}, f32[1,1,2,256,256]{4,3,2,1,0:T(8,128)}) fusion(f32[1,1,256,256]{3,2,1,0:T(8,128)S(1)} %fusion, f32[1,1,256,256]{3,2,1,0:T(8,128)S(1)} %fusion.1, f32[1,1,256,256]{3,2,1,0:T(8,128)S(1)} %get-tuple-element.18, f32[1,1,256,256]{3,2,1,0:T(8,128)S(1)} %get-tuple-element.17), kind=kLoop, calls=%fused_computation.27 | loop fusion | flops 262144 | bytes 2097152 | tf_op jit(solution)/shard_map/broadcast_in_dim | solution.py:248
  54.4 0.8 %maximum_select_fusion = f32[1,1,2,256,256]{4,3,2,1,0:T(8,128)} fusion(f32[1,1,2,128,256]{4,3,2,1,0:T(8,128)S(1)} %bitcast.194, f32[1,1,2,128,256]{4,3,2,1,0:T(8,128)S(1)} %bitcast.193, pred[]{:T(512)S(6)} %eq.18), kind=kLoop, calls=%fused_computation.29 | loop fusion | flops 393216 | bytes 1048577 | tf_op jit(solution)/shard_map/jit(_where)/select_n | solution.py:71
  (44 shorter events, 2.7 us)
Async XLA Ops:
  0.6 7.3 %copy-start.4 = (bf16[1,2,1,2,256,256]{5,4,3,2,1,0:T(8,128)(2,1)S(1)}, bf16[1,2,1,2,256,256]{5,4,3,2,1,0:T(8,128)(2,1)}, u32[]{:S(2)}) copy-start(bf16[1,2,1,2,256,256]{5,4,3,2,1,0:T(8,128)(2,1)} %param.14) | copy-start | bytes 1572868
  0.6 7.4 %collective-permute-start = (f32[1,2,256,256]{3,2,1,0:T(8,128)}, f32[1,2,256,256]{3,2,1,0:T(8,128)S(1)}, u32[]{:S(2)}, u32[]{:S(2)}) collective-permute-start(f32[1,2,256,256]{3,2,1,0:T(8,128)} %bitcast.197), channel_id=1, source_target_pairs={{8,0},{16,8},{24,16},{9,1},{17,9},{25,17},{10,2},{18,10},{26,18},{... | collective-permute-start | bytes 1572872 | tf_op jit(solution)/shard_map/ppermute | solution.py:205
  4.6 3.4 %copy-start.6 = (f32[1,256,256]{2,1,0:T(8,128)S(1)}, f32[1,256,256]{2,1,0:T(8,128)}, u32[]{:S(2)}) copy-start(f32[1,256,256]{2,1,0:T(8,128)} %param.15) | copy-start | bytes 786436
  8.2 1.1 %copy-start.1 = (f32[1,3,256,256]{3,2,1,0:T(8,128)S(1)}, f32[1,3,256,256]{3,2,1,0:T(8,128)}, u32[]{:S(2)}) copy-start(f32[1,3,256,256]{3,2,1,0:T(8,128)} %get-tuple-element.10) | copy-start | bytes 2359300
  10.8 6.0 %collective-permute-start.1 = (f32[1,2,256,64]{2,3,1,0:T(8,128)S(1)}, f32[1,2,256,64]{2,3,1,0:T(8,128)S(1)}, u32[]{:S(2)}, u32[]{:S(2)}) collective-permute-start(f32[1,2,256,64]{2,3,1,0:T(8,128)S(1)} %pad_maximum_fusion.4), channel_id=1, source_target_pairs={{0,4},{4,0},{1,5},{5,1},{2,6},{6,2},{3,7},{7,3},{8,12},{12,8},{9,1... | collective-permute-start | bytes 393224 | tf_op jit(solution)/shard_map/ppermute | solution.py:179
  14.2 2.6 %copy-start.3 = (f32[1,3,256,320]{3,2,1,0:T(8,128)S(1)}, f32[1,3,256,320]{3,2,1,0:T(8,128)}, u32[]{:S(2)}) copy-start(f32[1,3,256,320]{3,2,1,0:T(8,128)} %get-tuple-element.11) | copy-start | bytes 2949124
  18.5 2.3 %copy-start.7 = (f32[1,1,2,256,256]{4,3,2,1,0:T(8,128)S(1)}, f32[1,1,2,256,256]{4,3,2,1,0:T(8,128)}, u32[]{:S(2)}) copy-start(f32[1,1,2,256,256]{4,3,2,1,0:T(8,128)} %param.12) | copy-start | bytes 1572868
  18.6 7.7 %collective-permute-start.4 = (f32[2,128,256]{2,1,0:T(8,128)S(1)}, f32[2,128,256]{2,1,0:T(8,128)S(1)}, u32[]{:S(2)}, u32[]{:S(2)}) collective-permute-start(f32[2,128,256]{2,1,0:T(8,128)S(1)} %slice_select_fusion), channel_id=1, source_target_pairs={{0,1},{1,0},{2,3},{3,2},{4,5},{5,4},{6,7},{7,6},{8,9},{9,8},{10,11... | collective-permute-start | bytes 786440 | tf_op jit(solution)/shard_map/ppermute | solution.py:66
  20.8 16.6 %copy-start.5 = (bf16[2,256,256]{2,1,0:T(8,128)(2,1)S(1)}, bf16[2,256,256]{2,1,0:T(8,128)(2,1)}, u32[]{:S(2)}) copy-start(bf16[2,256,256]{2,1,0:T(8,128)(2,1)} %param.10) | copy-start | bytes 786436
  20.8 16.6 %collective-permute-start.2 = (f32[1,2,256,256]{3,2,1,0:T(8,128)S(1)}, f32[1,2,256,256]{3,2,1,0:T(8,128)S(1)}, u32[]{:S(2)}, u32[]{:S(2)}) collective-permute-start(f32[1,2,256,256]{3,2,1,0:T(8,128)S(1)} %bitcast.198), channel_id=1, source_target_pairs={{0,8},{8,16},{16,24},{1,9},{9,17},{17,25},{2,10},{10,18},{18,26},{... | collective-permute-start | bytes 1572872 | tf_op jit(solution)/shard_map/ppermute | solution.py:230
  26.3 10.4 %collective-permute-start.5 = (f32[2,64,256]{2,1,0:T(8,128)S(1)}, f32[2,64,256]{2,1,0:T(8,128)S(1)}, u32[]{:S(2)}, u32[]{:S(2)}) collective-permute-start(f32[2,64,256]{2,1,0:T(8,128)S(1)} %slice_select_fusion.1), channel_id=1, source_target_pairs={{0,2},{1,3},{2,0},{3,1},{4,6},{5,7},{6,4},{7,5},{8,10},{9,11},{10,... | collective-permute-start | bytes 393224 | tf_op jit(solution)/shard_map/ppermute | solution.py:66
  36.8 1.1 %copy-start = (f32[1,3,256,256]{3,2,1,0:T(8,128)S(1)}, f32[1,3,256,256]{3,2,1,0:T(8,128)}, u32[]{:S(2)}) copy-start(f32[1,3,256,256]{3,2,1,0:T(8,128)} %get-tuple-element.13) | copy-start | bytes 2359300
  36.8 9.3 %collective-permute-start.6 = (f32[2,64,256]{2,1,0:T(8,128)S(1)}, f32[2,64,256]{2,1,0:T(8,128)S(1)}, u32[]{:S(2)}, u32[]{:S(2)}) collective-permute-start(f32[2,64,256]{2,1,0:T(8,128)S(1)} %select_add_fusion.1), channel_id=1, source_target_pairs={{0,2},{1,3},{2,0},{3,1},{4,6},{5,7},{6,4},{7,5},{8,10},{9,11},{10,... | collective-permute-start | bytes 393224 | tf_op jit(solution)/shard_map/ppermute | solution.py:70
  46.1 8.3 %collective-permute-start.7 = (f32[2,128,256]{2,1,0:T(8,128)S(1)}, f32[2,128,256]{2,1,0:T(8,128)S(1)}, u32[]{:S(2)}, u32[]{:S(2)}) collective-permute-start(f32[2,128,256]{2,1,0:T(8,128)S(1)} %maximum_select_fusion.1), channel_id=1, source_target_pairs={{0,1},{1,0},{2,3},{3,2},{4,5},{5,4},{6,7},{7,6},{8,9},{9,8},{10,11... | collective-permute-start | bytes 786440 | tf_op jit(solution)/shard_map/ppermute | solution.py:70
  46.6 5.2 %copy-start.2 = (f32[1,3,256,320]{3,2,1,0:T(8,128)S(1)}, f32[1,3,256,320]{3,2,1,0:T(8,128)}, u32[]{:S(2)}) copy-start(f32[1,3,256,320]{3,2,1,0:T(8,128)} %get-tuple-element.15) | copy-start | bytes 2949124
  46.6 5.1 %collective-permute-start.3 = (f32[1,2,256,64]{2,3,1,0:T(8,128)S(1)}, f32[1,2,256,64]{2,3,1,0:T(8,128)S(1)}, u32[]{:S(2)}, u32[]{:S(2)}) collective-permute-start(f32[1,2,256,64]{2,3,1,0:T(8,128)S(1)} %pad_maximum_fusion.5), channel_id=1, source_target_pairs={{0,4},{4,0},{1,5},{5,1},{2,6},{6,2},{3,7},{7,3},{8,12},{12,8},{9,1... | collective-permute-start | bytes 393224 | tf_op jit(solution)/shard_map/ppermute | solution.py:179

commit v18 on v15

--- a/solution.py
+++ b/solution.py
@@ -192,6 +192,7 @@
     sine_part = jnp.sin(phase[0, 0])
     down = [(i + 1, i) for i in range(sections - 1)]
     up = [(i, i + 1) for i in range(sections - 1)]
+    rows_back, cols_back, adjoint_in = lax.optimization_barrier((rows_back, cols_back, adjoint_in))
     received_back = lax.ppermute(adjoint_in[0], "depth", down)
     exit_wave = held_waves[0, 1].astype(jnp.float32)
     intensity = exit_wave[:, 0] * exit_wave[:, 0] + exit_wave[:, 1] * exit_wave[:, 1]

time: 52.1 us -> 55.9 us (1.073)
  waiting for transfers between devices: 15.6 us -> 19.1 us
  starting transfers between devices: 17.6 us -> 18.3 us
    ppermute x1, starting transfers between devices: 4.81 us -> 7.52 us  [body(): received_fwd = lax.ppermute(forward_in[0], 'depth', up)]
    ppermute x1, waiting for transfers between devices: 0.01 us -> 2.54 us  [body(): received_back = lax.ppermute(adjoint_in[0], 'depth', down)]
    ppermute x2, waiting for transfers between devices: 2.59 us -> 3.55 us  [halving_allreduce(): held = keep + lax.ppermute(give, axis, pairs)]
    ppermute x2, starting transfers between devices: 5.21 us -> 4.56 us  [side_halo(): edges = lax.ppermute(edges, 'tile', [(0, 1), (1, 0)])]
    ppermute x2, starting transfers between devices: 5.45 us -> 4.83 us  [halving_allreduce(): held = keep + lax.ppermute(give, axis, pairs)]
  transfers between devices with their start and end apart: 8 -> 8, of which waited for: 4 -> 5; matrix products, arithmetic and copies ran while one was open for 10% -> 9% of each run, Pallas kernels for 13% -> 6%
where the time goes in v18:
time: 55.9 us; the launch traced here: 55.6 us
  waiting for transfers between devices  19.1 us (34%)
  starting transfers between devices  18.3 us (33%)
  Pallas kernels  6.59 us (12%)
  matrix products  5.5 us (10%)
  other arithmetic  2.49 us (4%)
  local copies, waits for them, and re-layouts  1.89 us (3%)
  between operations  1.74 us (3%)
    ppermute x2, waiting for transfers between devices, halving_allreduce(): other = lax.ppermute(held, axis, pairs)  11 us
    ppermute x1, starting transfers between devices, body(): received_fwd = lax.ppermute(forward_in[0], 'depth', up)  7.52 us
    pallas_call x2, Pallas kernels, build_tables(): pl.pallas_call(functools.partial(table_kernel, sign), out_shape=(rows, co...  6.59 us
    dot_general x12, matrix products, contract(): return jnp.einsum(form, left, right, precision=wave_precision)  5.5 us
    ppermute x2, starting transfers between devices, halving_allreduce(): held = keep + lax.ppermute(give, axis, pairs)  4.83 us
    ppermute x2, starting transfers between devices, side_halo(): edges = lax.ppermute(edges, 'tile', [(0, 1), (1, 0)])  4.56 us
    ppermute x2, waiting for transfers between devices, halving_allreduce(): held = keep + lax.ppermute(give, axis, pairs)  3.55 us
    ppermute x1, waiting for transfers between devices, body(): received_back = lax.ppermute(adjoint_in[0], 'depth', down)  2.54 us
  transfers between devices with their start and end apart: 8, of which 5 were waited for; matrix products, arithmetic and copies ran while one was open for 9% of the time, Pallas kernels for 6%

profile of v18, /device:TPU:0, one launch (start us, length us, event | category | flops | bytes accessed | tf_op | source)
XLA Modules:
  0.0 55.6 jit_solution(8472918376826915802)
XLA Ops:
  1.4 3.3 %shard_map.121 = (f32[1,3,256,256]{3,2,1,0:T(8,128)}, f32[1,3,256,320]{3,2,1,0:T(8,128)}) custom-call(s32[1]{0:T(128)S(6)} %copy.13.tilt_ref, s32[2]{0:T(128)} %bitcast.157, s32[1]{0:T(128)} %bitcast.1.first_ref, f32[320,640]{1,0:T(8,128)} %constant.16.clone.grid_ref), custom_call_target="tpu_custom_call" | custom-call | tf_op jit(solution)/shard_map/pallas_call | solution.py:154
  4.7 1.3 %collective-permute-start = (f32[1,2,256,256]{3,2,1,0:T(8,128)}, f32[1,2,256,256]{3,2,1,0:T(8,128)S(1)}, u32[]{:S(2)}, u32[]{:S(2)}) collective-permute-start(f32[1,2,256,256]{3,2,1,0:T(8,128)} %bitcast.159), channel_id=1, source_target_pairs={{8,0},{16,8},{24,16},{9,1},{17,9},{25,17},{10,2},{18,10},{26,18},{... | collective-permute-start | bytes 1572872 | tf_op jit(solution)/shard_map/ppermute | solution.py:196
  6.1 2.5 %collective-permute-done = f32[1,2,256,256]{3,2,1,0:T(8,128)S(1)} collective-permute-done((f32[1,2,256,256]{3,2,1,0:T(8,128)}, f32[1,2,256,256]{3,2,1,0:T(8,128)S(1)}, u32[]{:S(2)}, u32[]{:S(2)}) %collective-permute-start) | collective-permute-done | bytes 524320 | tf_op jit(solution)/shard_map/ppermute | solution.py:196
  8.8 0.4 fusion.55
  9.2 0.4 fusion.5
  9.6 0.4 fusion.4
  10.0 3.0 %collective-permute-start.1 = (f32[1,2,256,64]{2,3,1,0:T(8,128)S(1)}, f32[1,2,256,64]{2,3,1,0:T(8,128)S(1)}, u32[]{:S(2)}, u32[]{:S(2)}) collective-permute-start(f32[1,2,256,64]{2,3,1,0:T(8,128)S(1)} %fusion.77), channel_id=1, source_target_pairs={{0,4},{4,0},{1,5},{5,1},{2,6},{6,2},{3,7},{7,3},{8,12},{12,8},{9,1... | collective-permute-start | bytes 393224 | tf_op jit(solution)/shard_map/ppermute | solution.py:208
  13.0 0.9 %fusion.78 = (f32[1,1,256,256]{3,2,1,0:T(8,128)S(1)}, f32[1,1,256,256]{3,2,1,0:T(8,128)S(1)}) fusion(f32[1,1,256,256]{3,2,1,0:T(8,128)S(1)} %copy-done.5), kind=kLoop, calls=%fused_computation.118 | loop fusion | bytes 786432 | tf_op jit(solution)/shard_map/cos | solution.py:191
  14.0 2.0 %collective-permute-done.1 = f32[1,2,256,64]{2,3,1,0:T(8,128)S(1)} collective-permute-done((f32[1,2,256,64]{2,3,1,0:T(8,128)S(1)}, f32[1,2,256,64]{2,3,1,0:T(8,128)S(1)}, u32[]{:S(2)}, u32[]{:S(2)}) %collective-permute-start.1) | collective-permute-done | bytes 131104 | tf_op jit(solution)/shard_map/ppermute | solution.py:208
  16.0 0.5 fusion.12
  16.5 0.5 convolution_subtract_fusion.2
  17.1 0.6 %fusion.41 = (f32[1,1,256,256]{3,2,1,0:T(8,128)S(1)}, f32[1,1,256,256]{3,2,1,0:T(8,128)S(1)}, f32[1,256,256]{2,1,0:T(8,128)S(1)}, f32[1,256,256]{2,1,0:T(8,128)S(1)}) fusion(f32[1,1,256,256]{3,2,1,0:T(8,128)S(1)} %get-tuple-element.34, f32[256,256]{1,0:T(8,128)S(1)} %convolution_subtract_fusion.2, f32[1,1,256,256]{3,2,1,0:T(8,128)S(1)} %get-tuple-element.33, ...), kind=kOutput, calls=%fused_computation.64 | convolution fusion | flops 126681088 | bytes 3342336 | tf_op jit(solution)/shard_map/ajk,aik->aji/dot_general | solution.py:39
  17.8 2.2 %collective-permute-start.4 = (f32[2,128,256]{2,1,0:T(8,128)S(1)}, f32[2,128,256]{2,1,0:T(8,128)S(1)}, u32[]{:S(2)}, u32[]{:S(2)}) collective-permute-start(f32[2,128,256]{2,1,0:T(8,128)S(1)} %slice_select_fusion), channel_id=1, source_target_pairs={{0,1},{1,0},{2,3},{3,2},{4,5},{5,4},{6,7},{7,6},{8,9},{9,8},{10,11... | collective-permute-start | bytes 786440 | tf_op jit(solution)/shard_map/ppermute | solution.py:66
  20.0 7.5 %collective-permute-start.2 = (f32[1,2,256,256]{3,2,1,0:T(8,128)S(1)}, f32[1,2,256,256]{3,2,1,0:T(8,128)S(1)}, u32[]{:S(2)}, u32[]{:S(2)}) collective-permute-start(f32[1,2,256,256]{3,2,1,0:T(8,128)S(1)} %bitcast.160), channel_id=1, source_target_pairs={{0,8},{8,16},{16,24},{1,9},{9,17},{17,25},{2,10},{10,18},{18,26},{... | collective-permute-start | bytes 1572872 | tf_op jit(solution)/shard_map/ppermute | solution.py:221
  27.6 2.7 %collective-permute-start.5 = (f32[2,64,256]{2,1,0:T(8,128)S(1)}, f32[2,64,256]{2,1,0:T(8,128)S(1)}, u32[]{:S(2)}, u32[]{:S(2)}) collective-permute-start(f32[2,64,256]{2,1,0:T(8,128)S(1)} %slice_select_fusion.1), channel_id=1, source_target_pairs={{0,2},{1,3},{2,0},{3,1},{4,6},{5,7},{6,4},{7,5},{8,10},{9,11},{10,... | collective-permute-start | bytes 393224 | tf_op jit(solution)/shard_map/ppermute | solution.py:66
  30.2 3.3 %shard_map.122 = (f32[1,3,256,256]{3,2,1,0:T(8,128)}, f32[1,3,256,320]{3,2,1,0:T(8,128)}) custom-call(s32[1]{0:T(128)S(6)} %copy.13.tilt_ref, s32[2]{0:T(128)} %bitcast.158, s32[1]{0:T(128)} %bitcast.1.first_ref, f32[320,640]{1,0:T(8,128)} %constant.16.clone.grid_ref), custom_call_target="tpu_custom_call" | custom-call | tf_op jit(solution)/shard_map/pallas_call | solution.py:154
  33.5 3.5 %collective-permute-done.5 = f32[2,64,256]{2,1,0:T(8,128)S(1)} collective-permute-done((f32[2,64,256]{2,1,0:T(8,128)S(1)}, f32[2,64,256]{2,1,0:T(8,128)S(1)}, u32[]{:S(2)}, u32[]{:S(2)}) %collective-permute-start.5) | collective-permute-done | bytes 131104 | tf_op jit(solution)/shard_map/ppermute | solution.py:66
  37.1 0.1 collective-permute-start.6
  37.2 0.1 multiply_add_fusion
  37.3 0.9 %copy-done.3 = f32[1,3,256,256]{3,2,1,0:T(8,128)S(1)} copy-done((f32[1,3,256,256]{3,2,1,0:T(8,128)S(1)}, f32[1,3,256,256]{3,2,1,0:T(8,128)}, u32[]{:S(2)}) %copy-start.3) | copy-done | bytes 786456
  38.2 0.4 fusion.48
  38.6 0.4 fusion.3
  39.0 0.4 fusion.2
  39.4 1.6 %collective-permute-start.3 = (f32[1,2,256,64]{2,3,1,0:T(8,128)S(1)}, f32[1,2,256,64]{2,3,1,0:T(8,128)S(1)}, u32[]{:S(2)}, u32[]{:S(2)}) collective-permute-start(f32[1,2,256,64]{2,3,1,0:T(8,128)S(1)} %fusion.73), channel_id=1, source_target_pairs={{0,4},{4,0},{1,5},{5,1},{2,6},{6,2},{3,7},{7,3},{8,12},{12,8},{9,1... | collective-permute-start | bytes 393224 | tf_op jit(solution)/shard_map/ppermute | solution.py:208
  41.0 5.8 %collective-permute-done.6 = f32[2,64,256]{2,1,0:T(8,128)S(1)} collective-permute-done((f32[2,64,256]{2,1,0:T(8,128)S(1)}, f32[2,64,256]{2,1,0:T(8,128)S(1)}, u32[]{:S(2)}, u32[]{:S(2)}) %collective-permute-start.6) | collective-permute-done | bytes 131104 | tf_op jit(solution)/shard_map/ppermute | solution.py:70
  46.8 0.1 collective-permute-start.7
  47.0 0.5 fusion.8
  47.5 0.5 fusion.1
  48.0 0.5 fusion
  48.5 1.0 %maximum_bitcast_fusion = (f32[1,1,2,256,256]{4,3,2,1,0:T(8,128)}, f32[1,1,2,256,256]{4,3,2,1,0:T(8,128)}) fusion(f32[1,1,256,256]{3,2,1,0:T(8,128)S(1)} %fusion, f32[1,1,256,256]{3,2,1,0:T(8,128)S(1)} %fusion.1, f32[1,1,256,256]{3,2,1,0:T(8,128)S(1)} %get-tuple-element.24, f32[1,1,256,256]{3,2,1,0:T(8,128)S(1)} %get-tuple-element.23), kind=kLoop, calls=%fused_computation.17 | loop fusion | flops 262144 | bytes 2097152 | tf_op jit(solution)/shard_map/broadcast_in_dim | solution.py:239
  49.6 5.2 %collective-permute-done.7 = f32[2,128,256]{2,1,0:T(8,128)S(1)} collective-permute-done((f32[2,128,256]{2,1,0:T(8,128)S(1)}, f32[2,128,256]{2,1,0:T(8,128)S(1)}, u32[]{:S(2)}, u32[]{:S(2)}) %collective-permute-start.7) | collective-permute-done | bytes 262176 | tf_op jit(solution)/shard_map/ppermute | solution.py:70
  54.8 0.8 %maximum_select_fusion = f32[1,1,2,256,256]{4,3,2,1,0:T(8,128)} fusion(f32[1,1,2,128,256]{4,3,2,1,0:T(8,128)S(1)} %bitcast.156, f32[1,1,2,128,256]{4,3,2,1,0:T(8,128)S(1)} %bitcast.155, pred[]{:T(512)S(6)} %eq.18), kind=kLoop, calls=%fused_computation.19 | loop fusion | flops 393216 | bytes 1048577 | tf_op jit(solution)/shard_map/jit(_where)/select_n | solution.py:71
  (36 shorter events, 0.6 us)
Async XLA Ops:
  0.6 5.3 %copy-start.2 = (bf16[1,2,1,2,256,256]{5,4,3,2,1,0:T(8,128)(2,1)S(1)}, bf16[1,2,1,2,256,256]{5,4,3,2,1,0:T(8,128)(2,1)}, u32[]{:S(2)}) copy-start(bf16[1,2,1,2,256,256]{5,4,3,2,1,0:T(8,128)(2,1)} %param.14) | copy-start | bytes 1572868
  1.4 4.7 %copy-start.7 = (f32[1,256,256]{2,1,0:T(8,128)S(1)}, f32[1,256,256]{2,1,0:T(8,128)}, u32[]{:S(2)}) copy-start(f32[1,256,256]{2,1,0:T(8,128)} %param.15) | copy-start | bytes 786436
  4.7 4.0 %collective-permute-start = (f32[1,2,256,256]{3,2,1,0:T(8,128)}, f32[1,2,256,256]{3,2,1,0:T(8,128)S(1)}, u32[]{:S(2)}, u32[]{:S(2)}) collective-permute-start(f32[1,2,256,256]{3,2,1,0:T(8,128)} %bitcast.159), channel_id=1, source_target_pairs={{8,0},{16,8},{24,16},{9,1},{17,9},{25,17},{10,2},{18,10},{26,18},{... | collective-permute-start | bytes 1572872 | tf_op jit(solution)/shard_map/ppermute | solution.py:196
  6.1 2.7 %copy-start.4 = (f32[1,3,256,256]{3,2,1,0:T(8,128)S(1)}, f32[1,3,256,256]{3,2,1,0:T(8,128)}, u32[]{:S(2)}) copy-start(f32[1,3,256,256]{3,2,1,0:T(8,128)} %get-tuple-element.15) | copy-start | bytes 2359300
  9.2 3.8 %copy-start.5 = (f32[1,1,256,256]{3,2,1,0:T(8,128)S(1)}, f32[1,1,256,256]{3,2,1,0:T(8,128)}, u32[]{:S(2)}) copy-start(f32[1,1,256,256]{3,2,1,0:T(8,128)} %param.11) | copy-start | bytes 786436
  10.0 6.0 %copy-start.1 = (f32[1,3,256,320]{3,2,1,0:T(8,128)S(1)}, f32[1,3,256,320]{3,2,1,0:T(8,128)}, u32[]{:S(2)}) copy-start(f32[1,3,256,320]{3,2,1,0:T(8,128)} %get-tuple-element.17) | copy-start | bytes 2949124
  10.0 6.0 %collective-permute-start.1 = (f32[1,2,256,64]{2,3,1,0:T(8,128)S(1)}, f32[1,2,256,64]{2,3,1,0:T(8,128)S(1)}, u32[]{:S(2)}, u32[]{:S(2)}) collective-permute-start(f32[1,2,256,64]{2,3,1,0:T(8,128)S(1)} %fusion.77), channel_id=1, source_target_pairs={{0,4},{4,0},{1,5},{5,1},{2,6},{6,2},{3,7},{7,3},{8,12},{12,8},{9,1... | collective-permute-start | bytes 393224 | tf_op jit(solution)/shard_map/ppermute | solution.py:208
  17.7 2.3 %copy-start.8 = (f32[1,1,2,256,256]{4,3,2,1,0:T(8,128)S(1)}, f32[1,1,2,256,256]{4,3,2,1,0:T(8,128)}, u32[]{:S(2)}) copy-start(f32[1,1,2,256,256]{4,3,2,1,0:T(8,128)} %param.12) | copy-start | bytes 1572868
  17.8 9.7 %collective-permute-start.4 = (f32[2,128,256]{2,1,0:T(8,128)S(1)}, f32[2,128,256]{2,1,0:T(8,128)S(1)}, u32[]{:S(2)}, u32[]{:S(2)}) collective-permute-start(f32[2,128,256]{2,1,0:T(8,128)S(1)} %slice_select_fusion), channel_id=1, source_target_pairs={{0,1},{1,0},{2,3},{3,2},{4,5},{5,4},{6,7},{7,6},{8,9},{9,8},{10,11... | collective-permute-start | bytes 786440 | tf_op jit(solution)/shard_map/ppermute | solution.py:66
  19.9 17.2 %copy-start.6 = (bf16[2,256,256]{2,1,0:T(8,128)(2,1)S(1)}, bf16[2,256,256]{2,1,0:T(8,128)(2,1)}, u32[]{:S(2)}) copy-start(bf16[2,256,256]{2,1,0:T(8,128)(2,1)} %param.10) | copy-start | bytes 786436
  20.0 17.2 %collective-permute-start.2 = (f32[1,2,256,256]{3,2,1,0:T(8,128)S(1)}, f32[1,2,256,256]{3,2,1,0:T(8,128)S(1)}, u32[]{:S(2)}, u32[]{:S(2)}) collective-permute-start(f32[1,2,256,256]{3,2,1,0:T(8,128)S(1)} %bitcast.160), channel_id=1, source_target_pairs={{0,8},{8,16},{16,24},{1,9},{9,17},{17,25},{2,10},{10,18},{18,26},{... | collective-permute-start | bytes 1572872 | tf_op jit(solution)/shard_map/ppermute | solution.py:221
  27.6 9.5 %collective-permute-start.5 = (f32[2,64,256]{2,1,0:T(8,128)S(1)}, f32[2,64,256]{2,1,0:T(8,128)S(1)}, u32[]{:S(2)}, u32[]{:S(2)}) collective-permute-start(f32[2,64,256]{2,1,0:T(8,128)S(1)} %slice_select_fusion.1), channel_id=1, source_target_pairs={{0,2},{1,3},{2,0},{3,1},{4,6},{5,7},{6,4},{7,5},{8,10},{9,11},{10,... | collective-permute-start | bytes 393224 | tf_op jit(solution)/shard_map/ppermute | solution.py:66
  37.1 1.1 %copy-start.3 = (f32[1,3,256,256]{3,2,1,0:T(8,128)S(1)}, f32[1,3,256,256]{3,2,1,0:T(8,128)}, u32[]{:S(2)}) copy-start(f32[1,3,256,256]{3,2,1,0:T(8,128)} %get-tuple-element.19) | copy-start | bytes 2359300
  37.1 9.7 %collective-permute-start.6 = (f32[2,64,256]{2,1,0:T(8,128)S(1)}, f32[2,64,256]{2,1,0:T(8,128)S(1)}, u32[]{:S(2)}, u32[]{:S(2)}) collective-permute-start(f32[2,64,256]{2,1,0:T(8,128)S(1)} %select_add_fusion.1), channel_id=1, source_target_pairs={{0,2},{1,3},{2,0},{3,1},{4,6},{5,7},{6,4},{7,5},{8,10},{9,11},{10,... | collective-permute-start | bytes 393224 | tf_op jit(solution)/shard_map/ppermute | solution.py:70
  39.4 7.5 %copy-start = (f32[1,3,256,320]{3,2,1,0:T(8,128)S(1)}, f32[1,3,256,320]{3,2,1,0:T(8,128)}, u32[]{:S(2)}) copy-start(f32[1,3,256,320]{3,2,1,0:T(8,128)} %get-tuple-element.21) | copy-start | bytes 2949124
  39.4 7.4 %collective-permute-start.3 = (f32[1,2,256,64]{2,3,1,0:T(8,128)S(1)}, f32[1,2,256,64]{2,3,1,0:T(8,128)S(1)}, u32[]{:S(2)}, u32[]{:S(2)}) collective-permute-start(f32[1,2,256,64]{2,3,1,0:T(8,128)S(1)} %fusion.73), channel_id=1, source_target_pairs={{0,4},{4,0},{1,5},{5,1},{2,6},{6,2},{3,7},{7,3},{8,12},{12,8},{9,1... | collective-permute-start | bytes 393224 | tf_op jit(solution)/shard_map/ppermute | solution.py:208
  46.8 8.0 %collective-permute-start.7 = (f32[2,128,256]{2,1,0:T(8,128)S(1)}, f32[2,128,256]{2,1,0:T(8,128)S(1)}, u32[]{:S(2)}, u32[]{:S(2)}) collective-permute-start(f32[2,128,256]{2,1,0:T(8,128)S(1)} %maximum_select_fusion.1), channel_id=1, source_target_pairs={{0,1},{1,0},{2,3},{3,2},{4,5},{5,4},{6,7},{7,6},{8,9},{9,8},{10,11... | collective-permute-start | bytes 786440 | tf_op jit(solution)/shard_map/ppermute | solution.py:70
